TPU v7x, 256 devices: a whole 4x4x8 slice. The times are simulated.
256 devices in a mesh: vgrp: 4 (over y), samp: 64 (over z, x, core).
Axes of the slice: x: 4, y: 4, z: 8, core: 2. Of those that a mesh axis runs over, the one named last changes fastest.
Arguments:
- phenotype: float32 [196608], P(('vgrp', 'samp')), may hold values from -6 to 6
- exposures: float32 [196608, 128], P('samp'), may hold values from -6 to 6
- perms: int32 [16, 196608], P(None, 'samp'), may hold values from 0 to 196607, each once within a row
- genotypes: int32 [196608, 2048], P('samp', 'vgrp'), may hold values from 0 to 2
Outputs:
- statistics: float32 [2048, 16], P(('vgrp', 'samp'))
Inputs may be any that keep to these rules, and one draw needn't show every extreme that they name: Each row of perms holds every sample index once.
All inputs are finite; a program needn't handle non-finite values.
Results may differ from a plain program's by a relative error of at most 0.00075.
Values sent between devices are 32-bit elements; how exact they have to be, the bound alone decides.
No kernel may reach another device: no remote copies, remote signals or barrier semaphores. Data moves between devices by JAX's collectives and lax.ppermute only.
A program may use at most 64 MiB of HBM per device.

v0:
```python
import jax
import jax.numpy as jnp
from jax import lax
from jax.sharding import PartitionSpec as P


def chol_solve(factor, rhs):
    middle = lax.linalg.triangular_solve(factor, rhs, left_side=True, lower=True)
    return lax.linalg.triangular_solve(factor, middle, left_side=True, lower=True, transpose_a=True)


def permute_rows(pheno_full, perms):
    samples = pheno_full.shape[0]
    table = pheno_full.reshape(samples // 128, 128)
    lanes = lax.broadcasted_iota(jnp.int32, (1, 128), 1)

    def one_perm(index_row):
        picked_rows = table[index_row // 128]
        wanted = (index_row % 128)[:, None] == lanes
        return jnp.sum(jnp.where(wanted, picked_rows, jnp.float32(0.0)), axis=1)

    return lax.map(one_perm, perms)


def per_device(phenotype, exposures, perms, genotypes):
    hi = lax.Precision.HIGHEST
    pheno_full = lax.all_gather(phenotype, ("vgrp", "samp"), axis=0, tiled=True)
    samples = pheno_full.shape[0]
    local_rows = exposures.shape[0]
    width = exposures.shape[1]
    quarter = local_rows // lax.axis_size("vgrp")
    offset_rows = lax.axis_index("vgrp") * quarter
    perm_rows = permute_rows(pheno_full, perms)
    expo_part = lax.dynamic_slice_in_dim(exposures, offset_rows, quarter, 0)
    pheno_part = lax.dynamic_slice_in_dim(perm_rows, offset_rows, quarter, 1)
    gram_part = jnp.dot(expo_part.T, expo_part, precision=hi)
    cross_part = jnp.dot(expo_part.T, pheno_part.T, precision=hi)
    gram, cross = lax.psum((gram_part, cross_part), ("vgrp", "samp"))
    system = gram + 0.5 * samples * jnp.eye(width, dtype=jnp.float32)
    factor = jnp.linalg.cholesky(system)
    coefficients = chol_solve(factor, cross)
    permuted = jnp.transpose(perm_rows)
    residuals = permuted - jnp.dot(exposures, coefficients, precision=hi)
    nperm = residuals.shape[1]
    weighted = (
        (exposures[:, :, None] * residuals[:, None, :])
        .reshape(local_rows, width * nperm)
        .astype(jnp.bfloat16)
    )
    dosages = genotypes.astype(jnp.bfloat16)
    own_rows = genotypes.shape[1] // lax.axis_size("samp")
    summed = lax.psum(jnp.dot(dosages.T, weighted, preferred_element_type=jnp.float32), "samp")
    own_scores = lax.dynamic_slice_in_dim(summed, lax.axis_index("samp") * own_rows, own_rows, 0)
    shaped = own_scores.reshape(own_rows, width, nperm)
    return jnp.sum(shaped * shaped, axis=1) / (samples * width)


def solution(mesh):
    return jax.shard_map(
        per_device,
        mesh=mesh,
        in_specs=(P(("vgrp", "samp")), P("samp", None), P(None, "samp"), P("samp", "vgrp")),
        out_specs=P(("vgrp", "samp"), None),
        check_vma=False,
    )
```

profile of v0, /device:TPU:2, one launch (start us, length us, event | category | flops | bytes accessed | tf_op | source)
XLA Modules:
  0.0 586.8 jit_solution(16091386227517214379)
XLA Ops:
  6.5 2.5 fusion.7
  9.9 77.3 %all-gather = f32[256,1,768]{2,1,0:T(1,128)S(1)} all-gather(f32[1,1,768]{2,1,0:T(1,128)S(1)} %reshape.133), channel_id=1, replica_groups=mesh['vgrp'=4,'samp'=64] {'vgrp','samp'}, dimensions={0}, use_global_device_ids=true | all-gather | bytes 789504 | tf_op jit(solution)/shard_map/all_gather | solution.py:27
  87.1 181.6 %while.13 = (s32[]{:T(128)}, f32[16,3072]{1,0:T(8,128)S(1)}, s32[16,3072]{1,0:T(8,128)}, f32[1536,128]{1,0:T(8,128)S(1)}, s32[]{:T(128)}, /*index=5*/s32[]{:T(128)}) while((s32[]{:T(128)}, f32[16,3072]{1,0:T(8,128)S(1)}, s32[16,3072]{1,0:T(8,128)}, f32[1536,128]{1,0:T(8,128)S(1)}, s32[]{:T(128)}, /*index=5*/s32[]{:T(128)}) %tuple.39), condition=%wide.region_2.3_spmd.clone, body=%wide.region_0.2_spmd.clone.sunk | while | flops 1268738 | bytes 4866133 | solution.py:22
  88.1 8.1 %gather_fusion = f32[3072,128]{1,0:T(8,128)S(1)} fusion(f32[1536,128]{1,0:T(8,128)S(1)} %get-tuple-element.138, s32[3072]{0:T(1024)S(1)} %broadcast_clamp_fusion.2), kind=kCustom, calls=%fused_computation.clone.clone.1 | custom fusion | bytes 3158016 | tf_op jit(solution)/shard_map/while/body/eval_jaxpr/gather | solution.py:18
  96.2 1.9 select_reduce_fusion.3
  99.5 8.1 %gather_fusion = f32[3072,128]{1,0:T(8,128)S(1)} fusion(f32[1536,128]{1,0:T(8,128)S(1)} %get-tuple-element.138, s32[3072]{0:T(1024)S(1)} %broadcast_clamp_fusion.2), kind=kCustom, calls=%fused_computation.clone.clone.1 | custom fusion | bytes 3158016 | tf_op jit(solution)/shard_map/while/body/eval_jaxpr/gather | solution.py:18
  107.6 1.9 select_reduce_fusion.3
  110.8 8.1 %gather_fusion = f32[3072,128]{1,0:T(8,128)S(1)} fusion(f32[1536,128]{1,0:T(8,128)S(1)} %get-tuple-element.138, s32[3072]{0:T(1024)S(1)} %broadcast_clamp_fusion.2), kind=kCustom, calls=%fused_computation.clone.clone.1 | custom fusion | bytes 3158016 | tf_op jit(solution)/shard_map/while/body/eval_jaxpr/gather | solution.py:18
  119.0 1.9 select_reduce_fusion.3
  122.2 8.1 %gather_fusion = f32[3072,128]{1,0:T(8,128)S(1)} fusion(f32[1536,128]{1,0:T(8,128)S(1)} %get-tuple-element.138, s32[3072]{0:T(1024)S(1)} %broadcast_clamp_fusion.2), kind=kCustom, calls=%fused_computation.clone.clone.1 | custom fusion | bytes 3158016 | tf_op jit(solution)/shard_map/while/body/eval_jaxpr/gather | solution.py:18
  130.3 1.9 select_reduce_fusion.3
  132.5 1.0 compare_select_fusion.5
  133.5 8.1 %gather_fusion = f32[3072,128]{1,0:T(8,128)S(1)} fusion(f32[1536,128]{1,0:T(8,128)S(1)} %get-tuple-element.138, s32[3072]{0:T(1024)S(1)} %broadcast_clamp_fusion.2), kind=kCustom, calls=%fused_computation.clone.clone.1 | custom fusion | bytes 3158016 | tf_op jit(solution)/shard_map/while/body/eval_jaxpr/gather | solution.py:18
  141.7 1.9 select_reduce_fusion.3
  144.9 8.1 %gather_fusion = f32[3072,128]{1,0:T(8,128)S(1)} fusion(f32[1536,128]{1,0:T(8,128)S(1)} %get-tuple-element.138, s32[3072]{0:T(1024)S(1)} %broadcast_clamp_fusion.2), kind=kCustom, calls=%fused_computation.clone.clone.1 | custom fusion | bytes 3158016 | tf_op jit(solution)/shard_map/while/body/eval_jaxpr/gather | solution.py:18
  153.0 1.9 select_reduce_fusion.3
  156.2 8.1 %gather_fusion = f32[3072,128]{1,0:T(8,128)S(1)} fusion(f32[1536,128]{1,0:T(8,128)S(1)} %get-tuple-element.138, s32[3072]{0:T(1024)S(1)} %broadcast_clamp_fusion.2), kind=kCustom, calls=%fused_computation.clone.clone.1 | custom fusion | bytes 3158016 | tf_op jit(solution)/shard_map/while/body/eval_jaxpr/gather | solution.py:18
  164.4 1.9 select_reduce_fusion.3
  167.6 8.1 %gather_fusion = f32[3072,128]{1,0:T(8,128)S(1)} fusion(f32[1536,128]{1,0:T(8,128)S(1)} %get-tuple-element.138, s32[3072]{0:T(1024)S(1)} %broadcast_clamp_fusion.2), kind=kCustom, calls=%fused_computation.clone.clone.1 | custom fusion | bytes 3158016 | tf_op jit(solution)/shard_map/while/body/eval_jaxpr/gather | solution.py:18
  175.7 1.9 select_reduce_fusion.3
  178.9 8.1 %gather_fusion = f32[3072,128]{1,0:T(8,128)S(1)} fusion(f32[1536,128]{1,0:T(8,128)S(1)} %get-tuple-element.138, s32[3072]{0:T(1024)S(1)} %broadcast_clamp_fusion.2), kind=kCustom, calls=%fused_computation.clone.clone.1 | custom fusion | bytes 3158016 | tf_op jit(solution)/shard_map/while/body/eval_jaxpr/gather | solution.py:18
  187.1 1.9 select_reduce_fusion.3
  189.3 1.0 compare_select_fusion.5
  190.3 8.1 %gather_fusion = f32[3072,128]{1,0:T(8,128)S(1)} fusion(f32[1536,128]{1,0:T(8,128)S(1)} %get-tuple-element.138, s32[3072]{0:T(1024)S(1)} %broadcast_clamp_fusion.2), kind=kCustom, calls=%fused_computation.clone.clone.1 | custom fusion | bytes 3158016 | tf_op jit(solution)/shard_map/while/body/eval_jaxpr/gather | solution.py:18
  198.4 1.9 select_reduce_fusion.3
  201.6 8.1 %gather_fusion = f32[3072,128]{1,0:T(8,128)S(1)} fusion(f32[1536,128]{1,0:T(8,128)S(1)} %get-tuple-element.138, s32[3072]{0:T(1024)S(1)} %broadcast_clamp_fusion.2), kind=kCustom, calls=%fused_computation.clone.clone.1 | custom fusion | bytes 3158016 | tf_op jit(solution)/shard_map/while/body/eval_jaxpr/gather | solution.py:18
  209.8 1.9 select_reduce_fusion.3
  213.0 8.1 %gather_fusion = f32[3072,128]{1,0:T(8,128)S(1)} fusion(f32[1536,128]{1,0:T(8,128)S(1)} %get-tuple-element.138, s32[3072]{0:T(1024)S(1)} %broadcast_clamp_fusion.2), kind=kCustom, calls=%fused_computation.clone.clone.1 | custom fusion | bytes 3158016 | tf_op jit(solution)/shard_map/while/body/eval_jaxpr/gather | solution.py:18
  221.1 1.9 select_reduce_fusion.3
  223.3 1.0 compare_select_fusion.5
  224.3 8.1 %gather_fusion = f32[3072,128]{1,0:T(8,128)S(1)} fusion(f32[1536,128]{1,0:T(8,128)S(1)} %get-tuple-element.138, s32[3072]{0:T(1024)S(1)} %broadcast_clamp_fusion.2), kind=kCustom, calls=%fused_computation.clone.clone.1 | custom fusion | bytes 3158016 | tf_op jit(solution)/shard_map/while/body/eval_jaxpr/gather | solution.py:18
  232.5 1.9 select_reduce_fusion.3
  235.7 8.1 %gather_fusion = f32[3072,128]{1,0:T(8,128)S(1)} fusion(f32[1536,128]{1,0:T(8,128)S(1)} %get-tuple-element.138, s32[3072]{0:T(1024)S(1)} %broadcast_clamp_fusion.2), kind=kCustom, calls=%fused_computation.clone.clone.1 | custom fusion | bytes 3158016 | tf_op jit(solution)/shard_map/while/body/eval_jaxpr/gather | solution.py:18
  243.8 1.9 select_reduce_fusion.3
  247.1 8.1 %gather_fusion = f32[3072,128]{1,0:T(8,128)S(1)} fusion(f32[1536,128]{1,0:T(8,128)S(1)} %get-tuple-element.138, s32[3072]{0:T(1024)S(1)} %broadcast_clamp_fusion.2), kind=kCustom, calls=%fused_computation.clone.clone.1 | custom fusion | bytes 3158016 | tf_op jit(solution)/shard_map/while/body/eval_jaxpr/gather | solution.py:18
  255.2 1.9 select_reduce_fusion.3
  258.4 8.1 %gather_fusion = f32[3072,128]{1,0:T(8,128)S(1)} fusion(f32[1536,128]{1,0:T(8,128)S(1)} %get-tuple-element.138, s32[3072]{0:T(1024)S(1)} %broadcast_clamp_fusion.2), kind=kCustom, calls=%fused_computation.clone.clone.1 | custom fusion | bytes 3158016 | tf_op jit(solution)/shard_map/while/body/eval_jaxpr/gather | solution.py:18
  266.5 1.9 select_reduce_fusion.3
  268.7 1.3 fusion.5
  270.1 2.0 copy.12
  272.1 74.1 %psum.22 = f32[128,16]{0,1:T(8,128)S(1)} all-reduce(f32[128,16]{0,1:T(8,128)S(1)} %fusion.5), channel_id=1, replica_groups=mesh['vgrp'=4,'samp'=64] {'vgrp','samp'}, use_global_device_ids=true, to_apply=%region_6.7 | all-reduce | flops 2048 | bytes 16384 | tf_op jit(solution)/shard_map/psum | solution.py:38
  348.0 11.7 %cholesky.16 = f32[128,128]{1,0:T(8,128)S(1)} custom-call(f32[128,128]{1,0:T(8,128)S(1)} %fusion.14), custom_call_target="Cholesky" | custom-call | tf_op jit(solution)/shard_map/jit(cholesky)/cholesky | solution.py:40
  361.1 9.8 %custom-call.8 = f32[1,128,128]{1,2,0:T(8,128)S(1)} custom-call(f32[1,128,128]{2,1,0:T(8,128)S(1)} %fusion.9), custom_call_target="InvertDiagBlocksLowerTriangular" | custom-call | tf_op jit(solution)/shard_map/triangular_solve | solution.py:9
  371.3 1.4 fusion.3
  372.7 3.4 multiply_convert_fusion
  376.2 8.9 %convolution_bitcast_fusion = f32[512,2048]{0,1:T(8,128)} fusion(bf16[3072,2048]{0,1:T(8,128)(2,1)S(1)} %bitcast.45, s32[3072,512]{1,0:T(8,128)S(1)} %bitcast.51), kind=kOutput, calls=%fused_computation.19 | convolution fusion | flops 6444023808 | bytes 23068672 | tf_op jit(solution)/shard_map/dot_general | solution.py:52
  385.1 192.5 %all-reduce.5.cloned.1.call-done = f32[512,2048]{0,1:T(8,128)} async-done(((f32[512,2048]{0,1:T(8,128)}), f32[512,2048]{0,1:T(8,128)}) %all-reduce.5.cloned.1.call-update) | async-done | bytes 4194320 | tf_op jit(solution)/shard_map/psum | solution.py:52
  577.6 1.6 dynamic-slice_multiply_fusion
  (86 shorter events, 22.8 us)
Async XLA Ops:
  6.5 339.7 %all-reduce.3.cloned.1.call-start = ((), (), s32[]{:S(2)}) async-start(), calls=%async_computation | async-start | bytes 131072 | tf_op jit(solution)/shard_map/psum | solution.py:38
  9.1 568.5 %all-reduce.5.cloned.1.call-start = ((), (), s32[]{:S(2)}) async-start(), calls=%async_computation.1 | async-start | bytes 8388608 | tf_op jit(solution)/shard_map/psum | solution.py:52
  270.1 101.2 %copy-start = (f32[3072,128]{1,0:T(8,128)S(1)}, f32[3072,128]{1,0:T(8,128)}, u32[]{:S(2)}) copy-start(f32[3072,128]{1,0:T(8,128)} %param.7) | copy-start | bytes 4718596
  371.3 4.9 slice-start
  372.7 3.5 slice-start.1
Sparse Core Ops, SparseCore 0:
  12.8 243.7 all-reduce.2
  385.2 192.3 all-reduce.4
where the time goes:
time: 588 us; the launch traced here: 587 us
  waiting for transfers between devices  193 us (33%)
  blocking collectives  151 us (26%)
  local copies, waits for them, and re-layouts  138 us (23%)
  other arithmetic  76.4 us (13%)
  matrix products  14.5 us (2%)
  between operations  13.5 us (2%)
    psum x1, waiting for transfers between devices, per_device(): lax.psum(jnp.dot(dosages.T, weighted, preferred_element_type=jnp.float32)...  192 us
    gather x16, local copies, waits for them, and re-layouts, one_perm(): picked_rows = table[index_row // 128]  130 us
    all_gather x1, blocking collectives, per_device(): pheno_full = lax.all_gather(phenotype, ('vgrp', 'samp'), axis=0, tiled=True)  77.3 us
    psum x1, blocking collectives, per_device(): gram, cross = lax.psum((gram_part, cross_part), ('vgrp', 'samp'))  74.1 us
    reduce_sum x16, other arithmetic, one_perm(): return jnp.sum(jnp.where(wanted, picked_rows, jnp.float32(0.0)), axis=1)  30.2 us
    select_n x16, other arithmetic, one_perm(): picked_rows = table[index_row // 128]  15.6 us
    another operation x3, other arithmetic, per_device(): factor = jnp.linalg.cholesky(system)  12.4 us
  transfers between devices with their start and end apart: 2, of which 1 were waited for; matrix products, arithmetic and copies ran while one was open for 31% of the time, Pallas kernels for 0%

commit v1 on v0

v1 whole, which is shorter than its diff:
```python
import jax
import jax.numpy as jnp
from jax import lax
from jax.sharding import PartitionSpec as P


def chol_solve(factor, rhs):
    middle = lax.linalg.triangular_solve(factor, rhs, left_side=True, lower=True)
    return lax.linalg.triangular_solve(factor, middle, left_side=True, lower=True, transpose_a=True)


def per_device(phenotype, exposures, perms, genotypes):
    hi = lax.Precision.HIGHEST
    nv = lax.axis_size("vgrp")
    local_rows = exposures.shape[0]
    width = exposures.shape[1]
    quarter = local_rows // nv
    offset_rows = lax.axis_index("vgrp") * quarter
    expo_part = lax.dynamic_slice_in_dim(exposures, offset_rows, quarter, 0)
    gram_part = jnp.dot(expo_part.T, expo_part, precision=hi)
    gram = lax.psum(gram_part, ("vgrp", "samp"))
    pheno_full = lax.all_gather(phenotype, ("vgrp", "samp"), axis=0, tiled=True)
    samples = pheno_full.shape[0]
    system = gram + 0.5 * samples * jnp.eye(width, dtype=jnp.float32)
    factor = jnp.linalg.cholesky(system)
    perm_part = lax.dynamic_slice_in_dim(perms, offset_rows, quarter, 1)
    pheno_part = jnp.take(pheno_full, perm_part.T, axis=0, mode="clip")
    cross_part = jnp.dot(expo_part.T, pheno_part, precision=hi)
    cross = lax.psum(cross_part, ("vgrp", "samp"))
    coefficients = chol_solve(factor, cross)
    permuted = lax.all_gather(pheno_part, "vgrp", axis=0, tiled=True)
    residuals = permuted - jnp.dot(exposures, coefficients, precision=hi)
    nperm = residuals.shape[1]
    weighted = (
        (exposures[:, :, None] * residuals[:, None, :])
        .reshape(local_rows, width * nperm)
        .astype(jnp.bfloat16)
    )
    dosages = genotypes.astype(jnp.bfloat16)
    partial = jnp.dot(dosages.T, weighted, preferred_element_type=jnp.float32)
    own_scores = lax.psum_scatter(partial, "samp", scatter_dimension=0, tiled=True)
    own_rows = own_scores.shape[0]
    shaped = own_scores.reshape(own_rows, width, nperm)
    return jnp.sum(shaped * shaped, axis=1) / (samples * width)


def solution(mesh):
    return jax.shard_map(
        per_device,
        mesh=mesh,
        in_specs=(P(("vgrp", "samp")), P("samp", None), P(None, "samp"), P("samp", "vgrp")),
        out_specs=P(("vgrp", "samp"), None),
        check_vma=False,
    )
```

time: 588 us -> 511 us (0.87)
  local copies, waits for them, and re-layouts: 138 us -> 72.7 us
  other arithmetic: 76.4 us -> 36.8 us
  waiting for transfers between devices: 193 us -> 206 us
  blocking collectives: 151 us -> 162 us
    unnamed x2 -> x3, waiting for transfers between devices: 0.03 us -> 192 us
    psum x2 -> x1, waiting for transfers between devices: 192 us -> 14.5 us  [per_device(): gram = lax.psum(gram_part, ('vgrp', 'samp'))]
    gather x16 -> x3, local copies, waits for them, and re-layouts: 130 us -> 68.3 us  [per_device(): pheno_part = jnp.take(pheno_full, perm_part.T, axis=0, mode='clip')]
    reduce_sum x16 -> x0, other arithmetic: 30.2 us -> none  [one_perm(): return jnp.sum(jnp.where(wanted, picked_rows, jnp.float32(0.0)), axis=1)]
    select_n x32 -> x0, other arithmetic: 15.8 us -> none  [the longest x16 15.6 us: one_perm(): picked_rows = table[index_row // 128]]
    all_gather x0 -> x1, blocking collectives: none -> 12.1 us  [per_device(): permuted = lax.all_gather(pheno_part, 'vgrp', axis=0, tiled=True)]
  transfers between devices with their start and end apart: 2 -> 2, of which waited for: 1 -> 2; matrix products, arithmetic and copies ran while one was open for 31% -> 14% of each run, Pallas kernels for 0% -> 0%
where the time goes in v1:
time: 511 us; the launch traced here: 510 us
  waiting for transfers between devices  206 us (40%)
  blocking collectives  162 us (32%)
  local copies, waits for them, and re-layouts  72.7 us (14%)
  other arithmetic  36.8 us (7%)
  matrix products  17.6 us (3%)
  between operations  14.2 us (3%)
    unnamed x3, waiting for transfers between devices  192 us
    all_gather x1, blocking collectives, per_device(): pheno_full = lax.all_gather(phenotype, ('vgrp', 'samp'), axis=0, tiled=True)  77.3 us
    psum x1, blocking collectives, per_device(): cross = lax.psum(cross_part, ('vgrp', 'samp'))  73 us
    gather x3, local copies, waits for them, and re-layouts, per_device(): pheno_part = jnp.take(pheno_full, perm_part.T, axis=0, mode='clip')  68.3 us
    another operation x3, other arithmetic, per_device(): factor = jnp.linalg.cholesky(system)  14.7 us
    psum x1, waiting for transfers between devices, per_device(): gram = lax.psum(gram_part, ('vgrp', 'samp'))  14.5 us
    another operation x2, other arithmetic, chol_solve(): lax.linalg.triangular_solve(factor, middle, left_side=True, lower=True, t...  13.4 us
    all_gather x1, blocking collectives, per_device(): permuted = lax.all_gather(pheno_part, 'vgrp', axis=0, tiled=True)  12.1 us
  transfers between devices with their start and end apart: 2, of which 2 were waited for; matrix products, arithmetic and copies ran while one was open for 14% of the time, Pallas kernels for 0%

profile of v1, /device:TPU:2, one launch (start us, length us, event | category | flops | bytes accessed | tf_op | source)
XLA Modules:
  0.0 509.7 jit_solution(5372724521363424822)
XLA Ops:
  6.5 0.0 copy-start
  6.5 0.0 all-reduce.4.cloned.1.call-start
  6.5 2.6 fusion.4
  9.1 0.0 all-reduce.4.cloned.1.call-update
  9.1 0.0 all-reduce.6.cloned.1.call-start
  9.2 0.0 copy-done
  9.2 0.2 copy.17
  9.4 0.2 reshape.22
  9.6 0.7 reshape.31
  10.3 77.3 %all-gather.1 = f32[256,1,768]{2,1,0:T(1,128)S(1)} all-gather(f32[1,1,768]{2,1,0:T(1,128)S(1)} %reshape.31), channel_id=1, replica_groups=mesh['vgrp'=4,'samp'=64] {'vgrp','samp'}, dimensions={0}, use_global_device_ids=true | all-gather | bytes 789504 | tf_op jit(solution)/shard_map/all_gather | solution.py:22
  87.5 0.0 copy-start.1
  87.5 68.0 %gather_fusion = f32[12288]{0:T(1024)S(1)} fusion(f32[196608]{0:T(1024)S(1)} %bitcast.31, s32[12288]{0:T(1024)S(1)} %broadcast_clamp_fusion), kind=kCustom, calls=%fused_computation | custom fusion | bytes 147456 | tf_op jit(solution)/shard_map/jit(_take)/gather | solution.py:27
  155.6 0.2 reshape.21
  155.7 0.0 copy-done.1
  155.7 0.8 fusion.2
  156.5 0.1 copy.18
  156.6 12.1 %all-gather = f32[3072,16]{0,1:T(8,128)S(1)} all-gather(f32[768,16]{0,1:T(8,128)S(1)} %copy.18), channel_id=2, replica_groups=mesh['vgrp'=4,'samp'=64] {'vgrp'}, dimensions={0}, use_global_device_ids=true | all-gather | bytes 245760 | tf_op jit(solution)/shard_map/all_gather | solution.py:31
  168.8 0.5 copy.16
  169.2 73.0 %psum.15 = f32[128,16]{0,1:T(8,128)S(1)} all-reduce(f32[128,16]{0,1:T(8,128)S(1)} %fusion.2), channel_id=1, replica_groups=mesh['vgrp'=4,'samp'=64] {'vgrp','samp'}, use_global_device_ids=true, to_apply=%region_3.4 | all-reduce | flops 2048 | bytes 16384 | tf_op jit(solution)/shard_map/psum | solution.py:29
  242.2 14.5 %all-reduce.4.cloned.1.call-done = f32[128,128]{1,0:T(8,128)} async-done(((f32[128,128]{1,0:T(8,128)}), f32[128,128]{1,0:T(8,128)}) %all-reduce.4.cloned.1.call-update) | async-done | bytes 65552 | tf_op jit(solution)/shard_map/psum | solution.py:21
  256.7 1.5 select_add_fusion
  258.2 1.6 copy.19
  259.7 1.5 fusion.11
  261.3 13.2 %cholesky.16 = f32[128,128]{1,0:T(8,128)} custom-call(f32[128,128]{1,0:T(8,128)} %fusion.11), custom_call_target="Cholesky" | custom-call | tf_op jit(solution)/shard_map/jit(cholesky)/cholesky | solution.py:25
  274.4 0.9 select_reduce_fusion
  275.3 0.6 compare_reduce_fusion
  275.9 2.1 fusion.6
  278.1 11.3 %custom-call.8 = f32[1,128,128]{1,2,0:T(8,128)} custom-call(f32[1,128,128]{2,1,0:T(8,128)} %fusion.6), custom_call_target="InvertDiagBlocksLowerTriangular" | custom-call | tf_op jit(solution)/shard_map/triangular_solve | solution.py:9
  289.3 1.0 fusion.9
  290.3 1.0 fusion.7
  291.3 1.4 fusion
  292.8 3.4 multiply_convert_fusion
  296.2 10.8 %convolution_bitcast_fusion.1 = f32[512,2048]{0,1:T(8,128)} fusion(bf16[3072,2048]{0,1:T(8,128)(2,1)S(1)} %bitcast.32, s32[3072,512]{1,0:T(8,128)} %param.7), kind=kOutput, calls=%fused_computation.4 | convolution fusion | flops 6444023808 | bytes 23068672 | tf_op jit(solution)/shard_map/dot_general | solution.py:40
  307.0 0.0 copy-start.2
  307.0 0.0 all-reduce.6.cloned.1.call-update
  307.1 0.6 copy-done.2
  307.7 0.6 dynamic-slice
  308.9 191.6 %all-reduce.6.cloned.1.call-done = f32[512,2048]{0,1:T(8,128)} async-done(((f32[512,2048]{0,1:T(8,128)}), f32[512,2048]{0,1:T(8,128)}) %all-reduce.6.cloned.1.call-update) | async-done | bytes 4194320
  500.5 1.6 dynamic-slice_multiply_fusion
  502.1 0.1 reduce_sum.9
  502.2 0.1 copy.20
  502.3 0.6 broadcast_multiply_fusion
  (2 shorter events, 0.0 us)
Async XLA Ops:
  6.5 2.6 copy-start
  6.5 250.2 %all-reduce.4.cloned.1.call-start = ((), (), s32[]{:S(2)}) async-start(), calls=%async_computation | async-start | bytes 131072 | tf_op jit(solution)/shard_map/psum | solution.py:21
  9.1 491.4 %all-reduce.6.cloned.1.call-start = ((), (), s32[]{:S(2)}) async-start(), calls=%async_computation.1 | async-start | bytes 8388608
  87.5 68.2 %copy-start.1 = (f32[3072,128]{1,0:T(8,128)S(1)}, f32[3072,128]{1,0:T(8,128)}, u32[]{:S(2)}) copy-start(f32[3072,128]{1,0:T(8,128)} %param.5) | copy-start | bytes 4718596
  307.0 0.7 copy-start.2
Sparse Core Ops, SparseCore 0:
  12.8 243.8 all-reduce.3
  307.2 193.2 all-reduce.5

commit v2 on v1

v2 whole, which is shorter than its diff:
```python
import jax
import jax.numpy as jnp
from jax import lax
from jax.sharding import Mesh, PartitionSpec as P

SAMP = ("z", "x", "core")
ALL = ("vgrp",) + SAMP


def chol_solve(factor, rhs):
    middle = lax.linalg.triangular_solve(factor, rhs, left_side=True, lower=True)
    return lax.linalg.triangular_solve(factor, middle, left_side=True, lower=True, transpose_a=True)


def staged_psum(x):
    for axis in ("core", "x", "z", "vgrp"):
        x = lax.psum(x, axis)
    return x


def per_device(phenotype, exposures, perms, genotypes):
    hi = lax.Precision.HIGHEST
    nv = lax.axis_size("vgrp")
    local_rows = exposures.shape[0]
    width = exposures.shape[1]
    quarter = local_rows // nv
    offset_rows = lax.axis_index("vgrp") * quarter
    expo_part = lax.dynamic_slice_in_dim(exposures, offset_rows, quarter, 0)
    gram_part = jnp.dot(expo_part.T, expo_part, precision=hi)
    gram = staged_psum(gram_part)
    pheno_full = phenotype
    for axis in ("core", "x", "z", "vgrp"):
        pheno_full = lax.all_gather(pheno_full, axis, axis=0, tiled=True)
    samples = pheno_full.shape[0]
    system = gram + 0.5 * samples * jnp.eye(width, dtype=jnp.float32)
    factor = jnp.linalg.cholesky(system)
    perm_part = lax.dynamic_slice_in_dim(perms, offset_rows, quarter, 1)
    pheno_part = jnp.take(pheno_full, perm_part.T, axis=0, mode="clip")
    cross_part = jnp.dot(expo_part.T, pheno_part, precision=hi)
    cross = staged_psum(cross_part)
    coefficients = chol_solve(factor, cross)
    permuted = lax.all_gather(pheno_part, "vgrp", axis=0, tiled=True)
    residuals = permuted - jnp.dot(exposures, coefficients, precision=hi)
    nperm = residuals.shape[1]
    weighted = (
        (exposures[:, :, None] * residuals[:, None, :])
        .reshape(local_rows, width * nperm)
        .astype(jnp.bfloat16)
    )
    nz, nx, nc = (lax.axis_size(a) for a in SAMP)
    variants = genotypes.shape[1]
    own_rows = variants // (nz * nx * nc)
    order = genotypes.reshape(local_rows, nz, nx, nc, own_rows).transpose(0, 3, 2, 1, 4)
    dosages = order.reshape(local_rows, variants).astype(jnp.bfloat16)
    partial = jnp.dot(dosages.T, weighted, preferred_element_type=jnp.float32)
    blocks = partial.reshape(nc, nx, nz, own_rows * width * nperm)
    blocks = lax.psum_scatter(blocks, "core", scatter_dimension=0, tiled=False)
    blocks = lax.psum_scatter(blocks, "x", scatter_dimension=0, tiled=False)
    own_scores = lax.psum_scatter(blocks, "z", scatter_dimension=0, tiled=False)
    shaped = own_scores.reshape(own_rows, width, nperm)
    return jnp.sum(shaped * shaped, axis=1) / (samples * width)


def solution(mesh):
    nv, ns = mesh.devices.shape
    fine = Mesh(mesh.devices.reshape(nv, ns // 8, 4, 2), ALL)
    return jax.shard_map(
        per_device,
        mesh=fine,
        in_specs=(P(ALL), P(SAMP, None), P(None, SAMP), P(SAMP, "vgrp")),
        out_specs=P(ALL, None),
        check_vma=False,
    )
```

time: 511 us -> 452 us (0.88)
  blocking collectives: 162 us -> 107 us
  waiting for transfers between devices: 206 us -> 182 us
  local copies, waits for them, and re-layouts: 72.7 us -> 91.6 us
    unnamed x3 -> x8, waiting for transfers between devices: 192 us -> 76.6 us
    reduce_scatter x0 -> x2, waiting for transfers between devices: none -> 52.7 us  [the longest x1 34.7 us: per_device(): blocks = lax.psum_scatter(blocks, 'x', scatter_dimension=0, tiled=False)]
    psum x1 -> x4, waiting for transfers between devices: 14.5 us -> 52.7 us  [staged_psum(): x = lax.psum(x, axis)]
    psum x1 -> x4, blocking collectives: 73 us -> 38.1 us  [staged_psum(): x = lax.psum(x, axis)]
    all_gather x1 -> x4, blocking collectives: 77.3 us -> 56 us  [per_device(): pheno_full = lax.all_gather(pheno_full, axis, axis=0, tiled=True)]
    unnamed x9 -> x12, local copies, waits for them, and re-layouts: 2.4 us -> 8.37 us
    dot_general x0 -> x1, local copies, waits for them, and re-layouts: none -> 5.37 us  [per_device(): partial = jnp.dot(dosages.T, weighted, preferred_element_type=jnp.float32)]
  transfers between devices with their start and end apart: 2 -> 7, of which waited for: 2 -> 5; matrix products, arithmetic and copies ran while one was open for 14% -> 19% of each run, Pallas kernels for 0% -> 0%
where the time goes in v2:
time: 452 us; the launch traced here: 451 us
  waiting for transfers between devices  182 us (40%)
  blocking collectives  107 us (24%)
  local copies, waits for them, and re-layouts  91.6 us (20%)
  other arithmetic  40.5 us (9%)
  matrix products  15.8 us (3%)
  between operations  13.7 us (3%)
    unnamed x8, waiting for transfers between devices  76.6 us
    gather x3, local copies, waits for them, and re-layouts, per_device(): pheno_part = jnp.take(pheno_full, perm_part.T, axis=0, mode='clip')  68.9 us
    all_gather x4, blocking collectives, per_device(): pheno_full = lax.all_gather(pheno_full, axis, axis=0, tiled=True)  56 us
    psum x4, waiting for transfers between devices, staged_psum(): x = lax.psum(x, axis)  52.7 us
    psum x4, blocking collectives, staged_psum(): x = lax.psum(x, axis)  38.1 us
    reduce_scatter x1, waiting for transfers between devices, per_device(): blocks = lax.psum_scatter(blocks, 'x', scatter_dimension=0, tiled=False)  34.7 us
    reduce_scatter x1, waiting for transfers between devices, per_device(): blocks = lax.psum_scatter(blocks, 'core', scatter_dimension=0, tiled=False)  18 us
    another operation x3, other arithmetic, per_device(): factor = jnp.linalg.cholesky(system)  14.7 us
  transfers between devices with their start and end apart: 7, of which 5 were waited for; matrix products, arithmetic and copies ran while one was open for 19% of the time, Pallas kernels for 0%

profile of v2, /device:TPU:2, one launch (start us, length us, event | category | flops | bytes accessed | tf_op | source)
XLA Modules:
  0.0 450.7 jit_solution(5382359870029589654)
XLA Ops:
  6.5 2.6 fusion.3
  9.1 0.0 all-reduce.9.cloned.1.call-start
  9.2 0.7 reshape.46
  9.9 1.8 all-gather.1
  11.7 12.0 %all-gather.2 = f32[4,1,1536]{2,1,0:T(1,128)S(1)} all-gather(f32[1,1,1536]{2,1,0:T(1,128)S(1)} %bitcast.42), channel_id=1, replica_groups=mesh['vgrp'=4,'z'=8,'x'=4,'core'=2] {'x'}, dimensions={0}, use_global_device_ids=true | all-gather | bytes 30720 | tf_op jit(solution)/shard_map/all_gather | solution.py:33
  23.7 0.2 copy.15
  23.9 0.2 reshape.37
  24.0 28.4 %all_gather.17 = f32[49152]{0:T(1024)S(1)} all-gather(f32[6144]{0:T(1024)S(1)} %bitcast.41), channel_id=1, replica_groups=mesh['vgrp'=4,'z'=8,'x'=4,'core'=2] {'z'}, dimensions={0}, use_global_device_ids=true | all-gather | bytes 221184 | tf_op jit(solution)/shard_map/all_gather | solution.py:33
  52.5 13.8 %all_gather.18 = f32[196608]{0:T(1024)S(1)} all-gather(f32[49152]{0:T(1024)S(1)} %all_gather.17), channel_id=1, replica_groups=mesh['vgrp'=4,'z'=8,'x'=4,'core'=2] {'vgrp'}, dimensions={0}, use_global_device_ids=true | all-gather | bytes 983040 | tf_op jit(solution)/shard_map/all_gather | solution.py:33
  66.3 68.0 %gather_fusion = f32[12288]{0:T(1024)S(1)} fusion(f32[196608]{0:T(1024)S(1)} %all_gather.18, s32[12288]{0:T(1024)S(1)} %broadcast_clamp_fusion), kind=kCustom, calls=%fused_computation | custom fusion | bytes 147456 | tf_op jit(solution)/shard_map/jit(_take)/gather | solution.py:38
  134.4 0.2 reshape.36
  134.6 0.8 fusion.1
  135.4 0.8 copy.16
  136.2 0.5 copy.14
  136.6 6.6 %copy.18 = s32[3072,512]{0,1:T(8,128)} copy(s32[3072,512]{1,0:T(8,128)} %param.7) | data formatting | bytes 12582912 | tf_op args[3]
  143.2 3.5 convert_element_type.27
  146.8 1.9 copy.19
  148.6 2.5 psum.60
  151.1 8.6 %psum.61 = f32[128,16]{0,1:T(8,128)S(1)} all-reduce(f32[128,16]{0,1:T(8,128)S(1)} %psum.60), channel_id=1, replica_groups=mesh['vgrp'=4,'z'=8,'x'=4,'core'=2] {'x'}, use_global_device_ids=true, to_apply=%region_7.8 | all-reduce | flops 2048 | bytes 16384 | tf_op jit(solution)/shard_map/psum | solution.py:17
  159.7 16.6 %psum.62 = f32[128,16]{0,1:T(8,128)S(1)} all-reduce(f32[128,16]{0,1:T(8,128)S(1)} %psum.61), channel_id=1, replica_groups=mesh['vgrp'=4,'z'=8,'x'=4,'core'=2] {'z'}, use_global_device_ids=true, to_apply=%region_8.9 | all-reduce | flops 2048 | bytes 16384 | tf_op jit(solution)/shard_map/psum | solution.py:17
  176.4 10.3 %psum.63 = f32[128,16]{0,1:T(8,128)S(1)} all-reduce(f32[128,16]{0,1:T(8,128)S(1)} %psum.62), channel_id=1, replica_groups=mesh['vgrp'=4,'z'=8,'x'=4,'core'=2] {'vgrp'}, use_global_device_ids=true, to_apply=%region_9.10 | all-reduce | flops 2048 | bytes 16384 | tf_op jit(solution)/shard_map/psum | solution.py:17
  186.7 18.6 %all-reduce.11.cloned.1.call-done = f32[128,128]{1,0:T(8,128)} async-done(((f32[128,128]{1,0:T(8,128)}), f32[128,128]{1,0:T(8,128)}) %all-reduce.11.cloned.1.call-update) | async-done | bytes 65552 | tf_op jit(solution)/shard_map/psum | solution.py:17
  205.4 12.9 %all-gather = f32[3072,16]{0,1:T(8,128)S(1)} all-gather(f32[768,16]{0,1:T(8,128)} %copy.16), channel_id=2, replica_groups=mesh['vgrp'=4,'z'=8,'x'=4,'core'=2] {'vgrp'}, dimensions={0}, use_global_device_ids=true | all-gather | bytes 245760 | tf_op jit(solution)/shard_map/all_gather | solution.py:42
  218.3 34.1 %all-reduce.13.cloned.1.call-done = f32[128,128]{1,0:T(8,128)} async-done(((f32[128,128]{1,0:T(8,128)}), f32[128,128]{1,0:T(8,128)}) %all-reduce.13.cloned.1.call-update) | async-done | bytes 65552 | tf_op jit(solution)/shard_map/psum | solution.py:17
  252.4 1.5 select_add_fusion
  253.8 1.6 copy.17
  255.4 1.5 fusion.11
  256.9 13.2 %cholesky.16 = f32[128,128]{1,0:T(8,128)} custom-call(f32[128,128]{1,0:T(8,128)} %fusion.11), custom_call_target="Cholesky" | custom-call | tf_op jit(solution)/shard_map/jit(cholesky)/cholesky | solution.py:36
  270.1 0.9 select_reduce_fusion
  270.9 0.6 compare_reduce_fusion
  271.6 2.1 fusion.5
  273.7 11.3 %custom-call.8 = f32[1,128,128]{1,2,0:T(8,128)} custom-call(f32[1,128,128]{2,1,0:T(8,128)} %fusion.5), custom_call_target="InvertDiagBlocksLowerTriangular" | custom-call | tf_op jit(solution)/shard_map/triangular_solve | solution.py:12
  285.0 1.0 fusion.9
  286.0 1.0 fusion.7
  287.0 1.4 fusion
  288.4 3.4 multiply_convert_fusion
  291.9 9.0 %convolution_bitcast_fusion.1 = f32[512,2048]{0,1:T(8,128)} fusion(bf16[3072,2048]{0,1:T(8,128)(2,1)S(1)} %bitcast.36, bf16[3072,512]{0,1:T(8,128)(2,1)S(1)} %bitcast.38), kind=kOutput, calls=%fused_computation.4 | convolution fusion | flops 6442450944 | bytes 19922944 | tf_op jit(solution)/shard_map/dot_general | solution.py:55
  300.9 5.4 %copy.20 = f32[512,2048]{1,0:T(8,128)} copy(f32[512,2048]{0,1:T(8,128)} %convolution_bitcast_fusion.1) | data formatting | bytes 8388608 | tf_op jit(solution)/shard_map/dot_general | solution.py:55
  306.2 5.0 %reshape.34 = f32[2,4,8,16384]{3,2,1,0:T(8,128)} reshape(f32[512,2048]{1,0:T(8,128)} %copy.20) | data formatting | bytes 8388608 | tf_op jit(solution)/shard_map/reshape | solution.py:56
  311.2 0.0 reduce-scatter.5.cloned.1.call-start
  311.3 18.0 %reduce-scatter.3.cloned.1.call-done = f32[1,4,8,16384]{3,2,1,0:T(8,128)} async-done(((f32[2,4,8,16384]{3,2,1,0:T(8,128)}), f32[1,4,8,16384]{3,2,1,0:T(8,128)}) %reduce-scatter.3.cloned.1.call-update) | async-done | bytes 2097168 | tf_op jit(solution)/shard_map/reduce_scatter | solution.py:57
  329.3 0.0 all-reduce.15.cloned.1.call-start
  329.3 34.7 %reduce-scatter.5.cloned.1.call-done = f32[1,8,16384]{2,1,0:T(8,128)} async-done(((f32[4,8,16384]{2,1,0:T(8,128)}), f32[1,8,16384]{2,1,0:T(8,128)}) %reduce-scatter.5.cloned.1.call-update) | async-done | bytes 524304 | tf_op jit(solution)/shard_map/reduce_scatter | solution.py:58
  364.0 0.6 dynamic-slice
  364.6 76.5 %all-reduce.15.cloned.1.call-done = f32[8,16384]{1,0:T(8,128)} async-done(((f32[8,16384]{1,0:T(8,128)}), f32[8,16384]{1,0:T(8,128)}) %all-reduce.15.cloned.1.call-update) | async-done | bytes 524304
  441.1 1.9 fusion.6
  443.0 0.2 mul.47
  443.2 0.6 broadcast_multiply_fusion
  (24 shorter events, 0.3 us)
Async XLA Ops:
  6.5 17.1 %copy-start = (s32[16,3072]{1,0:T(8,128)S(1)}, s32[16,3072]{1,0:T(8,128)}, u32[]{:S(2)}) copy-start(s32[16,3072]{1,0:T(8,128)} %param.6) | copy-start | bytes 589828
  6.5 45.9 %all-reduce.7.cloned.1.call-start = ((), (), s32[]{:S(2)}) async-start(), calls=%async_computation.2 | async-start | bytes 131072 | tf_op jit(solution)/shard_map/psum | solution.py:17
  9.1 125.4 %all-reduce.9.cloned.1.call-start = ((), (), s32[]{:S(2)}) async-start(), calls=%async_computation.3 | async-start | bytes 131072 | tf_op jit(solution)/shard_map/psum | solution.py:17
  52.4 152.9 %all-reduce.11.cloned.1.call-start = ((), (), s32[]{:S(2)}) async-start(), calls=%async_computation.4 | async-start | bytes 131072 | tf_op jit(solution)/shard_map/psum | solution.py:17
  66.3 68.3 %copy-start.1 = (f32[3072,128]{1,0:T(8,128)S(1)}, f32[3072,128]{1,0:T(8,128)}, u32[]{:S(2)}) copy-start(f32[3072,128]{1,0:T(8,128)} %param.5) | copy-start | bytes 4718596
  134.6 117.8 %all-reduce.13.cloned.1.call-start = ((), (), s32[]{:S(2)}) async-start(), calls=%async_computation.5 | async-start | bytes 131072 | tf_op jit(solution)/shard_map/psum | solution.py:17
  205.4 123.9 %reduce-scatter.3.cloned.1.call-start = ((), (), s32[]{:S(2)}) async-start(), calls=%async_computation.6 | async-start | bytes 6291456 | tf_op jit(solution)/shard_map/reduce_scatter | solution.py:57
  288.4 3.5 copy-start.2
  311.2 52.8 %copy-start.3 = (u32[256]{0:T(256)S(1)}, u32[256]{0:T(256)}, u32[]{:S(2)}) copy-start(u32[256]{0:T(256)} %constant.66) | copy-start | bytes 3076
  311.2 52.8 %reduce-scatter.5.cloned.1.call-start = ((), (), s32[]{:S(2)}) async-start(), calls=%async_computation.7 | async-start | bytes 2621440 | tf_op jit(solution)/shard_map/reduce_scatter | solution.py:58
  329.3 111.8 %all-reduce.15.cloned.1.call-start = ((), (), s32[]{:S(2)}) async-start(), calls=%async_computation.8 | async-start | bytes 1048576
Sparse Core Ops, SparseCore 0:
  9.9 31.4 all-reduce.6
  52.6 44.1 all-reduce.8
  134.7 70.5 all-reduce.10
  207.5 44.8 all-reduce.12
  311.3 17.8 reduce-scatter.2
  331.7 32.2 reduce-scatter.4
  366.3 74.7 all-reduce.14

commit v3 on v2

--- a/solution.py
+++ b/solution.py
@@ -12,9 +12,14 @@
     return lax.linalg.triangular_solve(factor, middle, left_side=True, lower=True, transpose_a=True)
 
 
-def staged_psum(x):
-    for axis in ("core", "x", "z", "vgrp"):
-        x = lax.psum(x, axis)
+def doubling_psum(x, axes):
+    for axis in axes:
+        size = lax.axis_size(axis)
+        step = 1
+        while step < size:
+            pairs = [(i, i ^ step) for i in range(size)]
+            x = x + lax.ppermute(x, axis, pairs)
+            step *= 2
     return x
 
 
@@ -27,17 +32,17 @@
     offset_rows = lax.axis_index("vgrp") * quarter
     expo_part = lax.dynamic_slice_in_dim(exposures, offset_rows, quarter, 0)
     gram_part = jnp.dot(expo_part.T, expo_part, precision=hi)
-    gram = staged_psum(gram_part)
     pheno_full = phenotype
     for axis in ("core", "x", "z", "vgrp"):
         pheno_full = lax.all_gather(pheno_full, axis, axis=0, tiled=True)
     samples = pheno_full.shape[0]
-    system = gram + 0.5 * samples * jnp.eye(width, dtype=jnp.float32)
-    factor = jnp.linalg.cholesky(system)
     perm_part = lax.dynamic_slice_in_dim(perms, offset_rows, quarter, 1)
     pheno_part = jnp.take(pheno_full, perm_part.T, axis=0, mode="clip")
     cross_part = jnp.dot(expo_part.T, pheno_part, precision=hi)
-    cross = staged_psum(cross_part)
+    both = doubling_psum(jnp.concatenate([gram_part, cross_part], axis=1), ("core", "x", "z", "vgrp"))
+    gram, cross = both[:, :width], both[:, width:]
+    system = gram + 0.5 * samples * jnp.eye(width, dtype=jnp.float32)
+    factor = jnp.linalg.cholesky(system)
     coefficients = chol_solve(factor, cross)
     permuted = lax.all_gather(pheno_part, "vgrp", axis=0, tiled=True)
     residuals = permuted - jnp.dot(exposures, coefficients, precision=hi)
@@ -56,7 +61,7 @@
     blocks = partial.reshape(nc, nx, nz, own_rows * width * nperm)
     blocks = lax.psum_scatter(blocks, "core", scatter_dimension=0, tiled=False)
     blocks = lax.psum_scatter(blocks, "x", scatter_dimension=0, tiled=False)
-    own_scores = lax.psum_scatter(blocks, "z", scatter_dimension=0, tiled=False)
+    own_scores = jnp.sum(lax.all_to_all(blocks, "z", 0, 0, tiled=True), axis=0)
     shaped = own_scores.reshape(own_rows, width, nperm)
     return jnp.sum(shaped * shaped, axis=1) / (samples * width)
 

time: 452 us -> 340 us (0.75)
  waiting for transfers between devices: 182 us -> 76.8 us
  blocking collectives: 107 us -> 93.2 us
  starting transfers between devices: 0.24 us -> 13.1 us
  other arithmetic: 40.5 us -> 35.4 us
    unnamed x8 -> x2, waiting for transfers between devices: 76.6 us -> 0.03 us
    psum x4 -> x0, waiting for transfers between devices: 52.7 us -> none  [staged_psum(): x = lax.psum(x, axis)]
    psum x4 -> x0, blocking collectives: 38.1 us -> none  [staged_psum(): x = lax.psum(x, axis)]
    ppermute x0 -> x8, waiting for transfers between devices: none -> 27.4 us  [doubling_psum(): x = x + lax.ppermute(x, axis, pairs)]
    all_to_all x0 -> x1, blocking collectives: none -> 24.2 us  [per_device(): own_scores = jnp.sum(lax.all_to_all(blocks, 'z', 0, 0, tiled=True), axis=0)]
    ppermute x0 -> x8, starting transfers between devices: none -> 13.1 us  [doubling_psum(): x = x + lax.ppermute(x, axis, pairs)]
  transfers between devices with their start and end apart: 7 -> 10, of which waited for: 5 -> 8; matrix products, arithmetic and copies ran while one was open for 19% -> 4% of each run, Pallas kernels for 0% -> 0%
where the time goes in v3:
time: 340 us; the launch traced here: 338 us
  blocking collectives  93.2 us (27%)
  local copies, waits for them, and re-layouts  91.4 us (27%)
  waiting for transfers between devices  76.8 us (23%)
  other arithmetic  35.4 us (10%)
  matrix products  14.5 us (4%)
  between operations  13.6 us (4%)
  starting transfers between devices  13.1 us (4%)
    gather x3, local copies, waits for them, and re-layouts, per_device(): pheno_part = jnp.take(pheno_full, perm_part.T, axis=0, mode='clip')  68.3 us
    all_gather x4, blocking collectives, per_device(): pheno_full = lax.all_gather(pheno_full, axis, axis=0, tiled=True)  56 us
    reduce_scatter x1, waiting for transfers between devices, per_device(): blocks = lax.psum_scatter(blocks, 'x', scatter_dimension=0, tiled=False)  34.8 us
    ppermute x8, waiting for transfers between devices, doubling_psum(): x = x + lax.ppermute(x, axis, pairs)  27.4 us
    all_to_all x1, blocking collectives, per_device(): own_scores = jnp.sum(lax.all_to_all(blocks, 'z', 0, 0, tiled=True), axis=0)  24.2 us
    reduce_scatter x1, waiting for transfers between devices, per_device(): blocks = lax.psum_scatter(blocks, 'core', scatter_dimension=0, tiled=False)  14.5 us
    another operation x3, other arithmetic, per_device(): factor = jnp.linalg.cholesky(system)  13.2 us
    ppermute x8, starting transfers between devices, doubling_psum(): x = x + lax.ppermute(x, axis, pairs)  13.1 us
  transfers between devices with their start and end apart: 10, of which 8 were waited for; matrix products, arithmetic and copies ran while one was open for 4% of the time, Pallas kernels for 0%

profile of v3, /device:TPU:2, one launch (start us, length us, event | category | flops | bytes accessed | tf_op | source)
XLA Modules:
  0.0 338.0 jit_solution(11812765927203427328)
XLA Ops:
  6.5 0.7 reshape.50
  7.3 1.8 all-gather.1
  9.1 12.0 %all-gather.2 = f32[4,1,1536]{2,1,0:T(1,128)S(1)} all-gather(f32[1,1,1536]{2,1,0:T(1,128)S(1)} %bitcast.40), channel_id=1, replica_groups=mesh['vgrp'=4,'z'=8,'x'=4,'core'=2] {'x'}, dimensions={0}, use_global_device_ids=true | all-gather | bytes 30720 | tf_op jit(solution)/shard_map/all_gather | solution.py:37
  21.1 1.9 fusion.3
  23.0 28.4 %all_gather.17 = f32[49152]{0:T(1024)S(1)} all-gather(f32[6144]{0:T(1024)S(1)} %bitcast.39), channel_id=1, replica_groups=mesh['vgrp'=4,'z'=8,'x'=4,'core'=2] {'z'}, dimensions={0}, use_global_device_ids=true | all-gather | bytes 221184 | tf_op jit(solution)/shard_map/all_gather | solution.py:37
  51.7 13.8 %all_gather.18 = f32[196608]{0:T(1024)S(1)} all-gather(f32[49152]{0:T(1024)S(1)} %all_gather.17), channel_id=1, replica_groups=mesh['vgrp'=4,'z'=8,'x'=4,'core'=2] {'vgrp'}, dimensions={0}, use_global_device_ids=true | all-gather | bytes 983040 | tf_op jit(solution)/shard_map/all_gather | solution.py:37
  65.6 68.0 %gather_fusion = f32[12288]{0:T(1024)S(1)} fusion(f32[196608]{0:T(1024)S(1)} %all_gather.18, s32[12288]{0:T(1024)S(1)} %broadcast_clamp_fusion), kind=kCustom, calls=%fused_computation | custom fusion | bytes 147456 | tf_op jit(solution)/shard_map/jit(_take)/gather | solution.py:40
  133.8 0.8 fusion.1
  134.7 1.3 collective-permute-done
  136.0 0.9 collective-permute-start.1
  137.0 4.7 %collective-permute-done.1 = f32[128,144]{1,0:T(8,128)S(1)} collective-permute-done((f32[128,144]{1,0:T(8,128)S(1)}, f32[128,144]{1,0:T(8,128)S(1)}, u32[]{:S(2)}, u32[]{:S(2)}) %collective-permute-start.1) | collective-permute-done | bytes 73760 | tf_op jit(solution)/shard_map/ppermute | solution.py:21
  141.7 2.2 collective-permute-start.2
  143.9 4.4 %collective-permute-done.2 = f32[128,144]{1,0:T(8,128)S(1)} collective-permute-done((f32[128,144]{1,0:T(8,128)S(1)}, f32[128,144]{1,0:T(8,128)S(1)}, u32[]{:S(2)}, u32[]{:S(2)}) %collective-permute-start.2) | collective-permute-done | bytes 73760 | tf_op jit(solution)/shard_map/ppermute | solution.py:21
  148.3 1.1 collective-permute-start.3
  149.4 3.9 %collective-permute-done.3 = f32[128,144]{1,0:T(8,128)S(1)} collective-permute-done((f32[128,144]{1,0:T(8,128)S(1)}, f32[128,144]{1,0:T(8,128)S(1)}, u32[]{:S(2)}, u32[]{:S(2)}) %collective-permute-start.3) | collective-permute-done | bytes 73760 | tf_op jit(solution)/shard_map/ppermute | solution.py:21
  153.4 1.5 collective-permute-start.4
  154.9 5.9 %collective-permute-done.4 = f32[128,144]{1,0:T(8,128)S(1)} collective-permute-done((f32[128,144]{1,0:T(8,128)S(1)}, f32[128,144]{1,0:T(8,128)S(1)}, u32[]{:S(2)}, u32[]{:S(2)}) %collective-permute-start.4) | collective-permute-done | bytes 73760 | tf_op jit(solution)/shard_map/ppermute | solution.py:21
  160.8 3.1 collective-permute-start.5
  163.9 7.1 %collective-permute-done.5 = f32[128,144]{1,0:T(8,128)S(1)} collective-permute-done((f32[128,144]{1,0:T(8,128)S(1)}, f32[128,144]{1,0:T(8,128)S(1)}, u32[]{:S(2)}, u32[]{:S(2)}) %collective-permute-start.5) | collective-permute-done | bytes 73760 | tf_op jit(solution)/shard_map/ppermute | solution.py:21
  171.1 1.4 collective-permute-start.6
  172.6 0.5 copy.18
  173.0 6.6 %copy.24 = s32[3072,512]{0,1:T(8,128)} copy(s32[3072,512]{1,0:T(8,128)} %param.7) | data formatting | bytes 12582912 | tf_op args[3]
  179.7 3.5 %convert_element_type.27 = bf16[3072,512]{0,1:T(8,128)(2,1)S(1)} convert(s32[3072,512]{0,1:T(8,128)} %copy.24) | non-fusion elementwise | flops 1572864 | bytes 9437184 | tf_op jit(solution)/shard_map/convert_element_type | solution.py:59
  183.2 1.9 copy.25
  185.0 0.9 add.55
  186.0 2.8 collective-permute-start.7
  188.7 13.0 %all-gather = f32[3072,16]{0,1:T(8,128)} all-gather(f32[768,16]{0,1:T(8,128)S(1)} %copy.20), channel_id=2, replica_groups=mesh['vgrp'=4,'z'=8,'x'=4,'core'=2] {'vgrp'}, dimensions={0}, use_global_device_ids=true | all-gather | bytes 245760 | tf_op jit(solution)/shard_map/all_gather | solution.py:47
  201.8 0.6 slice_add_fusion
  202.4 0.9 copy.23
  203.3 0.6 fusion.11
  204.0 12.5 %cholesky.16 = f32[128,128]{1,0:T(8,128)S(1)} custom-call(f32[128,128]{1,0:T(8,128)} %fusion.11), custom_call_target="Cholesky" | custom-call | tf_op jit(solution)/shard_map/jit(cholesky)/cholesky | solution.py:45
  216.6 0.6 compare_reduce_fusion
  217.2 1.3 fusion.5
  218.5 10.6 %custom-call.8 = f32[1,128,128]{1,2,0:T(8,128)S(1)} custom-call(f32[1,128,128]{2,1,0:T(8,128)} %fusion.5), custom_call_target="InvertDiagBlocksLowerTriangular" | custom-call | tf_op jit(solution)/shard_map/triangular_solve | solution.py:12
  229.1 0.2 fusion.6
  229.3 0.2 fusion.8
  229.6 2.4 fusion
  231.9 3.4 %multiply_convert_fusion = bf16[3072,128,16]{0,2,1:T(8,128)(2,1)S(1)} fusion(f32[3072,16]{0,1:T(8,128)S(1)} %fusion, f32[3072,128]{0,1:T(8,128)S(1)} %copy.18), kind=kLoop, calls=%fused_computation.1 | loop fusion | flops 12582912 | bytes 14352384 | tf_op jit(solution)/shard_map/convert_element_type | solution.py:53
  235.4 9.0 %convolution_bitcast_fusion.1 = f32[512,2048]{0,1:T(8,128)} fusion(bf16[3072,2048]{0,1:T(8,128)(2,1)S(1)} %bitcast.34, bf16[3072,512]{0,1:T(8,128)(2,1)S(1)} %bitcast.36), kind=kOutput, calls=%fused_computation.4 | convolution fusion | flops 6442450944 | bytes 19922944 | tf_op jit(solution)/shard_map/dot_general | solution.py:60
  244.4 5.4 %copy.26 = f32[512,2048]{1,0:T(8,128)} copy(f32[512,2048]{0,1:T(8,128)} %convolution_bitcast_fusion.1) | data formatting | bytes 8388608 | tf_op jit(solution)/shard_map/dot_general | solution.py:60
  249.7 5.0 %reshape.38 = f32[2,4,8,16384]{3,2,1,0:T(8,128)} reshape(f32[512,2048]{1,0:T(8,128)} %copy.26) | data formatting | bytes 8388608 | tf_op jit(solution)/shard_map/reshape | solution.py:61
  254.8 14.5 %reduce-scatter.3.cloned.1.call-done = f32[1,4,8,16384]{3,2,1,0:T(8,128)} async-done(((f32[2,4,8,16384]{3,2,1,0:T(8,128)}), f32[1,4,8,16384]{3,2,1,0:T(8,128)}) %reduce-scatter.3.cloned.1.call-update) | async-done | bytes 2097168 | tf_op jit(solution)/shard_map/reduce_scatter | solution.py:62
  269.3 34.8 %reduce-scatter.5.cloned.1.call-done = f32[1,8,16384]{2,1,0:T(8,128)} async-done(((f32[4,8,16384]{2,1,0:T(8,128)}), f32[1,8,16384]{2,1,0:T(8,128)}) %reduce-scatter.5.cloned.1.call-update) | async-done | bytes 524304 | tf_op jit(solution)/shard_map/reduce_scatter | solution.py:63
  304.1 1.6 copy.27
  305.7 24.2 %all_to_all.9 = f32[8,1,16384]{2,1,0:T(1,128)S(1)} all-to-all(f32[8,1,16384]{2,1,0:T(1,128)S(1)} %copy.27), channel_id=1, replica_groups=mesh['vgrp'=4,'z'=8,'x'=4,'core'=2] {'z'}, dimensions={0} | all-to-all | bytes 1048576 | tf_op jit(solution)/shard_map/all_to_all | solution.py:64
  329.9 0.4 reduce_sum.18
  330.3 0.2 mul.43
  330.6 0.6 broadcast_multiply_fusion
  (30 shorter events, 1.0 us)
Async XLA Ops:
  6.5 14.5 %copy-start = (s32[16,3072]{1,0:T(8,128)S(1)}, s32[16,3072]{1,0:T(8,128)}, u32[]{:S(2)}) copy-start(s32[16,3072]{1,0:T(8,128)} %param.6) | copy-start | bytes 589828
  6.5 262.7 %reduce-scatter.3.cloned.1.call-start = ((), (), s32[]{:S(2)}) async-start(), calls=%async_computation.3 | async-start | bytes 6291456 | tf_op jit(solution)/shard_map/reduce_scatter | solution.py:62
  65.6 68.2 %copy-start.1 = (f32[3072,128]{1,0:T(8,128)S(1)}, f32[3072,128]{1,0:T(8,128)}, u32[]{:S(2)}) copy-start(f32[3072,128]{1,0:T(8,128)} %param.5) | copy-start | bytes 4718596
  134.6 1.4 collective-permute-start
  136.0 5.6 %collective-permute-start.1 = (f32[128,144]{1,0:T(8,128)S(1)}, f32[128,144]{1,0:T(8,128)S(1)}, u32[]{:S(2)}, u32[]{:S(2)}) collective-permute-start(f32[128,144]{1,0:T(8,128)S(1)} %fusion.14), channel_id=1, source_target_pairs={{0,2},{2,0},{4,6},{6,4},{1,3},{3,1},{5,7},{7,5},{8,10},{10,8},{12,... | collective-permute-start | bytes 221192 | tf_op jit(solution)/shard_map/ppermute | solution.py:21
  141.7 6.6 %collective-permute-start.2 = (f32[128,144]{1,0:T(8,128)S(1)}, f32[128,144]{1,0:T(8,128)S(1)}, u32[]{:S(2)}, u32[]{:S(2)}) collective-permute-start(f32[128,144]{1,0:T(8,128)S(1)} %add.50), channel_id=1, source_target_pairs={{0,4},{2,6},{4,0},{6,2},{1,5},{3,7},{5,1},{7,3},{8,12},{10,14},{12... | collective-permute-start | bytes 221192 | tf_op jit(solution)/shard_map/ppermute | solution.py:21
  148.3 5.1 %collective-permute-start.3 = (f32[128,144]{1,0:T(8,128)S(1)}, f32[128,144]{1,0:T(8,128)S(1)}, u32[]{:S(2)}, u32[]{:S(2)}) collective-permute-start(f32[128,144]{1,0:T(8,128)S(1)} %add.51), channel_id=1, source_target_pairs={{0,8},{8,0},{16,24},{24,16},{32,40},{40,32},{48,56},{56,48},{1,9},... | collective-permute-start | bytes 221192 | tf_op jit(solution)/shard_map/ppermute | solution.py:21
  153.4 7.4 %collective-permute-start.4 = (f32[128,144]{1,0:T(8,128)S(1)}, f32[128,144]{1,0:T(8,128)S(1)}, u32[]{:S(2)}, u32[]{:S(2)}) collective-permute-start(f32[128,144]{1,0:T(8,128)S(1)} %add.52), channel_id=1, source_target_pairs={{0,16},{8,24},{16,0},{24,8},{32,48},{40,56},{48,32},{56,40},{1,17}... | collective-permute-start | bytes 221192 | tf_op jit(solution)/shard_map/ppermute | solution.py:21
  160.8 10.2 %collective-permute-start.5 = (f32[128,144]{1,0:T(8,128)S(1)}, f32[128,144]{1,0:T(8,128)S(1)}, u32[]{:S(2)}, u32[]{:S(2)}) collective-permute-start(f32[128,144]{1,0:T(8,128)S(1)} %add.53), channel_id=1, source_target_pairs={{0,32},{8,40},{16,48},{24,56},{32,0},{40,8},{48,16},{56,24},{1,33}... | collective-permute-start | bytes 221192 | tf_op jit(solution)/shard_map/ppermute | solution.py:21
  171.1 14.0 %collective-permute-start.6 = (f32[128,144]{1,0:T(8,128)S(1)}, f32[128,144]{1,0:T(8,128)}, u32[]{:S(2)}, u32[]{:S(2)}) collective-permute-start(f32[128,144]{1,0:T(8,128)S(1)} %add.54), channel_id=1, source_target_pairs={{0,64},{64,0},{128,192},{192,128},{1,65},{65,1},{129,193},{193,129... | collective-permute-start | bytes 221192 | tf_op jit(solution)/shard_map/ppermute | solution.py:21
  186.0 15.8 %collective-permute-start.7 = (f32[128,144]{1,0:T(8,128)S(1)}, f32[128,144]{1,0:T(8,128)S(1)}, u32[]{:S(2)}, u32[]{:S(2)}) collective-permute-start(f32[128,144]{1,0:T(8,128)S(1)} %add.55), channel_id=1, source_target_pairs={{0,128},{64,192},{128,0},{192,64},{1,129},{65,193},{129,1},{193,65... | collective-permute-start | bytes 221192 | tf_op jit(solution)/shard_map/ppermute | solution.py:21
  231.9 3.5 %copy-start.2 = (bf16[3072,2,4,8,8]{0,4,3,2,1:T(8,128)(2,1)S(1)}, bf16[3072,2,4,8,8]{0,4,3,2,1:T(8,128)(2,1)}, u32[]{:S(2)}) copy-start(bf16[3072,2,4,8,8]{0,4,3,2,1:T(8,128)(2,1)} %copy.25) | copy-start | bytes 9437188
  254.7 49.4 %reduce-scatter.5.cloned.1.call-start = ((), (), s32[]{:S(2)}) async-start(), calls=%async_computation.4 | async-start | bytes 2621440 | tf_op jit(solution)/shard_map/reduce_scatter | solution.py:63
Sparse Core Ops, SparseCore 0:
  254.8 14.3 reduce-scatter.2
  271.8 32.2 reduce-scatter.4

commit v4 on v3

--- a/solution.py
+++ b/solution.py
@@ -1,6 +1,7 @@
 import jax
 import jax.numpy as jnp
 from jax import lax
+from jax.experimental import pallas as pl
 from jax.sharding import Mesh, PartitionSpec as P
 
 SAMP = ("z", "x", "core")
@@ -10,6 +11,50 @@
 def chol_solve(factor, rhs):
     middle = lax.linalg.triangular_solve(factor, rhs, left_side=True, lower=True)
     return lax.linalg.triangular_solve(factor, middle, left_side=True, lower=True, transpose_a=True)
+
+
+COLS = 256
+TILE = 512
+
+
+def gather_body(idx_ref, tab_ref, out_ref):
+    idx = idx_ref[...]
+    rows = tab_ref.shape[1]
+    row = idx // COLS
+    col = idx % COLS
+    hot = (lax.broadcasted_iota(jnp.int32, (rows, TILE), 0) == row).astype(jnp.bfloat16)
+    picked = jnp.dot(tab_ref[...], hot, preferred_element_type=jnp.float32)
+    value = picked[:COLS] + picked[COLS : 2 * COLS] + picked[2 * COLS :]
+    wanted = lax.broadcasted_iota(jnp.int32, (COLS, TILE), 0) == col
+    out_ref[...] = jnp.sum(jnp.where(wanted, value, jnp.float32(0.0)), axis=0, keepdims=True)
+
+
+def split_table(pheno_full):
+    table = pheno_full.reshape(-1, COLS)
+    top = lax.reduce_precision(table, exponent_bits=8, mantissa_bits=7)
+    rest = table - top
+    middle = lax.reduce_precision(rest, exponent_bits=8, mantissa_bits=7)
+    low = rest - middle
+    pieces = [piece.T.astype(jnp.bfloat16) for piece in (top, middle, low)]
+    return jnp.concatenate(pieces, axis=0)
+
+
+def gather_pheno(pheno_full, index, interpret=False):
+    stacked = split_table(pheno_full)
+    count = index.size
+    flat = index.reshape(1, count)
+    out = pl.pallas_call(
+        gather_body,
+        grid=(count // TILE,),
+        in_specs=[
+            pl.BlockSpec((1, TILE), lambda i: (0, i)),
+            pl.BlockSpec(stacked.shape, lambda i: (0, 0)),
+        ],
+        out_specs=pl.BlockSpec((1, TILE), lambda i: (0, i)),
+        out_shape=jax.ShapeDtypeStruct((1, count), jnp.float32),
+        interpret=interpret,
+    )(flat, stacked)
+    return out.reshape(index.shape)
 
 
 def doubling_psum(x, axes):
@@ -37,7 +82,7 @@
         pheno_full = lax.all_gather(pheno_full, axis, axis=0, tiled=True)
     samples = pheno_full.shape[0]
     perm_part = lax.dynamic_slice_in_dim(perms, offset_rows, quarter, 1)
-    pheno_part = jnp.take(pheno_full, perm_part.T, axis=0, mode="clip")
+    pheno_part = gather_pheno(pheno_full, perm_part).T
     cross_part = jnp.dot(expo_part.T, pheno_part, precision=hi)
     both = doubling_psum(jnp.concatenate([gram_part, cross_part], axis=1), ("core", "x", "z", "vgrp"))
     gram, cross = both[:, :width], both[:, width:]

time: 340 us -> 297 us (0.87)
  local copies, waits for them, and re-layouts: 91.4 us -> 24.4 us
  Pallas kernels: 0 us -> 21.3 us
    gather x3 -> x0, local copies, waits for them, and re-layouts: 68.3 us -> none  [per_device(): pheno_part = jnp.take(pheno_full, perm_part.T, axis=0, mode='clip')]
    pallas_call x0 -> x1, Pallas kernels: none -> 21.3 us  [gather_pheno(): pl.pallas_call(gather_body, grid=(count // TILE,), in_specs=[pl.BlockSpec...]
    unnamed x9 -> x11, local copies, waits for them, and re-layouts: 7.83 us -> 8.5 us
where the time goes in v4:
time: 297 us; the launch traced here: 295 us
  blocking collectives  93.2 us (31%)
  waiting for transfers between devices  76.7 us (26%)
  other arithmetic  38.2 us (13%)
  local copies, waits for them, and re-layouts  24.4 us (8%)
  Pallas kernels  21.3 us (7%)
  matrix products  14.5 us (5%)
  between operations  13.6 us (5%)
  starting transfers between devices  13.1 us (4%)
    all_gather x4, blocking collectives, per_device(): pheno_full = lax.all_gather(pheno_full, axis, axis=0, tiled=True)  56 us
    reduce_scatter x1, waiting for transfers between devices, per_device(): blocks = lax.psum_scatter(blocks, 'x', scatter_dimension=0, tiled=False)  34.8 us
    ppermute x8, waiting for transfers between devices, doubling_psum(): x = x + lax.ppermute(x, axis, pairs)  27.4 us
    all_to_all x1, blocking collectives, per_device(): own_scores = jnp.sum(lax.all_to_all(blocks, 'z', 0, 0, tiled=True), axis=0)  24.2 us
    pallas_call x1, Pallas kernels, gather_pheno(): pl.pallas_call(gather_body, grid=(count // TILE,), in_specs=[pl.BlockSpec...  21.3 us
    reduce_scatter x1, waiting for transfers between devices, per_device(): blocks = lax.psum_scatter(blocks, 'core', scatter_dimension=0, tiled=False)  14.5 us
    another operation x3, other arithmetic, per_device(): factor = jnp.linalg.cholesky(system)  13.2 us
    ppermute x8, starting transfers between devices, doubling_psum(): x = x + lax.ppermute(x, axis, pairs)  13.1 us
  transfers between devices with their start and end apart: 10, of which 8 were waited for; matrix products, arithmetic and copies ran while one was open for 4% of the time, Pallas kernels for 0%

profile of v4, /device:TPU:2, one launch (start us, length us, event | category | flops | bytes accessed | tf_op | source)
XLA Modules:
  0.0 295.2 jit_solution(10216900825642924638)
XLA Ops:
  6.5 0.7 reshape.51
  7.3 1.8 all-gather
  9.1 12.0 %all-gather.1 = f32[4,1,1536]{2,1,0:T(1,128)S(1)} all-gather(f32[1,1,1536]{2,1,0:T(1,128)S(1)} %bitcast.51), channel_id=1, replica_groups=mesh['vgrp'=4,'z'=8,'x'=4,'core'=2] {'x'}, dimensions={0}, use_global_device_ids=true | all-gather | bytes 30720 | tf_op jit(solution)/shard_map/all_gather | solution.py:82
  21.1 0.7 copy.30
  21.8 1.9 fusion.7
  23.7 28.4 %all_gather.17 = f32[49152]{0:T(1024)S(1)} all-gather(f32[6144]{0:T(1024)S(1)} %bitcast.50), channel_id=1, replica_groups=mesh['vgrp'=4,'z'=8,'x'=4,'core'=2] {'z'}, dimensions={0}, use_global_device_ids=true | all-gather | bytes 221184 | tf_op jit(solution)/shard_map/all_gather | solution.py:82
  52.1 13.8 %all_gather.18 = f32[196608]{0:T(1024)S(1)} all-gather(f32[49152]{0:T(1024)S(1)} %all_gather.17), channel_id=1, replica_groups=mesh['vgrp'=4,'z'=8,'x'=4,'core'=2] {'vgrp'}, dimensions={0}, use_global_device_ids=true | all-gather | bytes 983040 | tf_op jit(solution)/shard_map/all_gather | solution.py:82
  66.5 1.1 pad_maximum_fusion.tab_ref
  67.6 21.3 %shard_map.46 = f32[1,12288]{1,0:T(1,128)} custom-call(s32[1,12288]{1,0:T(1,128)} %bitcast.49, bf16[768,768]{1,0:T(8,128)(2,1)} %pad_maximum_fusion.tab_ref), custom_call_target="tpu_custom_call" | custom-call | tf_op jit(solution)/shard_map/pallas_call | solution.py:46
  89.0 0.5 broadcast.82
  89.5 1.6 reduce.10
  91.1 0.8 fusion.5
  92.0 1.3 collective-permute-done
  93.3 0.9 collective-permute-start.1
  94.3 4.7 %collective-permute-done.1 = f32[128,144]{1,0:T(8,128)S(1)} collective-permute-done((f32[128,144]{1,0:T(8,128)S(1)}, f32[128,144]{1,0:T(8,128)S(1)}, u32[]{:S(2)}, u32[]{:S(2)}) %collective-permute-start.1) | collective-permute-done | bytes 73760 | tf_op jit(solution)/shard_map/ppermute | solution.py:66
  99.0 2.2 collective-permute-start.2
  101.2 4.4 %collective-permute-done.2 = f32[128,144]{1,0:T(8,128)S(1)} collective-permute-done((f32[128,144]{1,0:T(8,128)S(1)}, f32[128,144]{1,0:T(8,128)S(1)}, u32[]{:S(2)}, u32[]{:S(2)}) %collective-permute-start.2) | collective-permute-done | bytes 73760 | tf_op jit(solution)/shard_map/ppermute | solution.py:66
  105.6 1.1 collective-permute-start.3
  106.7 3.9 %collective-permute-done.3 = f32[128,144]{1,0:T(8,128)S(1)} collective-permute-done((f32[128,144]{1,0:T(8,128)S(1)}, f32[128,144]{1,0:T(8,128)S(1)}, u32[]{:S(2)}, u32[]{:S(2)}) %collective-permute-start.3) | collective-permute-done | bytes 73760 | tf_op jit(solution)/shard_map/ppermute | solution.py:66
  110.7 1.5 collective-permute-start.4
  112.2 5.9 %collective-permute-done.4 = f32[128,144]{1,0:T(8,128)S(1)} collective-permute-done((f32[128,144]{1,0:T(8,128)S(1)}, f32[128,144]{1,0:T(8,128)S(1)}, u32[]{:S(2)}, u32[]{:S(2)}) %collective-permute-start.4) | collective-permute-done | bytes 73760 | tf_op jit(solution)/shard_map/ppermute | solution.py:66
  118.1 3.1 %collective-permute-start.5 = (f32[128,144]{1,0:T(8,128)S(1)}, f32[128,144]{1,0:T(8,128)S(1)}, u32[]{:S(2)}, u32[]{:S(2)}) collective-permute-start(f32[128,144]{1,0:T(8,128)S(1)} %add.53), channel_id=1, source_target_pairs={{0,32},{8,40},{16,48},{24,56},{32,0},{40,8},{48,16},{56,24},{1,33}... | collective-permute-start | bytes 221192 | tf_op jit(solution)/shard_map/ppermute | solution.py:66
  121.2 7.1 %collective-permute-done.5 = f32[128,144]{1,0:T(8,128)S(1)} collective-permute-done((f32[128,144]{1,0:T(8,128)S(1)}, f32[128,144]{1,0:T(8,128)S(1)}, u32[]{:S(2)}, u32[]{:S(2)}) %collective-permute-start.5) | collective-permute-done | bytes 73760 | tf_op jit(solution)/shard_map/ppermute | solution.py:66
  128.4 1.4 collective-permute-start.6
  129.7 0.5 copy.18
  130.2 6.6 %copy.24 = s32[3072,512]{0,1:T(8,128)} copy(s32[3072,512]{1,0:T(8,128)} %param.7) | data formatting | bytes 12582912 | tf_op args[3]
  136.8 3.5 %convert_element_type.51 = bf16[3072,512]{0,1:T(8,128)(2,1)S(1)} convert(s32[3072,512]{0,1:T(8,128)} %copy.24) | non-fusion elementwise | flops 1572864 | bytes 9437184 | tf_op jit(solution)/shard_map/convert_element_type | solution.py:104
  140.3 1.9 copy.25
  142.2 0.9 add.55
  143.1 2.8 collective-permute-start.7
  145.9 13.0 %all_gather.19 = f32[3072,16]{0,1:T(8,128)} all-gather(f32[768,16]{0,1:T(8,128)S(1)} %bitcast.48), channel_id=1, replica_groups=mesh['vgrp'=4,'z'=8,'x'=4,'core'=2] {'vgrp'}, dimensions={0}, use_global_device_ids=true | all-gather | bytes 245760 | tf_op jit(solution)/shard_map/all_gather | solution.py:92
  158.9 0.6 slice_add_fusion
  159.6 0.9 copy.23
  160.5 0.6 fusion.15
  161.1 12.5 %cholesky.16 = f32[128,128]{1,0:T(8,128)S(1)} custom-call(f32[128,128]{1,0:T(8,128)} %fusion.15), custom_call_target="Cholesky" | custom-call | tf_op jit(solution)/shard_map/jit(cholesky)/cholesky | solution.py:90
  173.7 0.6 compare_reduce_fusion
  174.4 1.3 fusion.9
  175.6 10.6 %custom-call.8 = f32[1,128,128]{1,2,0:T(8,128)S(1)} custom-call(f32[1,128,128]{2,1,0:T(8,128)} %fusion.9), custom_call_target="InvertDiagBlocksLowerTriangular" | custom-call | tf_op jit(solution)/shard_map/triangular_solve | solution.py:13
  186.7 2.4 fusion
  189.1 3.4 %multiply_convert_fusion = bf16[3072,128,16]{0,2,1:T(8,128)(2,1)S(1)} fusion(f32[3072,16]{0,1:T(8,128)S(1)} %fusion, f32[3072,128]{0,1:T(8,128)S(1)} %copy.18), kind=kLoop, calls=%fused_computation | loop fusion | flops 12582912 | bytes 14352384 | tf_op jit(solution)/shard_map/convert_element_type | solution.py:98
  192.5 9.0 %convolution_bitcast_fusion.1 = f32[512,2048]{0,1:T(8,128)} fusion(bf16[3072,2048]{0,1:T(8,128)(2,1)S(1)} %bitcast.43, bf16[3072,512]{0,1:T(8,128)(2,1)S(1)} %bitcast.45), kind=kOutput, calls=%fused_computation.3 | convolution fusion | flops 6442450944 | bytes 19922944 | tf_op jit(solution)/shard_map/dot_general | solution.py:105
  201.5 5.4 %copy.26 = f32[512,2048]{1,0:T(8,128)} copy(f32[512,2048]{0,1:T(8,128)} %convolution_bitcast_fusion.1) | data formatting | bytes 8388608 | tf_op jit(solution)/shard_map/dot_general | solution.py:105
  206.9 5.0 %reshape.50 = f32[2,4,8,16384]{3,2,1,0:T(8,128)} reshape(f32[512,2048]{1,0:T(8,128)} %copy.26) | data formatting | bytes 8388608 | tf_op jit(solution)/shard_map/reshape | solution.py:106
  211.9 14.5 %reduce-scatter.3.cloned.1.call-done = f32[1,4,8,16384]{3,2,1,0:T(8,128)} async-done(((f32[2,4,8,16384]{3,2,1,0:T(8,128)}), f32[1,4,8,16384]{3,2,1,0:T(8,128)}) %reduce-scatter.3.cloned.1.call-update) | async-done | bytes 2097168 | tf_op jit(solution)/shard_map/reduce_scatter | solution.py:107
  226.4 34.8 %reduce-scatter.5.cloned.1.call-done = f32[1,8,16384]{2,1,0:T(8,128)} async-done(((f32[4,8,16384]{2,1,0:T(8,128)}), f32[1,8,16384]{2,1,0:T(8,128)}) %reduce-scatter.5.cloned.1.call-update) | async-done | bytes 524304 | tf_op jit(solution)/shard_map/reduce_scatter | solution.py:108
  261.3 1.6 copy.27
  262.9 24.2 %all_to_all.9 = f32[8,1,16384]{2,1,0:T(1,128)S(1)} all-to-all(f32[8,1,16384]{2,1,0:T(1,128)S(1)} %copy.27), channel_id=1, replica_groups=mesh['vgrp'=4,'z'=8,'x'=4,'core'=2] {'z'}, dimensions={0} | all-to-all | bytes 1048576 | tf_op jit(solution)/shard_map/all_to_all | solution.py:109
  287.7 0.6 broadcast_multiply_fusion
  (33 shorter events, 2.1 us)
Async XLA Ops:
  6.5 14.5 %copy-start = (s32[16,3072]{1,0:T(8,128)S(1)}, s32[16,3072]{1,0:T(8,128)}, u32[]{:S(2)}) copy-start(s32[16,3072]{1,0:T(8,128)} %param.6) | copy-start | bytes 589828
  6.5 219.9 %reduce-scatter.3.cloned.1.call-start = ((), (), s32[]{:S(2)}) async-start(), calls=%async_computation.3 | async-start | bytes 6291456 | tf_op jit(solution)/shard_map/reduce_scatter | solution.py:107
  66.5 24.5 %copy-start.1 = (f32[3072,128]{1,0:T(8,128)S(1)}, f32[3072,128]{1,0:T(8,128)}, u32[]{:S(2)}) copy-start(f32[3072,128]{1,0:T(8,128)} %param.5) | copy-start | bytes 4718596
  91.9 1.4 collective-permute-start
  93.3 5.6 %collective-permute-start.1 = (f32[128,144]{1,0:T(8,128)S(1)}, f32[128,144]{1,0:T(8,128)S(1)}, u32[]{:S(2)}, u32[]{:S(2)}) collective-permute-start(f32[128,144]{1,0:T(8,128)S(1)} %fusion.18), channel_id=1, source_target_pairs={{0,2},{2,0},{4,6},{6,4},{1,3},{3,1},{5,7},{7,5},{8,10},{10,8},{12,... | collective-permute-start | bytes 221192 | tf_op jit(solution)/shard_map/ppermute | solution.py:66
  99.0 6.6 %collective-permute-start.2 = (f32[128,144]{1,0:T(8,128)S(1)}, f32[128,144]{1,0:T(8,128)S(1)}, u32[]{:S(2)}, u32[]{:S(2)}) collective-permute-start(f32[128,144]{1,0:T(8,128)S(1)} %add.50), channel_id=1, source_target_pairs={{0,4},{2,6},{4,0},{6,2},{1,5},{3,7},{5,1},{7,3},{8,12},{10,14},{12... | collective-permute-start | bytes 221192 | tf_op jit(solution)/shard_map/ppermute | solution.py:66
  105.6 5.1 %collective-permute-start.3 = (f32[128,144]{1,0:T(8,128)S(1)}, f32[128,144]{1,0:T(8,128)S(1)}, u32[]{:S(2)}, u32[]{:S(2)}) collective-permute-start(f32[128,144]{1,0:T(8,128)S(1)} %add.51), channel_id=1, source_target_pairs={{0,8},{8,0},{16,24},{24,16},{32,40},{40,32},{48,56},{56,48},{1,9},... | collective-permute-start | bytes 221192 | tf_op jit(solution)/shard_map/ppermute | solution.py:66
  110.7 7.4 %collective-permute-start.4 = (f32[128,144]{1,0:T(8,128)S(1)}, f32[128,144]{1,0:T(8,128)S(1)}, u32[]{:S(2)}, u32[]{:S(2)}) collective-permute-start(f32[128,144]{1,0:T(8,128)S(1)} %add.52), channel_id=1, source_target_pairs={{0,16},{8,24},{16,0},{24,8},{32,48},{40,56},{48,32},{56,40},{1,17}... | collective-permute-start | bytes 221192 | tf_op jit(solution)/shard_map/ppermute | solution.py:66
  118.1 10.2 %collective-permute-start.5 = (f32[128,144]{1,0:T(8,128)S(1)}, f32[128,144]{1,0:T(8,128)S(1)}, u32[]{:S(2)}, u32[]{:S(2)}) collective-permute-start(f32[128,144]{1,0:T(8,128)S(1)} %add.53), channel_id=1, source_target_pairs={{0,32},{8,40},{16,48},{24,56},{32,0},{40,8},{48,16},{56,24},{1,33}... | collective-permute-start | bytes 221192 | tf_op jit(solution)/shard_map/ppermute | solution.py:66
  128.4 13.8 %collective-permute-start.6 = (f32[128,144]{1,0:T(8,128)S(1)}, f32[128,144]{1,0:T(8,128)}, u32[]{:S(2)}, u32[]{:S(2)}) collective-permute-start(f32[128,144]{1,0:T(8,128)S(1)} %add.54), channel_id=1, source_target_pairs={{0,64},{64,0},{128,192},{192,128},{1,65},{65,1},{129,193},{193,129... | collective-permute-start | bytes 221192 | tf_op jit(solution)/shard_map/ppermute | solution.py:66
  143.1 15.8 %collective-permute-start.7 = (f32[128,144]{1,0:T(8,128)S(1)}, f32[128,144]{1,0:T(8,128)S(1)}, u32[]{:S(2)}, u32[]{:S(2)}) collective-permute-start(f32[128,144]{1,0:T(8,128)S(1)} %add.55), channel_id=1, source_target_pairs={{0,128},{64,192},{128,0},{192,64},{1,129},{65,193},{129,1},{193,65... | collective-permute-start | bytes 221192 | tf_op jit(solution)/shard_map/ppermute | solution.py:66
  189.1 3.5 %copy-start.2 = (bf16[3072,2,4,8,8]{0,4,3,2,1:T(8,128)(2,1)S(1)}, bf16[3072,2,4,8,8]{0,4,3,2,1:T(8,128)(2,1)}, u32[]{:S(2)}) copy-start(bf16[3072,2,4,8,8]{0,4,3,2,1:T(8,128)(2,1)} %copy.25) | copy-start | bytes 9437188
  211.9 49.4 %reduce-scatter.5.cloned.1.call-start = ((), (), s32[]{:S(2)}) async-start(), calls=%async_computation.4 | async-start | bytes 2621440 | tf_op jit(solution)/shard_map/reduce_scatter | solution.py:108
Sparse Core Ops, SparseCore 0:
  212.0 14.3 reduce-scatter.2
  229.0 32.2 reduce-scatter.4

commit v5 on v4

--- a/solution.py
+++ b/solution.py
@@ -68,6 +68,42 @@
     return x
 
 
+def split_bits():
+    bits = []
+    for axis, count in (("core", 1), ("x", 2), ("z", 3)):
+        for level in range(count):
+            bits.append((axis, level))
+    return bits
+
+
+def exchange(keep_lo, keep_hi, axis, level, along):
+    size = lax.axis_size(axis)
+    bit = (lax.axis_index(axis) >> level) & 1
+    flip = [(i, i ^ (1 << level)) for i in range(size)]
+    send = jnp.where(bit == 0, keep_hi, keep_lo)
+    mine = jnp.where(bit == 0, keep_lo, keep_hi)
+    return mine + lax.ppermute(send, axis, flip)
+
+
+def halving_scores(weighted, genotypes):
+    bits = split_bits()
+    local_rows, variants = genotypes.shape
+    nz, nx, nc = (lax.axis_size(a) for a in SAMP)
+    own_rows = variants // (nz * nx * nc)
+    order = genotypes.reshape(local_rows, 2, 2, 2, 2, 2, nc, own_rows)
+    order = order.transpose(0, 6, 5, 4, 3, 2, 1, 7)
+    dosages = order.reshape(local_rows, variants).astype(jnp.bfloat16)
+    cur = jnp.dot(weighted.T, dosages, preferred_element_type=jnp.float32)
+    for axis, level in bits[:2]:
+        half = cur.shape[1] // 2
+        cur = exchange(cur[:, :half], cur[:, half:], axis, level, 1)
+    cur = cur.T
+    for axis, level in bits[2:]:
+        half = cur.shape[0] // 2
+        cur = exchange(cur[:half], cur[half:], axis, level, 0)
+    return cur
+
+
 def per_device(phenotype, exposures, perms, genotypes):
     hi = lax.Precision.HIGHEST
     nv = lax.axis_size("vgrp")
@@ -97,17 +133,8 @@
         .reshape(local_rows, width * nperm)
         .astype(jnp.bfloat16)
     )
-    nz, nx, nc = (lax.axis_size(a) for a in SAMP)
-    variants = genotypes.shape[1]
-    own_rows = variants // (nz * nx * nc)
-    order = genotypes.reshape(local_rows, nz, nx, nc, own_rows).transpose(0, 3, 2, 1, 4)
-    dosages = order.reshape(local_rows, variants).astype(jnp.bfloat16)
-    partial = jnp.dot(dosages.T, weighted, preferred_element_type=jnp.float32)
-    blocks = partial.reshape(nc, nx, nz, own_rows * width * nperm)
-    blocks = lax.psum_scatter(blocks, "core", scatter_dimension=0, tiled=False)
-    blocks = lax.psum_scatter(blocks, "x", scatter_dimension=0, tiled=False)
-    own_scores = jnp.sum(lax.all_to_all(blocks, "z", 0, 0, tiled=True), axis=0)
-    shaped = own_scores.reshape(own_rows, width, nperm)
+    own_scores = halving_scores(weighted, genotypes)
+    shaped = own_scores.reshape(own_scores.shape[0], width, nperm)
     return jnp.sum(shaped * shaped, axis=1) / (samples * width)
 
 

time: 297 us -> 269 us (0.906)
  blocking collectives: 93.2 us -> 69 us
  between operations: 13.6 us -> 0.3 us
  waiting for transfers between devices: 76.7 us -> 87.2 us
  local copies, waits for them, and re-layouts: 24.4 us -> 14.1 us
  starting transfers between devices: 13.1 us -> 20.4 us
  other arithmetic: 38.2 us -> 43.5 us
    ppermute x0 -> x6, waiting for transfers between devices: none -> 59.8 us  [exchange(): return mine + lax.ppermute(send, axis, flip)]
    reduce_scatter x2 -> x0, waiting for transfers between devices: 49.3 us -> none  [the longest x1 34.8 us: per_device(): blocks = lax.psum_scatter(blocks, 'x', scatter_dimension=0, tiled=False)]
    all_to_all x1 -> x0, blocking collectives: 24.2 us -> none  [per_device(): own_scores = jnp.sum(lax.all_to_all(blocks, 'z', 0, 0, tiled=True), axis=0)]
    ppermute x0 -> x6, starting transfers between devices: none -> 7.31 us  [exchange(): return mine + lax.ppermute(send, axis, flip)]
    dot_general x1 -> x0, local copies, waits for them, and re-layouts: 5.37 us -> none  [per_device(): partial = jnp.dot(dosages.T, weighted, preferred_element_type=jnp.float32)]
    reshape x1 -> x0, local copies, waits for them, and re-layouts: 4.97 us -> none  [per_device(): blocks = partial.reshape(nc, nx, nz, own_rows * width * nperm)]
    add x0 -> x4, other arithmetic: none -> 3.52 us  [exchange(): return mine + lax.ppermute(send, axis, flip)]
    unnamed x11 -> x13, local copies, waits for them, and re-layouts: 8.5 us -> 10.1 us
  transfers between devices with their start and end apart: 10 -> 14, of which waited for: 8 -> 12; matrix products, arithmetic and copies ran while one was open for 4% -> 5% of each run, Pallas kernels for 0% -> 0%
where the time goes in v5:
time: 269 us; the launch traced here: 268 us
  waiting for transfers between devices  87.2 us (32%)
  blocking collectives  69 us (26%)
  other arithmetic  43.5 us (16%)
  Pallas kernels  21.3 us (8%)
  starting transfers between devices  20.4 us (8%)
  local copies, waits for them, and re-layouts  14.1 us (5%)
  matrix products  12.2 us (5%)
    ppermute x6, waiting for transfers between devices, exchange(): return mine + lax.ppermute(send, axis, flip)  59.8 us
    all_gather x4, blocking collectives, per_device(): pheno_full = lax.all_gather(pheno_full, axis, axis=0, tiled=True)  56 us
    ppermute x8, waiting for transfers between devices, doubling_psum(): x = x + lax.ppermute(x, axis, pairs)  27.4 us
    pallas_call x1, Pallas kernels, gather_pheno(): pl.pallas_call(gather_body, grid=(count // TILE,), in_specs=[pl.BlockSpec...  21.3 us
    another operation x3, other arithmetic, per_device(): factor = jnp.linalg.cholesky(system)  13.2 us
    ppermute x8, starting transfers between devices, doubling_psum(): x = x + lax.ppermute(x, axis, pairs)  13.1 us
    all_gather x1, blocking collectives, per_device(): permuted = lax.all_gather(pheno_part, 'vgrp', axis=0, tiled=True)  13 us
    another operation x2, other arithmetic, chol_solve(): lax.linalg.triangular_solve(factor, middle, left_side=True, lower=True, t...  11.9 us
  transfers between devices with their start and end apart: 14, of which 12 were waited for; matrix products, arithmetic and copies ran while one was open for 5% of the time, Pallas kernels for 0%

profile of v5, /device:TPU:2, one launch (start us, length us, event | category | flops | bytes accessed | tf_op | source)
XLA Modules:
  0.0 268.0 jit_solution(1735812914868352214)
XLA Ops:
  0.0 0.7 reshape.44
  0.7 1.8 all-gather
  2.5 12.0 %all-gather.1 = f32[4,1,1536]{2,1,0:T(1,128)S(1)} all-gather(f32[1,1,1536]{2,1,0:T(1,128)S(1)} %bitcast.47), channel_id=1, replica_groups=mesh['vgrp'=4,'z'=8,'x'=4,'core'=2] {'x'}, dimensions={0}, use_global_device_ids=true | all-gather | bytes 30720 | tf_op jit(solution)/shard_map/all_gather | solution.py:118
  15.2 1.9 fusion.7
  17.1 28.4 %all_gather.17 = f32[49152]{0:T(1024)S(1)} all-gather(f32[6144]{0:T(1024)S(1)} %bitcast.46), channel_id=1, replica_groups=mesh['vgrp'=4,'z'=8,'x'=4,'core'=2] {'z'}, dimensions={0}, use_global_device_ids=true | all-gather | bytes 221184 | tf_op jit(solution)/shard_map/all_gather | solution.py:118
  45.5 13.8 %all_gather.18 = f32[196608]{0:T(1024)S(1)} all-gather(f32[49152]{0:T(1024)S(1)} %all_gather.17), channel_id=1, replica_groups=mesh['vgrp'=4,'z'=8,'x'=4,'core'=2] {'vgrp'}, dimensions={0}, use_global_device_ids=true | all-gather | bytes 983040 | tf_op jit(solution)/shard_map/all_gather | solution.py:118
  60.0 1.1 pad_maximum_fusion.tab_ref
  61.1 21.3 %shard_map.46 = f32[1,12288]{1,0:T(1,128)} custom-call(s32[1,12288]{1,0:T(1,128)} %bitcast.45, bf16[768,768]{1,0:T(8,128)(2,1)} %pad_maximum_fusion.tab_ref), custom_call_target="tpu_custom_call" | custom-call | tf_op jit(solution)/shard_map/pallas_call | solution.py:46
  82.9 1.6 reduce.9
  84.5 0.8 fusion.5
  85.4 1.3 collective-permute-done
  86.8 0.9 collective-permute-start.1
  87.7 4.7 %collective-permute-done.1 = f32[128,144]{1,0:T(8,128)S(1)} collective-permute-done((f32[128,144]{1,0:T(8,128)S(1)}, f32[128,144]{1,0:T(8,128)S(1)}, u32[]{:S(2)}, u32[]{:S(2)}) %collective-permute-start.1) | collective-permute-done | bytes 73760 | tf_op jit(solution)/shard_map/ppermute | solution.py:66
  92.4 2.2 collective-permute-start.2
  94.6 4.4 %collective-permute-done.2 = f32[128,144]{1,0:T(8,128)S(1)} collective-permute-done((f32[128,144]{1,0:T(8,128)S(1)}, f32[128,144]{1,0:T(8,128)S(1)}, u32[]{:S(2)}, u32[]{:S(2)}) %collective-permute-start.2) | collective-permute-done | bytes 73760 | tf_op jit(solution)/shard_map/ppermute | solution.py:66
  99.0 1.1 collective-permute-start.3
  100.1 3.9 %collective-permute-done.3 = f32[128,144]{1,0:T(8,128)S(1)} collective-permute-done((f32[128,144]{1,0:T(8,128)S(1)}, f32[128,144]{1,0:T(8,128)S(1)}, u32[]{:S(2)}, u32[]{:S(2)}) %collective-permute-start.3) | collective-permute-done | bytes 73760 | tf_op jit(solution)/shard_map/ppermute | solution.py:66
  104.1 1.5 collective-permute-start.4
  105.6 5.9 %collective-permute-done.4 = f32[128,144]{1,0:T(8,128)S(1)} collective-permute-done((f32[128,144]{1,0:T(8,128)S(1)}, f32[128,144]{1,0:T(8,128)S(1)}, u32[]{:S(2)}, u32[]{:S(2)}) %collective-permute-start.4) | collective-permute-done | bytes 73760 | tf_op jit(solution)/shard_map/ppermute | solution.py:66
  111.6 3.1 %collective-permute-start.5 = (f32[128,144]{1,0:T(8,128)S(1)}, f32[128,144]{1,0:T(8,128)S(1)}, u32[]{:S(2)}, u32[]{:S(2)}) collective-permute-start(f32[128,144]{1,0:T(8,128)S(1)} %add.67), channel_id=1, source_target_pairs={{0,32},{8,40},{16,48},{24,56},{32,0},{40,8},{48,16},{56,24},{1,33}... | collective-permute-start | bytes 221192 | tf_op jit(solution)/shard_map/ppermute | solution.py:66
  114.7 7.1 %collective-permute-done.5 = f32[128,144]{1,0:T(8,128)S(1)} collective-permute-done((f32[128,144]{1,0:T(8,128)S(1)}, f32[128,144]{1,0:T(8,128)S(1)}, u32[]{:S(2)}, u32[]{:S(2)}) %collective-permute-start.5) | collective-permute-done | bytes 73760 | tf_op jit(solution)/shard_map/ppermute | solution.py:66
  121.8 1.4 collective-permute-start.6
  123.7 6.6 %copy.23 = s32[3072,512]{0,1:T(8,128)} copy(s32[3072,512]{1,0:T(8,128)} %param.7) | data formatting | bytes 12582912 | tf_op args[3]
  130.2 3.5 %convert_element_type.51 = bf16[3072,512]{0,1:T(8,128)(2,1)S(1)} convert(s32[3072,512]{0,1:T(8,128)} %copy.23) | non-fusion elementwise | flops 1572864 | bytes 9437184 | tf_op jit(solution)/shard_map/convert_element_type | solution.py:95
  133.7 1.8 copy.24
  135.6 0.9 add.69
  136.5 2.8 %collective-permute-start.7 = (f32[128,144]{1,0:T(8,128)S(1)}, f32[128,144]{1,0:T(8,128)S(1)}, u32[]{:S(2)}, u32[]{:S(2)}) collective-permute-start(f32[128,144]{1,0:T(8,128)S(1)} %add.69), channel_id=1, source_target_pairs={{0,128},{64,192},{128,0},{192,64},{1,129},{65,193},{129,1},{193,65... | collective-permute-start | bytes 221192 | tf_op jit(solution)/shard_map/ppermute | solution.py:66
  139.3 13.0 %all_gather.19 = f32[3072,16]{0,1:T(8,128)} all-gather(f32[768,16]{0,1:T(8,128)S(1)} %bitcast.44), channel_id=1, replica_groups=mesh['vgrp'=4,'z'=8,'x'=4,'core'=2] {'vgrp'}, dimensions={0}, use_global_device_ids=true | all-gather | bytes 245760 | tf_op jit(solution)/shard_map/all_gather | solution.py:128
  153.0 0.9 copy.22
  154.5 12.5 %cholesky.16 = f32[128,128]{1,0:T(8,128)S(1)} custom-call(f32[128,128]{1,0:T(8,128)} %fusion.15), custom_call_target="Cholesky" | custom-call | tf_op jit(solution)/shard_map/jit(cholesky)/cholesky | solution.py:126
  167.8 1.3 fusion.9
  169.0 10.6 %custom-call.8 = f32[1,128,128]{1,2,0:T(8,128)S(1)} custom-call(f32[1,128,128]{2,1,0:T(8,128)} %fusion.9), custom_call_target="InvertDiagBlocksLowerTriangular" | custom-call | tf_op jit(solution)/shard_map/triangular_solve | solution.py:13
  180.1 2.4 fusion
  182.5 3.6 %multiply_convert_fusion = bf16[3072,128,16]{0,2,1:T(8,128)(2,1)S(1)} fusion(f32[3072,16]{0,1:T(8,128)S(1)} %fusion, f32[3072,128]{0,1:T(8,128)S(1)} %copy.17), kind=kLoop, calls=%fused_computation | loop fusion | flops 12582912 | bytes 14352384 | tf_op jit(solution)/shard_map/convert_element_type | solution.py:134
  186.2 6.7 %fusion.19 = f32[2048,512]{0,1:T(8,128)S(1)} fusion(bf16[3072,2048]{0,1:T(8,128)(2,1)S(1)} %bitcast.41, bf16[3072,512]{0,1:T(8,128)(2,1)S(1)} %bitcast.43), kind=kOutput, calls=%fused_computation.48 | convolution fusion | flops 6442450944 | bytes 19922944 | tf_op jit(solution)/shard_map/dot_general | solution.py:96
  193.2 1.7 copy-done.1
  194.8 4.3 %collective-permute-done.8 = f32[2048,256]{0,1:T(8,128)} collective-permute-done((f32[2048,256]{0,1:T(8,128)S(1)}, f32[2048,256]{0,1:T(8,128)}, u32[]{:S(2)}, u32[]{:S(2)}) %collective-permute-start.8) | collective-permute-done | bytes 2097184 | tf_op jit(solution)/shard_map/ppermute | solution.py:85
  199.1 3.4 %select_add_fusion = f32[2048,256]{0,1:T(8,128)S(1)} fusion(f32[2048,256]{0,1:T(8,128)} %collective-permute-done.8, f32[2048,512]{0,1:T(8,128)} %copy-done.1, pred[]{:T(512)S(6)} %eq.30), kind=kLoop, calls=%fused_computation.3 | loop fusion | flops 1048576 | bytes 8388609 | tf_op jit(solution)/shard_map/add | solution.py:85
  202.6 0.9 collective-permute-start.9
  203.6 24.5 %collective-permute-done.9 = f32[2048,128]{0,1:T(8,128)} collective-permute-done((f32[2048,128]{0,1:T(8,128)S(1)}, f32[2048,128]{0,1:T(8,128)}, u32[]{:S(2)}, u32[]{:S(2)}) %collective-permute-start.9) | collective-permute-done | bytes 1048608 | tf_op jit(solution)/shard_map/ppermute | solution.py:85
  228.0 1.4 add_bitcast_fusion
  229.5 2.2 collective-permute-start.10
  231.7 12.5 %collective-permute-done.10 = f32[64,2048]{1,0:T(8,128)S(1)} collective-permute-done((f32[64,2048]{1,0:T(8,128)S(1)}, f32[64,2048]{1,0:T(8,128)S(1)}, u32[]{:S(2)}, u32[]{:S(2)}) %collective-permute-start.10) | collective-permute-done | bytes 524320 | tf_op jit(solution)/shard_map/ppermute | solution.py:85
  244.4 6.6 %collective-permute-done.11 = f32[32,2048]{1,0:T(8,128)S(1)} collective-permute-done((f32[32,2048]{1,0:T(8,128)S(1)}, f32[32,2048]{1,0:T(8,128)S(1)}, u32[]{:S(2)}, u32[]{:S(2)}) %collective-permute-start.11) | collective-permute-done | bytes 262176 | tf_op jit(solution)/shard_map/ppermute | solution.py:85
  251.1 0.8 collective-permute-start.12
  251.9 6.3 %collective-permute-done.12 = f32[16,2048]{1,0:T(8,128)S(1)} collective-permute-done((f32[16,2048]{1,0:T(8,128)S(1)}, f32[16,2048]{1,0:T(8,128)S(1)}, u32[]{:S(2)}, u32[]{:S(2)}) %collective-permute-start.12) | collective-permute-done | bytes 131104 | tf_op jit(solution)/shard_map/ppermute | solution.py:85
  258.2 3.3 %collective-permute-start.13 = (f32[8,2048]{1,0:T(8,128)S(1)}, f32[8,2048]{1,0:T(8,128)S(1)}, u32[]{:S(2)}, u32[]{:S(2)}) collective-permute-start(f32[8,2048]{1,0:T(8,128)S(1)} %slice_select_fusion.5), channel_id=1, source_target_pairs={{0,32},{8,40},{16,48},{24,56},{32,0},{40,8},{48,16},{56,24},{1,33}... | collective-permute-start | bytes 196616 | tf_op jit(solution)/shard_map/ppermute | solution.py:85
  261.5 5.6 %collective-permute-done.13 = f32[8,2048]{1,0:T(8,128)S(1)} collective-permute-done((f32[8,2048]{1,0:T(8,128)S(1)}, f32[8,2048]{1,0:T(8,128)S(1)}, u32[]{:S(2)}, u32[]{:S(2)}) %collective-permute-start.13) | collective-permute-done | bytes 65568 | tf_op jit(solution)/shard_map/ppermute | solution.py:85
  (47 shorter events, 6.5 us)
Async XLA Ops:
  0.0 14.5 %copy-start = (s32[16,3072]{1,0:T(8,128)S(1)}, s32[16,3072]{1,0:T(8,128)}, u32[]{:S(2)}) copy-start(s32[16,3072]{1,0:T(8,128)} %param.6) | copy-start | bytes 589828
  60.0 24.5 %copy-start.2 = (f32[3072,128]{1,0:T(8,128)S(1)}, f32[3072,128]{1,0:T(8,128)}, u32[]{:S(2)}) copy-start(f32[3072,128]{1,0:T(8,128)} %param.5) | copy-start | bytes 4718596
  85.3 1.4 collective-permute-start
  86.8 5.6 %collective-permute-start.1 = (f32[128,144]{1,0:T(8,128)S(1)}, f32[128,144]{1,0:T(8,128)S(1)}, u32[]{:S(2)}, u32[]{:S(2)}) collective-permute-start(f32[128,144]{1,0:T(8,128)S(1)} %fusion.18), channel_id=1, source_target_pairs={{0,2},{2,0},{4,6},{6,4},{1,3},{3,1},{5,7},{7,5},{8,10},{10,8},{12,... | collective-permute-start | bytes 221192 | tf_op jit(solution)/shard_map/ppermute | solution.py:66
  92.4 6.6 %collective-permute-start.2 = (f32[128,144]{1,0:T(8,128)S(1)}, f32[128,144]{1,0:T(8,128)S(1)}, u32[]{:S(2)}, u32[]{:S(2)}) collective-permute-start(f32[128,144]{1,0:T(8,128)S(1)} %add.64), channel_id=1, source_target_pairs={{0,4},{2,6},{4,0},{6,2},{1,5},{3,7},{5,1},{7,3},{8,12},{10,14},{12... | collective-permute-start | bytes 221192 | tf_op jit(solution)/shard_map/ppermute | solution.py:66
  99.0 5.1 %collective-permute-start.3 = (f32[128,144]{1,0:T(8,128)S(1)}, f32[128,144]{1,0:T(8,128)S(1)}, u32[]{:S(2)}, u32[]{:S(2)}) collective-permute-start(f32[128,144]{1,0:T(8,128)S(1)} %add.65), channel_id=1, source_target_pairs={{0,8},{8,0},{16,24},{24,16},{32,40},{40,32},{48,56},{56,48},{1,9},... | collective-permute-start | bytes 221192 | tf_op jit(solution)/shard_map/ppermute | solution.py:66
  104.1 7.4 %collective-permute-start.4 = (f32[128,144]{1,0:T(8,128)S(1)}, f32[128,144]{1,0:T(8,128)S(1)}, u32[]{:S(2)}, u32[]{:S(2)}) collective-permute-start(f32[128,144]{1,0:T(8,128)S(1)} %add.66), channel_id=1, source_target_pairs={{0,16},{8,24},{16,0},{24,8},{32,48},{40,56},{48,32},{56,40},{1,17}... | collective-permute-start | bytes 221192 | tf_op jit(solution)/shard_map/ppermute | solution.py:66
  111.6 10.2 %collective-permute-start.5 = (f32[128,144]{1,0:T(8,128)S(1)}, f32[128,144]{1,0:T(8,128)S(1)}, u32[]{:S(2)}, u32[]{:S(2)}) collective-permute-start(f32[128,144]{1,0:T(8,128)S(1)} %add.67), channel_id=1, source_target_pairs={{0,32},{8,40},{16,48},{24,56},{32,0},{40,8},{48,16},{56,24},{1,33}... | collective-permute-start | bytes 221192 | tf_op jit(solution)/shard_map/ppermute | solution.py:66
  121.8 13.8 %collective-permute-start.6 = (f32[128,144]{1,0:T(8,128)S(1)}, f32[128,144]{1,0:T(8,128)}, u32[]{:S(2)}, u32[]{:S(2)}) collective-permute-start(f32[128,144]{1,0:T(8,128)S(1)} %add.68), channel_id=1, source_target_pairs={{0,64},{64,0},{128,192},{192,128},{1,65},{65,1},{129,193},{193,129... | collective-permute-start | bytes 221192 | tf_op jit(solution)/shard_map/ppermute | solution.py:66
  136.5 15.8 %collective-permute-start.7 = (f32[128,144]{1,0:T(8,128)S(1)}, f32[128,144]{1,0:T(8,128)S(1)}, u32[]{:S(2)}, u32[]{:S(2)}) collective-permute-start(f32[128,144]{1,0:T(8,128)S(1)} %add.69), channel_id=1, source_target_pairs={{0,128},{64,192},{128,0},{192,64},{1,129},{65,193},{129,1},{193,65... | collective-permute-start | bytes 221192 | tf_op jit(solution)/shard_map/ppermute | solution.py:66
  182.5 3.7 %copy-start.3 = (bf16[3072,2,2,2,2,2,2,8]{0,7,6,5,4,3,2,1:T(8,128)(2,1)S(1)}, bf16[3072,2,2,2,2,2,2,8]{0,7,6,5,4,3,2,1:T(8,128)(2,1)}, u32[]{:S(2)}) copy-start(bf16[3072,2,2,2,2,2,2,8]{0,7,6,5,4,3,2,1:T(8,128)(2,1)} %copy.24) | copy-start | bytes 9437188
  192.9 1.9 copy-start.1
  194.8 4.3 %collective-permute-start.8 = (f32[2048,256]{0,1:T(8,128)S(1)}, f32[2048,256]{0,1:T(8,128)}, u32[]{:S(2)}, u32[]{:S(2)}) collective-permute-start(f32[2048,256]{0,1:T(8,128)S(1)} %slice_select_fusion), channel_id=1, source_target_pairs={{0,1},{1,0},{2,3},{3,2},{4,5},{5,4},{6,7},{7,6},{8,9},{9,8},{10,11... | collective-permute-start | bytes 6291464 | tf_op jit(solution)/shard_map/ppermute | solution.py:85
  202.6 25.4 %collective-permute-start.9 = (f32[2048,128]{0,1:T(8,128)S(1)}, f32[2048,128]{0,1:T(8,128)}, u32[]{:S(2)}, u32[]{:S(2)}) collective-permute-start(f32[2048,128]{0,1:T(8,128)S(1)} %slice_select_fusion.1), channel_id=1, source_target_pairs={{0,2},{2,0},{4,6},{6,4},{1,3},{3,1},{5,7},{7,5},{8,10},{10,8},{12,... | collective-permute-start | bytes 3145736 | tf_op jit(solution)/shard_map/ppermute | solution.py:85
  229.5 14.7 %collective-permute-start.10 = (f32[64,2048]{1,0:T(8,128)S(1)}, f32[64,2048]{1,0:T(8,128)S(1)}, u32[]{:S(2)}, u32[]{:S(2)}) collective-permute-start(f32[64,2048]{1,0:T(8,128)S(1)} %slice_select_fusion.2), channel_id=1, source_target_pairs={{0,4},{2,6},{4,0},{6,2},{1,5},{3,7},{5,1},{7,3},{8,12},{10,14},{12... | collective-permute-start | bytes 1572872 | tf_op jit(solution)/shard_map/ppermute | solution.py:85
  244.3 6.7 %collective-permute-start.11 = (f32[32,2048]{1,0:T(8,128)S(1)}, f32[32,2048]{1,0:T(8,128)S(1)}, u32[]{:S(2)}, u32[]{:S(2)}) collective-permute-start(f32[32,2048]{1,0:T(8,128)S(1)} %slice_select_fusion.3), channel_id=1, source_target_pairs={{0,8},{8,0},{16,24},{24,16},{32,40},{40,32},{48,56},{56,48},{1,9},... | collective-permute-start | bytes 786440 | tf_op jit(solution)/shard_map/ppermute | solution.py:85
  251.1 7.1 %collective-permute-start.12 = (f32[16,2048]{1,0:T(8,128)S(1)}, f32[16,2048]{1,0:T(8,128)S(1)}, u32[]{:S(2)}, u32[]{:S(2)}) collective-permute-start(f32[16,2048]{1,0:T(8,128)S(1)} %slice_select_fusion.4), channel_id=1, source_target_pairs={{0,16},{8,24},{16,0},{24,8},{32,48},{40,56},{48,32},{56,40},{1,17}... | collective-permute-start | bytes 393224 | tf_op jit(solution)/shard_map/ppermute | solution.py:85
  258.2 8.9 %collective-permute-start.13 = (f32[8,2048]{1,0:T(8,128)S(1)}, f32[8,2048]{1,0:T(8,128)S(1)}, u32[]{:S(2)}, u32[]{:S(2)}) collective-permute-start(f32[8,2048]{1,0:T(8,128)S(1)} %slice_select_fusion.5), channel_id=1, source_target_pairs={{0,32},{8,40},{16,48},{24,56},{32,0},{40,8},{48,16},{56,24},{1,33}... | collective-permute-start | bytes 196616 | tf_op jit(solution)/shard_map/ppermute | solution.py:85

commit v6 on v5

--- a/solution.py
+++ b/solution.py
@@ -68,6 +68,28 @@
     return x
 
 
+def doubling_gather(x, steps):
+    for axis, level in steps:
+        size = lax.axis_size(axis)
+        bit = (lax.axis_index(axis) >> level) & 1
+        flip = [(i, i ^ (1 << level)) for i in range(size)]
+        other = lax.ppermute(x, axis, flip)
+        low = jnp.where(bit == 0, x, other)
+        high = jnp.where(bit == 0, other, x)
+        x = jnp.concatenate([low, high], axis=0)
+    return x
+
+
+def axis_bits(axes):
+    steps = []
+    for axis in axes:
+        level = 0
+        while (1 << level) < lax.axis_size(axis):
+            steps.append((axis, level))
+            level += 1
+    return steps
+
+
 def split_bits():
     bits = []
     for axis, count in (("core", 1), ("x", 2), ("z", 3)):
@@ -113,19 +135,17 @@
     offset_rows = lax.axis_index("vgrp") * quarter
     expo_part = lax.dynamic_slice_in_dim(exposures, offset_rows, quarter, 0)
     gram_part = jnp.dot(expo_part.T, expo_part, precision=hi)
-    pheno_full = phenotype
-    for axis in ("core", "x", "z", "vgrp"):
-        pheno_full = lax.all_gather(pheno_full, axis, axis=0, tiled=True)
+    gram = doubling_psum(gram_part, ("core", "x", "z", "vgrp"))
+    pheno_full = doubling_gather(phenotype, axis_bits(("core", "x", "z", "vgrp")))
     samples = pheno_full.shape[0]
+    system = gram + 0.5 * samples * jnp.eye(width, dtype=jnp.float32)
+    factor = jnp.linalg.cholesky(system)
     perm_part = lax.dynamic_slice_in_dim(perms, offset_rows, quarter, 1)
     pheno_part = gather_pheno(pheno_full, perm_part).T
     cross_part = jnp.dot(expo_part.T, pheno_part, precision=hi)
-    both = doubling_psum(jnp.concatenate([gram_part, cross_part], axis=1), ("core", "x", "z", "vgrp"))
-    gram, cross = both[:, :width], both[:, width:]
-    system = gram + 0.5 * samples * jnp.eye(width, dtype=jnp.float32)
-    factor = jnp.linalg.cholesky(system)
+    cross = doubling_psum(cross_part, ("core", "x", "z", "vgrp"))
     coefficients = chol_solve(factor, cross)
-    permuted = lax.all_gather(pheno_part, "vgrp", axis=0, tiled=True)
+    permuted = doubling_gather(pheno_part, axis_bits(("vgrp",)))
     residuals = permuted - jnp.dot(exposures, coefficients, precision=hi)
     nperm = residuals.shape[1]
     weighted = (

time: 269 us -> 262 us (0.974); the launches traced: 268 us -> 257 us
  blocking collectives: 69 us -> 0 us
  starting transfers between devices: 20.4 us -> 63.7 us
  waiting for transfers between devices: 87.2 us -> 111 us
  other arithmetic: 43.5 us -> 38.9 us
  local copies, waits for them, and re-layouts: 14.1 us -> 11 us
    all_gather x5 -> x0, blocking collectives: 69 us -> none  [the longest x4 56 us: per_device(): pheno_full = lax.all_gather(pheno_full, axis, axis=0, tiled=True)]
    ppermute x0 -> x10, starting transfers between devices: none -> 25.8 us  [doubling_gather(): other = lax.ppermute(x, axis, flip)]
    ppermute x8 -> x16, starting transfers between devices: 13.1 us -> 34 us  [doubling_psum(): x = x + lax.ppermute(x, axis, pairs)]
    ppermute x0 -> x10, waiting for transfers between devices: none -> 14.6 us  [doubling_gather(): other = lax.ppermute(x, axis, flip)]
    ppermute x8 -> x16, waiting for transfers between devices: 27.4 us -> 32.6 us  [doubling_psum(): x = x + lax.ppermute(x, axis, pairs)]
    ppermute x6, waiting for transfers between devices: 59.8 us -> 63.3 us  [exchange(): return mine + lax.ppermute(send, axis, flip)]
    ppermute x6, starting transfers between devices: 7.31 us -> 3.91 us  [exchange(): return mine + lax.ppermute(send, axis, flip)]
    add x4, other arithmetic: 3.52 us -> 0.71 us  [exchange(): return mine + lax.ppermute(send, axis, flip)]
  transfers between devices with their start and end apart: 14 -> 32, of which waited for: 12 -> 26; matrix products, arithmetic and copies ran while one was open for 5% -> 18% of each run, Pallas kernels for 0% -> 8%
where the time goes in v6:
time: 262 us; the launch traced here: 257 us
  waiting for transfers between devices  111 us (42%)
  starting transfers between devices  63.7 us (24%)
  other arithmetic  38.9 us (15%)
  Pallas kernels  21.3 us (8%)
  local copies, waits for them, and re-layouts  11 us (4%)
  matrix products  10.9 us (4%)
    ppermute x6, waiting for transfers between devices, exchange(): return mine + lax.ppermute(send, axis, flip)  63.3 us
    ppermute x16, starting transfers between devices, doubling_psum(): x = x + lax.ppermute(x, axis, pairs)  34 us
    ppermute x16, waiting for transfers between devices, doubling_psum(): x = x + lax.ppermute(x, axis, pairs)  32.6 us
    ppermute x10, starting transfers between devices, doubling_gather(): other = lax.ppermute(x, axis, flip)  25.8 us
    pallas_call x1, Pallas kernels, gather_pheno(): pl.pallas_call(gather_body, grid=(count // TILE,), in_specs=[pl.BlockSpec...  21.3 us
    ppermute x10, waiting for transfers between devices, doubling_gather(): other = lax.ppermute(x, axis, flip)  14.6 us
    another operation x3, other arithmetic, per_device(): factor = jnp.linalg.cholesky(system)  13.2 us
    another operation x2, other arithmetic, chol_solve(): lax.linalg.triangular_solve(factor, middle, left_side=True, lower=True, t...  10.5 us
  transfers between devices with their start and end apart: 32, of which 26 were waited for; matrix products, arithmetic and copies ran while one was open for 18% of the time, Pallas kernels for 8%

profile of v6, /device:TPU:2, one launch (start us, length us, event | category | flops | bytes accessed | tf_op | source)
XLA Modules:
  0.0 257.0 jit_solution(17765283544369270025)
XLA Ops:
  0.0 1.4 collective-permute-done
  2.1 2.3 collective-permute-start.1
  4.4 1.6 collective-permute-done.1
  6.1 2.0 collective-permute-start.2
  8.0 3.3 %collective-permute-done.2 = f32[3072]{0:T(1024)S(1)} collective-permute-done((f32[3072]{0:T(1024)S(1)}, f32[3072]{0:T(1024)S(1)}, u32[]{:S(2)}, u32[]{:S(2)}) %collective-permute-start.2) | collective-permute-done | bytes 12320 | tf_op jit(solution)/shard_map/ppermute | solution.py:76
  11.4 1.8 collective-permute-start.3
  13.1 2.1 collective-permute-done.3
  15.3 3.4 %collective-permute-start.4 = (f32[12288]{0:T(1024)S(1)}, f32[12288]{0:T(1024)S(1)}, u32[]{:S(2)}, u32[]{:S(2)}) collective-permute-start(f32[12288]{0:T(1024)S(1)} %pad_maximum_fusion.6), channel_id=1, source_target_pairs={{0,16},{8,24},{16,0},{24,8},{32,48},{40,56},{48,32},{56,40},{1,17}... | collective-permute-start | bytes 147464 | tf_op jit(solution)/shard_map/ppermute | solution.py:76
  18.7 2.1 collective-permute-done.4
  20.8 8.2 %collective-permute-start.5 = (f32[24576]{0:T(1024)S(1)}, f32[24576]{0:T(1024)S(1)}, u32[]{:S(2)}, u32[]{:S(2)}) collective-permute-start(f32[24576]{0:T(1024)S(1)} %pad_maximum_fusion.4), channel_id=1, source_target_pairs={{0,32},{8,40},{16,48},{24,56},{32,0},{40,8},{48,16},{56,24},{1,33}... | collective-permute-start | bytes 294920 | tf_op jit(solution)/shard_map/ppermute | solution.py:76
  29.0 2.6 %collective-permute-done.5 = f32[24576]{0:T(1024)S(1)} collective-permute-done((f32[24576]{0:T(1024)S(1)}, f32[24576]{0:T(1024)S(1)}, u32[]{:S(2)}, u32[]{:S(2)}) %collective-permute-start.5) | collective-permute-done | bytes 98336 | tf_op jit(solution)/shard_map/ppermute | solution.py:76
  31.7 1.7 collective-permute-start.6
  33.3 1.9 fusion.6
  37.5 3.3 %collective-permute-start.7 = (f32[98304]{0:T(1024)S(1)}, f32[98304]{0:T(1024)S(1)}, u32[]{:S(2)}, u32[]{:S(2)}) collective-permute-start(f32[98304]{0:T(1024)S(1)} %pad_maximum_fusion.2), channel_id=1, source_target_pairs={{0,128},{64,192},{128,0},{192,64},{1,129},{65,193},{129,1},{193,65... | collective-permute-start | bytes 1179656 | tf_op jit(solution)/shard_map/ppermute | solution.py:76
  41.0 2.2 collective-permute-start.12
  43.2 3.6 %collective-permute-done.12 = f32[128,128]{1,0:T(8,128)S(1)} collective-permute-done((f32[128,128]{1,0:T(8,128)S(1)}, f32[128,128]{1,0:T(8,128)S(1)}, u32[]{:S(2)}, u32[]{:S(2)}) %collective-permute-start.12) | collective-permute-done | bytes 65568 | tf_op jit(solution)/shard_map/ppermute | solution.py:66
  47.8 3.5 %collective-permute-done.13 = f32[128,128]{1,0:T(8,128)S(1)} collective-permute-done((f32[128,128]{1,0:T(8,128)S(1)}, f32[128,128]{1,0:T(8,128)S(1)}, u32[]{:S(2)}, u32[]{:S(2)}) %collective-permute-start.13) | collective-permute-done | bytes 65568 | tf_op jit(solution)/shard_map/ppermute | solution.py:66
  52.0 5.2 %collective-permute-done.14 = f32[128,128]{1,0:T(8,128)S(1)} collective-permute-done((f32[128,128]{1,0:T(8,128)S(1)}, f32[128,128]{1,0:T(8,128)S(1)}, u32[]{:S(2)}, u32[]{:S(2)}) %collective-permute-start.14) | collective-permute-done | bytes 65568 | tf_op jit(solution)/shard_map/ppermute | solution.py:66
  57.2 6.7 %collective-permute-start.15 = (f32[128,128]{1,0:T(8,128)S(1)}, f32[128,128]{1,0:T(8,128)S(1)}, u32[]{:S(2)}, u32[]{:S(2)}) collective-permute-start(f32[128,128]{1,0:T(8,128)S(1)} %add.91), channel_id=1, source_target_pairs={{0,32},{8,40},{16,48},{24,56},{32,0},{40,8},{48,16},{56,24},{1,33}... | collective-permute-start | bytes 196616 | tf_op jit(solution)/shard_map/ppermute | solution.py:66
  63.9 2.2 collective-permute-done.15
  67.4 3.1 %collective-permute-done.16 = f32[128,128]{1,0:T(8,128)S(1)} collective-permute-done((f32[128,128]{1,0:T(8,128)S(1)}, f32[128,128]{1,0:T(8,128)S(1)}, u32[]{:S(2)}, u32[]{:S(2)}) %collective-permute-start.16) | collective-permute-done | bytes 65568 | tf_op jit(solution)/shard_map/ppermute | solution.py:66
  70.5 3.0 %collective-permute-start.17 = (f32[128,128]{1,0:T(8,128)S(1)}, f32[128,128]{1,0:T(8,128)}, u32[]{:S(2)}, u32[]{:S(2)}) collective-permute-start(f32[128,128]{1,0:T(8,128)S(1)} %add.93), channel_id=1, source_target_pairs={{0,128},{64,192},{128,0},{192,64},{1,129},{65,193},{129,1},{193,65... | collective-permute-start | bytes 196616 | tf_op jit(solution)/shard_map/ppermute | solution.py:66
  75.4 21.3 %shard_map.46 = f32[1,12288]{1,0:T(1,128)} custom-call(s32[1,12288]{1,0:T(1,128)} %bitcast.43, bf16[768,768]{1,0:T(8,128)(2,1)} %pad_maximum_fusion.tab_ref), custom_call_target="tpu_custom_call" | custom-call | tf_op jit(solution)/shard_map/pallas_call | solution.py:46
  97.3 1.6 reduce.9
  100.0 6.6 %copy.11 = s32[3072,512]{0,1:T(8,128)} copy(s32[3072,512]{1,0:T(8,128)} %param.7) | data formatting | bytes 12582912 | tf_op args[3]
  106.6 3.5 %convert_element_type.51 = bf16[3072,512]{0,1:T(8,128)(2,1)S(1)} convert(s32[3072,512]{0,1:T(8,128)} %copy.11) | non-fusion elementwise | flops 1572864 | bytes 9437184 | tf_op jit(solution)/shard_map/convert_element_type | solution.py:117
  110.1 1.8 copy.12
  113.4 2.3 collective-permute-done.19
  115.6 2.0 collective-permute-start.20
  118.3 12.5 %cholesky.16 = f32[128,128]{1,0:T(8,128)S(1)} custom-call(f32[128,128]{1,0:T(8,128)} %fusion.13), custom_call_target="Cholesky" | custom-call | tf_op jit(solution)/shard_map/jit(cholesky)/cholesky | solution.py:142
  131.1 3.5 %collective-permute-done.21 = f32[128,16]{0,1:T(8,128)S(1)} collective-permute-done((f32[128,16]{0,1:T(8,128)S(1)}, f32[128,16]{0,1:T(8,128)S(1)}, u32[]{:S(2)}, u32[]{:S(2)}) %collective-permute-start.21) | collective-permute-done | bytes 8224 | tf_op jit(solution)/shard_map/ppermute | solution.py:66
  135.5 3.7 %collective-permute-done.22 = f32[128,16]{0,1:T(8,128)S(1)} collective-permute-done((f32[128,16]{0,1:T(8,128)S(1)}, f32[128,16]{0,1:T(8,128)S(1)}, u32[]{:S(2)}, u32[]{:S(2)}) %collective-permute-start.22) | collective-permute-done | bytes 8224 | tf_op jit(solution)/shard_map/ppermute | solution.py:66
  139.2 5.9 %collective-permute-start.23 = (f32[128,16]{0,1:T(8,128)S(1)}, f32[128,16]{0,1:T(8,128)S(1)}, u32[]{:S(2)}, u32[]{:S(2)}) collective-permute-start(f32[128,16]{0,1:T(8,128)S(1)} %add.101), channel_id=1, source_target_pairs={{0,32},{8,40},{16,48},{24,56},{32,0},{40,8},{48,16},{56,24},{1,33}... | collective-permute-start | bytes 24584 | tf_op jit(solution)/shard_map/ppermute | solution.py:66
  145.8 9.8 %custom-call.8 = f32[1,128,128]{1,2,0:T(8,128)S(1)} custom-call(f32[1,128,128]{2,1,0:T(8,128)S(1)} %fusion.8), custom_call_target="InvertDiagBlocksLowerTriangular" | custom-call | tf_op jit(solution)/shard_map/triangular_solve | solution.py:13
  156.7 2.6 %collective-permute-done.24 = f32[128,16]{0,1:T(8,128)S(1)} collective-permute-done((f32[128,16]{0,1:T(8,128)S(1)}, f32[128,16]{0,1:T(8,128)S(1)}, u32[]{:S(2)}, u32[]{:S(2)}) %collective-permute-start.24) | collective-permute-done | bytes 8224 | tf_op jit(solution)/shard_map/ppermute | solution.py:66
  159.3 9.9 %collective-permute-start.25 = (f32[128,16]{0,1:T(8,128)S(1)}, f32[128,16]{0,1:T(8,128)S(1)}, u32[]{:S(2)}, u32[]{:S(2)}) collective-permute-start(f32[128,16]{0,1:T(8,128)S(1)} %add.103), channel_id=1, source_target_pairs={{0,128},{64,192},{128,0},{192,64},{1,129},{65,193},{129,1},{193,65... | collective-permute-start | bytes 24584 | tf_op jit(solution)/shard_map/ppermute | solution.py:66
  169.2 2.9 %collective-permute-start.9 = (f32[1536,16]{0,1:T(8,128)S(1)}, f32[1536,16]{0,1:T(8,128)S(1)}, u32[]{:S(2)}, u32[]{:S(2)}) collective-permute-start(f32[1536,16]{0,1:T(8,128)S(1)} %pad_maximum_fusion.5), channel_id=1, source_target_pairs={{0,128},{64,192},{128,0},{192,64},{1,129},{65,193},{129,1},{193,65... | collective-permute-start | bytes 294920 | tf_op jit(solution)/shard_map/ppermute | solution.py:76
  172.1 1.5 collective-permute-done.25
  175.5 1.4 maximum_subtract_fusion
  176.9 3.4 %multiply_convert_fusion = bf16[3072,128,16]{0,2,1:T(8,128)(2,1)S(1)} fusion(f32[3072,16]{0,1:T(8,128)S(1)} %maximum_subtract_fusion, f32[3072,128]{0,1:T(8,128)S(1)} %copy.7), kind=kLoop, calls=%fused_computation | loop fusion | flops 12582912 | bytes 14352384 | tf_op jit(solution)/shard_map/convert_element_type | solution.py:154
  180.3 6.7 %fusion.17 = f32[2048,512]{0,1:T(8,128)S(1)} fusion(bf16[3072,2048]{0,1:T(8,128)(2,1)S(1)} %bitcast.39, bf16[3072,512]{0,1:T(8,128)(2,1)S(1)} %bitcast.41), kind=kOutput, calls=%fused_computation.75 | convolution fusion | flops 6442450944 | bytes 19922944 | tf_op jit(solution)/shard_map/dot_general | solution.py:118
  187.5 4.1 %collective-permute-done.26 = f32[2048,256]{0,1:T(8,128)S(1)} collective-permute-done((f32[2048,256]{0,1:T(8,128)S(1)}, f32[2048,256]{0,1:T(8,128)S(1)}, u32[]{:S(2)}, u32[]{:S(2)}) %collective-permute-start.26) | collective-permute-done | bytes 2097184 | tf_op jit(solution)/shard_map/ppermute | solution.py:107
  193.2 24.4 %collective-permute-done.27 = f32[2048,128]{0,1:T(8,128)S(1)} collective-permute-done((f32[2048,128]{0,1:T(8,128)S(1)}, f32[2048,128]{0,1:T(8,128)S(1)}, u32[]{:S(2)}, u32[]{:S(2)}) %collective-permute-start.27) | collective-permute-done | bytes 1048608 | tf_op jit(solution)/shard_map/ppermute | solution.py:107
  217.9 1.5 collective-permute-start.28
  219.4 13.2 %collective-permute-done.28 = f32[64,2048]{1,0:T(8,128)S(1)} collective-permute-done((f32[64,2048]{1,0:T(8,128)S(1)}, f32[64,2048]{1,0:T(8,128)S(1)}, u32[]{:S(2)}, u32[]{:S(2)}) %collective-permute-start.28) | collective-permute-done | bytes 524320 | tf_op jit(solution)/shard_map/ppermute | solution.py:107
  234.0 5.5 %collective-permute-done.29 = f32[32,2048]{1,0:T(8,128)S(1)} collective-permute-done((f32[32,2048]{1,0:T(8,128)S(1)}, f32[32,2048]{1,0:T(8,128)S(1)}, u32[]{:S(2)}, u32[]{:S(2)}) %collective-permute-start.29) | collective-permute-done | bytes 262176 | tf_op jit(solution)/shard_map/ppermute | solution.py:107
  239.6 8.0 %collective-permute-done.30 = f32[16,2048]{1,0:T(8,128)S(1)} collective-permute-done((f32[16,2048]{1,0:T(8,128)S(1)}, f32[16,2048]{1,0:T(8,128)S(1)}, u32[]{:S(2)}, u32[]{:S(2)}) %collective-permute-start.30) | collective-permute-done | bytes 131104 | tf_op jit(solution)/shard_map/ppermute | solution.py:107
  247.7 8.2 %collective-permute-done.31 = f32[8,2048]{1,0:T(8,128)S(1)} collective-permute-done((f32[8,2048]{1,0:T(8,128)S(1)}, f32[8,2048]{1,0:T(8,128)S(1)}, u32[]{:S(2)}, u32[]{:S(2)}) %collective-permute-start.31) | collective-permute-done | bytes 65568 | tf_op jit(solution)/shard_map/ppermute | solution.py:107
  (100 shorter events, 21.3 us)
Async XLA Ops:
  0.0 66.7 %copy-start = (s32[16,3072]{1,0:T(8,128)S(1)}, s32[16,3072]{1,0:T(8,128)}, u32[]{:S(2)}) copy-start(s32[16,3072]{1,0:T(8,128)} %param.6) | copy-start | bytes 589828
  0.0 1.4 collective-permute-start
  2.1 4.0 %collective-permute-start.1 = (f32[1536]{0:T(1024)S(1)}, f32[1536]{0:T(1024)S(1)}, u32[]{:S(2)}, u32[]{:S(2)}) collective-permute-start(f32[1536]{0:T(1024)S(1)} %pad_maximum_fusion.9), channel_id=1, source_target_pairs={{0,2},{2,0},{4,6},{6,4},{1,3},{3,1},{5,7},{7,5},{8,10},{10,8},{12,... | collective-permute-start | bytes 18440 | tf_op jit(solution)/shard_map/ppermute | solution.py:76
  6.1 5.3 %collective-permute-start.2 = (f32[3072]{0:T(1024)S(1)}, f32[3072]{0:T(1024)S(1)}, u32[]{:S(2)}, u32[]{:S(2)}) collective-permute-start(f32[3072]{0:T(1024)S(1)} %pad_maximum_fusion.8), channel_id=1, source_target_pairs={{0,4},{2,6},{4,0},{6,2},{1,5},{3,7},{5,1},{7,3},{8,12},{10,14},{12... | collective-permute-start | bytes 36872 | tf_op jit(solution)/shard_map/ppermute | solution.py:76
  11.4 3.9 %collective-permute-start.3 = (f32[6144]{0:T(1024)S(1)}, f32[6144]{0:T(1024)S(1)}, u32[]{:S(2)}, u32[]{:S(2)}) collective-permute-start(f32[6144]{0:T(1024)S(1)} %pad_maximum_fusion.7), channel_id=1, source_target_pairs={{0,8},{8,0},{16,24},{24,16},{32,40},{40,32},{48,56},{56,48},{1,9},... | collective-permute-start | bytes 73736 | tf_op jit(solution)/shard_map/ppermute | solution.py:76
  15.3 5.5 %collective-permute-start.4 = (f32[12288]{0:T(1024)S(1)}, f32[12288]{0:T(1024)S(1)}, u32[]{:S(2)}, u32[]{:S(2)}) collective-permute-start(f32[12288]{0:T(1024)S(1)} %pad_maximum_fusion.6), channel_id=1, source_target_pairs={{0,16},{8,24},{16,0},{24,8},{32,48},{40,56},{48,32},{56,40},{1,17}... | collective-permute-start | bytes 147464 | tf_op jit(solution)/shard_map/ppermute | solution.py:76
  20.8 10.8 %collective-permute-start.5 = (f32[24576]{0:T(1024)S(1)}, f32[24576]{0:T(1024)S(1)}, u32[]{:S(2)}, u32[]{:S(2)}) collective-permute-start(f32[24576]{0:T(1024)S(1)} %pad_maximum_fusion.4), channel_id=1, source_target_pairs={{0,32},{8,40},{16,48},{24,56},{32,0},{40,8},{48,16},{56,24},{1,33}... | collective-permute-start | bytes 294920 | tf_op jit(solution)/shard_map/ppermute | solution.py:76
  31.7 5.8 %collective-permute-start.6 = (f32[49152]{0:T(1024)S(1)}, f32[49152]{0:T(1024)S(1)}, u32[]{:S(2)}, u32[]{:S(2)}) collective-permute-start(f32[49152]{0:T(1024)S(1)} %pad_maximum_fusion.3), channel_id=1, source_target_pairs={{0,64},{64,0},{128,192},{192,128},{1,65},{65,1},{129,193},{193,129... | collective-permute-start | bytes 589832 | tf_op jit(solution)/shard_map/ppermute | solution.py:76
  35.3 1.3 collective-permute-start.10
  36.6 4.4 %collective-permute-start.11 = (f32[128,128]{1,0:T(8,128)S(1)}, f32[128,128]{1,0:T(8,128)S(1)}, u32[]{:S(2)}, u32[]{:S(2)}) collective-permute-start(f32[128,128]{1,0:T(8,128)S(1)} %add.87), channel_id=1, source_target_pairs={{0,2},{2,0},{4,6},{6,4},{1,3},{3,1},{5,7},{7,5},{8,10},{10,8},{12,... | collective-permute-start | bytes 196616 | tf_op jit(solution)/shard_map/ppermute | solution.py:66
  37.5 36.0 %collective-permute-start.7 = (f32[98304]{0:T(1024)S(1)}, f32[98304]{0:T(1024)S(1)}, u32[]{:S(2)}, u32[]{:S(2)}) collective-permute-start(f32[98304]{0:T(1024)S(1)} %pad_maximum_fusion.2), channel_id=1, source_target_pairs={{0,128},{64,192},{128,0},{192,64},{1,129},{65,193},{129,1},{193,65... | collective-permute-start | bytes 1179656 | tf_op jit(solution)/shard_map/ppermute | solution.py:76
  41.0 5.9 %collective-permute-start.12 = (f32[128,128]{1,0:T(8,128)S(1)}, f32[128,128]{1,0:T(8,128)S(1)}, u32[]{:S(2)}, u32[]{:S(2)}) collective-permute-start(f32[128,128]{1,0:T(8,128)S(1)} %add.88), channel_id=1, source_target_pairs={{0,4},{2,6},{4,0},{6,2},{1,5},{3,7},{5,1},{7,3},{8,12},{10,14},{12... | collective-permute-start | bytes 196616 | tf_op jit(solution)/shard_map/ppermute | solution.py:66
  46.9 4.4 %collective-permute-start.13 = (f32[128,128]{1,0:T(8,128)S(1)}, f32[128,128]{1,0:T(8,128)S(1)}, u32[]{:S(2)}, u32[]{:S(2)}) collective-permute-start(f32[128,128]{1,0:T(8,128)S(1)} %add.89), channel_id=1, source_target_pairs={{0,8},{8,0},{16,24},{24,16},{32,40},{40,32},{48,56},{56,48},{1,9},... | collective-permute-start | bytes 196616 | tf_op jit(solution)/shard_map/ppermute | solution.py:66
  51.2 6.0 %collective-permute-start.14 = (f32[128,128]{1,0:T(8,128)S(1)}, f32[128,128]{1,0:T(8,128)S(1)}, u32[]{:S(2)}, u32[]{:S(2)}) collective-permute-start(f32[128,128]{1,0:T(8,128)S(1)} %add.90), channel_id=1, source_target_pairs={{0,16},{8,24},{16,0},{24,8},{32,48},{40,56},{48,32},{56,40},{1,17}... | collective-permute-start | bytes 196616 | tf_op jit(solution)/shard_map/ppermute | solution.py:66
  57.2 9.0 %collective-permute-start.15 = (f32[128,128]{1,0:T(8,128)S(1)}, f32[128,128]{1,0:T(8,128)S(1)}, u32[]{:S(2)}, u32[]{:S(2)}) collective-permute-start(f32[128,128]{1,0:T(8,128)S(1)} %add.91), channel_id=1, source_target_pairs={{0,32},{8,40},{16,48},{24,56},{32,0},{40,8},{48,16},{56,24},{1,33}... | collective-permute-start | bytes 196616 | tf_op jit(solution)/shard_map/ppermute | solution.py:66
  66.2 4.4 %collective-permute-start.16 = (f32[128,128]{1,0:T(8,128)S(1)}, f32[128,128]{1,0:T(8,128)S(1)}, u32[]{:S(2)}, u32[]{:S(2)}) collective-permute-start(f32[128,128]{1,0:T(8,128)S(1)} %add.92), channel_id=1, source_target_pairs={{0,64},{64,0},{128,192},{192,128},{1,65},{65,1},{129,193},{193,129... | collective-permute-start | bytes 196616 | tf_op jit(solution)/shard_map/ppermute | solution.py:66
  70.5 41.9 %collective-permute-start.17 = (f32[128,128]{1,0:T(8,128)S(1)}, f32[128,128]{1,0:T(8,128)}, u32[]{:S(2)}, u32[]{:S(2)}) collective-permute-start(f32[128,128]{1,0:T(8,128)S(1)} %add.93), channel_id=1, source_target_pairs={{0,128},{64,192},{128,0},{192,64},{1,129},{65,193},{129,1},{193,65... | collective-permute-start | bytes 196616 | tf_op jit(solution)/shard_map/ppermute | solution.py:66
  74.3 24.6 %copy-start.1 = (f32[3072,128]{1,0:T(8,128)S(1)}, f32[3072,128]{1,0:T(8,128)}, u32[]{:S(2)}) copy-start(f32[3072,128]{1,0:T(8,128)} %param.5) | copy-start | bytes 4718596
  99.2 12.8 %collective-permute-start.18 = (f32[128,16]{0,1:T(8,128)S(1)}, f32[128,16]{0,1:T(8,128)S(1)}, u32[]{:S(2)}, u32[]{:S(2)}) collective-permute-start(f32[128,16]{0,1:T(8,128)S(1)} %fusion.4), channel_id=1, source_target_pairs={{0,1},{1,0},{2,3},{3,2},{4,5},{5,4},{6,7},{7,6},{8,9},{9,8},{10,11... | collective-permute-start | bytes 24584 | tf_op jit(solution)/shard_map/ppermute | solution.py:66
  112.0 3.7 %collective-permute-start.19 = (f32[128,16]{0,1:T(8,128)S(1)}, f32[128,16]{0,1:T(8,128)S(1)}, u32[]{:S(2)}, u32[]{:S(2)}) collective-permute-start(f32[128,16]{0,1:T(8,128)S(1)} %add.97), channel_id=1, source_target_pairs={{0,2},{2,0},{4,6},{6,4},{1,3},{3,1},{5,7},{7,5},{8,10},{10,8},{12,... | collective-permute-start | bytes 24584 | tf_op jit(solution)/shard_map/ppermute | solution.py:66
  115.6 15.2 %collective-permute-start.20 = (f32[128,16]{0,1:T(8,128)S(1)}, f32[128,16]{0,1:T(8,128)S(1)}, u32[]{:S(2)}, u32[]{:S(2)}) collective-permute-start(f32[128,16]{0,1:T(8,128)S(1)} %add.98), channel_id=1, source_target_pairs={{0,4},{2,6},{4,0},{6,2},{1,5},{3,7},{5,1},{7,3},{8,12},{10,14},{12... | collective-permute-start | bytes 24584 | tf_op jit(solution)/shard_map/ppermute | solution.py:66
  130.9 3.7 %collective-permute-start.21 = (f32[128,16]{0,1:T(8,128)S(1)}, f32[128,16]{0,1:T(8,128)S(1)}, u32[]{:S(2)}, u32[]{:S(2)}) collective-permute-start(f32[128,16]{0,1:T(8,128)S(1)} %add.99), channel_id=1, source_target_pairs={{0,8},{8,0},{16,24},{24,16},{32,40},{40,32},{48,56},{56,48},{1,9},... | collective-permute-start | bytes 24584 | tf_op jit(solution)/shard_map/ppermute | solution.py:66
  134.6 4.5 %collective-permute-start.22 = (f32[128,16]{0,1:T(8,128)S(1)}, f32[128,16]{0,1:T(8,128)S(1)}, u32[]{:S(2)}, u32[]{:S(2)}) collective-permute-start(f32[128,16]{0,1:T(8,128)S(1)} %add.100), channel_id=1, source_target_pairs={{0,16},{8,24},{16,0},{24,8},{32,48},{40,56},{48,32},{56,40},{1,17}... | collective-permute-start | bytes 24584 | tf_op jit(solution)/shard_map/ppermute | solution.py:66
  135.3 20.7 %collective-permute-start.8 = (f32[768,16]{0,1:T(8,128)S(1)}, f32[768,16]{0,1:T(8,128)}, u32[]{:S(2)}, u32[]{:S(2)}) collective-permute-start(f32[768,16]{0,1:T(8,128)S(1)} %bitcast.42), channel_id=1, source_target_pairs={{0,64},{64,0},{128,192},{192,128},{1,65},{65,1},{129,193},{193,129... | collective-permute-start | bytes 147464 | tf_op jit(solution)/shard_map/ppermute | solution.py:76
  139.2 16.4 %collective-permute-start.23 = (f32[128,16]{0,1:T(8,128)S(1)}, f32[128,16]{0,1:T(8,128)S(1)}, u32[]{:S(2)}, u32[]{:S(2)}) collective-permute-start(f32[128,16]{0,1:T(8,128)S(1)} %add.101), channel_id=1, source_target_pairs={{0,32},{8,40},{16,48},{24,56},{32,0},{40,8},{48,16},{56,24},{1,33}... | collective-permute-start | bytes 24584 | tf_op jit(solution)/shard_map/ppermute | solution.py:66
  155.6 3.7 %collective-permute-start.24 = (f32[128,16]{0,1:T(8,128)S(1)}, f32[128,16]{0,1:T(8,128)S(1)}, u32[]{:S(2)}, u32[]{:S(2)}) collective-permute-start(f32[128,16]{0,1:T(8,128)S(1)} %add.102), channel_id=1, source_target_pairs={{0,64},{64,0},{128,192},{192,128},{1,65},{65,1},{129,193},{193,129... | collective-permute-start | bytes 24584 | tf_op jit(solution)/shard_map/ppermute | solution.py:66
  159.3 14.3 %collective-permute-start.25 = (f32[128,16]{0,1:T(8,128)S(1)}, f32[128,16]{0,1:T(8,128)S(1)}, u32[]{:S(2)}, u32[]{:S(2)}) collective-permute-start(f32[128,16]{0,1:T(8,128)S(1)} %add.103), channel_id=1, source_target_pairs={{0,128},{64,192},{128,0},{192,64},{1,129},{65,193},{129,1},{193,65... | collective-permute-start | bytes 24584 | tf_op jit(solution)/shard_map/ppermute | solution.py:66
  169.2 6.2 %collective-permute-start.9 = (f32[1536,16]{0,1:T(8,128)S(1)}, f32[1536,16]{0,1:T(8,128)S(1)}, u32[]{:S(2)}, u32[]{:S(2)}) collective-permute-start(f32[1536,16]{0,1:T(8,128)S(1)} %pad_maximum_fusion.5), channel_id=1, source_target_pairs={{0,128},{64,192},{128,0},{192,64},{1,129},{65,193},{129,1},{193,65... | collective-permute-start | bytes 294920 | tf_op jit(solution)/shard_map/ppermute | solution.py:76
  176.9 3.4 %copy-start.2 = (bf16[3072,2,2,2,2,2,2,8]{0,7,6,5,4,3,2,1:T(8,128)(2,1)S(1)}, bf16[3072,2,2,2,2,2,2,8]{0,7,6,5,4,3,2,1:T(8,128)(2,1)}, u32[]{:S(2)}) copy-start(bf16[3072,2,2,2,2,2,2,8]{0,7,6,5,4,3,2,1:T(8,128)(2,1)} %copy.12) | copy-start | bytes 9437188
  187.4 4.2 %collective-permute-start.26 = (f32[2048,256]{0,1:T(8,128)S(1)}, f32[2048,256]{0,1:T(8,128)S(1)}, u32[]{:S(2)}, u32[]{:S(2)}) collective-permute-start(f32[2048,256]{0,1:T(8,128)S(1)} %slice_select_fusion), channel_id=1, source_target_pairs={{0,1},{1,0},{2,3},{3,2},{4,5},{5,4},{6,7},{7,6},{8,9},{9,8},{10,11... | collective-permute-start | bytes 6291464 | tf_op jit(solution)/shard_map/ppermute | solution.py:107
  192.3 25.3 %collective-permute-start.27 = (f32[2048,128]{0,1:T(8,128)S(1)}, f32[2048,128]{0,1:T(8,128)S(1)}, u32[]{:S(2)}, u32[]{:S(2)}) collective-permute-start(f32[2048,128]{0,1:T(8,128)S(1)} %slice_select_fusion.1), channel_id=1, source_target_pairs={{0,2},{2,0},{4,6},{6,4},{1,3},{3,1},{5,7},{7,5},{8,10},{10,8},{12,... | collective-permute-start | bytes 3145736 | tf_op jit(solution)/shard_map/ppermute | solution.py:107
  217.9 14.7 %collective-permute-start.28 = (f32[64,2048]{1,0:T(8,128)S(1)}, f32[64,2048]{1,0:T(8,128)S(1)}, u32[]{:S(2)}, u32[]{:S(2)}) collective-permute-start(f32[64,2048]{1,0:T(8,128)S(1)} %slice_select_fusion.2), channel_id=1, source_target_pairs={{0,4},{2,6},{4,0},{6,2},{1,5},{3,7},{5,1},{7,3},{8,12},{10,14},{12... | collective-permute-start | bytes 1572872 | tf_op jit(solution)/shard_map/ppermute | solution.py:107
  232.7 6.7 %collective-permute-start.29 = (f32[32,2048]{1,0:T(8,128)S(1)}, f32[32,2048]{1,0:T(8,128)S(1)}, u32[]{:S(2)}, u32[]{:S(2)}) collective-permute-start(f32[32,2048]{1,0:T(8,128)S(1)} %slice_select_fusion.3), channel_id=1, source_target_pairs={{0,8},{8,0},{16,24},{24,16},{32,40},{40,32},{48,56},{56,48},{1,9},... | collective-permute-start | bytes 786440 | tf_op jit(solution)/shard_map/ppermute | solution.py:107
  239.5 8.1 %collective-permute-start.30 = (f32[16,2048]{1,0:T(8,128)S(1)}, f32[16,2048]{1,0:T(8,128)S(1)}, u32[]{:S(2)}, u32[]{:S(2)}) collective-permute-start(f32[16,2048]{1,0:T(8,128)S(1)} %slice_select_fusion.4), channel_id=1, source_target_pairs={{0,16},{8,24},{16,0},{24,8},{32,48},{40,56},{48,32},{56,40},{1,17}... | collective-permute-start | bytes 393224 | tf_op jit(solution)/shard_map/ppermute | solution.py:107
  247.6 8.3 %collective-permute-start.31 = (f32[8,2048]{1,0:T(8,128)S(1)}, f32[8,2048]{1,0:T(8,128)S(1)}, u32[]{:S(2)}, u32[]{:S(2)}) collective-permute-start(f32[8,2048]{1,0:T(8,128)S(1)} %slice_select_fusion.5), channel_id=1, source_target_pairs={{0,32},{8,40},{16,48},{24,56},{32,0},{40,8},{48,16},{56,24},{1,33}... | collective-permute-start | bytes 196616 | tf_op jit(solution)/shard_map/ppermute | solution.py:107

commit v7 on v6

--- a/solution.py
+++ b/solution.py
@@ -107,8 +107,22 @@
     return mine + lax.ppermute(send, axis, flip)
 
 
+def halve_bit(cur, names, name):
+    position = len(names) - 1 - names.index(name) + 3
+    rows, cols = cur.shape
+    axis, level = name
+    size = lax.axis_size(axis)
+    bit = (lax.axis_index(axis) >> level) & 1
+    flip = [(i, i ^ (1 << level)) for i in range(size)]
+    split = cur.reshape(rows >> (position + 1), 2, 1 << position, cols)
+    low, high = split[:, 0], split[:, 1]
+    send = jnp.where(bit == 0, high, low)
+    mine = jnp.where(bit == 0, low, high)
+    kept = mine + lax.ppermute(send, axis, flip)
+    return kept.reshape(rows // 2, cols), [n for n in names if n != name]
+
+
 def halving_scores(weighted, genotypes):
-    bits = split_bits()
     local_rows, variants = genotypes.shape
     nz, nx, nc = (lax.axis_size(a) for a in SAMP)
     own_rows = variants // (nz * nx * nc)
@@ -116,13 +130,18 @@
     order = order.transpose(0, 6, 5, 4, 3, 2, 1, 7)
     dosages = order.reshape(local_rows, variants).astype(jnp.bfloat16)
     cur = jnp.dot(weighted.T, dosages, preferred_element_type=jnp.float32)
-    for axis, level in bits[:2]:
-        half = cur.shape[1] // 2
-        cur = exchange(cur[:, :half], cur[:, half:], axis, level, 1)
-    cur = cur.T
-    for axis, level in bits[2:]:
-        half = cur.shape[0] // 2
-        cur = exchange(cur[:half], cur[half:], axis, level, 0)
+    half = cur.shape[1] // 2
+    cur = exchange(cur[:, :half], cur[:, half:], "core", 0, 1).T
+    names = [("x", 0), ("x", 1), ("z", 0), ("z", 1), ("z", 2)]
+    cols = cur.shape[1] // 2
+    part_a, names_a = cur[:, :cols], list(names)
+    part_b, names_b = cur[:, cols:], list(names)
+    plan = [(("x", 0), ("z", 0)), (("z", 0), ("x", 0)), (("x", 1), ("z", 1)), (("z", 1), ("x", 1))]
+    for step_a, step_b in plan:
+        part_a, names_a = halve_bit(part_a, names_a, step_a)
+        part_b, names_b = halve_bit(part_b, names_b, step_b)
+    cur = jnp.concatenate([part_a, part_b], axis=1)
+    cur, _ = halve_bit(cur, names_a, ("z", 2))
     return cur
 
 

time: 262 us -> 245 us (0.935)
  the two profiles are of different devices: /device:TPU:2 before, /device:TPU:6 now
where the time goes in v7:
time: 245 us; the launch traced here: 240 us
  waiting for transfers between devices  93.4 us (38%)
  starting transfers between devices  64.2 us (26%)
  other arithmetic  38.9 us (16%)
  Pallas kernels  21.3 us (9%)
  local copies, waits for them, and re-layouts  11.2 us (5%)
  matrix products  10.7 us (4%)
    ppermute x9, waiting for transfers between devices, halve_bit(): kept = mine + lax.ppermute(send, axis, flip)  40.5 us
    ppermute x16, waiting for transfers between devices, doubling_psum(): x = x + lax.ppermute(x, axis, pairs)  33 us
    ppermute x16, starting transfers between devices, doubling_psum(): x = x + lax.ppermute(x, axis, pairs)  32.8 us
    ppermute x10, starting transfers between devices, doubling_gather(): other = lax.ppermute(x, axis, flip)  24.4 us
    pallas_call x1, Pallas kernels, gather_pheno(): pl.pallas_call(gather_body, grid=(count // TILE,), in_specs=[pl.BlockSpec...  21.3 us
    ppermute x10, waiting for transfers between devices, doubling_gather(): other = lax.ppermute(x, axis, flip)  15.7 us
    another operation x3, other arithmetic, per_device(): factor = jnp.linalg.cholesky(system)  13.2 us
    another operation x2, other arithmetic, chol_solve(): lax.linalg.triangular_solve(factor, middle, left_side=True, lower=True, t...  10.5 us
  transfers between devices with their start and end apart: 36, of which 26 were waited for; matrix products, arithmetic and copies ran while one was open for 19% of the time, Pallas kernels for 9%

profile of v7, /device:TPU:6, one launch (start us, length us, event | category | flops | bytes accessed | tf_op | source)
XLA Modules:
  0.0 240.4 jit_solution(16645318361332931239)
XLA Ops:
  3.0 2.8 %collective-permute-done.1 = f32[1536]{0:T(1024)S(1)} collective-permute-done((f32[1536]{0:T(1024)S(1)}, f32[1536]{0:T(1024)S(1)}, u32[]{:S(2)}, u32[]{:S(2)}) %collective-permute-start.1) | collective-permute-done | bytes 6176 | tf_op jit(solution)/shard_map/ppermute | solution.py:76
  5.8 1.7 collective-permute-start.2
  7.5 3.6 %collective-permute-done.2 = f32[3072]{0:T(1024)S(1)} collective-permute-done((f32[3072]{0:T(1024)S(1)}, f32[3072]{0:T(1024)S(1)}, u32[]{:S(2)}, u32[]{:S(2)}) %collective-permute-start.2) | collective-permute-done | bytes 12320 | tf_op jit(solution)/shard_map/ppermute | solution.py:76
  11.1 2.0 collective-permute-start.3
  13.1 1.9 collective-permute-done.3
  15.1 3.6 %collective-permute-start.4 = (f32[12288]{0:T(1024)S(1)}, f32[12288]{0:T(1024)S(1)}, u32[]{:S(2)}, u32[]{:S(2)}) collective-permute-start(f32[12288]{0:T(1024)S(1)} %pad_maximum_fusion.7), channel_id=1, source_target_pairs={{0,16},{8,24},{16,0},{24,8},{32,48},{40,56},{48,32},{56,40},{1,17}... | collective-permute-start | bytes 147464 | tf_op jit(solution)/shard_map/ppermute | solution.py:76
  18.7 2.1 collective-permute-done.4
  20.8 8.2 %collective-permute-start.5 = (f32[24576]{0:T(1024)S(1)}, f32[24576]{0:T(1024)S(1)}, u32[]{:S(2)}, u32[]{:S(2)}) collective-permute-start(f32[24576]{0:T(1024)S(1)} %pad_maximum_fusion.4), channel_id=1, source_target_pairs={{0,32},{8,40},{16,48},{24,56},{32,0},{40,8},{48,16},{56,24},{1,33}... | collective-permute-start | bytes 294920 | tf_op jit(solution)/shard_map/ppermute | solution.py:76
  29.0 2.6 %collective-permute-done.5 = f32[24576]{0:T(1024)S(1)} collective-permute-done((f32[24576]{0:T(1024)S(1)}, f32[24576]{0:T(1024)S(1)}, u32[]{:S(2)}, u32[]{:S(2)}) %collective-permute-start.5) | collective-permute-done | bytes 98336 | tf_op jit(solution)/shard_map/ppermute | solution.py:76
  31.7 1.7 collective-permute-start.6
  33.3 1.9 fusion.8
  37.6 3.2 %collective-permute-start.7 = (f32[98304]{0:T(1024)S(1)}, f32[98304]{0:T(1024)S(1)}, u32[]{:S(2)}, u32[]{:S(2)}) collective-permute-start(f32[98304]{0:T(1024)S(1)} %pad_maximum_fusion.2), channel_id=1, source_target_pairs={{0,128},{64,192},{128,0},{192,64},{1,129},{65,193},{129,1},{193,65... | collective-permute-start | bytes 1179656 | tf_op jit(solution)/shard_map/ppermute | solution.py:76
  41.0 1.5 collective-permute-start.12
  42.5 4.4 %collective-permute-done.12 = f32[128,128]{1,0:T(8,128)S(1)} collective-permute-done((f32[128,128]{1,0:T(8,128)S(1)}, f32[128,128]{1,0:T(8,128)S(1)}, u32[]{:S(2)}, u32[]{:S(2)}) %collective-permute-start.12) | collective-permute-done | bytes 65568 | tf_op jit(solution)/shard_map/ppermute | solution.py:66
  47.8 3.5 %collective-permute-done.13 = f32[128,128]{1,0:T(8,128)S(1)} collective-permute-done((f32[128,128]{1,0:T(8,128)S(1)}, f32[128,128]{1,0:T(8,128)S(1)}, u32[]{:S(2)}, u32[]{:S(2)}) %collective-permute-start.13) | collective-permute-done | bytes 65568 | tf_op jit(solution)/shard_map/ppermute | solution.py:66
  52.0 5.2 %collective-permute-done.14 = f32[128,128]{1,0:T(8,128)S(1)} collective-permute-done((f32[128,128]{1,0:T(8,128)S(1)}, f32[128,128]{1,0:T(8,128)S(1)}, u32[]{:S(2)}, u32[]{:S(2)}) %collective-permute-start.14) | collective-permute-done | bytes 65568 | tf_op jit(solution)/shard_map/ppermute | solution.py:66
  57.2 6.7 %collective-permute-start.15 = (f32[128,128]{1,0:T(8,128)S(1)}, f32[128,128]{1,0:T(8,128)S(1)}, u32[]{:S(2)}, u32[]{:S(2)}) collective-permute-start(f32[128,128]{1,0:T(8,128)S(1)} %add.103), channel_id=1, source_target_pairs={{0,32},{8,40},{16,48},{24,56},{32,0},{40,8},{48,16},{56,24},{1,33}... | collective-permute-start | bytes 196616 | tf_op jit(solution)/shard_map/ppermute | solution.py:66
  63.9 2.2 collective-permute-done.15
  67.3 3.2 %collective-permute-done.16 = f32[128,128]{1,0:T(8,128)S(1)} collective-permute-done((f32[128,128]{1,0:T(8,128)S(1)}, f32[128,128]{1,0:T(8,128)S(1)}, u32[]{:S(2)}, u32[]{:S(2)}) %collective-permute-start.16) | collective-permute-done | bytes 65568 | tf_op jit(solution)/shard_map/ppermute | solution.py:66
  70.5 2.9 %collective-permute-start.17 = (f32[128,128]{1,0:T(8,128)S(1)}, f32[128,128]{1,0:T(8,128)}, u32[]{:S(2)}, u32[]{:S(2)}) collective-permute-start(f32[128,128]{1,0:T(8,128)S(1)} %add.105), channel_id=1, source_target_pairs={{0,128},{64,192},{128,0},{192,64},{1,129},{65,193},{129,1},{193,65... | collective-permute-start | bytes 196616 | tf_op jit(solution)/shard_map/ppermute | solution.py:66
  75.3 21.3 %shard_map.46 = f32[1,12288]{1,0:T(1,128)} custom-call(s32[1,12288]{1,0:T(1,128)} %bitcast.161, bf16[768,768]{1,0:T(8,128)(2,1)} %pad_maximum_fusion.tab_ref), custom_call_target="tpu_custom_call" | custom-call | tf_op jit(solution)/shard_map/pallas_call | solution.py:46
  97.2 1.6 reduce.9
  99.9 6.6 %copy.37 = s32[3072,512]{0,1:T(8,128)} copy(s32[3072,512]{1,0:T(8,128)} %param.7) | data formatting | bytes 12582912 | tf_op args[3]
  106.6 3.5 %convert_element_type.51 = bf16[3072,512]{0,1:T(8,128)(2,1)S(1)} convert(s32[3072,512]{0,1:T(8,128)} %copy.37) | non-fusion elementwise | flops 1572864 | bytes 9437184 | tf_op jit(solution)/shard_map/convert_element_type | solution.py:131
  110.1 1.8 copy.38
  113.8 1.8 collective-permute-done.19
  115.6 1.5 collective-permute-start.20
  117.7 12.5 %cholesky.16 = f32[128,128]{1,0:T(8,128)S(1)} custom-call(f32[128,128]{1,0:T(8,128)} %fusion.25), custom_call_target="Cholesky" | custom-call | tf_op jit(solution)/shard_map/jit(cholesky)/cholesky | solution.py:161
  130.7 3.3 %collective-permute-done.21 = f32[128,16]{0,1:T(8,128)S(1)} collective-permute-done((f32[128,16]{0,1:T(8,128)S(1)}, f32[128,16]{0,1:T(8,128)S(1)}, u32[]{:S(2)}, u32[]{:S(2)}) %collective-permute-start.21) | collective-permute-done | bytes 8224 | tf_op jit(solution)/shard_map/ppermute | solution.py:66
  134.8 3.8 %collective-permute-done.22 = f32[128,16]{0,1:T(8,128)S(1)} collective-permute-done((f32[128,16]{0,1:T(8,128)S(1)}, f32[128,16]{0,1:T(8,128)S(1)}, u32[]{:S(2)}, u32[]{:S(2)}) %collective-permute-start.22) | collective-permute-done | bytes 8224 | tf_op jit(solution)/shard_map/ppermute | solution.py:66
  138.6 5.9 %collective-permute-start.23 = (f32[128,16]{0,1:T(8,128)S(1)}, f32[128,16]{0,1:T(8,128)S(1)}, u32[]{:S(2)}, u32[]{:S(2)}) collective-permute-start(f32[128,16]{0,1:T(8,128)S(1)} %add.113), channel_id=1, source_target_pairs={{0,32},{8,40},{16,48},{24,56},{32,0},{40,8},{48,16},{56,24},{1,33}... | collective-permute-start | bytes 24584 | tf_op jit(solution)/shard_map/ppermute | solution.py:66
  145.2 9.8 %custom-call.8 = f32[1,128,128]{1,2,0:T(8,128)S(1)} custom-call(f32[1,128,128]{2,1,0:T(8,128)S(1)} %fusion.16), custom_call_target="InvertDiagBlocksLowerTriangular" | custom-call | tf_op jit(solution)/shard_map/triangular_solve | solution.py:13
  156.1 2.7 %collective-permute-done.24 = f32[128,16]{0,1:T(8,128)S(1)} collective-permute-done((f32[128,16]{0,1:T(8,128)S(1)}, f32[128,16]{0,1:T(8,128)S(1)}, u32[]{:S(2)}, u32[]{:S(2)}) %collective-permute-start.24) | collective-permute-done | bytes 8224 | tf_op jit(solution)/shard_map/ppermute | solution.py:66
  158.8 9.3 %collective-permute-start.25 = (f32[128,16]{0,1:T(8,128)S(1)}, f32[128,16]{0,1:T(8,128)S(1)}, u32[]{:S(2)}, u32[]{:S(2)}) collective-permute-start(f32[128,16]{0,1:T(8,128)S(1)} %add.115), channel_id=1, source_target_pairs={{0,128},{64,192},{128,0},{192,64},{1,129},{65,193},{129,1},{193,65... | collective-permute-start | bytes 24584 | tf_op jit(solution)/shard_map/ppermute | solution.py:66
  168.1 3.0 %collective-permute-start.9 = (f32[1536,16]{0,1:T(8,128)S(1)}, f32[1536,16]{0,1:T(8,128)S(1)}, u32[]{:S(2)}, u32[]{:S(2)}) collective-permute-start(f32[1536,16]{0,1:T(8,128)S(1)} %pad_maximum_fusion.5), channel_id=1, source_target_pairs={{0,128},{64,192},{128,0},{192,64},{1,129},{65,193},{129,1},{193,65... | collective-permute-start | bytes 294920 | tf_op jit(solution)/shard_map/ppermute | solution.py:76
  171.0 1.5 collective-permute-done.25
  175.7 3.4 %multiply_convert_fusion = bf16[3072,128,16]{0,2,1:T(8,128)(2,1)S(1)} fusion(f32[3072,16]{0,1:T(8,128)S(1)} %maximum_subtract_fusion, f32[3072,128]{0,1:T(8,128)S(1)} %copy.33), kind=kLoop, calls=%fused_computation | loop fusion | flops 12582912 | bytes 14352384 | tf_op jit(solution)/shard_map/convert_element_type | solution.py:173
  179.1 6.7 %fusion.30 = f32[2048,512]{0,1:T(8,128)S(1)} fusion(bf16[3072,2048]{0,1:T(8,128)(2,1)S(1)} %bitcast.145, bf16[3072,512]{0,1:T(8,128)(2,1)S(1)} %bitcast.155), kind=kOutput, calls=%fused_computation.99 | convolution fusion | flops 6442450944 | bytes 19922944 | tf_op jit(solution)/shard_map/dot_general | solution.py:132
  186.3 4.1 %collective-permute-done.26 = f32[2048,256]{0,1:T(8,128)S(1)} collective-permute-done((f32[2048,256]{0,1:T(8,128)S(1)}, f32[2048,256]{0,1:T(8,128)S(1)}, u32[]{:S(2)}, u32[]{:S(2)}) %collective-permute-start.26) | collective-permute-done | bytes 2097184 | tf_op jit(solution)/shard_map/ppermute | solution.py:107
  191.4 1.4 collective-permute-start.31
  192.9 12.5 %collective-permute-done.27 = f32[1,128,1024]{2,1,0:T(8,128)S(1)} collective-permute-done((f32[1,128,1024]{2,1,0:T(8,128)S(1)}, f32[1,128,1024]{2,1,0:T(8,128)S(1)}, u32[]{:S(2)}, u32[]{:S(2)}) %collective-permute-start.27) | collective-permute-done | bytes 524320 | tf_op jit(solution)/shard_map/ppermute | solution.py:121
  206.0 1.5 collective-permute-start.32
  207.5 5.6 %collective-permute-done.28 = f32[2,32,1024]{2,1,0:T(8,128)S(1)} collective-permute-done((f32[2,32,1024]{2,1,0:T(8,128)S(1)}, f32[2,32,1024]{2,1,0:T(8,128)S(1)}, u32[]{:S(2)}, u32[]{:S(2)}) %collective-permute-start.28) | collective-permute-done | bytes 262176 | tf_op jit(solution)/shard_map/ppermute | solution.py:121
  213.1 2.4 %collective-permute-start.29 = (f32[1,32,1024]{2,1,0:T(8,128)S(1)}, f32[1,32,1024]{2,1,0:T(8,128)S(1)}, u32[]{:S(2)}, u32[]{:S(2)}) collective-permute-start(f32[1,32,1024]{2,1,0:T(8,128)S(1)} %select_bitcast_fusion.5), channel_id=1, source_target_pairs={{0,4},{2,6},{4,0},{6,2},{1,5},{3,7},{5,1},{7,3},{8,12},{10,14},{12... | collective-permute-start | bytes 393224 | tf_op jit(solution)/shard_map/ppermute | solution.py:121
  215.7 4.2 %collective-permute-done.29 = f32[1,32,1024]{2,1,0:T(8,128)S(1)} collective-permute-done((f32[1,32,1024]{2,1,0:T(8,128)S(1)}, f32[1,32,1024]{2,1,0:T(8,128)S(1)}, u32[]{:S(2)}, u32[]{:S(2)}) %collective-permute-start.29) | collective-permute-done | bytes 131104 | tf_op jit(solution)/shard_map/ppermute | solution.py:121
  220.1 5.0 %collective-permute-done.33 = f32[2,16,1024]{2,1,0:T(8,128)S(1)} collective-permute-done((f32[2,16,1024]{2,1,0:T(8,128)S(1)}, f32[2,16,1024]{2,1,0:T(8,128)S(1)}, u32[]{:S(2)}, u32[]{:S(2)}) %collective-permute-start.33) | collective-permute-done | bytes 131104 | tf_op jit(solution)/shard_map/ppermute | solution.py:121
  225.8 5.2 %collective-permute-done.34 = f32[1,16,1024]{2,1,0:T(8,128)S(1)} collective-permute-done((f32[1,16,1024]{2,1,0:T(8,128)S(1)}, f32[1,16,1024]{2,1,0:T(8,128)S(1)}, u32[]{:S(2)}, u32[]{:S(2)}) %collective-permute-start.34) | collective-permute-done | bytes 65568 | tf_op jit(solution)/shard_map/ppermute | solution.py:121
  231.2 8.1 %collective-permute-done.35 = f32[1,8,2048]{2,1,0:T(8,128)S(1)} collective-permute-done((f32[1,8,2048]{2,1,0:T(8,128)S(1)}, f32[1,8,2048]{2,1,0:T(8,128)S(1)}, u32[]{:S(2)}, u32[]{:S(2)}) %collective-permute-start.35) | collective-permute-done | bytes 65568 | tf_op jit(solution)/shard_map/ppermute | solution.py:121
  (117 shorter events, 24.8 us)
Async XLA Ops:
  0.0 66.6 %copy-start = (s32[16,3072]{1,0:T(8,128)S(1)}, s32[16,3072]{1,0:T(8,128)}, u32[]{:S(2)}) copy-start(s32[16,3072]{1,0:T(8,128)} %param.6) | copy-start | bytes 589828
  0.0 1.4 collective-permute-start
  2.1 3.7 %collective-permute-start.1 = (f32[1536]{0:T(1024)S(1)}, f32[1536]{0:T(1024)S(1)}, u32[]{:S(2)}, u32[]{:S(2)}) collective-permute-start(f32[1536]{0:T(1024)S(1)} %pad_maximum_fusion.10), channel_id=1, source_target_pairs={{0,2},{2,0},{4,6},{6,4},{1,3},{3,1},{5,7},{7,5},{8,10},{10,8},{12,... | collective-permute-start | bytes 18440 | tf_op jit(solution)/shard_map/ppermute | solution.py:76
  5.8 5.3 %collective-permute-start.2 = (f32[3072]{0:T(1024)S(1)}, f32[3072]{0:T(1024)S(1)}, u32[]{:S(2)}, u32[]{:S(2)}) collective-permute-start(f32[3072]{0:T(1024)S(1)} %pad_maximum_fusion.9), channel_id=1, source_target_pairs={{0,4},{2,6},{4,0},{6,2},{1,5},{3,7},{5,1},{7,3},{8,12},{10,14},{12... | collective-permute-start | bytes 36872 | tf_op jit(solution)/shard_map/ppermute | solution.py:76
  11.1 3.9 %collective-permute-start.3 = (f32[6144]{0:T(1024)S(1)}, f32[6144]{0:T(1024)S(1)}, u32[]{:S(2)}, u32[]{:S(2)}) collective-permute-start(f32[6144]{0:T(1024)S(1)} %pad_maximum_fusion.8), channel_id=1, source_target_pairs={{0,8},{8,0},{16,24},{24,16},{32,40},{40,32},{48,56},{56,48},{1,9},... | collective-permute-start | bytes 73736 | tf_op jit(solution)/shard_map/ppermute | solution.py:76
  15.1 5.7 %collective-permute-start.4 = (f32[12288]{0:T(1024)S(1)}, f32[12288]{0:T(1024)S(1)}, u32[]{:S(2)}, u32[]{:S(2)}) collective-permute-start(f32[12288]{0:T(1024)S(1)} %pad_maximum_fusion.7), channel_id=1, source_target_pairs={{0,16},{8,24},{16,0},{24,8},{32,48},{40,56},{48,32},{56,40},{1,17}... | collective-permute-start | bytes 147464 | tf_op jit(solution)/shard_map/ppermute | solution.py:76
  20.8 10.8 %collective-permute-start.5 = (f32[24576]{0:T(1024)S(1)}, f32[24576]{0:T(1024)S(1)}, u32[]{:S(2)}, u32[]{:S(2)}) collective-permute-start(f32[24576]{0:T(1024)S(1)} %pad_maximum_fusion.4), channel_id=1, source_target_pairs={{0,32},{8,40},{16,48},{24,56},{32,0},{40,8},{48,16},{56,24},{1,33}... | collective-permute-start | bytes 294920 | tf_op jit(solution)/shard_map/ppermute | solution.py:76
  31.7 5.9 %collective-permute-start.6 = (f32[49152]{0:T(1024)S(1)}, f32[49152]{0:T(1024)S(1)}, u32[]{:S(2)}, u32[]{:S(2)}) collective-permute-start(f32[49152]{0:T(1024)S(1)} %pad_maximum_fusion.3), channel_id=1, source_target_pairs={{0,64},{64,0},{128,192},{192,128},{1,65},{65,1},{129,193},{193,129... | collective-permute-start | bytes 589832 | tf_op jit(solution)/shard_map/ppermute | solution.py:76
  35.3 1.3 collective-permute-start.10
  36.6 4.4 %collective-permute-start.11 = (f32[128,128]{1,0:T(8,128)S(1)}, f32[128,128]{1,0:T(8,128)S(1)}, u32[]{:S(2)}, u32[]{:S(2)}) collective-permute-start(f32[128,128]{1,0:T(8,128)S(1)} %add.99), channel_id=1, source_target_pairs={{0,2},{2,0},{4,6},{6,4},{1,3},{3,1},{5,7},{7,5},{8,10},{10,8},{12,... | collective-permute-start | bytes 196616 | tf_op jit(solution)/shard_map/ppermute | solution.py:66
  37.6 35.8 %collective-permute-start.7 = (f32[98304]{0:T(1024)S(1)}, f32[98304]{0:T(1024)S(1)}, u32[]{:S(2)}, u32[]{:S(2)}) collective-permute-start(f32[98304]{0:T(1024)S(1)} %pad_maximum_fusion.2), channel_id=1, source_target_pairs={{0,128},{64,192},{128,0},{192,64},{1,129},{65,193},{129,1},{193,65... | collective-permute-start | bytes 1179656 | tf_op jit(solution)/shard_map/ppermute | solution.py:76
  41.0 5.9 %collective-permute-start.12 = (f32[128,128]{1,0:T(8,128)S(1)}, f32[128,128]{1,0:T(8,128)S(1)}, u32[]{:S(2)}, u32[]{:S(2)}) collective-permute-start(f32[128,128]{1,0:T(8,128)S(1)} %add.100), channel_id=1, source_target_pairs={{0,4},{2,6},{4,0},{6,2},{1,5},{3,7},{5,1},{7,3},{8,12},{10,14},{12... | collective-permute-start | bytes 196616 | tf_op jit(solution)/shard_map/ppermute | solution.py:66
  46.9 4.4 %collective-permute-start.13 = (f32[128,128]{1,0:T(8,128)S(1)}, f32[128,128]{1,0:T(8,128)S(1)}, u32[]{:S(2)}, u32[]{:S(2)}) collective-permute-start(f32[128,128]{1,0:T(8,128)S(1)} %add.101), channel_id=1, source_target_pairs={{0,8},{8,0},{16,24},{24,16},{32,40},{40,32},{48,56},{56,48},{1,9},... | collective-permute-start | bytes 196616 | tf_op jit(solution)/shard_map/ppermute | solution.py:66
  51.2 6.0 %collective-permute-start.14 = (f32[128,128]{1,0:T(8,128)S(1)}, f32[128,128]{1,0:T(8,128)S(1)}, u32[]{:S(2)}, u32[]{:S(2)}) collective-permute-start(f32[128,128]{1,0:T(8,128)S(1)} %add.102), channel_id=1, source_target_pairs={{0,16},{8,24},{16,0},{24,8},{32,48},{40,56},{48,32},{56,40},{1,17}... | collective-permute-start | bytes 196616 | tf_op jit(solution)/shard_map/ppermute | solution.py:66
  57.2 9.0 %collective-permute-start.15 = (f32[128,128]{1,0:T(8,128)S(1)}, f32[128,128]{1,0:T(8,128)S(1)}, u32[]{:S(2)}, u32[]{:S(2)}) collective-permute-start(f32[128,128]{1,0:T(8,128)S(1)} %add.103), channel_id=1, source_target_pairs={{0,32},{8,40},{16,48},{24,56},{32,0},{40,8},{48,16},{56,24},{1,33}... | collective-permute-start | bytes 196616 | tf_op jit(solution)/shard_map/ppermute | solution.py:66
  66.2 4.4 %collective-permute-start.16 = (f32[128,128]{1,0:T(8,128)S(1)}, f32[128,128]{1,0:T(8,128)S(1)}, u32[]{:S(2)}, u32[]{:S(2)}) collective-permute-start(f32[128,128]{1,0:T(8,128)S(1)} %add.104), channel_id=1, source_target_pairs={{0,64},{64,0},{128,192},{192,128},{1,65},{65,1},{129,193},{193,129... | collective-permute-start | bytes 196616 | tf_op jit(solution)/shard_map/ppermute | solution.py:66
  70.5 42.3 %collective-permute-start.17 = (f32[128,128]{1,0:T(8,128)S(1)}, f32[128,128]{1,0:T(8,128)}, u32[]{:S(2)}, u32[]{:S(2)}) collective-permute-start(f32[128,128]{1,0:T(8,128)S(1)} %add.105), channel_id=1, source_target_pairs={{0,128},{64,192},{128,0},{192,64},{1,129},{65,193},{129,1},{193,65... | collective-permute-start | bytes 196616 | tf_op jit(solution)/shard_map/ppermute | solution.py:66
  74.2 24.6 %copy-start.1 = (f32[3072,128]{1,0:T(8,128)S(1)}, f32[3072,128]{1,0:T(8,128)}, u32[]{:S(2)}) copy-start(f32[3072,128]{1,0:T(8,128)} %param.5) | copy-start | bytes 4718596
  99.1 12.8 %collective-permute-start.18 = (f32[128,16]{0,1:T(8,128)S(1)}, f32[128,16]{0,1:T(8,128)S(1)}, u32[]{:S(2)}, u32[]{:S(2)}) collective-permute-start(f32[128,16]{0,1:T(8,128)S(1)} %fusion.6), channel_id=1, source_target_pairs={{0,1},{1,0},{2,3},{3,2},{4,5},{5,4},{6,7},{7,6},{8,9},{9,8},{10,11... | collective-permute-start | bytes 24584 | tf_op jit(solution)/shard_map/ppermute | solution.py:66
  111.9 3.7 %collective-permute-start.19 = (f32[128,16]{0,1:T(8,128)S(1)}, f32[128,16]{0,1:T(8,128)S(1)}, u32[]{:S(2)}, u32[]{:S(2)}) collective-permute-start(f32[128,16]{0,1:T(8,128)S(1)} %add.109), channel_id=1, source_target_pairs={{0,2},{2,0},{4,6},{6,4},{1,3},{3,1},{5,7},{7,5},{8,10},{10,8},{12,... | collective-permute-start | bytes 24584 | tf_op jit(solution)/shard_map/ppermute | solution.py:66
  115.6 14.7 %collective-permute-start.20 = (f32[128,16]{0,1:T(8,128)S(1)}, f32[128,16]{0,1:T(8,128)S(1)}, u32[]{:S(2)}, u32[]{:S(2)}) collective-permute-start(f32[128,16]{0,1:T(8,128)S(1)} %add.110), channel_id=1, source_target_pairs={{0,4},{2,6},{4,0},{6,2},{1,5},{3,7},{5,1},{7,3},{8,12},{10,14},{12... | collective-permute-start | bytes 24584 | tf_op jit(solution)/shard_map/ppermute | solution.py:66
  130.3 3.7 %collective-permute-start.21 = (f32[128,16]{0,1:T(8,128)S(1)}, f32[128,16]{0,1:T(8,128)S(1)}, u32[]{:S(2)}, u32[]{:S(2)}) collective-permute-start(f32[128,16]{0,1:T(8,128)S(1)} %add.111), channel_id=1, source_target_pairs={{0,8},{8,0},{16,24},{24,16},{32,40},{40,32},{48,56},{56,48},{1,9},... | collective-permute-start | bytes 24584 | tf_op jit(solution)/shard_map/ppermute | solution.py:66
  134.0 4.5 %collective-permute-start.22 = (f32[128,16]{0,1:T(8,128)S(1)}, f32[128,16]{0,1:T(8,128)S(1)}, u32[]{:S(2)}, u32[]{:S(2)}) collective-permute-start(f32[128,16]{0,1:T(8,128)S(1)} %add.112), channel_id=1, source_target_pairs={{0,16},{8,24},{16,0},{24,8},{32,48},{40,56},{48,32},{56,40},{1,17}... | collective-permute-start | bytes 24584 | tf_op jit(solution)/shard_map/ppermute | solution.py:66
  134.7 20.6 %collective-permute-start.8 = (f32[768,16]{0,1:T(8,128)S(1)}, f32[768,16]{0,1:T(8,128)}, u32[]{:S(2)}, u32[]{:S(2)}) collective-permute-start(f32[768,16]{0,1:T(8,128)S(1)} %bitcast.160), channel_id=1, source_target_pairs={{0,64},{64,0},{128,192},{192,128},{1,65},{65,1},{129,193},{193,129... | collective-permute-start | bytes 147464 | tf_op jit(solution)/shard_map/ppermute | solution.py:76
  138.6 16.4 %collective-permute-start.23 = (f32[128,16]{0,1:T(8,128)S(1)}, f32[128,16]{0,1:T(8,128)S(1)}, u32[]{:S(2)}, u32[]{:S(2)}) collective-permute-start(f32[128,16]{0,1:T(8,128)S(1)} %add.113), channel_id=1, source_target_pairs={{0,32},{8,40},{16,48},{24,56},{32,0},{40,8},{48,16},{56,24},{1,33}... | collective-permute-start | bytes 24584 | tf_op jit(solution)/shard_map/ppermute | solution.py:66
  155.0 3.7 %collective-permute-start.24 = (f32[128,16]{0,1:T(8,128)S(1)}, f32[128,16]{0,1:T(8,128)S(1)}, u32[]{:S(2)}, u32[]{:S(2)}) collective-permute-start(f32[128,16]{0,1:T(8,128)S(1)} %add.114), channel_id=1, source_target_pairs={{0,64},{64,0},{128,192},{192,128},{1,65},{65,1},{129,193},{193,129... | collective-permute-start | bytes 24584 | tf_op jit(solution)/shard_map/ppermute | solution.py:66
  158.8 13.8 %collective-permute-start.25 = (f32[128,16]{0,1:T(8,128)S(1)}, f32[128,16]{0,1:T(8,128)S(1)}, u32[]{:S(2)}, u32[]{:S(2)}) collective-permute-start(f32[128,16]{0,1:T(8,128)S(1)} %add.115), channel_id=1, source_target_pairs={{0,128},{64,192},{128,0},{192,64},{1,129},{65,193},{129,1},{193,65... | collective-permute-start | bytes 24584 | tf_op jit(solution)/shard_map/ppermute | solution.py:66
  168.1 6.2 %collective-permute-start.9 = (f32[1536,16]{0,1:T(8,128)S(1)}, f32[1536,16]{0,1:T(8,128)S(1)}, u32[]{:S(2)}, u32[]{:S(2)}) collective-permute-start(f32[1536,16]{0,1:T(8,128)S(1)} %pad_maximum_fusion.5), channel_id=1, source_target_pairs={{0,128},{64,192},{128,0},{192,64},{1,129},{65,193},{129,1},{193,65... | collective-permute-start | bytes 294920 | tf_op jit(solution)/shard_map/ppermute | solution.py:76
  175.7 3.5 %copy-start.2 = (bf16[3072,2,2,2,2,2,2,8]{0,7,6,5,4,3,2,1:T(8,128)(2,1)S(1)}, bf16[3072,2,2,2,2,2,2,8]{0,7,6,5,4,3,2,1:T(8,128)(2,1)}, u32[]{:S(2)}) copy-start(bf16[3072,2,2,2,2,2,2,8]{0,7,6,5,4,3,2,1:T(8,128)(2,1)} %copy.38) | copy-start | bytes 9437188
  186.2 4.2 %collective-permute-start.26 = (f32[2048,256]{0,1:T(8,128)S(1)}, f32[2048,256]{0,1:T(8,128)S(1)}, u32[]{:S(2)}, u32[]{:S(2)}) collective-permute-start(f32[2048,256]{0,1:T(8,128)S(1)} %slice_select_fusion), channel_id=1, source_target_pairs={{0,1},{1,0},{2,3},{3,2},{4,5},{5,4},{6,7},{7,6},{8,9},{9,8},{10,11... | collective-permute-start | bytes 6291464 | tf_op jit(solution)/shard_map/ppermute | solution.py:107
  191.3 14.1 %collective-permute-start.27 = (f32[1,128,1024]{2,1,0:T(8,128)S(1)}, f32[1,128,1024]{2,1,0:T(8,128)S(1)}, u32[]{:S(2)}, u32[]{:S(2)}) collective-permute-start(f32[1,128,1024]{2,1,0:T(8,128)S(1)} %select_bitcast_fusion.1), channel_id=1, source_target_pairs={{0,2},{2,0},{4,6},{6,4},{1,3},{3,1},{5,7},{7,5},{8,10},{10,8},{12,... | collective-permute-start | bytes 1572872 | tf_op jit(solution)/shard_map/ppermute | solution.py:121
  191.4 14.4 %collective-permute-start.31 = (f32[4,32,1024]{2,1,0:T(8,128)S(1)}, f32[4,32,1024]{2,1,0:T(8,128)S(1)}, u32[]{:S(2)}, u32[]{:S(2)}) collective-permute-start(f32[4,32,1024]{2,1,0:T(8,128)S(1)} %select_bitcast_fusion), channel_id=1, source_target_pairs={{0,8},{8,0},{16,24},{24,16},{32,40},{40,32},{48,56},{56,48},{1,9},... | collective-permute-start | bytes 1572872 | tf_op jit(solution)/shard_map/ppermute | solution.py:121
  205.5 7.6 %collective-permute-start.28 = (f32[2,32,1024]{2,1,0:T(8,128)S(1)}, f32[2,32,1024]{2,1,0:T(8,128)S(1)}, u32[]{:S(2)}, u32[]{:S(2)}) collective-permute-start(f32[2,32,1024]{2,1,0:T(8,128)S(1)} %select_bitcast_fusion.3), channel_id=1, source_target_pairs={{0,8},{8,0},{16,24},{24,16},{32,40},{40,32},{48,56},{56,48},{1,9},... | collective-permute-start | bytes 786440 | tf_op jit(solution)/shard_map/ppermute | solution.py:121
  206.0 9.5 %collective-permute-start.32 = (f32[1,64,1024]{2,1,0:T(8,128)S(1)}, f32[1,64,1024]{2,1,0:T(8,128)S(1)}, u32[]{:S(2)}, u32[]{:S(2)}) collective-permute-start(f32[1,64,1024]{2,1,0:T(8,128)S(1)} %select_bitcast_fusion.2), channel_id=1, source_target_pairs={{0,2},{2,0},{4,6},{6,4},{1,3},{3,1},{5,7},{7,5},{8,10},{10,8},{12,... | collective-permute-start | bytes 786440 | tf_op jit(solution)/shard_map/ppermute | solution.py:121
  213.1 6.8 %collective-permute-start.29 = (f32[1,32,1024]{2,1,0:T(8,128)S(1)}, f32[1,32,1024]{2,1,0:T(8,128)S(1)}, u32[]{:S(2)}, u32[]{:S(2)}) collective-permute-start(f32[1,32,1024]{2,1,0:T(8,128)S(1)} %select_bitcast_fusion.5), channel_id=1, source_target_pairs={{0,4},{2,6},{4,0},{6,2},{1,5},{3,7},{5,1},{7,3},{8,12},{10,14},{12... | collective-permute-start | bytes 393224 | tf_op jit(solution)/shard_map/ppermute | solution.py:121
  215.6 9.5 %collective-permute-start.33 = (f32[2,16,1024]{2,1,0:T(8,128)S(1)}, f32[2,16,1024]{2,1,0:T(8,128)S(1)}, u32[]{:S(2)}, u32[]{:S(2)}) collective-permute-start(f32[2,16,1024]{2,1,0:T(8,128)S(1)} %select_bitcast_fusion.4), channel_id=1, source_target_pairs={{0,16},{8,24},{16,0},{24,8},{32,48},{40,56},{48,32},{56,40},{1,17}... | collective-permute-start | bytes 393224 | tf_op jit(solution)/shard_map/ppermute | solution.py:121
  219.9 5.9 %collective-permute-start.30 = (f32[1,16,1024]{2,1,0:T(8,128)S(1)}, f32[1,16,1024]{2,1,0:T(8,128)S(1)}, u32[]{:S(2)}, u32[]{:S(2)}) collective-permute-start(f32[1,16,1024]{2,1,0:T(8,128)S(1)} %select_bitcast_fusion.8), channel_id=1, source_target_pairs={{0,16},{8,24},{16,0},{24,8},{32,48},{40,56},{48,32},{56,40},{1,17}... | collective-permute-start | bytes 196616 | tf_op jit(solution)/shard_map/ppermute | solution.py:121
  225.1 5.9 %collective-permute-start.34 = (f32[1,16,1024]{2,1,0:T(8,128)S(1)}, f32[1,16,1024]{2,1,0:T(8,128)S(1)}, u32[]{:S(2)}, u32[]{:S(2)}) collective-permute-start(f32[1,16,1024]{2,1,0:T(8,128)S(1)} %select_bitcast_fusion.7), channel_id=1, source_target_pairs={{0,4},{2,6},{4,0},{6,2},{1,5},{3,7},{5,1},{7,3},{8,12},{10,14},{12... | collective-permute-start | bytes 196616 | tf_op jit(solution)/shard_map/ppermute | solution.py:121
  231.0 8.3 %collective-permute-start.35 = (f32[1,8,2048]{2,1,0:T(8,128)S(1)}, f32[1,8,2048]{2,1,0:T(8,128)S(1)}, u32[]{:S(2)}, u32[]{:S(2)}) collective-permute-start(f32[1,8,2048]{2,1,0:T(8,128)S(1)} %select_bitcast_fusion.6), channel_id=1, source_target_pairs={{0,32},{8,40},{16,48},{24,56},{32,0},{40,8},{48,16},{56,24},{1,33}... | collective-permute-start | bytes 196616 | tf_op jit(solution)/shard_map/ppermute | solution.py:121

commit v8 on v7

--- a/solution.py
+++ b/solution.py
@@ -123,16 +123,10 @@
 
 
 def halving_scores(weighted, genotypes):
-    local_rows, variants = genotypes.shape
-    nz, nx, nc = (lax.axis_size(a) for a in SAMP)
-    own_rows = variants // (nz * nx * nc)
-    order = genotypes.reshape(local_rows, 2, 2, 2, 2, 2, nc, own_rows)
-    order = order.transpose(0, 6, 5, 4, 3, 2, 1, 7)
-    dosages = order.reshape(local_rows, variants).astype(jnp.bfloat16)
-    cur = jnp.dot(weighted.T, dosages, preferred_element_type=jnp.float32)
-    half = cur.shape[1] // 2
-    cur = exchange(cur[:, :half], cur[:, half:], "core", 0, 1).T
-    names = [("x", 0), ("x", 1), ("z", 0), ("z", 1), ("z", 2)]
+    dosages = genotypes.astype(jnp.bfloat16)
+    cur = jnp.dot(weighted.T, dosages, preferred_element_type=jnp.float32).T
+    names = [("z", 2), ("z", 1), ("z", 0), ("x", 1), ("x", 0), ("core", 0)]
+    cur, names = halve_bit(cur, names, ("core", 0))
     cols = cur.shape[1] // 2
     part_a, names_a = cur[:, :cols], list(names)
     part_b, names_b = cur[:, cols:], list(names)
@@ -159,11 +153,12 @@
     samples = pheno_full.shape[0]
     system = gram + 0.5 * samples * jnp.eye(width, dtype=jnp.float32)
     factor = jnp.linalg.cholesky(system)
+    inverse = chol_solve(factor, jnp.eye(width, dtype=jnp.float32))
     perm_part = lax.dynamic_slice_in_dim(perms, offset_rows, quarter, 1)
     pheno_part = gather_pheno(pheno_full, perm_part).T
     cross_part = jnp.dot(expo_part.T, pheno_part, precision=hi)
     cross = doubling_psum(cross_part, ("core", "x", "z", "vgrp"))
-    coefficients = chol_solve(factor, cross)
+    coefficients = jnp.dot(inverse, cross, precision=hi)
     permuted = doubling_gather(pheno_part, axis_bits(("vgrp",)))
     residuals = permuted - jnp.dot(exposures, coefficients, precision=hi)
     nperm = residuals.shape[1]

time: 245 us -> 257 us (1.049)
  the two profiles are of different devices: /device:TPU:6 before, /device:TPU:2 now
where the time goes in v8:
time: 257 us; the launch traced here: 253 us
  waiting for transfers between devices  93.7 us (36%)
  starting transfers between devices  64.4 us (25%)
  other arithmetic  45.3 us (18%)
  Pallas kernels  21.3 us (8%)
  matrix products  15.8 us (6%)
  local copies, waits for them, and re-layouts  12 us (5%)
    ppermute x16, waiting for transfers between devices, doubling_psum(): x = x + lax.ppermute(x, axis, pairs)  42.5 us
    ppermute x10, waiting for transfers between devices, halve_bit(): kept = mine + lax.ppermute(send, axis, flip)  39.2 us
    ppermute x16, starting transfers between devices, doubling_psum(): x = x + lax.ppermute(x, axis, pairs)  29 us
    ppermute x10, starting transfers between devices, doubling_gather(): other = lax.ppermute(x, axis, flip)  22.8 us
    pallas_call x1, Pallas kernels, gather_pheno(): pl.pallas_call(gather_body, grid=(count // TILE,), in_specs=[pl.BlockSpec...  21.3 us
    another operation x3, other arithmetic, per_device(): factor = jnp.linalg.cholesky(system)  13.2 us
    ppermute x10, starting transfers between devices, halve_bit(): kept = mine + lax.ppermute(send, axis, flip)  12.6 us
    ppermute x10, waiting for transfers between devices, doubling_gather(): other = lax.ppermute(x, axis, flip)  12 us
  transfers between devices with their start and end apart: 36, of which 24 were waited for; matrix products, arithmetic and copies ran while one was open for 13% of the time, Pallas kernels for 0%

profile of v8, /device:TPU:2, one launch (start us, length us, event | category | flops | bytes accessed | tf_op | source)
XLA Modules:
  0.0 253.2 jit_solution(130054431967826506)
XLA Ops:
  2.1 2.3 collective-permute-start.1
  6.1 2.0 collective-permute-start.2
  8.0 3.3 %collective-permute-done.2 = f32[3072]{0:T(1024)S(1)} collective-permute-done((f32[3072]{0:T(1024)S(1)}, f32[3072]{0:T(1024)S(1)}, u32[]{:S(2)}, u32[]{:S(2)}) %collective-permute-start.2) | collective-permute-done | bytes 12320 | tf_op jit(solution)/shard_map/ppermute | solution.py:76
  11.4 1.8 collective-permute-start.3
  13.1 2.1 collective-permute-done.3
  15.3 3.4 %collective-permute-start.4 = (f32[12288]{0:T(1024)S(1)}, f32[12288]{0:T(1024)S(1)}, u32[]{:S(2)}, u32[]{:S(2)}) collective-permute-start(f32[12288]{0:T(1024)S(1)} %pad_maximum_fusion.7), channel_id=1, source_target_pairs={{0,16},{8,24},{16,0},{24,8},{32,48},{40,56},{48,32},{56,40},{1,17}... | collective-permute-start | bytes 147464 | tf_op jit(solution)/shard_map/ppermute | solution.py:76
  18.7 1.9 fusion.15
  20.8 6.7 %collective-permute-start.5 = (f32[24576]{0:T(1024)S(1)}, f32[24576]{0:T(1024)S(1)}, u32[]{:S(2)}, u32[]{:S(2)}) collective-permute-start(f32[24576]{0:T(1024)S(1)} %pad_maximum_fusion.4), channel_id=1, source_target_pairs={{0,32},{8,40},{16,48},{24,56},{32,0},{40,8},{48,16},{56,24},{1,33}... | collective-permute-start | bytes 294920 | tf_op jit(solution)/shard_map/ppermute | solution.py:76
  28.1 3.7 %collective-permute-done.11 = f32[128,128]{1,0:T(8,128)S(1)} collective-permute-done((f32[128,128]{1,0:T(8,128)S(1)}, f32[128,128]{1,0:T(8,128)S(1)}, u32[]{:S(2)}, u32[]{:S(2)}) %collective-permute-start.11) | collective-permute-done | bytes 65568 | tf_op jit(solution)/shard_map/ppermute | solution.py:66
  31.8 2.2 collective-permute-start.12
  35.7 1.9 collective-permute-done.12
  38.9 3.5 %collective-permute-done.13 = f32[128,128]{1,0:T(8,128)S(1)} collective-permute-done((f32[128,128]{1,0:T(8,128)S(1)}, f32[128,128]{1,0:T(8,128)S(1)}, u32[]{:S(2)}, u32[]{:S(2)}) %collective-permute-start.13) | collective-permute-done | bytes 65568 | tf_op jit(solution)/shard_map/ppermute | solution.py:66
  44.0 4.4 %collective-permute-done.14 = f32[128,128]{1,0:T(8,128)S(1)} collective-permute-done((f32[128,128]{1,0:T(8,128)S(1)}, f32[128,128]{1,0:T(8,128)S(1)}, u32[]{:S(2)}, u32[]{:S(2)}) %collective-permute-start.14) | collective-permute-done | bytes 65568 | tf_op jit(solution)/shard_map/ppermute | solution.py:66
  48.9 7.8 %collective-permute-done.15 = f32[128,128]{1,0:T(8,128)S(1)} collective-permute-done((f32[128,128]{1,0:T(8,128)S(1)}, f32[128,128]{1,0:T(8,128)S(1)}, u32[]{:S(2)}, u32[]{:S(2)}) %collective-permute-start.15) | collective-permute-done | bytes 65568 | tf_op jit(solution)/shard_map/ppermute | solution.py:66
  57.3 2.3 collective-permute-start.16
  60.4 2.9 %collective-permute-start.7 = (f32[98304]{0:T(1024)}, f32[98304]{0:T(1024)}, u32[]{:S(2)}, u32[]{:S(2)}) collective-permute-start(f32[98304]{0:T(1024)} %pad_maximum_fusion.2), channel_id=1, source_target_pairs={{0,128},{64,192},{128,0},{192,64},{1,129},{65,193},{129,1},{193,65... | collective-permute-start | bytes 1179656 | tf_op jit(solution)/shard_map/ppermute | solution.py:76
  64.7 2.4 collective-permute-start.17
  67.7 3.1 %collective-permute-done.17 = f32[128,128]{1,0:T(8,128)S(1)} collective-permute-done((f32[128,128]{1,0:T(8,128)S(1)}, f32[128,128]{1,0:T(8,128)S(1)}, u32[]{:S(2)}, u32[]{:S(2)}) %collective-permute-start.17) | collective-permute-done | bytes 65568 | tf_op jit(solution)/shard_map/ppermute | solution.py:66
  73.0 2.0 broadcast_select_fusion.1
  75.0 1.9 concatenate.53
  76.8 1.9 copy.164
  78.8 1.9 concatenate.54
  80.6 1.9 copy.165
  84.9 21.3 %shard_map.46 = f32[1,12288]{1,0:T(1,128)} custom-call(s32[1,12288]{1,0:T(1,128)} %bitcast.252, bf16[768,768]{1,0:T(8,128)(2,1)} %pad_maximum_fusion.tab_ref), custom_call_target="tpu_custom_call" | custom-call | tf_op jit(solution)/shard_map/pallas_call | solution.py:46
  106.8 2.2 reduce.9
  110.9 12.5 %cholesky.17 = f32[128,128]{1,0:T(8,128)S(1)} custom-call(f32[128,128]{1,0:T(8,128)} %fusion.38), custom_call_target="Cholesky" | custom-call | tf_op jit(solution)/shard_map/jit(cholesky)/cholesky | solution.py:155
  124.4 2.8 %collective-permute-done.19 = f32[128,16]{0,1:T(8,128)S(1)} collective-permute-done((f32[128,16]{0,1:T(8,128)S(1)}, f32[128,16]{0,1:T(8,128)S(1)}, u32[]{:S(2)}, u32[]{:S(2)}) %collective-permute-start.19) | collective-permute-done | bytes 8224 | tf_op jit(solution)/shard_map/ppermute | solution.py:66
  127.2 2.1 collective-permute-start.20
  129.9 2.4 collective-permute-done.20
  133.6 10.6 %custom-call.8 = f32[1,128,128]{1,2,0:T(8,128)S(1)} custom-call(f32[1,128,128]{2,1,0:T(8,128)} %fusion.27), custom_call_target="InvertDiagBlocksLowerTriangular" | custom-call | tf_op jit(solution)/shard_map/triangular_solve | solution.py:13
  144.3 1.8 collective-permute-start.22
  149.4 7.1 %collective-permute-done.23 = f32[128,16]{0,1:T(8,128)S(1)} collective-permute-done((f32[128,16]{0,1:T(8,128)S(1)}, f32[128,16]{0,1:T(8,128)S(1)}, u32[]{:S(2)}, u32[]{:S(2)}) %collective-permute-start.23) | collective-permute-done | bytes 8224 | tf_op jit(solution)/shard_map/ppermute | solution.py:66
  156.5 10.2 %collective-permute-start.24 = (f32[128,16]{0,1:T(8,128)S(1)}, f32[128,16]{0,1:T(8,128)S(1)}, u32[]{:S(2)}, u32[]{:S(2)}) collective-permute-start(f32[128,16]{0,1:T(8,128)S(1)} %add.114), channel_id=1, source_target_pairs={{0,64},{64,0},{128,192},{192,128},{1,65},{65,1},{129,193},{193,129... | collective-permute-start | bytes 24584 | tf_op jit(solution)/shard_map/ppermute | solution.py:66
  166.7 2.9 %collective-permute-done.24 = f32[128,16]{0,1:T(8,128)S(1)} collective-permute-done((f32[128,16]{0,1:T(8,128)S(1)}, f32[128,16]{0,1:T(8,128)S(1)}, u32[]{:S(2)}, u32[]{:S(2)}) %collective-permute-start.24) | collective-permute-done | bytes 8224 | tf_op jit(solution)/shard_map/ppermute | solution.py:66
  169.7 2.7 %collective-permute-start.25 = (f32[128,16]{0,1:T(8,128)S(1)}, f32[128,16]{0,1:T(8,128)S(1)}, u32[]{:S(2)}, u32[]{:S(2)}) collective-permute-start(f32[128,16]{0,1:T(8,128)S(1)} %add.115), channel_id=1, source_target_pairs={{0,128},{64,192},{128,0},{192,64},{1,129},{65,193},{129,1},{193,65... | collective-permute-start | bytes 24584 | tf_op jit(solution)/shard_map/ppermute | solution.py:66
  175.0 3.6 %collective-permute-done.9 = f32[1536,16]{0,1:T(8,128)S(1)} collective-permute-done((f32[1536,16]{0,1:T(8,128)S(1)}, f32[1536,16]{0,1:T(8,128)S(1)}, u32[]{:S(2)}, u32[]{:S(2)}) %collective-permute-start.9) | collective-permute-done | bytes 98336 | tf_op jit(solution)/shard_map/ppermute | solution.py:76
  180.0 6.9 %multiply_convert_fusion = bf16[3072,128,16]{0,2,1:T(8,128)(2,1)} fusion(f32[3072,16]{0,1:T(8,128)S(1)} %maximum_subtract_fusion, f32[3072,128]{0,1:T(8,128)S(1)} %copy.163), kind=kLoop, calls=%fused_computation | loop fusion | flops 12582912 | bytes 14352384 | tf_op jit(solution)/shard_map/convert_element_type | solution.py:168
  186.9 11.5 %fusion = f32[2048,512]{0,1:T(8,128)S(1)} fusion(bf16[3072,2048]{0,1:T(8,128)(2,1)} %bitcast.238, s32[3072,512]{1,0:T(8,128)} %param.7), kind=kOutput, calls=%fused_computation.2 | convolution fusion | flops 6444023808 | bytes 23068672 | tf_op jit(solution)/shard_map/dot_general | solution.py:127
  198.9 4.1 %collective-permute-done.26 = f32[32,8,2048]{2,1,0:T(8,128)S(1)} collective-permute-done((f32[32,8,2048]{2,1,0:T(8,128)S(1)}, f32[32,8,2048]{2,1,0:T(8,128)S(1)}, u32[]{:S(2)}, u32[]{:S(2)}) %collective-permute-start.26) | collective-permute-done | bytes 2097184 | tf_op jit(solution)/shard_map/ppermute | solution.py:121
  204.9 2.2 collective-permute-start.31
  207.1 11.0 %collective-permute-done.27 = f32[16,8,1024]{2,1,0:T(8,128)S(1)} collective-permute-done((f32[16,8,1024]{2,1,0:T(8,128)S(1)}, f32[16,8,1024]{2,1,0:T(8,128)S(1)}, u32[]{:S(2)}, u32[]{:S(2)}) %collective-permute-start.27) | collective-permute-done | bytes 524320 | tf_op jit(solution)/shard_map/ppermute | solution.py:121
  218.2 2.1 collective-permute-start.28
  221.4 4.7 %collective-permute-done.28 = f32[4,16,1024]{2,1,0:T(8,128)S(1)} collective-permute-done((f32[4,16,1024]{2,1,0:T(8,128)S(1)}, f32[4,16,1024]{2,1,0:T(8,128)S(1)}, u32[]{:S(2)}, u32[]{:S(2)}) %collective-permute-start.28) | collective-permute-done | bytes 262176 | tf_op jit(solution)/shard_map/ppermute | solution.py:121
  226.1 3.0 %collective-permute-start.29 = (f32[4,8,1024]{2,1,0:T(8,128)S(1)}, f32[4,8,1024]{2,1,0:T(8,128)S(1)}, u32[]{:S(2)}, u32[]{:S(2)}) collective-permute-start(f32[4,8,1024]{2,1,0:T(8,128)S(1)} %select_bitcast_fusion.6), channel_id=1, source_target_pairs={{0,4},{2,6},{4,0},{6,2},{1,5},{3,7},{5,1},{7,3},{8,12},{10,14},{12... | collective-permute-start | bytes 393224 | tf_op jit(solution)/shard_map/ppermute | solution.py:121
  229.4 3.3 %collective-permute-done.29 = f32[4,8,1024]{2,1,0:T(8,128)S(1)} collective-permute-done((f32[4,8,1024]{2,1,0:T(8,128)S(1)}, f32[4,8,1024]{2,1,0:T(8,128)S(1)}, u32[]{:S(2)}, u32[]{:S(2)}) %collective-permute-start.29) | collective-permute-done | bytes 131104 | tf_op jit(solution)/shard_map/ppermute | solution.py:121
  234.3 3.7 %collective-permute-done.33 = f32[2,16,1024]{2,1,0:T(8,128)S(1)} collective-permute-done((f32[2,16,1024]{2,1,0:T(8,128)S(1)}, f32[2,16,1024]{2,1,0:T(8,128)S(1)}, u32[]{:S(2)}, u32[]{:S(2)}) %collective-permute-start.33) | collective-permute-done | bytes 131104 | tf_op jit(solution)/shard_map/ppermute | solution.py:121
  239.5 4.4 %collective-permute-done.34 = f32[2,8,1024]{2,1,0:T(8,128)S(1)} collective-permute-done((f32[2,8,1024]{2,1,0:T(8,128)S(1)}, f32[2,8,1024]{2,1,0:T(8,128)S(1)}, u32[]{:S(2)}, u32[]{:S(2)}) %collective-permute-start.34) | collective-permute-done | bytes 65568 | tf_op jit(solution)/shard_map/ppermute | solution.py:121
  244.0 8.1 %collective-permute-done.35 = f32[1,8,2048]{2,1,0:T(8,128)S(1)} collective-permute-done((f32[1,8,2048]{2,1,0:T(8,128)S(1)}, f32[1,8,2048]{2,1,0:T(8,128)S(1)}, u32[]{:S(2)}, u32[]{:S(2)}) %collective-permute-start.35) | collective-permute-done | bytes 65568 | tf_op jit(solution)/shard_map/ppermute | solution.py:121
  (119 shorter events, 38.1 us)
Async XLA Ops:
  0.0 67.0 %copy-start = (s32[16,3072]{1,0:T(8,128)S(1)}, s32[16,3072]{1,0:T(8,128)}, u32[]{:S(2)}) copy-start(s32[16,3072]{1,0:T(8,128)} %param.6) | copy-start | bytes 589828
  0.0 1.4 collective-permute-start
  2.1 4.0 %collective-permute-start.1 = (f32[1536]{0:T(1024)S(1)}, f32[1536]{0:T(1024)S(1)}, u32[]{:S(2)}, u32[]{:S(2)}) collective-permute-start(f32[1536]{0:T(1024)S(1)} %pad_maximum_fusion.10), channel_id=1, source_target_pairs={{0,2},{2,0},{4,6},{6,4},{1,3},{3,1},{5,7},{7,5},{8,10},{10,8},{12,... | collective-permute-start | bytes 18440 | tf_op jit(solution)/shard_map/ppermute | solution.py:76
  6.1 5.3 %collective-permute-start.2 = (f32[3072]{0:T(1024)S(1)}, f32[3072]{0:T(1024)S(1)}, u32[]{:S(2)}, u32[]{:S(2)}) collective-permute-start(f32[3072]{0:T(1024)S(1)} %pad_maximum_fusion.9), channel_id=1, source_target_pairs={{0,4},{2,6},{4,0},{6,2},{1,5},{3,7},{5,1},{7,3},{8,12},{10,14},{12... | collective-permute-start | bytes 36872 | tf_op jit(solution)/shard_map/ppermute | solution.py:76
  11.4 3.9 %collective-permute-start.3 = (f32[6144]{0:T(1024)S(1)}, f32[6144]{0:T(1024)S(1)}, u32[]{:S(2)}, u32[]{:S(2)}) collective-permute-start(f32[6144]{0:T(1024)S(1)} %pad_maximum_fusion.8), channel_id=1, source_target_pairs={{0,8},{8,0},{16,24},{24,16},{32,40},{40,32},{48,56},{56,48},{1,9},... | collective-permute-start | bytes 73736 | tf_op jit(solution)/shard_map/ppermute | solution.py:76
  15.3 5.5 %collective-permute-start.4 = (f32[12288]{0:T(1024)S(1)}, f32[12288]{0:T(1024)S(1)}, u32[]{:S(2)}, u32[]{:S(2)}) collective-permute-start(f32[12288]{0:T(1024)S(1)} %pad_maximum_fusion.7), channel_id=1, source_target_pairs={{0,16},{8,24},{16,0},{24,8},{32,48},{40,56},{48,32},{56,40},{1,17}... | collective-permute-start | bytes 147464 | tf_op jit(solution)/shard_map/ppermute | solution.py:76
  20.6 42.7 %copy-start.1 = (f32[3072,128]{1,0:T(8,128)S(1)}, f32[3072,128]{1,0:T(8,128)}, u32[]{:S(2)}) copy-start(f32[3072,128]{1,0:T(8,128)} %param.5) | copy-start | bytes 4718596
  20.6 6.8 %collective-permute-start.10 = (f32[128,128]{1,0:T(8,128)S(1)}, f32[128,128]{1,0:T(8,128)S(1)}, u32[]{:S(2)}, u32[]{:S(2)}) collective-permute-start(f32[128,128]{1,0:T(8,128)S(1)} %fusion.15), channel_id=1, source_target_pairs={{0,1},{1,0},{2,3},{3,2},{4,5},{5,4},{6,7},{7,6},{8,9},{9,8},{10,11... | collective-permute-start | bytes 196616 | tf_op jit(solution)/shard_map/ppermute | solution.py:66
  20.8 13.3 %collective-permute-start.5 = (f32[24576]{0:T(1024)S(1)}, f32[24576]{0:T(1024)S(1)}, u32[]{:S(2)}, u32[]{:S(2)}) collective-permute-start(f32[24576]{0:T(1024)S(1)} %pad_maximum_fusion.4), channel_id=1, source_target_pairs={{0,32},{8,40},{16,48},{24,56},{32,0},{40,8},{48,16},{56,24},{1,33}... | collective-permute-start | bytes 294920 | tf_op jit(solution)/shard_map/ppermute | solution.py:76
  27.5 4.4 %collective-permute-start.11 = (f32[128,128]{1,0:T(8,128)S(1)}, f32[128,128]{1,0:T(8,128)S(1)}, u32[]{:S(2)}, u32[]{:S(2)}) collective-permute-start(f32[128,128]{1,0:T(8,128)S(1)} %add.99), channel_id=1, source_target_pairs={{0,2},{2,0},{4,6},{6,4},{1,3},{3,1},{5,7},{7,5},{8,10},{10,8},{12,... | collective-permute-start | bytes 196616 | tf_op jit(solution)/shard_map/ppermute | solution.py:66
  31.8 5.9 %collective-permute-start.12 = (f32[128,128]{1,0:T(8,128)S(1)}, f32[128,128]{1,0:T(8,128)S(1)}, u32[]{:S(2)}, u32[]{:S(2)}) collective-permute-start(f32[128,128]{1,0:T(8,128)S(1)} %add.100), channel_id=1, source_target_pairs={{0,4},{2,6},{4,0},{6,2},{1,5},{3,7},{5,1},{7,3},{8,12},{10,14},{12... | collective-permute-start | bytes 196616 | tf_op jit(solution)/shard_map/ppermute | solution.py:66
  34.1 14.8 %collective-permute-start.6 = (f32[49152]{0:T(1024)S(1)}, f32[49152]{0:T(1024)S(1)}, u32[]{:S(2)}, u32[]{:S(2)}) collective-permute-start(f32[49152]{0:T(1024)S(1)} %pad_maximum_fusion.3), channel_id=1, source_target_pairs={{0,64},{64,0},{128,192},{192,128},{1,65},{65,1},{129,193},{193,129... | collective-permute-start | bytes 589832 | tf_op jit(solution)/shard_map/ppermute | solution.py:76
  37.7 4.8 %collective-permute-start.13 = (f32[128,128]{1,0:T(8,128)S(1)}, f32[128,128]{1,0:T(8,128)S(1)}, u32[]{:S(2)}, u32[]{:S(2)}) collective-permute-start(f32[128,128]{1,0:T(8,128)S(1)} %add.101), channel_id=1, source_target_pairs={{0,8},{8,0},{16,24},{24,16},{32,40},{40,32},{48,56},{56,48},{1,9},... | collective-permute-start | bytes 196616 | tf_op jit(solution)/shard_map/ppermute | solution.py:66
  42.5 6.0 %collective-permute-start.14 = (f32[128,128]{1,0:T(8,128)S(1)}, f32[128,128]{1,0:T(8,128)S(1)}, u32[]{:S(2)}, u32[]{:S(2)}) collective-permute-start(f32[128,128]{1,0:T(8,128)S(1)} %add.102), channel_id=1, source_target_pairs={{0,16},{8,24},{16,0},{24,8},{32,48},{40,56},{48,32},{56,40},{1,17}... | collective-permute-start | bytes 196616 | tf_op jit(solution)/shard_map/ppermute | solution.py:66
  48.4 8.3 %collective-permute-start.15 = (f32[128,128]{1,0:T(8,128)S(1)}, f32[128,128]{1,0:T(8,128)S(1)}, u32[]{:S(2)}, u32[]{:S(2)}) collective-permute-start(f32[128,128]{1,0:T(8,128)S(1)} %add.103), channel_id=1, source_target_pairs={{0,32},{8,40},{16,48},{24,56},{32,0},{40,8},{48,16},{56,24},{1,33}... | collective-permute-start | bytes 196616 | tf_op jit(solution)/shard_map/ppermute | solution.py:66
  48.9 14.4 %copy-start.2 = (f32[49152]{0:T(1024)}, f32[49152]{0:T(1024)S(1)}, u32[]{:S(2)}) copy-start(f32[49152]{0:T(1024)S(1)} %get-tuple-element.13) | copy-start | bytes 589828
  57.3 6.5 %collective-permute-start.16 = (f32[128,128]{1,0:T(8,128)}, f32[128,128]{1,0:T(8,128)}, u32[]{:S(2)}, u32[]{:S(2)}) collective-permute-start(f32[128,128]{1,0:T(8,128)} %add.104), channel_id=1, source_target_pairs={{0,64},{64,0},{128,192},{192,128},{1,65},{65,1},{129,193},{193,129... | collective-permute-start | bytes 196616 | tf_op jit(solution)/shard_map/ppermute | solution.py:66
  60.4 12.6 %collective-permute-start.7 = (f32[98304]{0:T(1024)}, f32[98304]{0:T(1024)}, u32[]{:S(2)}, u32[]{:S(2)}) collective-permute-start(f32[98304]{0:T(1024)} %pad_maximum_fusion.2), channel_id=1, source_target_pairs={{0,128},{64,192},{128,0},{192,64},{1,129},{65,193},{129,1},{193,65... | collective-permute-start | bytes 1179656 | tf_op jit(solution)/shard_map/ppermute | solution.py:76
  64.7 6.1 %collective-permute-start.17 = (f32[128,128]{1,0:T(8,128)S(1)}, f32[128,128]{1,0:T(8,128)S(1)}, u32[]{:S(2)}, u32[]{:S(2)}) collective-permute-start(f32[128,128]{1,0:T(8,128)S(1)} %add.105), channel_id=1, source_target_pairs={{0,128},{64,192},{128,0},{192,64},{1,129},{65,193},{129,1},{193,65... | collective-permute-start | bytes 196616 | tf_op jit(solution)/shard_map/ppermute | solution.py:66
  83.8 26.4 %copy-start.3 = (f32[128,128]{1,0:T(8,128)S(1)}, f32[128,128]{1,0:T(8,128)}, u32[]{:S(2)}) copy-start(f32[128,128]{1,0:T(8,128)} %select_add_fusion) | copy-start | bytes 196612
  83.8 26.4 %copy-start.4 = (f32[128,128]{0,1:T(8,128)S(1)}, f32[128,128]{0,1:T(8,128)}, u32[]{:S(2)}) copy-start(f32[128,128]{0,1:T(8,128)} %copy.166) | copy-start | bytes 196612
  110.1 13.3 %collective-permute-start.18 = (f32[128,16]{0,1:T(8,128)S(1)}, f32[128,16]{0,1:T(8,128)S(1)}, u32[]{:S(2)}, u32[]{:S(2)}) collective-permute-start(f32[128,16]{0,1:T(8,128)S(1)} %fusion.13), channel_id=1, source_target_pairs={{0,1},{1,0},{2,3},{3,2},{4,5},{5,4},{6,7},{7,6},{8,9},{9,8},{10,11... | collective-permute-start | bytes 24584 | tf_op jit(solution)/shard_map/ppermute | solution.py:66
  123.4 3.7 %collective-permute-start.19 = (f32[128,16]{0,1:T(8,128)S(1)}, f32[128,16]{0,1:T(8,128)S(1)}, u32[]{:S(2)}, u32[]{:S(2)}) collective-permute-start(f32[128,16]{0,1:T(8,128)S(1)} %add.109), channel_id=1, source_target_pairs={{0,2},{2,0},{4,6},{6,4},{1,3},{3,1},{5,7},{7,5},{8,10},{10,8},{12,... | collective-permute-start | bytes 24584 | tf_op jit(solution)/shard_map/ppermute | solution.py:66
  127.2 5.2 %collective-permute-start.20 = (f32[128,16]{0,1:T(8,128)S(1)}, f32[128,16]{0,1:T(8,128)S(1)}, u32[]{:S(2)}, u32[]{:S(2)}) collective-permute-start(f32[128,16]{0,1:T(8,128)S(1)} %add.110), channel_id=1, source_target_pairs={{0,4},{2,6},{4,0},{6,2},{1,5},{3,7},{5,1},{7,3},{8,12},{10,14},{12... | collective-permute-start | bytes 24584 | tf_op jit(solution)/shard_map/ppermute | solution.py:66
  132.3 11.9 %collective-permute-start.21 = (f32[128,16]{0,1:T(8,128)S(1)}, f32[128,16]{0,1:T(8,128)S(1)}, u32[]{:S(2)}, u32[]{:S(2)}) collective-permute-start(f32[128,16]{0,1:T(8,128)S(1)} %add.111), channel_id=1, source_target_pairs={{0,8},{8,0},{16,24},{24,16},{32,40},{40,32},{48,56},{56,48},{1,9},... | collective-permute-start | bytes 24584 | tf_op jit(solution)/shard_map/ppermute | solution.py:66
  144.3 4.6 %collective-permute-start.22 = (f32[128,16]{0,1:T(8,128)S(1)}, f32[128,16]{0,1:T(8,128)S(1)}, u32[]{:S(2)}, u32[]{:S(2)}) collective-permute-start(f32[128,16]{0,1:T(8,128)S(1)} %add.112), channel_id=1, source_target_pairs={{0,16},{8,24},{16,0},{24,8},{32,48},{40,56},{48,32},{56,40},{1,17}... | collective-permute-start | bytes 24584 | tf_op jit(solution)/shard_map/ppermute | solution.py:66
  146.4 20.3 %collective-permute-start.8 = (f32[768,16]{0,1:T(8,128)S(1)}, f32[768,16]{0,1:T(8,128)S(1)}, u32[]{:S(2)}, u32[]{:S(2)}) collective-permute-start(f32[768,16]{0,1:T(8,128)S(1)} %bitcast.251), channel_id=1, source_target_pairs={{0,64},{64,0},{128,192},{192,128},{1,65},{65,1},{129,193},{193,129... | collective-permute-start | bytes 147464 | tf_op jit(solution)/shard_map/ppermute | solution.py:76
  148.9 7.6 %collective-permute-start.23 = (f32[128,16]{0,1:T(8,128)S(1)}, f32[128,16]{0,1:T(8,128)S(1)}, u32[]{:S(2)}, u32[]{:S(2)}) collective-permute-start(f32[128,16]{0,1:T(8,128)S(1)} %add.113), channel_id=1, source_target_pairs={{0,32},{8,40},{16,48},{24,56},{32,0},{40,8},{48,16},{56,24},{1,33}... | collective-permute-start | bytes 24584 | tf_op jit(solution)/shard_map/ppermute | solution.py:66
  156.5 13.2 %collective-permute-start.24 = (f32[128,16]{0,1:T(8,128)S(1)}, f32[128,16]{0,1:T(8,128)S(1)}, u32[]{:S(2)}, u32[]{:S(2)}) collective-permute-start(f32[128,16]{0,1:T(8,128)S(1)} %add.114), channel_id=1, source_target_pairs={{0,64},{64,0},{128,192},{192,128},{1,65},{65,1},{129,193},{193,129... | collective-permute-start | bytes 24584 | tf_op jit(solution)/shard_map/ppermute | solution.py:66
  169.7 5.2 %collective-permute-start.25 = (f32[128,16]{0,1:T(8,128)S(1)}, f32[128,16]{0,1:T(8,128)S(1)}, u32[]{:S(2)}, u32[]{:S(2)}) collective-permute-start(f32[128,16]{0,1:T(8,128)S(1)} %add.115), channel_id=1, source_target_pairs={{0,128},{64,192},{128,0},{192,64},{1,129},{65,193},{129,1},{193,65... | collective-permute-start | bytes 24584 | tf_op jit(solution)/shard_map/ppermute | solution.py:66
  172.4 6.2 %collective-permute-start.9 = (f32[1536,16]{0,1:T(8,128)S(1)}, f32[1536,16]{0,1:T(8,128)S(1)}, u32[]{:S(2)}, u32[]{:S(2)}) collective-permute-start(f32[1536,16]{0,1:T(8,128)S(1)} %pad_maximum_fusion.5), channel_id=1, source_target_pairs={{0,128},{64,192},{128,0},{192,64},{1,129},{65,193},{129,1},{193,65... | collective-permute-start | bytes 294920 | tf_op jit(solution)/shard_map/ppermute | solution.py:76
  198.8 4.2 %collective-permute-start.26 = (f32[32,8,2048]{2,1,0:T(8,128)S(1)}, f32[32,8,2048]{2,1,0:T(8,128)S(1)}, u32[]{:S(2)}, u32[]{:S(2)}) collective-permute-start(f32[32,8,2048]{2,1,0:T(8,128)S(1)} %select_bitcast_fusion), channel_id=1, source_target_pairs={{0,1},{1,0},{2,3},{3,2},{4,5},{5,4},{6,7},{7,6},{8,9},{9,8},{10,11... | collective-permute-start | bytes 6291464 | tf_op jit(solution)/shard_map/ppermute | solution.py:121
  204.0 14.1 %collective-permute-start.27 = (f32[16,8,1024]{2,1,0:T(8,128)S(1)}, f32[16,8,1024]{2,1,0:T(8,128)S(1)}, u32[]{:S(2)}, u32[]{:S(2)}) collective-permute-start(f32[16,8,1024]{2,1,0:T(8,128)S(1)} %select_bitcast_fusion.2), channel_id=1, source_target_pairs={{0,2},{2,0},{4,6},{6,4},{1,3},{3,1},{5,7},{7,5},{8,10},{10,8},{12,... | collective-permute-start | bytes 1572872 | tf_op jit(solution)/shard_map/ppermute | solution.py:121
  204.9 15.4 %collective-permute-start.31 = (f32[4,32,1024]{2,1,0:T(8,128)S(1)}, f32[4,32,1024]{2,1,0:T(8,128)S(1)}, u32[]{:S(2)}, u32[]{:S(2)}) collective-permute-start(f32[4,32,1024]{2,1,0:T(8,128)S(1)} %select_bitcast_fusion.1), channel_id=1, source_target_pairs={{0,8},{8,0},{16,24},{24,16},{32,40},{40,32},{48,56},{56,48},{1,9},... | collective-permute-start | bytes 1572872 | tf_op jit(solution)/shard_map/ppermute | solution.py:121
  218.2 7.9 %collective-permute-start.28 = (f32[4,16,1024]{2,1,0:T(8,128)S(1)}, f32[4,16,1024]{2,1,0:T(8,128)S(1)}, u32[]{:S(2)}, u32[]{:S(2)}) collective-permute-start(f32[4,16,1024]{2,1,0:T(8,128)S(1)} %select_bitcast_fusion.4), channel_id=1, source_target_pairs={{0,8},{8,0},{16,24},{24,16},{32,40},{40,32},{48,56},{56,48},{1,9},... | collective-permute-start | bytes 786440 | tf_op jit(solution)/shard_map/ppermute | solution.py:121
  220.4 8.7 %collective-permute-start.32 = (f32[8,8,1024]{2,1,0:T(8,128)S(1)}, f32[8,8,1024]{2,1,0:T(8,128)S(1)}, u32[]{:S(2)}, u32[]{:S(2)}) collective-permute-start(f32[8,8,1024]{2,1,0:T(8,128)S(1)} %select_bitcast_fusion.3), channel_id=1, source_target_pairs={{0,2},{2,0},{4,6},{6,4},{1,3},{3,1},{5,7},{7,5},{8,10},{10,8},{12,... | collective-permute-start | bytes 786440 | tf_op jit(solution)/shard_map/ppermute | solution.py:121
  226.1 6.6 %collective-permute-start.29 = (f32[4,8,1024]{2,1,0:T(8,128)S(1)}, f32[4,8,1024]{2,1,0:T(8,128)S(1)}, u32[]{:S(2)}, u32[]{:S(2)}) collective-permute-start(f32[4,8,1024]{2,1,0:T(8,128)S(1)} %select_bitcast_fusion.6), channel_id=1, source_target_pairs={{0,4},{2,6},{4,0},{6,2},{1,5},{3,7},{5,1},{7,3},{8,12},{10,14},{12... | collective-permute-start | bytes 393224 | tf_op jit(solution)/shard_map/ppermute | solution.py:121
  229.2 8.8 %collective-permute-start.33 = (f32[2,16,1024]{2,1,0:T(8,128)S(1)}, f32[2,16,1024]{2,1,0:T(8,128)S(1)}, u32[]{:S(2)}, u32[]{:S(2)}) collective-permute-start(f32[2,16,1024]{2,1,0:T(8,128)S(1)} %select_bitcast_fusion.5), channel_id=1, source_target_pairs={{0,16},{8,24},{16,0},{24,8},{32,48},{40,56},{48,32},{56,40},{1,17}... | collective-permute-start | bytes 393224 | tf_op jit(solution)/shard_map/ppermute | solution.py:121
  232.7 6.8 %collective-permute-start.30 = (f32[2,8,1024]{2,1,0:T(8,128)S(1)}, f32[2,8,1024]{2,1,0:T(8,128)S(1)}, u32[]{:S(2)}, u32[]{:S(2)}) collective-permute-start(f32[2,8,1024]{2,1,0:T(8,128)S(1)} %select_bitcast_fusion.9), channel_id=1, source_target_pairs={{0,16},{8,24},{16,0},{24,8},{32,48},{40,56},{48,32},{56,40},{1,17}... | collective-permute-start | bytes 196616 | tf_op jit(solution)/shard_map/ppermute | solution.py:121
  238.0 5.9 %collective-permute-start.34 = (f32[2,8,1024]{2,1,0:T(8,128)S(1)}, f32[2,8,1024]{2,1,0:T(8,128)S(1)}, u32[]{:S(2)}, u32[]{:S(2)}) collective-permute-start(f32[2,8,1024]{2,1,0:T(8,128)S(1)} %select_bitcast_fusion.8), channel_id=1, source_target_pairs={{0,4},{2,6},{4,0},{6,2},{1,5},{3,7},{5,1},{7,3},{8,12},{10,14},{12... | collective-permute-start | bytes 196616 | tf_op jit(solution)/shard_map/ppermute | solution.py:121
  243.9 8.3 %collective-permute-start.35 = (f32[1,8,2048]{2,1,0:T(8,128)S(1)}, f32[1,8,2048]{2,1,0:T(8,128)S(1)}, u32[]{:S(2)}, u32[]{:S(2)}) collective-permute-start(f32[1,8,2048]{2,1,0:T(8,128)S(1)} %select_bitcast_fusion.7), channel_id=1, source_target_pairs={{0,32},{8,40},{16,48},{24,56},{32,0},{40,8},{48,16},{56,24},{1,33}... | collective-permute-start | bytes 196616 | tf_op jit(solution)/shard_map/ppermute | solution.py:121

commit v9 on v7

--- a/solution.py
+++ b/solution.py
@@ -78,6 +78,21 @@
         high = jnp.where(bit == 0, other, x)
         x = jnp.concatenate([low, high], axis=0)
     return x
+
+
+def front_chain(pheno, gram, steps):
+    for axis, level in steps:
+        size = lax.axis_size(axis)
+        bit = (lax.axis_index(axis) >> level) & 1
+        flip = [(i, i ^ (1 << level)) for i in range(size)]
+        count = pheno.shape[0]
+        packed = lax.ppermute(jnp.concatenate([pheno, gram.reshape(-1)]), axis, flip)
+        other, other_gram = packed[:count], packed[count:].reshape(gram.shape)
+        low = jnp.where(bit == 0, pheno, other)
+        high = jnp.where(bit == 0, other, pheno)
+        pheno = jnp.concatenate([low, high], axis=0)
+        gram = gram + other_gram
+    return pheno, gram
 
 
 def axis_bits(axes):
@@ -154,8 +169,7 @@
     offset_rows = lax.axis_index("vgrp") * quarter
     expo_part = lax.dynamic_slice_in_dim(exposures, offset_rows, quarter, 0)
     gram_part = jnp.dot(expo_part.T, expo_part, precision=hi)
-    gram = doubling_psum(gram_part, ("core", "x", "z", "vgrp"))
-    pheno_full = doubling_gather(phenotype, axis_bits(("core", "x", "z", "vgrp")))
+    pheno_full, gram = front_chain(phenotype, gram_part, axis_bits(("core", "x", "z", "vgrp")))
     samples = pheno_full.shape[0]
     system = gram + 0.5 * samples * jnp.eye(width, dtype=jnp.float32)
     factor = jnp.linalg.cholesky(system)

time: 245 us -> 226 us (0.922)
  the two profiles are of different devices: /device:TPU:6 before, /device:TPU:2 now
where the time goes in v9:
time: 226 us; the launch traced here: 224 us
  waiting for transfers between devices  85.4 us (38%)
  starting transfers between devices  47 us (21%)
  other arithmetic  45.3 us (20%)
  Pallas kernels  21.3 us (9%)
  local copies, waits for them, and re-layouts  13.3 us (6%)
  matrix products  11.3 us (5%)
    ppermute x9, waiting for transfers between devices, halve_bit(): kept = mine + lax.ppermute(send, axis, flip)  36.4 us
    ppermute x8, waiting for transfers between devices, front_chain(): lax.ppermute(jnp.concatenate([pheno, gram.reshape(-1)]), axis, flip)  33.2 us
    ppermute x8, starting transfers between devices, front_chain(): lax.ppermute(jnp.concatenate([pheno, gram.reshape(-1)]), axis, flip)  22.5 us
    pallas_call x1, Pallas kernels, gather_pheno(): pl.pallas_call(gather_body, grid=(count // TILE,), in_specs=[pl.BlockSpec...  21.3 us
    another operation x3, other arithmetic, per_device(): factor = jnp.linalg.cholesky(system)  13.2 us
    ppermute x8, starting transfers between devices, doubling_psum(): x = x + lax.ppermute(x, axis, pairs)  11.7 us
    another operation x2, other arithmetic, chol_solve(): lax.linalg.triangular_solve(factor, middle, left_side=True, lower=True, t...  10.5 us
    ppermute x9, starting transfers between devices, halve_bit(): kept = mine + lax.ppermute(send, axis, flip)  9.32 us
  transfers between devices with their start and end apart: 28, of which 22 were waited for; matrix products, arithmetic and copies ran while one was open for 20% of the time, Pallas kernels for 0%

profile of v9, /device:TPU:2, one launch (start us, length us, event | category | flops | bytes accessed | tf_op | source)
XLA Modules:
  0.0 224.2 jit_solution(6873363109316254098)
XLA Ops:
  0.0 1.9 fusion.8
  4.6 2.3 %collective-permute-start.1 = (f32[17920]{0:T(1024)S(1)}, f32[17920]{0:T(1024)S(1)}, u32[]{:S(2)}, u32[]{:S(2)}) collective-permute-start(f32[17920]{0:T(1024)S(1)} %pad_maximum_fusion.14), channel_id=1, source_target_pairs={{0,2},{2,0},{4,6},{6,4},{1,3},{3,1},{5,7},{7,5},{8,10},{10,8},{12,... | collective-permute-start | bytes 215048 | tf_op jit(solution)/shard_map/ppermute | solution.py:89
  7.0 2.6 %collective-permute-done.1 = f32[17920]{0:T(1024)S(1)} collective-permute-done((f32[17920]{0:T(1024)S(1)}, f32[17920]{0:T(1024)S(1)}, u32[]{:S(2)}, u32[]{:S(2)}) %collective-permute-start.1) | collective-permute-done | bytes 71712 | tf_op jit(solution)/shard_map/ppermute | solution.py:89
  9.6 1.7 collective-permute-start.2
  11.3 4.3 %collective-permute-done.2 = f32[19456]{0:T(1024)S(1)} collective-permute-done((f32[19456]{0:T(1024)S(1)}, f32[19456]{0:T(1024)S(1)}, u32[]{:S(2)}, u32[]{:S(2)}) %collective-permute-start.2) | collective-permute-done | bytes 77856 | tf_op jit(solution)/shard_map/ppermute | solution.py:89
  15.7 1.5 collective-permute-start.3
  17.2 3.1 %collective-permute-done.3 = f32[22528]{0:T(1024)S(1)} collective-permute-done((f32[22528]{0:T(1024)S(1)}, f32[22528]{0:T(1024)S(1)}, u32[]{:S(2)}, u32[]{:S(2)}) %collective-permute-start.3) | collective-permute-done | bytes 90144 | tf_op jit(solution)/shard_map/ppermute | solution.py:89
  20.3 3.2 %collective-permute-start.4 = (f32[28672]{0:T(1024)S(1)}, f32[28672]{0:T(1024)S(1)}, u32[]{:S(2)}, u32[]{:S(2)}) collective-permute-start(f32[28672]{0:T(1024)S(1)} %pad_maximum_fusion.9), channel_id=1, source_target_pairs={{0,16},{8,24},{16,0},{24,8},{32,48},{40,56},{48,32},{56,40},{1,17}... | collective-permute-start | bytes 344072 | tf_op jit(solution)/shard_map/ppermute | solution.py:89
  23.6 4.0 %collective-permute-done.4 = f32[28672]{0:T(1024)S(1)} collective-permute-done((f32[28672]{0:T(1024)S(1)}, f32[28672]{0:T(1024)S(1)}, u32[]{:S(2)}, u32[]{:S(2)}) %collective-permute-start.4) | collective-permute-done | bytes 114720 | tf_op jit(solution)/shard_map/ppermute | solution.py:89
  27.7 10.1 %collective-permute-start.5 = (f32[40960]{0:T(1024)S(1)}, f32[40960]{0:T(1024)S(1)}, u32[]{:S(2)}, u32[]{:S(2)}) collective-permute-start(f32[40960]{0:T(1024)S(1)} %pad_maximum_fusion.7), channel_id=1, source_target_pairs={{0,32},{8,40},{16,48},{24,56},{32,0},{40,8},{48,16},{56,24},{1,33}... | collective-permute-start | bytes 491528 | tf_op jit(solution)/shard_map/ppermute | solution.py:89
  38.5 4.3 %collective-permute-done.5 = f32[40960]{0:T(1024)S(1)} collective-permute-done((f32[40960]{0:T(1024)S(1)}, f32[40960]{0:T(1024)S(1)}, u32[]{:S(2)}, u32[]{:S(2)}) %collective-permute-start.5) | collective-permute-done | bytes 163872 | tf_op jit(solution)/shard_map/ppermute | solution.py:89
  42.9 1.7 collective-permute-start.6
  45.0 6.0 %collective-permute-done.6 = f32[65536]{0:T(1024)S(1)} collective-permute-done((f32[65536]{0:T(1024)S(1)}, f32[65536]{0:T(1024)S(1)}, u32[]{:S(2)}, u32[]{:S(2)}) %collective-permute-start.6) | collective-permute-done | bytes 262176 | tf_op jit(solution)/shard_map/ppermute | solution.py:89
  51.2 1.9 collective-permute-start.7
  53.5 7.7 %collective-permute-done.7 = f32[114688]{0:T(1024)S(1)} collective-permute-done((f32[114688]{0:T(1024)S(1)}, f32[114688]{0:T(1024)S(1)}, u32[]{:S(2)}, u32[]{:S(2)}) %collective-permute-start.7) | collective-permute-done | bytes 458784 | tf_op jit(solution)/shard_map/ppermute | solution.py:89
  63.3 21.3 %shard_map.46 = f32[1,12288]{1,0:T(1,128)} custom-call(s32[1,12288]{1,0:T(1,128)} %bitcast.303, bf16[768,768]{1,0:T(8,128)(2,1)} %pad_maximum_fusion.tab_ref), custom_call_target="tpu_custom_call" | custom-call | tf_op jit(solution)/shard_map/pallas_call | solution.py:46
  85.2 1.6 reduce.9
  88.2 6.6 %copy.79 = s32[3072,512]{0,1:T(8,128)} copy(s32[3072,512]{1,0:T(8,128)} %param.7) | data formatting | bytes 12582912 | tf_op args[3]
  94.8 3.5 %convert_element_type.51 = bf16[3072,512]{0,1:T(8,128)(2,1)S(1)} convert(s32[3072,512]{0,1:T(8,128)} %copy.79) | non-fusion elementwise | flops 1572864 | bytes 9437184 | tf_op jit(solution)/shard_map/convert_element_type | solution.py:146
  98.3 1.8 copy.80
  102.0 1.6 fusion.27
  103.6 1.6 copy.78
  106.7 2.1 collective-permute-start.12
  108.8 1.7 fusion.42
  110.5 12.5 %cholesky.16 = f32[128,128]{1,0:T(8,128)S(1)} custom-call(f32[128,128]{1,0:T(8,128)} %fusion.42), custom_call_target="Cholesky" | custom-call | tf_op jit(solution)/shard_map/jit(cholesky)/cholesky | solution.py:175
  123.9 3.6 %collective-permute-done.13 = f32[128,16]{0,1:T(8,128)S(1)} collective-permute-done((f32[128,16]{0,1:T(8,128)S(1)}, f32[128,16]{0,1:T(8,128)S(1)}, u32[]{:S(2)}, u32[]{:S(2)}) %collective-permute-start.13) | collective-permute-done | bytes 8224 | tf_op jit(solution)/shard_map/ppermute | solution.py:66
  129.9 2.1 collective-permute-done.14
  132.0 5.3 %collective-permute-start.15 = (f32[128,16]{0,1:T(8,128)S(1)}, f32[128,16]{0,1:T(8,128)S(1)}, u32[]{:S(2)}, u32[]{:S(2)}) collective-permute-start(f32[128,16]{0,1:T(8,128)S(1)} %add.113), channel_id=1, source_target_pairs={{0,32},{8,40},{16,48},{24,56},{32,0},{40,8},{48,16},{56,24},{1,33}... | collective-permute-start | bytes 24584 | tf_op jit(solution)/shard_map/ppermute | solution.py:66
  138.0 9.8 %custom-call.8 = f32[1,128,128]{1,2,0:T(8,128)S(1)} custom-call(f32[1,128,128]{2,1,0:T(8,128)S(1)} %fusion.24), custom_call_target="InvertDiagBlocksLowerTriangular" | custom-call | tf_op jit(solution)/shard_map/triangular_solve | solution.py:13
  147.9 1.4 collective-permute-start.16
  150.1 1.5 collective-permute-done.16
  151.6 1.8 collective-permute-start.17
  153.5 2.0 collective-permute-start.9
  157.1 2.8 %collective-permute-done.9 = f32[1536,16]{0,1:T(8,128)S(1)} collective-permute-done((f32[1536,16]{0,1:T(8,128)S(1)}, f32[1536,16]{0,1:T(8,128)S(1)}, u32[]{:S(2)}, u32[]{:S(2)}) %collective-permute-start.9) | collective-permute-done | bytes 98336 | tf_op jit(solution)/shard_map/ppermute | solution.py:76
  159.9 1.4 maximum_subtract_fusion
  161.3 3.5 %multiply_convert_fusion = bf16[3072,128,16]{0,2,1:T(8,128)(2,1)S(1)} fusion(f32[3072,16]{0,1:T(8,128)S(1)} %maximum_subtract_fusion, f32[3072,128]{0,1:T(8,128)S(1)} %copy.67), kind=kLoop, calls=%fused_computation | loop fusion | flops 12582912 | bytes 14352384 | tf_op jit(solution)/shard_map/convert_element_type | solution.py:187
  164.8 6.7 %fusion.53 = f32[2048,512]{0,1:T(8,128)S(1)} fusion(bf16[3072,2048]{0,1:T(8,128)(2,1)S(1)} %bitcast.286, bf16[3072,512]{0,1:T(8,128)(2,1)S(1)} %bitcast.297), kind=kOutput, calls=%fused_computation.136 | convolution fusion | flops 6442450944 | bytes 19922944 | tf_op jit(solution)/shard_map/dot_general | solution.py:147
  172.0 4.1 %collective-permute-done.18 = f32[2048,256]{0,1:T(8,128)S(1)} collective-permute-done((f32[2048,256]{0,1:T(8,128)S(1)}, f32[2048,256]{0,1:T(8,128)S(1)}, u32[]{:S(2)}, u32[]{:S(2)}) %collective-permute-start.18) | collective-permute-done | bytes 2097184 | tf_op jit(solution)/shard_map/ppermute | solution.py:122
  177.0 1.9 collective-permute-start.19
  179.0 12.1 %collective-permute-done.19 = f32[1,128,1024]{2,1,0:T(8,128)S(1)} collective-permute-done((f32[1,128,1024]{2,1,0:T(8,128)S(1)}, f32[1,128,1024]{2,1,0:T(8,128)S(1)}, u32[]{:S(2)}, u32[]{:S(2)}) %collective-permute-start.19) | collective-permute-done | bytes 524320 | tf_op jit(solution)/shard_map/ppermute | solution.py:136
  191.3 1.4 collective-permute-done.23
  193.3 5.5 %collective-permute-done.20 = f32[2,32,1024]{2,1,0:T(8,128)S(1)} collective-permute-done((f32[2,32,1024]{2,1,0:T(8,128)S(1)}, f32[2,32,1024]{2,1,0:T(8,128)S(1)}, u32[]{:S(2)}, u32[]{:S(2)}) %collective-permute-start.20) | collective-permute-done | bytes 262176 | tf_op jit(solution)/shard_map/ppermute | solution.py:136
  198.9 1.4 collective-permute-start.21
  201.3 4.2 %collective-permute-done.21 = f32[1,32,1024]{2,1,0:T(8,128)S(1)} collective-permute-done((f32[1,32,1024]{2,1,0:T(8,128)S(1)}, f32[1,32,1024]{2,1,0:T(8,128)S(1)}, u32[]{:S(2)}, u32[]{:S(2)}) %collective-permute-start.21) | collective-permute-done | bytes 131104 | tf_op jit(solution)/shard_map/ppermute | solution.py:136
  206.2 2.9 %collective-permute-done.25 = f32[2,16,1024]{2,1,0:T(8,128)S(1)} collective-permute-done((f32[2,16,1024]{2,1,0:T(8,128)S(1)}, f32[2,16,1024]{2,1,0:T(8,128)S(1)}, u32[]{:S(2)}, u32[]{:S(2)}) %collective-permute-start.25) | collective-permute-done | bytes 131104 | tf_op jit(solution)/shard_map/ppermute | solution.py:136
  209.2 3.1 %collective-permute-start.26 = (f32[1,16,1024]{2,1,0:T(8,128)S(1)}, f32[1,16,1024]{2,1,0:T(8,128)S(1)}, u32[]{:S(2)}, u32[]{:S(2)}) collective-permute-start(f32[1,16,1024]{2,1,0:T(8,128)S(1)} %select_bitcast_fusion.7), channel_id=1, source_target_pairs={{0,4},{2,6},{4,0},{6,2},{1,5},{3,7},{5,1},{7,3},{8,12},{10,14},{12... | collective-permute-start | bytes 196616 | tf_op jit(solution)/shard_map/ppermute | solution.py:136
  212.3 2.8 %collective-permute-done.26 = f32[1,16,1024]{2,1,0:T(8,128)S(1)} collective-permute-done((f32[1,16,1024]{2,1,0:T(8,128)S(1)}, f32[1,16,1024]{2,1,0:T(8,128)S(1)}, u32[]{:S(2)}, u32[]{:S(2)}) %collective-permute-start.26) | collective-permute-done | bytes 65568 | tf_op jit(solution)/shard_map/ppermute | solution.py:136
  215.8 7.6 %collective-permute-done.27 = f32[1,8,2048]{2,1,0:T(8,128)S(1)} collective-permute-done((f32[1,8,2048]{2,1,0:T(8,128)S(1)}, f32[1,8,2048]{2,1,0:T(8,128)S(1)}, u32[]{:S(2)}, u32[]{:S(2)}) %collective-permute-start.27) | collective-permute-done | bytes 65568 | tf_op jit(solution)/shard_map/ppermute | solution.py:136
  (134 shorter events, 24.0 us)
Async XLA Ops:
  0.0 37.8 %copy-start = (s32[16,3072]{1,0:T(8,128)S(1)}, s32[16,3072]{1,0:T(8,128)}, u32[]{:S(2)}) copy-start(s32[16,3072]{1,0:T(8,128)} %param.6) | copy-start | bytes 589828
  2.7 1.3 collective-permute-start
  4.6 4.9 %collective-permute-start.1 = (f32[17920]{0:T(1024)S(1)}, f32[17920]{0:T(1024)S(1)}, u32[]{:S(2)}, u32[]{:S(2)}) collective-permute-start(f32[17920]{0:T(1024)S(1)} %pad_maximum_fusion.14), channel_id=1, source_target_pairs={{0,2},{2,0},{4,6},{6,4},{1,3},{3,1},{5,7},{7,5},{8,10},{10,8},{12,... | collective-permute-start | bytes 215048 | tf_op jit(solution)/shard_map/ppermute | solution.py:89
  9.6 6.0 %collective-permute-start.2 = (f32[19456]{0:T(1024)S(1)}, f32[19456]{0:T(1024)S(1)}, u32[]{:S(2)}, u32[]{:S(2)}) collective-permute-start(f32[19456]{0:T(1024)S(1)} %pad_maximum_fusion.13), channel_id=1, source_target_pairs={{0,4},{2,6},{4,0},{6,2},{1,5},{3,7},{5,1},{7,3},{8,12},{10,14},{12... | collective-permute-start | bytes 233480 | tf_op jit(solution)/shard_map/ppermute | solution.py:89
  15.6 35.4 %copy-start.3 = (f32[19456]{0:T(1024)}, f32[19456]{0:T(1024)S(1)}, u32[]{:S(2)}) copy-start(f32[19456]{0:T(1024)S(1)} %collective-permute-done.2) | copy-start | bytes 233476
  15.7 4.6 %collective-permute-start.3 = (f32[22528]{0:T(1024)S(1)}, f32[22528]{0:T(1024)S(1)}, u32[]{:S(2)}, u32[]{:S(2)}) collective-permute-start(f32[22528]{0:T(1024)S(1)} %pad_maximum_fusion.12), channel_id=1, source_target_pairs={{0,8},{8,0},{16,24},{24,16},{32,40},{40,32},{48,56},{56,48},{1,9},... | collective-permute-start | bytes 270344 | tf_op jit(solution)/shard_map/ppermute | solution.py:89
  20.3 30.7 %copy-start.5 = (f32[22528]{0:T(1024)}, f32[22528]{0:T(1024)S(1)}, u32[]{:S(2)}) copy-start(f32[22528]{0:T(1024)S(1)} %collective-permute-done.3) | copy-start | bytes 270340
  20.3 7.2 %collective-permute-start.4 = (f32[28672]{0:T(1024)S(1)}, f32[28672]{0:T(1024)S(1)}, u32[]{:S(2)}, u32[]{:S(2)}) collective-permute-start(f32[28672]{0:T(1024)S(1)} %pad_maximum_fusion.9), channel_id=1, source_target_pairs={{0,16},{8,24},{16,0},{24,8},{32,48},{40,56},{48,32},{56,40},{1,17}... | collective-permute-start | bytes 344072 | tf_op jit(solution)/shard_map/ppermute | solution.py:89
  27.6 23.4 %copy-start.7 = (f32[28672]{0:T(1024)}, f32[28672]{0:T(1024)S(1)}, u32[]{:S(2)}) copy-start(f32[28672]{0:T(1024)S(1)} %collective-permute-done.4) | copy-start | bytes 344068
  27.7 15.1 %collective-permute-start.5 = (f32[40960]{0:T(1024)S(1)}, f32[40960]{0:T(1024)S(1)}, u32[]{:S(2)}, u32[]{:S(2)}) collective-permute-start(f32[40960]{0:T(1024)S(1)} %pad_maximum_fusion.7), channel_id=1, source_target_pairs={{0,32},{8,40},{16,48},{24,56},{32,0},{40,8},{48,16},{56,24},{1,33}... | collective-permute-start | bytes 491528 | tf_op jit(solution)/shard_map/ppermute | solution.py:89
  42.8 8.3 %copy-start.9 = (f32[40960]{0:T(1024)}, f32[40960]{0:T(1024)S(1)}, u32[]{:S(2)}) copy-start(f32[40960]{0:T(1024)S(1)} %collective-permute-done.5) | copy-start | bytes 491524
  42.9 8.1 %collective-permute-start.6 = (f32[65536]{0:T(1024)S(1)}, f32[65536]{0:T(1024)S(1)}, u32[]{:S(2)}, u32[]{:S(2)}) collective-permute-start(f32[65536]{0:T(1024)S(1)} %pad_maximum_fusion.5), channel_id=1, source_target_pairs={{0,64},{64,0},{128,192},{192,128},{1,65},{65,1},{129,193},{193,129... | collective-permute-start | bytes 786440 | tf_op jit(solution)/shard_map/ppermute | solution.py:89
  51.0 2.4 %copy-start.11 = (f32[65536]{0:T(1024)}, f32[65536]{0:T(1024)S(1)}, u32[]{:S(2)}) copy-start(f32[65536]{0:T(1024)S(1)} %collective-permute-done.6) | copy-start | bytes 786436
  51.2 10.1 %collective-permute-start.7 = (f32[114688]{0:T(1024)S(1)}, f32[114688]{0:T(1024)S(1)}, u32[]{:S(2)}, u32[]{:S(2)}) collective-permute-start(f32[114688]{0:T(1024)S(1)} %pad_maximum_fusion.2), channel_id=1, source_target_pairs={{0,128},{64,192},{128,0},{192,64},{1,129},{65,193},{129,1},{193,65... | collective-permute-start | bytes 1376264 | tf_op jit(solution)/shard_map/ppermute | solution.py:89
  61.2 0.8 copy-start.10
  62.2 24.6 %copy-start.1 = (f32[3072,128]{1,0:T(8,128)S(1)}, f32[3072,128]{1,0:T(8,128)}, u32[]{:S(2)}) copy-start(f32[3072,128]{1,0:T(8,128)} %param.5) | copy-start | bytes 4718596
  86.7 0.9 copy-start.12
  87.7 12.5 %collective-permute-start.10 = (f32[128,16]{0,1:T(8,128)}, f32[128,16]{0,1:T(8,128)}, u32[]{:S(2)}, u32[]{:S(2)}) collective-permute-start(f32[128,16]{0,1:T(8,128)} %fusion.6), channel_id=1, source_target_pairs={{0,1},{1,0},{2,3},{3,2},{4,5},{5,4},{6,7},{7,6},{8,9},{9,8},{10,11... | collective-permute-start | bytes 24584 | tf_op jit(solution)/shard_map/ppermute | solution.py:66
  98.3 3.7 %copy-start.4 = (f32[19456]{0:T(1024)S(1)}, f32[19456]{0:T(1024)}, u32[]{:S(2)}) copy-start(f32[19456]{0:T(1024)} %copy-done.3) | copy-start | bytes 233476
  98.3 3.7 %copy-start.6 = (f32[22528]{0:T(1024)S(1)}, f32[22528]{0:T(1024)}, u32[]{:S(2)}) copy-start(f32[22528]{0:T(1024)} %copy-done.5) | copy-start | bytes 270340
  98.3 3.7 %copy-start.8 = (f32[28672]{0:T(1024)S(1)}, f32[28672]{0:T(1024)}, u32[]{:S(2)}) copy-start(f32[28672]{0:T(1024)} %copy-done.7) | copy-start | bytes 344068
  101.4 4.0 %collective-permute-start.11 = (f32[128,16]{0,1:T(8,128)}, f32[128,16]{0,1:T(8,128)}, u32[]{:S(2)}, u32[]{:S(2)}) collective-permute-start(f32[128,16]{0,1:T(8,128)} %add.109), channel_id=1, source_target_pairs={{0,2},{2,0},{4,6},{6,4},{1,3},{3,1},{5,7},{7,5},{8,10},{10,8},{12,... | collective-permute-start | bytes 24584 | tf_op jit(solution)/shard_map/ppermute | solution.py:66
  106.7 16.4 %collective-permute-start.12 = (f32[128,16]{0,1:T(8,128)}, f32[128,16]{0,1:T(8,128)}, u32[]{:S(2)}, u32[]{:S(2)}) collective-permute-start(f32[128,16]{0,1:T(8,128)} %add.110), channel_id=1, source_target_pairs={{0,4},{2,6},{4,0},{6,2},{1,5},{3,7},{5,1},{7,3},{8,12},{10,14},{12... | collective-permute-start | bytes 24584 | tf_op jit(solution)/shard_map/ppermute | solution.py:66
  123.8 3.7 %collective-permute-start.13 = (f32[128,16]{0,1:T(8,128)S(1)}, f32[128,16]{0,1:T(8,128)S(1)}, u32[]{:S(2)}, u32[]{:S(2)}) collective-permute-start(f32[128,16]{0,1:T(8,128)S(1)} %add.111), channel_id=1, source_target_pairs={{0,8},{8,0},{16,24},{24,16},{32,40},{40,32},{48,56},{56,48},{1,9},... | collective-permute-start | bytes 24584 | tf_op jit(solution)/shard_map/ppermute | solution.py:66
  127.5 4.5 %collective-permute-start.14 = (f32[128,16]{0,1:T(8,128)S(1)}, f32[128,16]{0,1:T(8,128)S(1)}, u32[]{:S(2)}, u32[]{:S(2)}) collective-permute-start(f32[128,16]{0,1:T(8,128)S(1)} %add.112), channel_id=1, source_target_pairs={{0,16},{8,24},{16,0},{24,8},{32,48},{40,56},{48,32},{56,40},{1,17}... | collective-permute-start | bytes 24584 | tf_op jit(solution)/shard_map/ppermute | solution.py:66
  128.5 20.8 %collective-permute-start.8 = (f32[768,16]{0,1:T(8,128)}, f32[768,16]{0,1:T(8,128)S(1)}, u32[]{:S(2)}, u32[]{:S(2)}) collective-permute-start(f32[768,16]{0,1:T(8,128)} %bitcast.302), channel_id=1, source_target_pairs={{0,64},{64,0},{128,192},{192,128},{1,65},{65,1},{129,193},{193,129... | collective-permute-start | bytes 147464 | tf_op jit(solution)/shard_map/ppermute | solution.py:76
  132.0 15.8 %collective-permute-start.15 = (f32[128,16]{0,1:T(8,128)S(1)}, f32[128,16]{0,1:T(8,128)S(1)}, u32[]{:S(2)}, u32[]{:S(2)}) collective-permute-start(f32[128,16]{0,1:T(8,128)S(1)} %add.113), channel_id=1, source_target_pairs={{0,32},{8,40},{16,48},{24,56},{32,0},{40,8},{48,16},{56,24},{1,33}... | collective-permute-start | bytes 24584 | tf_op jit(solution)/shard_map/ppermute | solution.py:66
  147.9 3.7 %collective-permute-start.16 = (f32[128,16]{0,1:T(8,128)S(1)}, f32[128,16]{0,1:T(8,128)S(1)}, u32[]{:S(2)}, u32[]{:S(2)}) collective-permute-start(f32[128,16]{0,1:T(8,128)S(1)} %add.114), channel_id=1, source_target_pairs={{0,64},{64,0},{128,192},{192,128},{1,65},{65,1},{129,193},{193,129... | collective-permute-start | bytes 24584 | tf_op jit(solution)/shard_map/ppermute | solution.py:66
  151.6 5.2 %collective-permute-start.17 = (f32[128,16]{0,1:T(8,128)S(1)}, f32[128,16]{0,1:T(8,128)S(1)}, u32[]{:S(2)}, u32[]{:S(2)}) collective-permute-start(f32[128,16]{0,1:T(8,128)S(1)} %add.115), channel_id=1, source_target_pairs={{0,128},{64,192},{128,0},{192,64},{1,129},{65,193},{129,1},{193,65... | collective-permute-start | bytes 24584 | tf_op jit(solution)/shard_map/ppermute | solution.py:66
  153.5 6.4 %collective-permute-start.9 = (f32[1536,16]{0,1:T(8,128)S(1)}, f32[1536,16]{0,1:T(8,128)S(1)}, u32[]{:S(2)}, u32[]{:S(2)}) collective-permute-start(f32[1536,16]{0,1:T(8,128)S(1)} %pad_maximum_fusion.11), channel_id=1, source_target_pairs={{0,128},{64,192},{128,0},{192,64},{1,129},{65,193},{129,1},{193,65... | collective-permute-start | bytes 294920 | tf_op jit(solution)/shard_map/ppermute | solution.py:76
  161.3 3.5 %copy-start.2 = (bf16[3072,2,2,2,2,2,2,8]{0,7,6,5,4,3,2,1:T(8,128)(2,1)S(1)}, bf16[3072,2,2,2,2,2,2,8]{0,7,6,5,4,3,2,1:T(8,128)(2,1)}, u32[]{:S(2)}) copy-start(bf16[3072,2,2,2,2,2,2,8]{0,7,6,5,4,3,2,1:T(8,128)(2,1)} %copy.80) | copy-start | bytes 9437188
  171.9 4.2 %collective-permute-start.18 = (f32[2048,256]{0,1:T(8,128)S(1)}, f32[2048,256]{0,1:T(8,128)S(1)}, u32[]{:S(2)}, u32[]{:S(2)}) collective-permute-start(f32[2048,256]{0,1:T(8,128)S(1)} %slice_select_fusion), channel_id=1, source_target_pairs={{0,1},{1,0},{2,3},{3,2},{4,5},{5,4},{6,7},{7,6},{8,9},{9,8},{10,11... | collective-permute-start | bytes 6291464 | tf_op jit(solution)/shard_map/ppermute | solution.py:122
  177.0 14.1 %collective-permute-start.19 = (f32[1,128,1024]{2,1,0:T(8,128)S(1)}, f32[1,128,1024]{2,1,0:T(8,128)S(1)}, u32[]{:S(2)}, u32[]{:S(2)}) collective-permute-start(f32[1,128,1024]{2,1,0:T(8,128)S(1)} %select_bitcast_fusion.1), channel_id=1, source_target_pairs={{0,2},{2,0},{4,6},{6,4},{1,3},{3,1},{5,7},{7,5},{8,10},{10,8},{12,... | collective-permute-start | bytes 1572872 | tf_op jit(solution)/shard_map/ppermute | solution.py:136
  178.9 13.8 %collective-permute-start.23 = (f32[4,32,1024]{2,1,0:T(8,128)S(1)}, f32[4,32,1024]{2,1,0:T(8,128)S(1)}, u32[]{:S(2)}, u32[]{:S(2)}) collective-permute-start(f32[4,32,1024]{2,1,0:T(8,128)S(1)} %select_bitcast_fusion), channel_id=1, source_target_pairs={{0,8},{8,0},{16,24},{24,16},{32,40},{40,32},{48,56},{56,48},{1,9},... | collective-permute-start | bytes 1572872 | tf_op jit(solution)/shard_map/ppermute | solution.py:136
  191.2 7.6 %collective-permute-start.20 = (f32[2,32,1024]{2,1,0:T(8,128)S(1)}, f32[2,32,1024]{2,1,0:T(8,128)S(1)}, u32[]{:S(2)}, u32[]{:S(2)}) collective-permute-start(f32[2,32,1024]{2,1,0:T(8,128)S(1)} %select_bitcast_fusion.3), channel_id=1, source_target_pairs={{0,8},{8,0},{16,24},{24,16},{32,40},{40,32},{48,56},{56,48},{1,9},... | collective-permute-start | bytes 786440 | tf_op jit(solution)/shard_map/ppermute | solution.py:136
  192.8 7.5 %collective-permute-start.24 = (f32[1,64,1024]{2,1,0:T(8,128)S(1)}, f32[1,64,1024]{2,1,0:T(8,128)S(1)}, u32[]{:S(2)}, u32[]{:S(2)}) collective-permute-start(f32[1,64,1024]{2,1,0:T(8,128)S(1)} %select_bitcast_fusion.2), channel_id=1, source_target_pairs={{0,2},{2,0},{4,6},{6,4},{1,3},{3,1},{5,7},{7,5},{8,10},{10,8},{12,... | collective-permute-start | bytes 786440 | tf_op jit(solution)/shard_map/ppermute | solution.py:136
  198.9 6.6 %collective-permute-start.21 = (f32[1,32,1024]{2,1,0:T(8,128)S(1)}, f32[1,32,1024]{2,1,0:T(8,128)S(1)}, u32[]{:S(2)}, u32[]{:S(2)}) collective-permute-start(f32[1,32,1024]{2,1,0:T(8,128)S(1)} %select_bitcast_fusion.5), channel_id=1, source_target_pairs={{0,4},{2,6},{4,0},{6,2},{1,5},{3,7},{5,1},{7,3},{8,12},{10,14},{12... | collective-permute-start | bytes 393224 | tf_op jit(solution)/shard_map/ppermute | solution.py:136
  200.4 8.7 %collective-permute-start.25 = (f32[2,16,1024]{2,1,0:T(8,128)S(1)}, f32[2,16,1024]{2,1,0:T(8,128)S(1)}, u32[]{:S(2)}, u32[]{:S(2)}) collective-permute-start(f32[2,16,1024]{2,1,0:T(8,128)S(1)} %select_bitcast_fusion.4), channel_id=1, source_target_pairs={{0,16},{8,24},{16,0},{24,8},{32,48},{40,56},{48,32},{56,40},{1,17}... | collective-permute-start | bytes 393224 | tf_op jit(solution)/shard_map/ppermute | solution.py:136
  205.5 6.7 %collective-permute-start.22 = (f32[1,16,1024]{2,1,0:T(8,128)S(1)}, f32[1,16,1024]{2,1,0:T(8,128)S(1)}, u32[]{:S(2)}, u32[]{:S(2)}) collective-permute-start(f32[1,16,1024]{2,1,0:T(8,128)S(1)} %select_bitcast_fusion.8), channel_id=1, source_target_pairs={{0,16},{8,24},{16,0},{24,8},{32,48},{40,56},{48,32},{56,40},{1,17}... | collective-permute-start | bytes 196616 | tf_op jit(solution)/shard_map/ppermute | solution.py:136
  209.2 5.9 %collective-permute-start.26 = (f32[1,16,1024]{2,1,0:T(8,128)S(1)}, f32[1,16,1024]{2,1,0:T(8,128)S(1)}, u32[]{:S(2)}, u32[]{:S(2)}) collective-permute-start(f32[1,16,1024]{2,1,0:T(8,128)S(1)} %select_bitcast_fusion.7), channel_id=1, source_target_pairs={{0,4},{2,6},{4,0},{6,2},{1,5},{3,7},{5,1},{7,3},{8,12},{10,14},{12... | collective-permute-start | bytes 196616 | tf_op jit(solution)/shard_map/ppermute | solution.py:136
  215.1 8.3 %collective-permute-start.27 = (f32[1,8,2048]{2,1,0:T(8,128)S(1)}, f32[1,8,2048]{2,1,0:T(8,128)S(1)}, u32[]{:S(2)}, u32[]{:S(2)}) collective-permute-start(f32[1,8,2048]{2,1,0:T(8,128)S(1)} %select_bitcast_fusion.6), channel_id=1, source_target_pairs={{0,32},{8,40},{16,48},{24,56},{32,0},{40,8},{48,16},{56,24},{1,33}... | collective-permute-start | bytes 196616 | tf_op jit(solution)/shard_map/ppermute | solution.py:136

commit v10 on v9

--- a/solution.py
+++ b/solution.py
@@ -80,8 +80,10 @@
     return x
 
 
-def front_chain(pheno, gram, steps):
-    for axis, level in steps:
+def front_chain(pheno, gram, steps, side, tie_after):
+    for index, (axis, level) in enumerate(steps):
+        if index == tie_after:
+            pheno, gram, side = lax.optimization_barrier((pheno, gram, side))
         size = lax.axis_size(axis)
         bit = (lax.axis_index(axis) >> level) & 1
         flip = [(i, i ^ (1 << level)) for i in range(size)]
@@ -92,7 +94,7 @@
         high = jnp.where(bit == 0, other, pheno)
         pheno = jnp.concatenate([low, high], axis=0)
         gram = gram + other_gram
-    return pheno, gram
+    return pheno, gram, side
 
 
 def axis_bits(axes):
@@ -137,13 +139,16 @@
     return kept.reshape(rows // 2, cols), [n for n in names if n != name]
 
 
-def halving_scores(weighted, genotypes):
+def reorder_dosages(genotypes):
     local_rows, variants = genotypes.shape
     nz, nx, nc = (lax.axis_size(a) for a in SAMP)
     own_rows = variants // (nz * nx * nc)
     order = genotypes.reshape(local_rows, 2, 2, 2, 2, 2, nc, own_rows)
     order = order.transpose(0, 6, 5, 4, 3, 2, 1, 7)
-    dosages = order.reshape(local_rows, variants).astype(jnp.bfloat16)
+    return order.reshape(local_rows, variants).astype(jnp.bfloat16)
+
+
+def halving_scores(weighted, dosages):
     cur = jnp.dot(weighted.T, dosages, preferred_element_type=jnp.float32)
     half = cur.shape[1] // 2
     cur = exchange(cur[:, :half], cur[:, half:], "core", 0, 1).T
@@ -169,7 +174,8 @@
     offset_rows = lax.axis_index("vgrp") * quarter
     expo_part = lax.dynamic_slice_in_dim(exposures, offset_rows, quarter, 0)
     gram_part = jnp.dot(expo_part.T, expo_part, precision=hi)
-    pheno_full, gram = front_chain(phenotype, gram_part, axis_bits(("core", "x", "z", "vgrp")))
+    steps = axis_bits(("core", "x", "z", "vgrp"))
+    pheno_full, gram, dosages = front_chain(phenotype, gram_part, steps, reorder_dosages(genotypes), 5)
     samples = pheno_full.shape[0]
     system = gram + 0.5 * samples * jnp.eye(width, dtype=jnp.float32)
     factor = jnp.linalg.cholesky(system)
@@ -186,7 +192,7 @@
         .reshape(local_rows, width * nperm)
         .astype(jnp.bfloat16)
     )
-    own_scores = halving_scores(weighted, genotypes)
+    own_scores = halving_scores(weighted, dosages)
     shaped = own_scores.reshape(own_scores.shape[0], width, nperm)
     return jnp.sum(shaped * shaped, axis=1) / (samples * width)
 

time: 226 us -> 214 us (0.947)
  waiting for transfers between devices: 85.4 us -> 73.1 us
  starting transfers between devices: 47 us -> 54.4 us
  other arithmetic: 45.3 us -> 39.5 us
    ppermute x9, waiting for transfers between devices: 36.4 us -> 28.3 us  [halve_bit(): kept = mine + lax.ppermute(send, axis, flip)]
    ppermute x9, starting transfers between devices: 9.32 us -> 17.2 us  [halve_bit(): kept = mine + lax.ppermute(send, axis, flip)]
    ppermute x8, waiting for transfers between devices: 33.2 us -> 27.2 us  [front_chain(): lax.ppermute(jnp.concatenate([pheno, gram.reshape(-1)]), axis, flip)]
    add x7, other arithmetic: 3.34 us -> 0.03 us  [doubling_psum(): x = x + lax.ppermute(x, axis, pairs)]
    ppermute x8, starting transfers between devices: 11.7 us -> 14.9 us  [doubling_psum(): x = x + lax.ppermute(x, axis, pairs)]
    ppermute x8, starting transfers between devices: 22.5 us -> 20.2 us  [front_chain(): lax.ppermute(jnp.concatenate([pheno, gram.reshape(-1)]), axis, flip)]
    unnamed x30 -> x16, local copies, waits for them, and re-layouts: 8.12 us -> 8.52 us
  transfers between devices with their start and end apart: 28 -> 28, of which waited for: 22 -> 22; matrix products, arithmetic and copies ran while one was open for 20% -> 19% of each run, Pallas kernels for 0% -> 0%
where the time goes in v10:
time: 214 us; the launch traced here: 212 us
  waiting for transfers between devices  73.1 us (34%)
  starting transfers between devices  54.4 us (25%)
  other arithmetic  39.5 us (18%)
  Pallas kernels  21.3 us (10%)
  local copies, waits for them, and re-layouts  12.8 us (6%)
  matrix products  10.7 us (5%)
    ppermute x9, waiting for transfers between devices, halve_bit(): kept = mine + lax.ppermute(send, axis, flip)  28.3 us
    ppermute x8, waiting for transfers between devices, front_chain(): lax.ppermute(jnp.concatenate([pheno, gram.reshape(-1)]), axis, flip)  27.2 us
    pallas_call x1, Pallas kernels, gather_pheno(): pl.pallas_call(gather_body, grid=(count // TILE,), in_specs=[pl.BlockSpec...  21.3 us
    ppermute x8, starting transfers between devices, front_chain(): lax.ppermute(jnp.concatenate([pheno, gram.reshape(-1)]), axis, flip)  20.2 us
    ppermute x9, starting transfers between devices, halve_bit(): kept = mine + lax.ppermute(send, axis, flip)  17.2 us
    ppermute x8, starting transfers between devices, doubling_psum(): x = x + lax.ppermute(x, axis, pairs)  14.9 us
    another operation x3, other arithmetic, per_device(): factor = jnp.linalg.cholesky(system)  12.4 us
    another operation x2, other arithmetic, chol_solve(): lax.linalg.triangular_solve(factor, middle, left_side=True, lower=True, t...  10.5 us
  transfers between devices with their start and end apart: 28, of which 22 were waited for; matrix products, arithmetic and copies ran while one was open for 19% of the time, Pallas kernels for 0%

profile of v10, /device:TPU:2, one launch (start us, length us, event | category | flops | bytes accessed | tf_op | source)
XLA Modules:
  0.0 212.3 jit_solution(14694626900867558835)
XLA Ops:
  0.0 1.9 fusion.8
  4.6 2.3 %collective-permute-start.1 = (f32[17920]{0:T(1024)S(1)}, f32[17920]{0:T(1024)S(1)}, u32[]{:S(2)}, u32[]{:S(2)}) collective-permute-start(f32[17920]{0:T(1024)S(1)} %pad_maximum_fusion.13), channel_id=1, source_target_pairs={{0,2},{2,0},{4,6},{6,4},{1,3},{3,1},{5,7},{7,5},{8,10},{10,8},{12,... | collective-permute-start | bytes 215048 | tf_op jit(solution)/shard_map/ppermute | solution.py:91
  7.0 2.6 %collective-permute-done.1 = f32[17920]{0:T(1024)S(1)} collective-permute-done((f32[17920]{0:T(1024)S(1)}, f32[17920]{0:T(1024)S(1)}, u32[]{:S(2)}, u32[]{:S(2)}) %collective-permute-start.1) | collective-permute-done | bytes 71712 | tf_op jit(solution)/shard_map/ppermute | solution.py:91
  9.6 1.7 collective-permute-start.2
  11.3 4.3 %collective-permute-done.2 = f32[19456]{0:T(1024)S(1)} collective-permute-done((f32[19456]{0:T(1024)S(1)}, f32[19456]{0:T(1024)S(1)}, u32[]{:S(2)}, u32[]{:S(2)}) %collective-permute-start.2) | collective-permute-done | bytes 77856 | tf_op jit(solution)/shard_map/ppermute | solution.py:91
  15.7 1.5 collective-permute-start.3
  17.2 3.1 %collective-permute-done.3 = f32[22528]{0:T(1024)S(1)} collective-permute-done((f32[22528]{0:T(1024)S(1)}, f32[22528]{0:T(1024)S(1)}, u32[]{:S(2)}, u32[]{:S(2)}) %collective-permute-start.3) | collective-permute-done | bytes 90144 | tf_op jit(solution)/shard_map/ppermute | solution.py:91
  20.3 3.2 %collective-permute-start.4 = (f32[28672]{0:T(1024)S(1)}, f32[28672]{0:T(1024)S(1)}, u32[]{:S(2)}, u32[]{:S(2)}) collective-permute-start(f32[28672]{0:T(1024)S(1)} %pad_maximum_fusion.8), channel_id=1, source_target_pairs={{0,16},{8,24},{16,0},{24,8},{32,48},{40,56},{48,32},{56,40},{1,17}... | collective-permute-start | bytes 344072 | tf_op jit(solution)/shard_map/ppermute | solution.py:91
  23.6 6.6 %copy.38 = s32[3072,512]{0,1:T(8,128)} copy(s32[3072,512]{1,0:T(8,128)} %param.7) | data formatting | bytes 12582912 | tf_op args[3]
  30.2 3.5 %convert_element_type.37 = bf16[3072,512]{0,1:T(8,128)(2,1)S(1)} convert(s32[3072,512]{0,1:T(8,128)} %copy.38) | non-fusion elementwise | flops 1572864 | bytes 9437184 | tf_op jit(solution)/shard_map/convert_element_type | solution.py:148
  33.7 1.8 copy.39
  35.6 5.2 %collective-permute-start.5 = (f32[40960]{0:T(1024)S(1)}, f32[40960]{0:T(1024)S(1)}, u32[]{:S(2)}, u32[]{:S(2)}) collective-permute-start(f32[40960]{0:T(1024)S(1)} %pad_maximum_fusion.7), channel_id=1, source_target_pairs={{0,32},{8,40},{16,48},{24,56},{32,0},{40,8},{48,16},{56,24},{1,33}... | collective-permute-start | bytes 491528 | tf_op jit(solution)/shard_map/ppermute | solution.py:91
  40.8 4.4 %collective-permute-done.5 = f32[40960]{0:T(1024)S(1)} collective-permute-done((f32[40960]{0:T(1024)S(1)}, f32[40960]{0:T(1024)S(1)}, u32[]{:S(2)}, u32[]{:S(2)}) %collective-permute-start.5) | collective-permute-done | bytes 163872 | tf_op jit(solution)/shard_map/ppermute | solution.py:91
  45.3 1.7 collective-permute-start.6
  47.0 6.4 %collective-permute-done.6 = f32[65536]{0:T(1024)S(1)} collective-permute-done((f32[65536]{0:T(1024)S(1)}, f32[65536]{0:T(1024)S(1)}, u32[]{:S(2)}, u32[]{:S(2)}) %collective-permute-start.6) | collective-permute-done | bytes 262176 | tf_op jit(solution)/shard_map/ppermute | solution.py:91
  53.5 4.5 %collective-permute-start.7 = (f32[114688]{0:T(1024)S(1)}, f32[114688]{0:T(1024)S(1)}, u32[]{:S(2)}, u32[]{:S(2)}) collective-permute-start(f32[114688]{0:T(1024)S(1)} %pad_maximum_fusion.2), channel_id=1, source_target_pairs={{0,128},{64,192},{128,0},{192,64},{1,129},{65,193},{129,1},{193,65... | collective-permute-start | bytes 1376264 | tf_op jit(solution)/shard_map/ppermute | solution.py:91
  59.3 5.2 %collective-permute-done.7 = f32[114688]{0:T(1024)S(1)} collective-permute-done((f32[114688]{0:T(1024)S(1)}, f32[114688]{0:T(1024)S(1)}, u32[]{:S(2)}, u32[]{:S(2)}) %collective-permute-start.7) | collective-permute-done | bytes 458784 | tf_op jit(solution)/shard_map/ppermute | solution.py:91
  66.9 21.3 %shard_map.46 = f32[1,12288]{1,0:T(1,128)} custom-call(s32[1,12288]{1,0:T(1,128)} %bitcast.261, bf16[768,768]{1,0:T(8,128)(2,1)} %pad_maximum_fusion.tab_ref), custom_call_target="tpu_custom_call" | custom-call | tf_op jit(solution)/shard_map/pallas_call | solution.py:46
  88.8 1.6 reduce.9
  94.1 1.5 collective-permute-done.11
  95.6 2.1 %collective-permute-start.12 = (f32[128,16]{0,1:T(8,128)S(1)}, f32[128,16]{0,1:T(8,128)S(1)}, u32[]{:S(2)}, u32[]{:S(2)}) collective-permute-start(f32[128,16]{0,1:T(8,128)S(1)} %add.110), channel_id=1, source_target_pairs={{0,4},{2,6},{4,0},{6,2},{1,5},{3,7},{5,1},{7,3},{8,12},{10,14},{12... | collective-permute-start | bytes 24584 | tf_op jit(solution)/shard_map/ppermute | solution.py:66
  98.7 11.7 %cholesky.16 = f32[128,128]{1,0:T(8,128)S(1)} custom-call(f32[128,128]{1,0:T(8,128)S(1)} %fusion.40), custom_call_target="Cholesky" | custom-call | tf_op jit(solution)/shard_map/jit(cholesky)/cholesky | solution.py:181
  110.4 2.9 %collective-permute-start.13 = (f32[128,16]{0,1:T(8,128)S(1)}, f32[128,16]{0,1:T(8,128)S(1)}, u32[]{:S(2)}, u32[]{:S(2)}) collective-permute-start(f32[128,16]{0,1:T(8,128)S(1)} %add.111), channel_id=1, source_target_pairs={{0,8},{8,0},{16,24},{24,16},{32,40},{40,32},{48,56},{56,48},{1,9},... | collective-permute-start | bytes 24584 | tf_op jit(solution)/shard_map/ppermute | solution.py:66
  113.4 1.6 collective-permute-done.13
  115.9 1.7 collective-permute-start.8
  117.6 2.0 collective-permute-done.14
  119.6 4.3 %collective-permute-start.15 = (f32[128,16]{0,1:T(8,128)S(1)}, f32[128,16]{0,1:T(8,128)S(1)}, u32[]{:S(2)}, u32[]{:S(2)}) collective-permute-start(f32[128,16]{0,1:T(8,128)S(1)} %add.113), channel_id=1, source_target_pairs={{0,32},{8,40},{16,48},{24,56},{32,0},{40,8},{48,16},{56,24},{1,33}... | collective-permute-start | bytes 24584 | tf_op jit(solution)/shard_map/ppermute | solution.py:66
  124.5 9.8 %custom-call.8 = f32[1,128,128]{1,2,0:T(8,128)S(1)} custom-call(f32[1,128,128]{2,1,0:T(8,128)S(1)} %fusion.22), custom_call_target="InvertDiagBlocksLowerTriangular" | custom-call | tf_op jit(solution)/shard_map/triangular_solve | solution.py:13
  136.2 1.9 collective-permute-done.16
  138.1 3.7 %collective-permute-start.17 = (f32[128,16]{0,1:T(8,128)S(1)}, f32[128,16]{0,1:T(8,128)S(1)}, u32[]{:S(2)}, u32[]{:S(2)}) collective-permute-start(f32[128,16]{0,1:T(8,128)S(1)} %add.115), channel_id=1, source_target_pairs={{0,128},{64,192},{128,0},{192,64},{1,129},{65,193},{129,1},{193,65... | collective-permute-start | bytes 24584 | tf_op jit(solution)/shard_map/ppermute | solution.py:66
  143.8 4.5 %collective-permute-done.9 = f32[1536,16]{0,1:T(8,128)S(1)} collective-permute-done((f32[1536,16]{0,1:T(8,128)S(1)}, f32[1536,16]{0,1:T(8,128)S(1)}, u32[]{:S(2)}, u32[]{:S(2)}) %collective-permute-start.9) | collective-permute-done | bytes 98336 | tf_op jit(solution)/shard_map/ppermute | solution.py:76
  149.7 3.4 %multiply_convert_fusion = bf16[3072,128,16]{0,2,1:T(8,128)(2,1)S(1)} fusion(f32[3072,16]{0,1:T(8,128)S(1)} %maximum_subtract_fusion, f32[3072,128]{0,1:T(8,128)S(1)} %copy.37), kind=kLoop, calls=%fused_computation | loop fusion | flops 12582912 | bytes 14352384 | tf_op jit(solution)/shard_map/convert_element_type | solution.py:193
  153.1 6.7 %fusion.50 = f32[2048,512]{0,1:T(8,128)S(1)} fusion(bf16[3072,2048]{0,1:T(8,128)(2,1)S(1)} %bitcast.243, bf16[3072,512]{0,1:T(8,128)(2,1)S(1)} %bitcast.254), kind=kOutput, calls=%fused_computation.131 | convolution fusion | flops 6442450944 | bytes 19922944 | tf_op jit(solution)/shard_map/dot_general | solution.py:152
  160.3 4.1 %collective-permute-done.18 = f32[2048,256]{0,1:T(8,128)S(1)} collective-permute-done((f32[2048,256]{0,1:T(8,128)S(1)}, f32[2048,256]{0,1:T(8,128)S(1)}, u32[]{:S(2)}, u32[]{:S(2)}) %collective-permute-start.18) | collective-permute-done | bytes 2097184 | tf_op jit(solution)/shard_map/ppermute | solution.py:124
  165.2 1.5 collective-permute-start.19
  166.8 1.9 collective-permute-start.23
  168.8 10.5 %collective-permute-done.19 = f32[1,128,1024]{2,1,0:T(8,128)S(1)} collective-permute-done((f32[1,128,1024]{2,1,0:T(8,128)S(1)}, f32[1,128,1024]{2,1,0:T(8,128)S(1)}, u32[]{:S(2)}, u32[]{:S(2)}) %collective-permute-start.19) | collective-permute-done | bytes 524320 | tf_op jit(solution)/shard_map/ppermute | solution.py:138
  179.5 1.9 collective-permute-start.20
  181.6 1.5 collective-permute-start.24
  183.1 4.1 %collective-permute-done.20 = f32[2,32,1024]{2,1,0:T(8,128)S(1)} collective-permute-done((f32[2,32,1024]{2,1,0:T(8,128)S(1)}, f32[2,32,1024]{2,1,0:T(8,128)S(1)}, u32[]{:S(2)}, u32[]{:S(2)}) %collective-permute-start.20) | collective-permute-done | bytes 262176 | tf_op jit(solution)/shard_map/ppermute | solution.py:138
  187.2 1.5 collective-permute-start.21
  188.9 2.2 %collective-permute-start.25 = (f32[2,16,1024]{2,1,0:T(8,128)S(1)}, f32[2,16,1024]{2,1,0:T(8,128)S(1)}, u32[]{:S(2)}, u32[]{:S(2)}) collective-permute-start(f32[2,16,1024]{2,1,0:T(8,128)S(1)} %select_bitcast_fusion.4), channel_id=1, source_target_pairs={{0,16},{8,24},{16,0},{24,8},{32,48},{40,56},{48,32},{56,40},{1,17}... | collective-permute-start | bytes 393224 | tf_op jit(solution)/shard_map/ppermute | solution.py:138
  191.2 2.6 %collective-permute-done.21 = f32[1,32,1024]{2,1,0:T(8,128)S(1)} collective-permute-done((f32[1,32,1024]{2,1,0:T(8,128)S(1)}, f32[1,32,1024]{2,1,0:T(8,128)S(1)}, u32[]{:S(2)}, u32[]{:S(2)}) %collective-permute-start.21) | collective-permute-done | bytes 131104 | tf_op jit(solution)/shard_map/ppermute | solution.py:138
  193.8 2.4 %collective-permute-start.22 = (f32[1,16,1024]{2,1,0:T(8,128)S(1)}, f32[1,16,1024]{2,1,0:T(8,128)S(1)}, u32[]{:S(2)}, u32[]{:S(2)}) collective-permute-start(f32[1,16,1024]{2,1,0:T(8,128)S(1)} %select_bitcast_fusion.8), channel_id=1, source_target_pairs={{0,16},{8,24},{16,0},{24,8},{32,48},{40,56},{48,32},{56,40},{1,17}... | collective-permute-start | bytes 196616 | tf_op jit(solution)/shard_map/ppermute | solution.py:138
  197.3 2.2 %collective-permute-start.26 = (f32[1,16,1024]{2,1,0:T(8,128)S(1)}, f32[1,16,1024]{2,1,0:T(8,128)S(1)}, u32[]{:S(2)}, u32[]{:S(2)}) collective-permute-start(f32[1,16,1024]{2,1,0:T(8,128)S(1)} %select_bitcast_fusion.7), channel_id=1, source_target_pairs={{0,4},{2,6},{4,0},{6,2},{1,5},{3,7},{5,1},{7,3},{8,12},{10,14},{12... | collective-permute-start | bytes 196616 | tf_op jit(solution)/shard_map/ppermute | solution.py:138
  199.6 3.6 %collective-permute-done.26 = f32[1,16,1024]{2,1,0:T(8,128)S(1)} collective-permute-done((f32[1,16,1024]{2,1,0:T(8,128)S(1)}, f32[1,16,1024]{2,1,0:T(8,128)S(1)}, u32[]{:S(2)}, u32[]{:S(2)}) %collective-permute-start.26) | collective-permute-done | bytes 65568 | tf_op jit(solution)/shard_map/ppermute | solution.py:138
  203.2 2.0 collective-permute-start.27
  205.2 6.3 %collective-permute-done.27 = f32[1,8,2048]{2,1,0:T(8,128)S(1)} collective-permute-done((f32[1,8,2048]{2,1,0:T(8,128)S(1)}, f32[1,8,2048]{2,1,0:T(8,128)S(1)}, u32[]{:S(2)}, u32[]{:S(2)}) %collective-permute-start.27) | collective-permute-done | bytes 65568 | tf_op jit(solution)/shard_map/ppermute | solution.py:138
  (115 shorter events, 22.6 us)
Async XLA Ops:
  0.0 57.9 %copy-start = (s32[16,3072]{1,0:T(8,128)S(1)}, s32[16,3072]{1,0:T(8,128)}, u32[]{:S(2)}) copy-start(s32[16,3072]{1,0:T(8,128)} %param.6) | copy-start | bytes 589828
  2.7 1.3 collective-permute-start
  4.6 4.9 %collective-permute-start.1 = (f32[17920]{0:T(1024)S(1)}, f32[17920]{0:T(1024)S(1)}, u32[]{:S(2)}, u32[]{:S(2)}) collective-permute-start(f32[17920]{0:T(1024)S(1)} %pad_maximum_fusion.13), channel_id=1, source_target_pairs={{0,2},{2,0},{4,6},{6,4},{1,3},{3,1},{5,7},{7,5},{8,10},{10,8},{12,... | collective-permute-start | bytes 215048 | tf_op jit(solution)/shard_map/ppermute | solution.py:91
  9.6 6.0 %collective-permute-start.2 = (f32[19456]{0:T(1024)S(1)}, f32[19456]{0:T(1024)S(1)}, u32[]{:S(2)}, u32[]{:S(2)}) collective-permute-start(f32[19456]{0:T(1024)S(1)} %pad_maximum_fusion.12), channel_id=1, source_target_pairs={{0,4},{2,6},{4,0},{6,2},{1,5},{3,7},{5,1},{7,3},{8,12},{10,14},{12... | collective-permute-start | bytes 233480 | tf_op jit(solution)/shard_map/ppermute | solution.py:91
  15.7 4.6 %collective-permute-start.3 = (f32[22528]{0:T(1024)S(1)}, f32[22528]{0:T(1024)S(1)}, u32[]{:S(2)}, u32[]{:S(2)}) collective-permute-start(f32[22528]{0:T(1024)S(1)} %pad_maximum_fusion.11), channel_id=1, source_target_pairs={{0,8},{8,0},{16,24},{24,16},{32,40},{40,32},{48,56},{56,48},{1,9},... | collective-permute-start | bytes 270344 | tf_op jit(solution)/shard_map/ppermute | solution.py:91
  20.3 15.2 %collective-permute-start.4 = (f32[28672]{0:T(1024)S(1)}, f32[28672]{0:T(1024)S(1)}, u32[]{:S(2)}, u32[]{:S(2)}) collective-permute-start(f32[28672]{0:T(1024)S(1)} %pad_maximum_fusion.8), channel_id=1, source_target_pairs={{0,16},{8,24},{16,0},{24,8},{32,48},{40,56},{48,32},{56,40},{1,17}... | collective-permute-start | bytes 344072 | tf_op jit(solution)/shard_map/ppermute | solution.py:91
  35.6 9.6 %collective-permute-start.5 = (f32[40960]{0:T(1024)S(1)}, f32[40960]{0:T(1024)S(1)}, u32[]{:S(2)}, u32[]{:S(2)}) collective-permute-start(f32[40960]{0:T(1024)S(1)} %pad_maximum_fusion.7), channel_id=1, source_target_pairs={{0,32},{8,40},{16,48},{24,56},{32,0},{40,8},{48,16},{56,24},{1,33}... | collective-permute-start | bytes 491528 | tf_op jit(solution)/shard_map/ppermute | solution.py:91
  45.2 13.7 %copy-start.3 = (f32[40960]{0:T(1024)}, f32[40960]{0:T(1024)S(1)}, u32[]{:S(2)}) copy-start(f32[40960]{0:T(1024)S(1)} %collective-permute-done.5) | copy-start | bytes 491524
  45.3 8.1 %collective-permute-start.6 = (f32[65536]{0:T(1024)S(1)}, f32[65536]{0:T(1024)S(1)}, u32[]{:S(2)}, u32[]{:S(2)}) collective-permute-start(f32[65536]{0:T(1024)S(1)} %pad_maximum_fusion.5), channel_id=1, source_target_pairs={{0,64},{64,0},{128,192},{192,128},{1,65},{65,1},{129,193},{193,129... | collective-permute-start | bytes 786440 | tf_op jit(solution)/shard_map/ppermute | solution.py:91
  53.4 5.5 %copy-start.5 = (f32[65536]{0:T(1024)}, f32[65536]{0:T(1024)S(1)}, u32[]{:S(2)}) copy-start(f32[65536]{0:T(1024)S(1)} %collective-permute-done.6) | copy-start | bytes 786436
  53.5 10.9 %collective-permute-start.7 = (f32[114688]{0:T(1024)S(1)}, f32[114688]{0:T(1024)S(1)}, u32[]{:S(2)}, u32[]{:S(2)}) collective-permute-start(f32[114688]{0:T(1024)S(1)} %pad_maximum_fusion.2), channel_id=1, source_target_pairs={{0,128},{64,192},{128,0},{192,64},{1,129},{65,193},{129,1},{193,65... | collective-permute-start | bytes 1376264 | tf_op jit(solution)/shard_map/ppermute | solution.py:91
  64.4 0.8 copy-start.4
  65.8 24.6 %copy-start.1 = (f32[3072,128]{1,0:T(8,128)S(1)}, f32[3072,128]{1,0:T(8,128)}, u32[]{:S(2)}) copy-start(f32[3072,128]{1,0:T(8,128)} %param.5) | copy-start | bytes 4718596
  90.7 1.3 collective-permute-start.10
  92.0 3.7 %collective-permute-start.11 = (f32[128,16]{0,1:T(8,128)S(1)}, f32[128,16]{0,1:T(8,128)S(1)}, u32[]{:S(2)}, u32[]{:S(2)}) collective-permute-start(f32[128,16]{0,1:T(8,128)S(1)} %add.109), channel_id=1, source_target_pairs={{0,2},{2,0},{4,6},{6,4},{1,3},{3,1},{5,7},{7,5},{8,10},{10,8},{12,... | collective-permute-start | bytes 24584 | tf_op jit(solution)/shard_map/ppermute | solution.py:66
  95.6 14.8 %collective-permute-start.12 = (f32[128,16]{0,1:T(8,128)S(1)}, f32[128,16]{0,1:T(8,128)S(1)}, u32[]{:S(2)}, u32[]{:S(2)}) collective-permute-start(f32[128,16]{0,1:T(8,128)S(1)} %add.110), channel_id=1, source_target_pairs={{0,4},{2,6},{4,0},{6,2},{1,5},{3,7},{5,1},{7,3},{8,12},{10,14},{12... | collective-permute-start | bytes 24584 | tf_op jit(solution)/shard_map/ppermute | solution.py:66
  110.4 4.6 %collective-permute-start.13 = (f32[128,16]{0,1:T(8,128)S(1)}, f32[128,16]{0,1:T(8,128)S(1)}, u32[]{:S(2)}, u32[]{:S(2)}) collective-permute-start(f32[128,16]{0,1:T(8,128)S(1)} %add.111), channel_id=1, source_target_pairs={{0,8},{8,0},{16,24},{24,16},{32,40},{40,32},{48,56},{56,48},{1,9},... | collective-permute-start | bytes 24584 | tf_op jit(solution)/shard_map/ppermute | solution.py:66
  115.0 4.5 %collective-permute-start.14 = (f32[128,16]{0,1:T(8,128)S(1)}, f32[128,16]{0,1:T(8,128)S(1)}, u32[]{:S(2)}, u32[]{:S(2)}) collective-permute-start(f32[128,16]{0,1:T(8,128)S(1)} %add.112), channel_id=1, source_target_pairs={{0,16},{8,24},{16,0},{24,8},{32,48},{40,56},{48,32},{56,40},{1,17}... | collective-permute-start | bytes 24584 | tf_op jit(solution)/shard_map/ppermute | solution.py:66
  115.9 19.5 %collective-permute-start.8 = (f32[768,16]{0,1:T(8,128)S(1)}, f32[768,16]{0,1:T(8,128)}, u32[]{:S(2)}, u32[]{:S(2)}) collective-permute-start(f32[768,16]{0,1:T(8,128)S(1)} %bitcast.260), channel_id=1, source_target_pairs={{0,64},{64,0},{128,192},{192,128},{1,65},{65,1},{129,193},{193,129... | collective-permute-start | bytes 147464 | tf_op jit(solution)/shard_map/ppermute | solution.py:76
  119.6 14.8 %collective-permute-start.15 = (f32[128,16]{0,1:T(8,128)S(1)}, f32[128,16]{0,1:T(8,128)S(1)}, u32[]{:S(2)}, u32[]{:S(2)}) collective-permute-start(f32[128,16]{0,1:T(8,128)S(1)} %add.113), channel_id=1, source_target_pairs={{0,32},{8,40},{16,48},{24,56},{32,0},{40,8},{48,16},{56,24},{1,33}... | collective-permute-start | bytes 24584 | tf_op jit(solution)/shard_map/ppermute | solution.py:66
  134.4 3.7 %collective-permute-start.16 = (f32[128,16]{0,1:T(8,128)S(1)}, f32[128,16]{0,1:T(8,128)S(1)}, u32[]{:S(2)}, u32[]{:S(2)}) collective-permute-start(f32[128,16]{0,1:T(8,128)S(1)} %add.114), channel_id=1, source_target_pairs={{0,64},{64,0},{128,192},{192,128},{1,65},{65,1},{129,193},{193,129... | collective-permute-start | bytes 24584 | tf_op jit(solution)/shard_map/ppermute | solution.py:66
  138.1 5.3 %collective-permute-start.17 = (f32[128,16]{0,1:T(8,128)S(1)}, f32[128,16]{0,1:T(8,128)S(1)}, u32[]{:S(2)}, u32[]{:S(2)}) collective-permute-start(f32[128,16]{0,1:T(8,128)S(1)} %add.115), channel_id=1, source_target_pairs={{0,128},{64,192},{128,0},{192,64},{1,129},{65,193},{129,1},{193,65... | collective-permute-start | bytes 24584 | tf_op jit(solution)/shard_map/ppermute | solution.py:66
  141.8 6.4 %collective-permute-start.9 = (f32[1536,16]{0,1:T(8,128)S(1)}, f32[1536,16]{0,1:T(8,128)S(1)}, u32[]{:S(2)}, u32[]{:S(2)}) collective-permute-start(f32[1536,16]{0,1:T(8,128)S(1)} %pad_maximum_fusion.10), channel_id=1, source_target_pairs={{0,128},{64,192},{128,0},{192,64},{1,129},{65,193},{129,1},{193,65... | collective-permute-start | bytes 294920 | tf_op jit(solution)/shard_map/ppermute | solution.py:76
  149.7 3.5 %copy-start.2 = (bf16[3072,2,2,2,2,2,2,8]{0,7,6,5,4,3,2,1:T(8,128)(2,1)S(1)}, bf16[3072,2,2,2,2,2,2,8]{0,7,6,5,4,3,2,1:T(8,128)(2,1)}, u32[]{:S(2)}) copy-start(bf16[3072,2,2,2,2,2,2,8]{0,7,6,5,4,3,2,1:T(8,128)(2,1)} %copy.39) | copy-start | bytes 9437188
  160.2 4.2 %collective-permute-start.18 = (f32[2048,256]{0,1:T(8,128)S(1)}, f32[2048,256]{0,1:T(8,128)S(1)}, u32[]{:S(2)}, u32[]{:S(2)}) collective-permute-start(f32[2048,256]{0,1:T(8,128)S(1)} %slice_select_fusion), channel_id=1, source_target_pairs={{0,1},{1,0},{2,3},{3,2},{4,5},{5,4},{6,7},{7,6},{8,9},{9,8},{10,11... | collective-permute-start | bytes 6291464 | tf_op jit(solution)/shard_map/ppermute | solution.py:124
  165.2 14.1 %collective-permute-start.19 = (f32[1,128,1024]{2,1,0:T(8,128)S(1)}, f32[1,128,1024]{2,1,0:T(8,128)S(1)}, u32[]{:S(2)}, u32[]{:S(2)}) collective-permute-start(f32[1,128,1024]{2,1,0:T(8,128)S(1)} %select_bitcast_fusion.1), channel_id=1, source_target_pairs={{0,2},{2,0},{4,6},{6,4},{1,3},{3,1},{5,7},{7,5},{8,10},{10,8},{12,... | collective-permute-start | bytes 1572872 | tf_op jit(solution)/shard_map/ppermute | solution.py:138
  166.8 14.6 %collective-permute-start.23 = (f32[4,32,1024]{2,1,0:T(8,128)S(1)}, f32[4,32,1024]{2,1,0:T(8,128)S(1)}, u32[]{:S(2)}, u32[]{:S(2)}) collective-permute-start(f32[4,32,1024]{2,1,0:T(8,128)S(1)} %select_bitcast_fusion), channel_id=1, source_target_pairs={{0,8},{8,0},{16,24},{24,16},{32,40},{40,32},{48,56},{56,48},{1,9},... | collective-permute-start | bytes 1572872 | tf_op jit(solution)/shard_map/ppermute | solution.py:138
  179.5 7.7 %collective-permute-start.20 = (f32[2,32,1024]{2,1,0:T(8,128)S(1)}, f32[2,32,1024]{2,1,0:T(8,128)S(1)}, u32[]{:S(2)}, u32[]{:S(2)}) collective-permute-start(f32[2,32,1024]{2,1,0:T(8,128)S(1)} %select_bitcast_fusion.3), channel_id=1, source_target_pairs={{0,8},{8,0},{16,24},{24,16},{32,40},{40,32},{48,56},{56,48},{1,9},... | collective-permute-start | bytes 786440 | tf_op jit(solution)/shard_map/ppermute | solution.py:138
  181.6 7.3 %collective-permute-start.24 = (f32[1,64,1024]{2,1,0:T(8,128)S(1)}, f32[1,64,1024]{2,1,0:T(8,128)S(1)}, u32[]{:S(2)}, u32[]{:S(2)}) collective-permute-start(f32[1,64,1024]{2,1,0:T(8,128)S(1)} %select_bitcast_fusion.2), channel_id=1, source_target_pairs={{0,2},{2,0},{4,6},{6,4},{1,3},{3,1},{5,7},{7,5},{8,10},{10,8},{12,... | collective-permute-start | bytes 786440 | tf_op jit(solution)/shard_map/ppermute | solution.py:138
  187.2 6.6 %collective-permute-start.21 = (f32[1,32,1024]{2,1,0:T(8,128)S(1)}, f32[1,32,1024]{2,1,0:T(8,128)S(1)}, u32[]{:S(2)}, u32[]{:S(2)}) collective-permute-start(f32[1,32,1024]{2,1,0:T(8,128)S(1)} %select_bitcast_fusion.5), channel_id=1, source_target_pairs={{0,4},{2,6},{4,0},{6,2},{1,5},{3,7},{5,1},{7,3},{8,12},{10,14},{12... | collective-permute-start | bytes 393224 | tf_op jit(solution)/shard_map/ppermute | solution.py:138
  188.9 8.3 %collective-permute-start.25 = (f32[2,16,1024]{2,1,0:T(8,128)S(1)}, f32[2,16,1024]{2,1,0:T(8,128)S(1)}, u32[]{:S(2)}, u32[]{:S(2)}) collective-permute-start(f32[2,16,1024]{2,1,0:T(8,128)S(1)} %select_bitcast_fusion.4), channel_id=1, source_target_pairs={{0,16},{8,24},{16,0},{24,8},{32,48},{40,56},{48,32},{56,40},{1,17}... | collective-permute-start | bytes 393224 | tf_op jit(solution)/shard_map/ppermute | solution.py:138
  193.8 5.7 %collective-permute-start.22 = (f32[1,16,1024]{2,1,0:T(8,128)S(1)}, f32[1,16,1024]{2,1,0:T(8,128)S(1)}, u32[]{:S(2)}, u32[]{:S(2)}) collective-permute-start(f32[1,16,1024]{2,1,0:T(8,128)S(1)} %select_bitcast_fusion.8), channel_id=1, source_target_pairs={{0,16},{8,24},{16,0},{24,8},{32,48},{40,56},{48,32},{56,40},{1,17}... | collective-permute-start | bytes 196616 | tf_op jit(solution)/shard_map/ppermute | solution.py:138
  197.3 5.9 %collective-permute-start.26 = (f32[1,16,1024]{2,1,0:T(8,128)S(1)}, f32[1,16,1024]{2,1,0:T(8,128)S(1)}, u32[]{:S(2)}, u32[]{:S(2)}) collective-permute-start(f32[1,16,1024]{2,1,0:T(8,128)S(1)} %select_bitcast_fusion.7), channel_id=1, source_target_pairs={{0,4},{2,6},{4,0},{6,2},{1,5},{3,7},{5,1},{7,3},{8,12},{10,14},{12... | collective-permute-start | bytes 196616 | tf_op jit(solution)/shard_map/ppermute | solution.py:138
  203.2 8.3 %collective-permute-start.27 = (f32[1,8,2048]{2,1,0:T(8,128)S(1)}, f32[1,8,2048]{2,1,0:T(8,128)S(1)}, u32[]{:S(2)}, u32[]{:S(2)}) collective-permute-start(f32[1,8,2048]{2,1,0:T(8,128)S(1)} %select_bitcast_fusion.6), channel_id=1, source_target_pairs={{0,32},{8,40},{16,48},{24,56},{32,0},{40,8},{48,16},{56,24},{1,33}... | collective-permute-start | bytes 196616 | tf_op jit(solution)/shard_map/ppermute | solution.py:138

commit v11 on v10

--- a/solution.py
+++ b/solution.py
@@ -14,7 +14,7 @@
 
 
 COLS = 256
-TILE = 512
+TILE = 1024
 
 
 def gather_body(idx_ref, tab_ref, out_ref):
@@ -24,7 +24,7 @@
     col = idx % COLS
     hot = (lax.broadcasted_iota(jnp.int32, (rows, TILE), 0) == row).astype(jnp.bfloat16)
     picked = jnp.dot(tab_ref[...], hot, preferred_element_type=jnp.float32)
-    value = picked[:COLS] + picked[COLS : 2 * COLS] + picked[2 * COLS :]
+    value = picked[:COLS] + picked[COLS:]
     wanted = lax.broadcasted_iota(jnp.int32, (COLS, TILE), 0) == col
     out_ref[...] = jnp.sum(jnp.where(wanted, value, jnp.float32(0.0)), axis=0, keepdims=True)
 
@@ -33,9 +33,7 @@
     table = pheno_full.reshape(-1, COLS)
     top = lax.reduce_precision(table, exponent_bits=8, mantissa_bits=7)
     rest = table - top
-    middle = lax.reduce_precision(rest, exponent_bits=8, mantissa_bits=7)
-    low = rest - middle
-    pieces = [piece.T.astype(jnp.bfloat16) for piece in (top, middle, low)]
+    pieces = [piece.T.astype(jnp.bfloat16) for piece in (top, rest)]
     return jnp.concatenate(pieces, axis=0)
 
 

time: 214 us -> 206 us (0.963)
  Pallas kernels: 21.3 us -> 13.9 us
    pallas_call x1, Pallas kernels: 21.3 us -> 13.9 us  [gather_pheno(): pl.pallas_call(gather_body, grid=(count // TILE,), in_specs=[pl.BlockSpec...]
  transfers between devices with their start and end apart: 28 -> 28, of which waited for: 22 -> 22; matrix products, arithmetic and copies ran while one was open for 19% -> 20% of each run, Pallas kernels for 0% -> 0%
where the time goes in v11:
time: 206 us; the launch traced here: 205 us
  waiting for transfers between devices  73.1 us (35%)
  starting transfers between devices  54.4 us (26%)
  other arithmetic  39.3 us (19%)
  Pallas kernels  13.9 us (7%)
  local copies, waits for them, and re-layouts  12.8 us (6%)
  matrix products  10.7 us (5%)
    ppermute x9, waiting for transfers between devices, halve_bit(): kept = mine + lax.ppermute(send, axis, flip)  28.3 us
    ppermute x8, waiting for transfers between devices, front_chain(): lax.ppermute(jnp.concatenate([pheno, gram.reshape(-1)]), axis, flip)  27.2 us
    ppermute x8, starting transfers between devices, front_chain(): lax.ppermute(jnp.concatenate([pheno, gram.reshape(-1)]), axis, flip)  20.2 us
    ppermute x9, starting transfers between devices, halve_bit(): kept = mine + lax.ppermute(send, axis, flip)  17.2 us
    ppermute x8, starting transfers between devices, doubling_psum(): x = x + lax.ppermute(x, axis, pairs)  14.9 us
    pallas_call x1, Pallas kernels, gather_pheno(): pl.pallas_call(gather_body, grid=(count // TILE,), in_specs=[pl.BlockSpec...  13.9 us
    another operation x3, other arithmetic, per_device(): factor = jnp.linalg.cholesky(system)  12.4 us
    another operation x2, other arithmetic, chol_solve(): lax.linalg.triangular_solve(factor, middle, left_side=True, lower=True, t...  10.5 us
  transfers between devices with their start and end apart: 28, of which 22 were waited for; matrix products, arithmetic and copies ran while one was open for 20% of the time, Pallas kernels for 0%

profile of v11, /device:TPU:2, one launch (start us, length us, event | category | flops | bytes accessed | tf_op | source)
XLA Modules:
  0.0 204.7 jit_solution(11755840722706189870)
XLA Ops:
  0.0 1.9 fusion.7
  4.6 2.3 %collective-permute-start.1 = (f32[17920]{0:T(1024)S(1)}, f32[17920]{0:T(1024)S(1)}, u32[]{:S(2)}, u32[]{:S(2)}) collective-permute-start(f32[17920]{0:T(1024)S(1)} %pad_maximum_fusion.13), channel_id=1, source_target_pairs={{0,2},{2,0},{4,6},{6,4},{1,3},{3,1},{5,7},{7,5},{8,10},{10,8},{12,... | collective-permute-start | bytes 215048 | tf_op jit(solution)/shard_map/ppermute | solution.py:89
  7.0 2.6 %collective-permute-done.1 = f32[17920]{0:T(1024)S(1)} collective-permute-done((f32[17920]{0:T(1024)S(1)}, f32[17920]{0:T(1024)S(1)}, u32[]{:S(2)}, u32[]{:S(2)}) %collective-permute-start.1) | collective-permute-done | bytes 71712 | tf_op jit(solution)/shard_map/ppermute | solution.py:89
  9.6 1.7 collective-permute-start.2
  11.3 4.3 %collective-permute-done.2 = f32[19456]{0:T(1024)S(1)} collective-permute-done((f32[19456]{0:T(1024)S(1)}, f32[19456]{0:T(1024)S(1)}, u32[]{:S(2)}, u32[]{:S(2)}) %collective-permute-start.2) | collective-permute-done | bytes 77856 | tf_op jit(solution)/shard_map/ppermute | solution.py:89
  15.7 1.5 collective-permute-start.3
  17.2 3.1 %collective-permute-done.3 = f32[22528]{0:T(1024)S(1)} collective-permute-done((f32[22528]{0:T(1024)S(1)}, f32[22528]{0:T(1024)S(1)}, u32[]{:S(2)}, u32[]{:S(2)}) %collective-permute-start.3) | collective-permute-done | bytes 90144 | tf_op jit(solution)/shard_map/ppermute | solution.py:89
  20.3 3.2 %collective-permute-start.4 = (f32[28672]{0:T(1024)S(1)}, f32[28672]{0:T(1024)S(1)}, u32[]{:S(2)}, u32[]{:S(2)}) collective-permute-start(f32[28672]{0:T(1024)S(1)} %pad_maximum_fusion.8), channel_id=1, source_target_pairs={{0,16},{8,24},{16,0},{24,8},{32,48},{40,56},{48,32},{56,40},{1,17}... | collective-permute-start | bytes 344072 | tf_op jit(solution)/shard_map/ppermute | solution.py:89
  23.6 6.6 %copy.38 = s32[3072,512]{0,1:T(8,128)} copy(s32[3072,512]{1,0:T(8,128)} %param.7) | data formatting | bytes 12582912 | tf_op args[3]
  30.2 3.5 %convert_element_type.31 = bf16[3072,512]{0,1:T(8,128)(2,1)S(1)} convert(s32[3072,512]{0,1:T(8,128)} %copy.38) | non-fusion elementwise | flops 1572864 | bytes 9437184 | tf_op jit(solution)/shard_map/convert_element_type | solution.py:146
  33.7 1.8 copy.39
  35.6 5.2 %collective-permute-start.5 = (f32[40960]{0:T(1024)S(1)}, f32[40960]{0:T(1024)S(1)}, u32[]{:S(2)}, u32[]{:S(2)}) collective-permute-start(f32[40960]{0:T(1024)S(1)} %pad_maximum_fusion.7), channel_id=1, source_target_pairs={{0,32},{8,40},{16,48},{24,56},{32,0},{40,8},{48,16},{56,24},{1,33}... | collective-permute-start | bytes 491528 | tf_op jit(solution)/shard_map/ppermute | solution.py:89
  40.8 4.4 %collective-permute-done.5 = f32[40960]{0:T(1024)S(1)} collective-permute-done((f32[40960]{0:T(1024)S(1)}, f32[40960]{0:T(1024)S(1)}, u32[]{:S(2)}, u32[]{:S(2)}) %collective-permute-start.5) | collective-permute-done | bytes 163872 | tf_op jit(solution)/shard_map/ppermute | solution.py:89
  45.3 1.7 collective-permute-start.6
  47.0 6.4 %collective-permute-done.6 = f32[65536]{0:T(1024)S(1)} collective-permute-done((f32[65536]{0:T(1024)S(1)}, f32[65536]{0:T(1024)S(1)}, u32[]{:S(2)}, u32[]{:S(2)}) %collective-permute-start.6) | collective-permute-done | bytes 262176 | tf_op jit(solution)/shard_map/ppermute | solution.py:89
  53.5 4.5 %collective-permute-start.7 = (f32[114688]{0:T(1024)S(1)}, f32[114688]{0:T(1024)S(1)}, u32[]{:S(2)}, u32[]{:S(2)}) collective-permute-start(f32[114688]{0:T(1024)S(1)} %pad_maximum_fusion.2), channel_id=1, source_target_pairs={{0,128},{64,192},{128,0},{192,64},{1,129},{65,193},{129,1},{193,65... | collective-permute-start | bytes 1376264 | tf_op jit(solution)/shard_map/ppermute | solution.py:89
  59.3 5.2 %collective-permute-done.7 = f32[114688]{0:T(1024)S(1)} collective-permute-done((f32[114688]{0:T(1024)S(1)}, f32[114688]{0:T(1024)S(1)}, u32[]{:S(2)}, u32[]{:S(2)}) %collective-permute-start.7) | collective-permute-done | bytes 458784 | tf_op jit(solution)/shard_map/ppermute | solution.py:89
  66.7 13.9 %shard_map.46 = f32[1,12288]{1,0:T(1,128)} custom-call(s32[1,12288]{1,0:T(1,128)} %bitcast.259, bf16[512,768]{1,0:T(8,128)(2,1)} %pad_maximum_fusion.1.tab_ref), custom_call_target="tpu_custom_call" | custom-call | tf_op jit(solution)/shard_map/pallas_call | solution.py:44
  81.1 1.6 reduce.9
  86.4 1.5 collective-permute-done.11
  87.9 2.1 %collective-permute-start.12 = (f32[128,16]{0,1:T(8,128)S(1)}, f32[128,16]{0,1:T(8,128)S(1)}, u32[]{:S(2)}, u32[]{:S(2)}) collective-permute-start(f32[128,16]{0,1:T(8,128)S(1)} %add.110), channel_id=1, source_target_pairs={{0,4},{2,6},{4,0},{6,2},{1,5},{3,7},{5,1},{7,3},{8,12},{10,14},{12... | collective-permute-start | bytes 24584 | tf_op jit(solution)/shard_map/ppermute | solution.py:64
  91.0 11.7 %cholesky.16 = f32[128,128]{1,0:T(8,128)S(1)} custom-call(f32[128,128]{1,0:T(8,128)S(1)} %fusion.39), custom_call_target="Cholesky" | custom-call | tf_op jit(solution)/shard_map/jit(cholesky)/cholesky | solution.py:179
  102.7 2.9 %collective-permute-start.13 = (f32[128,16]{0,1:T(8,128)S(1)}, f32[128,16]{0,1:T(8,128)S(1)}, u32[]{:S(2)}, u32[]{:S(2)}) collective-permute-start(f32[128,16]{0,1:T(8,128)S(1)} %add.111), channel_id=1, source_target_pairs={{0,8},{8,0},{16,24},{24,16},{32,40},{40,32},{48,56},{56,48},{1,9},... | collective-permute-start | bytes 24584 | tf_op jit(solution)/shard_map/ppermute | solution.py:64
  105.7 1.6 collective-permute-done.13
  108.2 1.7 collective-permute-start.8
  109.9 2.0 collective-permute-done.14
  111.9 4.3 %collective-permute-start.15 = (f32[128,16]{0,1:T(8,128)S(1)}, f32[128,16]{0,1:T(8,128)S(1)}, u32[]{:S(2)}, u32[]{:S(2)}) collective-permute-start(f32[128,16]{0,1:T(8,128)S(1)} %add.113), channel_id=1, source_target_pairs={{0,32},{8,40},{16,48},{24,56},{32,0},{40,8},{48,16},{56,24},{1,33}... | collective-permute-start | bytes 24584 | tf_op jit(solution)/shard_map/ppermute | solution.py:64
  116.9 9.8 %custom-call.8 = f32[1,128,128]{1,2,0:T(8,128)S(1)} custom-call(f32[1,128,128]{2,1,0:T(8,128)S(1)} %fusion.21), custom_call_target="InvertDiagBlocksLowerTriangular" | custom-call | tf_op jit(solution)/shard_map/triangular_solve | solution.py:13
  128.5 1.9 collective-permute-done.16
  130.4 3.7 %collective-permute-start.17 = (f32[128,16]{0,1:T(8,128)S(1)}, f32[128,16]{0,1:T(8,128)S(1)}, u32[]{:S(2)}, u32[]{:S(2)}) collective-permute-start(f32[128,16]{0,1:T(8,128)S(1)} %add.115), channel_id=1, source_target_pairs={{0,128},{64,192},{128,0},{192,64},{1,129},{65,193},{129,1},{193,65... | collective-permute-start | bytes 24584 | tf_op jit(solution)/shard_map/ppermute | solution.py:64
  136.1 4.5 %collective-permute-done.9 = f32[1536,16]{0,1:T(8,128)S(1)} collective-permute-done((f32[1536,16]{0,1:T(8,128)S(1)}, f32[1536,16]{0,1:T(8,128)S(1)}, u32[]{:S(2)}, u32[]{:S(2)}) %collective-permute-start.9) | collective-permute-done | bytes 98336 | tf_op jit(solution)/shard_map/ppermute | solution.py:74
  142.0 3.4 %multiply_convert_fusion = bf16[3072,128,16]{0,2,1:T(8,128)(2,1)S(1)} fusion(f32[3072,16]{0,1:T(8,128)S(1)} %maximum_subtract_fusion, f32[3072,128]{0,1:T(8,128)S(1)} %copy.37), kind=kLoop, calls=%fused_computation | loop fusion | flops 12582912 | bytes 14352384 | tf_op jit(solution)/shard_map/convert_element_type | solution.py:191
  145.4 6.7 %fusion.49 = f32[2048,512]{0,1:T(8,128)S(1)} fusion(bf16[3072,2048]{0,1:T(8,128)(2,1)S(1)} %bitcast.241, bf16[3072,512]{0,1:T(8,128)(2,1)S(1)} %bitcast.252), kind=kOutput, calls=%fused_computation.128 | convolution fusion | flops 6442450944 | bytes 19922944 | tf_op jit(solution)/shard_map/dot_general | solution.py:150
  152.6 4.1 %collective-permute-done.18 = f32[2048,256]{0,1:T(8,128)S(1)} collective-permute-done((f32[2048,256]{0,1:T(8,128)S(1)}, f32[2048,256]{0,1:T(8,128)S(1)}, u32[]{:S(2)}, u32[]{:S(2)}) %collective-permute-start.18) | collective-permute-done | bytes 2097184 | tf_op jit(solution)/shard_map/ppermute | solution.py:122
  157.6 1.5 collective-permute-start.19
  159.1 1.9 collective-permute-start.23
  161.1 10.5 %collective-permute-done.19 = f32[1,128,1024]{2,1,0:T(8,128)S(1)} collective-permute-done((f32[1,128,1024]{2,1,0:T(8,128)S(1)}, f32[1,128,1024]{2,1,0:T(8,128)S(1)}, u32[]{:S(2)}, u32[]{:S(2)}) %collective-permute-start.19) | collective-permute-done | bytes 524320 | tf_op jit(solution)/shard_map/ppermute | solution.py:136
  171.8 1.9 collective-permute-start.20
  173.9 1.5 collective-permute-start.24
  175.4 4.1 %collective-permute-done.20 = f32[2,32,1024]{2,1,0:T(8,128)S(1)} collective-permute-done((f32[2,32,1024]{2,1,0:T(8,128)S(1)}, f32[2,32,1024]{2,1,0:T(8,128)S(1)}, u32[]{:S(2)}, u32[]{:S(2)}) %collective-permute-start.20) | collective-permute-done | bytes 262176 | tf_op jit(solution)/shard_map/ppermute | solution.py:136
  179.5 1.5 collective-permute-start.21
  181.3 2.2 %collective-permute-start.25 = (f32[2,16,1024]{2,1,0:T(8,128)S(1)}, f32[2,16,1024]{2,1,0:T(8,128)S(1)}, u32[]{:S(2)}, u32[]{:S(2)}) collective-permute-start(f32[2,16,1024]{2,1,0:T(8,128)S(1)} %select_bitcast_fusion.4), channel_id=1, source_target_pairs={{0,16},{8,24},{16,0},{24,8},{32,48},{40,56},{48,32},{56,40},{1,17}... | collective-permute-start | bytes 393224 | tf_op jit(solution)/shard_map/ppermute | solution.py:136
  183.5 2.6 %collective-permute-done.21 = f32[1,32,1024]{2,1,0:T(8,128)S(1)} collective-permute-done((f32[1,32,1024]{2,1,0:T(8,128)S(1)}, f32[1,32,1024]{2,1,0:T(8,128)S(1)}, u32[]{:S(2)}, u32[]{:S(2)}) %collective-permute-start.21) | collective-permute-done | bytes 131104 | tf_op jit(solution)/shard_map/ppermute | solution.py:136
  186.1 2.4 %collective-permute-start.22 = (f32[1,16,1024]{2,1,0:T(8,128)S(1)}, f32[1,16,1024]{2,1,0:T(8,128)S(1)}, u32[]{:S(2)}, u32[]{:S(2)}) collective-permute-start(f32[1,16,1024]{2,1,0:T(8,128)S(1)} %select_bitcast_fusion.8), channel_id=1, source_target_pairs={{0,16},{8,24},{16,0},{24,8},{32,48},{40,56},{48,32},{56,40},{1,17}... | collective-permute-start | bytes 196616 | tf_op jit(solution)/shard_map/ppermute | solution.py:136
  189.6 2.2 %collective-permute-start.26 = (f32[1,16,1024]{2,1,0:T(8,128)S(1)}, f32[1,16,1024]{2,1,0:T(8,128)S(1)}, u32[]{:S(2)}, u32[]{:S(2)}) collective-permute-start(f32[1,16,1024]{2,1,0:T(8,128)S(1)} %select_bitcast_fusion.7), channel_id=1, source_target_pairs={{0,4},{2,6},{4,0},{6,2},{1,5},{3,7},{5,1},{7,3},{8,12},{10,14},{12... | collective-permute-start | bytes 196616 | tf_op jit(solution)/shard_map/ppermute | solution.py:136
  191.9 3.6 %collective-permute-done.26 = f32[1,16,1024]{2,1,0:T(8,128)S(1)} collective-permute-done((f32[1,16,1024]{2,1,0:T(8,128)S(1)}, f32[1,16,1024]{2,1,0:T(8,128)S(1)}, u32[]{:S(2)}, u32[]{:S(2)}) %collective-permute-start.26) | collective-permute-done | bytes 65568 | tf_op jit(solution)/shard_map/ppermute | solution.py:136
  195.5 2.0 collective-permute-start.27
  197.5 6.3 %collective-permute-done.27 = f32[1,8,2048]{2,1,0:T(8,128)S(1)} collective-permute-done((f32[1,8,2048]{2,1,0:T(8,128)S(1)}, f32[1,8,2048]{2,1,0:T(8,128)S(1)}, u32[]{:S(2)}, u32[]{:S(2)}) %collective-permute-start.27) | collective-permute-done | bytes 65568 | tf_op jit(solution)/shard_map/ppermute | solution.py:136
  (115 shorter events, 22.4 us)
Async XLA Ops:
  0.0 57.9 %copy-start = (s32[16,3072]{1,0:T(8,128)S(1)}, s32[16,3072]{1,0:T(8,128)}, u32[]{:S(2)}) copy-start(s32[16,3072]{1,0:T(8,128)} %param.6) | copy-start | bytes 589828
  2.7 1.3 collective-permute-start
  4.6 4.9 %collective-permute-start.1 = (f32[17920]{0:T(1024)S(1)}, f32[17920]{0:T(1024)S(1)}, u32[]{:S(2)}, u32[]{:S(2)}) collective-permute-start(f32[17920]{0:T(1024)S(1)} %pad_maximum_fusion.13), channel_id=1, source_target_pairs={{0,2},{2,0},{4,6},{6,4},{1,3},{3,1},{5,7},{7,5},{8,10},{10,8},{12,... | collective-permute-start | bytes 215048 | tf_op jit(solution)/shard_map/ppermute | solution.py:89
  9.6 6.0 %collective-permute-start.2 = (f32[19456]{0:T(1024)S(1)}, f32[19456]{0:T(1024)S(1)}, u32[]{:S(2)}, u32[]{:S(2)}) collective-permute-start(f32[19456]{0:T(1024)S(1)} %pad_maximum_fusion.12), channel_id=1, source_target_pairs={{0,4},{2,6},{4,0},{6,2},{1,5},{3,7},{5,1},{7,3},{8,12},{10,14},{12... | collective-permute-start | bytes 233480 | tf_op jit(solution)/shard_map/ppermute | solution.py:89
  15.7 4.6 %collective-permute-start.3 = (f32[22528]{0:T(1024)S(1)}, f32[22528]{0:T(1024)S(1)}, u32[]{:S(2)}, u32[]{:S(2)}) collective-permute-start(f32[22528]{0:T(1024)S(1)} %pad_maximum_fusion.11), channel_id=1, source_target_pairs={{0,8},{8,0},{16,24},{24,16},{32,40},{40,32},{48,56},{56,48},{1,9},... | collective-permute-start | bytes 270344 | tf_op jit(solution)/shard_map/ppermute | solution.py:89
  20.3 15.2 %collective-permute-start.4 = (f32[28672]{0:T(1024)S(1)}, f32[28672]{0:T(1024)S(1)}, u32[]{:S(2)}, u32[]{:S(2)}) collective-permute-start(f32[28672]{0:T(1024)S(1)} %pad_maximum_fusion.8), channel_id=1, source_target_pairs={{0,16},{8,24},{16,0},{24,8},{32,48},{40,56},{48,32},{56,40},{1,17}... | collective-permute-start | bytes 344072 | tf_op jit(solution)/shard_map/ppermute | solution.py:89
  35.6 9.6 %collective-permute-start.5 = (f32[40960]{0:T(1024)S(1)}, f32[40960]{0:T(1024)S(1)}, u32[]{:S(2)}, u32[]{:S(2)}) collective-permute-start(f32[40960]{0:T(1024)S(1)} %pad_maximum_fusion.7), channel_id=1, source_target_pairs={{0,32},{8,40},{16,48},{24,56},{32,0},{40,8},{48,16},{56,24},{1,33}... | collective-permute-start | bytes 491528 | tf_op jit(solution)/shard_map/ppermute | solution.py:89
  45.2 13.7 %copy-start.3 = (f32[40960]{0:T(1024)}, f32[40960]{0:T(1024)S(1)}, u32[]{:S(2)}) copy-start(f32[40960]{0:T(1024)S(1)} %collective-permute-done.5) | copy-start | bytes 491524
  45.3 8.1 %collective-permute-start.6 = (f32[65536]{0:T(1024)S(1)}, f32[65536]{0:T(1024)S(1)}, u32[]{:S(2)}, u32[]{:S(2)}) collective-permute-start(f32[65536]{0:T(1024)S(1)} %pad_maximum_fusion.5), channel_id=1, source_target_pairs={{0,64},{64,0},{128,192},{192,128},{1,65},{65,1},{129,193},{193,129... | collective-permute-start | bytes 786440 | tf_op jit(solution)/shard_map/ppermute | solution.py:89
  53.4 5.5 %copy-start.5 = (f32[65536]{0:T(1024)}, f32[65536]{0:T(1024)S(1)}, u32[]{:S(2)}) copy-start(f32[65536]{0:T(1024)S(1)} %collective-permute-done.6) | copy-start | bytes 786436
  53.5 10.9 %collective-permute-start.7 = (f32[114688]{0:T(1024)S(1)}, f32[114688]{0:T(1024)S(1)}, u32[]{:S(2)}, u32[]{:S(2)}) collective-permute-start(f32[114688]{0:T(1024)S(1)} %pad_maximum_fusion.2), channel_id=1, source_target_pairs={{0,128},{64,192},{128,0},{192,64},{1,129},{65,193},{129,1},{193,65... | collective-permute-start | bytes 1376264 | tf_op jit(solution)/shard_map/ppermute | solution.py:89
  64.4 0.8 copy-start.4
  65.6 17.0 %copy-start.1 = (f32[3072,128]{1,0:T(8,128)S(1)}, f32[3072,128]{1,0:T(8,128)}, u32[]{:S(2)}) copy-start(f32[3072,128]{1,0:T(8,128)} %param.5) | copy-start | bytes 4718596
  83.0 1.3 collective-permute-start.10
  84.3 3.7 %collective-permute-start.11 = (f32[128,16]{0,1:T(8,128)S(1)}, f32[128,16]{0,1:T(8,128)S(1)}, u32[]{:S(2)}, u32[]{:S(2)}) collective-permute-start(f32[128,16]{0,1:T(8,128)S(1)} %add.109), channel_id=1, source_target_pairs={{0,2},{2,0},{4,6},{6,4},{1,3},{3,1},{5,7},{7,5},{8,10},{10,8},{12,... | collective-permute-start | bytes 24584 | tf_op jit(solution)/shard_map/ppermute | solution.py:64
  87.9 14.8 %collective-permute-start.12 = (f32[128,16]{0,1:T(8,128)S(1)}, f32[128,16]{0,1:T(8,128)S(1)}, u32[]{:S(2)}, u32[]{:S(2)}) collective-permute-start(f32[128,16]{0,1:T(8,128)S(1)} %add.110), channel_id=1, source_target_pairs={{0,4},{2,6},{4,0},{6,2},{1,5},{3,7},{5,1},{7,3},{8,12},{10,14},{12... | collective-permute-start | bytes 24584 | tf_op jit(solution)/shard_map/ppermute | solution.py:64
  102.7 4.6 %collective-permute-start.13 = (f32[128,16]{0,1:T(8,128)S(1)}, f32[128,16]{0,1:T(8,128)S(1)}, u32[]{:S(2)}, u32[]{:S(2)}) collective-permute-start(f32[128,16]{0,1:T(8,128)S(1)} %add.111), channel_id=1, source_target_pairs={{0,8},{8,0},{16,24},{24,16},{32,40},{40,32},{48,56},{56,48},{1,9},... | collective-permute-start | bytes 24584 | tf_op jit(solution)/shard_map/ppermute | solution.py:64
  107.3 4.5 %collective-permute-start.14 = (f32[128,16]{0,1:T(8,128)S(1)}, f32[128,16]{0,1:T(8,128)S(1)}, u32[]{:S(2)}, u32[]{:S(2)}) collective-permute-start(f32[128,16]{0,1:T(8,128)S(1)} %add.112), channel_id=1, source_target_pairs={{0,16},{8,24},{16,0},{24,8},{32,48},{40,56},{48,32},{56,40},{1,17}... | collective-permute-start | bytes 24584 | tf_op jit(solution)/shard_map/ppermute | solution.py:64
  108.2 19.5 %collective-permute-start.8 = (f32[768,16]{0,1:T(8,128)S(1)}, f32[768,16]{0,1:T(8,128)}, u32[]{:S(2)}, u32[]{:S(2)}) collective-permute-start(f32[768,16]{0,1:T(8,128)S(1)} %bitcast.258), channel_id=1, source_target_pairs={{0,64},{64,0},{128,192},{192,128},{1,65},{65,1},{129,193},{193,129... | collective-permute-start | bytes 147464 | tf_op jit(solution)/shard_map/ppermute | solution.py:74
  111.9 14.8 %collective-permute-start.15 = (f32[128,16]{0,1:T(8,128)S(1)}, f32[128,16]{0,1:T(8,128)S(1)}, u32[]{:S(2)}, u32[]{:S(2)}) collective-permute-start(f32[128,16]{0,1:T(8,128)S(1)} %add.113), channel_id=1, source_target_pairs={{0,32},{8,40},{16,48},{24,56},{32,0},{40,8},{48,16},{56,24},{1,33}... | collective-permute-start | bytes 24584 | tf_op jit(solution)/shard_map/ppermute | solution.py:64
  126.7 3.7 %collective-permute-start.16 = (f32[128,16]{0,1:T(8,128)S(1)}, f32[128,16]{0,1:T(8,128)S(1)}, u32[]{:S(2)}, u32[]{:S(2)}) collective-permute-start(f32[128,16]{0,1:T(8,128)S(1)} %add.114), channel_id=1, source_target_pairs={{0,64},{64,0},{128,192},{192,128},{1,65},{65,1},{129,193},{193,129... | collective-permute-start | bytes 24584 | tf_op jit(solution)/shard_map/ppermute | solution.py:64
  130.4 5.3 %collective-permute-start.17 = (f32[128,16]{0,1:T(8,128)S(1)}, f32[128,16]{0,1:T(8,128)S(1)}, u32[]{:S(2)}, u32[]{:S(2)}) collective-permute-start(f32[128,16]{0,1:T(8,128)S(1)} %add.115), channel_id=1, source_target_pairs={{0,128},{64,192},{128,0},{192,64},{1,129},{65,193},{129,1},{193,65... | collective-permute-start | bytes 24584 | tf_op jit(solution)/shard_map/ppermute | solution.py:64
  134.1 6.4 %collective-permute-start.9 = (f32[1536,16]{0,1:T(8,128)S(1)}, f32[1536,16]{0,1:T(8,128)S(1)}, u32[]{:S(2)}, u32[]{:S(2)}) collective-permute-start(f32[1536,16]{0,1:T(8,128)S(1)} %pad_maximum_fusion.10), channel_id=1, source_target_pairs={{0,128},{64,192},{128,0},{192,64},{1,129},{65,193},{129,1},{193,65... | collective-permute-start | bytes 294920 | tf_op jit(solution)/shard_map/ppermute | solution.py:74
  142.0 3.5 %copy-start.2 = (bf16[3072,2,2,2,2,2,2,8]{0,7,6,5,4,3,2,1:T(8,128)(2,1)S(1)}, bf16[3072,2,2,2,2,2,2,8]{0,7,6,5,4,3,2,1:T(8,128)(2,1)}, u32[]{:S(2)}) copy-start(bf16[3072,2,2,2,2,2,2,8]{0,7,6,5,4,3,2,1:T(8,128)(2,1)} %copy.39) | copy-start | bytes 9437188
  152.5 4.2 %collective-permute-start.18 = (f32[2048,256]{0,1:T(8,128)S(1)}, f32[2048,256]{0,1:T(8,128)S(1)}, u32[]{:S(2)}, u32[]{:S(2)}) collective-permute-start(f32[2048,256]{0,1:T(8,128)S(1)} %slice_select_fusion), channel_id=1, source_target_pairs={{0,1},{1,0},{2,3},{3,2},{4,5},{5,4},{6,7},{7,6},{8,9},{9,8},{10,11... | collective-permute-start | bytes 6291464 | tf_op jit(solution)/shard_map/ppermute | solution.py:122
  157.6 14.1 %collective-permute-start.19 = (f32[1,128,1024]{2,1,0:T(8,128)S(1)}, f32[1,128,1024]{2,1,0:T(8,128)S(1)}, u32[]{:S(2)}, u32[]{:S(2)}) collective-permute-start(f32[1,128,1024]{2,1,0:T(8,128)S(1)} %select_bitcast_fusion.1), channel_id=1, source_target_pairs={{0,2},{2,0},{4,6},{6,4},{1,3},{3,1},{5,7},{7,5},{8,10},{10,8},{12,... | collective-permute-start | bytes 1572872 | tf_op jit(solution)/shard_map/ppermute | solution.py:136
  159.1 14.6 %collective-permute-start.23 = (f32[4,32,1024]{2,1,0:T(8,128)S(1)}, f32[4,32,1024]{2,1,0:T(8,128)S(1)}, u32[]{:S(2)}, u32[]{:S(2)}) collective-permute-start(f32[4,32,1024]{2,1,0:T(8,128)S(1)} %select_bitcast_fusion), channel_id=1, source_target_pairs={{0,8},{8,0},{16,24},{24,16},{32,40},{40,32},{48,56},{56,48},{1,9},... | collective-permute-start | bytes 1572872 | tf_op jit(solution)/shard_map/ppermute | solution.py:136
  171.8 7.7 %collective-permute-start.20 = (f32[2,32,1024]{2,1,0:T(8,128)S(1)}, f32[2,32,1024]{2,1,0:T(8,128)S(1)}, u32[]{:S(2)}, u32[]{:S(2)}) collective-permute-start(f32[2,32,1024]{2,1,0:T(8,128)S(1)} %select_bitcast_fusion.3), channel_id=1, source_target_pairs={{0,8},{8,0},{16,24},{24,16},{32,40},{40,32},{48,56},{56,48},{1,9},... | collective-permute-start | bytes 786440 | tf_op jit(solution)/shard_map/ppermute | solution.py:136
  173.9 7.3 %collective-permute-start.24 = (f32[1,64,1024]{2,1,0:T(8,128)S(1)}, f32[1,64,1024]{2,1,0:T(8,128)S(1)}, u32[]{:S(2)}, u32[]{:S(2)}) collective-permute-start(f32[1,64,1024]{2,1,0:T(8,128)S(1)} %select_bitcast_fusion.2), channel_id=1, source_target_pairs={{0,2},{2,0},{4,6},{6,4},{1,3},{3,1},{5,7},{7,5},{8,10},{10,8},{12,... | collective-permute-start | bytes 786440 | tf_op jit(solution)/shard_map/ppermute | solution.py:136
  179.5 6.6 %collective-permute-start.21 = (f32[1,32,1024]{2,1,0:T(8,128)S(1)}, f32[1,32,1024]{2,1,0:T(8,128)S(1)}, u32[]{:S(2)}, u32[]{:S(2)}) collective-permute-start(f32[1,32,1024]{2,1,0:T(8,128)S(1)} %select_bitcast_fusion.5), channel_id=1, source_target_pairs={{0,4},{2,6},{4,0},{6,2},{1,5},{3,7},{5,1},{7,3},{8,12},{10,14},{12... | collective-permute-start | bytes 393224 | tf_op jit(solution)/shard_map/ppermute | solution.py:136
  181.3 8.3 %collective-permute-start.25 = (f32[2,16,1024]{2,1,0:T(8,128)S(1)}, f32[2,16,1024]{2,1,0:T(8,128)S(1)}, u32[]{:S(2)}, u32[]{:S(2)}) collective-permute-start(f32[2,16,1024]{2,1,0:T(8,128)S(1)} %select_bitcast_fusion.4), channel_id=1, source_target_pairs={{0,16},{8,24},{16,0},{24,8},{32,48},{40,56},{48,32},{56,40},{1,17}... | collective-permute-start | bytes 393224 | tf_op jit(solution)/shard_map/ppermute | solution.py:136
  186.1 5.7 %collective-permute-start.22 = (f32[1,16,1024]{2,1,0:T(8,128)S(1)}, f32[1,16,1024]{2,1,0:T(8,128)S(1)}, u32[]{:S(2)}, u32[]{:S(2)}) collective-permute-start(f32[1,16,1024]{2,1,0:T(8,128)S(1)} %select_bitcast_fusion.8), channel_id=1, source_target_pairs={{0,16},{8,24},{16,0},{24,8},{32,48},{40,56},{48,32},{56,40},{1,17}... | collective-permute-start | bytes 196616 | tf_op jit(solution)/shard_map/ppermute | solution.py:136
  189.6 5.9 %collective-permute-start.26 = (f32[1,16,1024]{2,1,0:T(8,128)S(1)}, f32[1,16,1024]{2,1,0:T(8,128)S(1)}, u32[]{:S(2)}, u32[]{:S(2)}) collective-permute-start(f32[1,16,1024]{2,1,0:T(8,128)S(1)} %select_bitcast_fusion.7), channel_id=1, source_target_pairs={{0,4},{2,6},{4,0},{6,2},{1,5},{3,7},{5,1},{7,3},{8,12},{10,14},{12... | collective-permute-start | bytes 196616 | tf_op jit(solution)/shard_map/ppermute | solution.py:136
  195.5 8.3 %collective-permute-start.27 = (f32[1,8,2048]{2,1,0:T(8,128)S(1)}, f32[1,8,2048]{2,1,0:T(8,128)S(1)}, u32[]{:S(2)}, u32[]{:S(2)}) collective-permute-start(f32[1,8,2048]{2,1,0:T(8,128)S(1)} %select_bitcast_fusion.6), channel_id=1, source_target_pairs={{0,32},{8,40},{16,48},{24,56},{32,0},{40,8},{48,16},{56,24},{1,33}... | collective-permute-start | bytes 196616 | tf_op jit(solution)/shard_map/ppermute | solution.py:136

commit v12 on v11

--- a/solution.py
+++ b/solution.py
@@ -173,7 +173,7 @@
     expo_part = lax.dynamic_slice_in_dim(exposures, offset_rows, quarter, 0)
     gram_part = jnp.dot(expo_part.T, expo_part, precision=hi)
     steps = axis_bits(("core", "x", "z", "vgrp"))
-    pheno_full, gram, dosages = front_chain(phenotype, gram_part, steps, reorder_dosages(genotypes), 5)
+    pheno_full, gram, dosages = front_chain(phenotype, gram_part, steps, reorder_dosages(genotypes), 7)
     samples = pheno_full.shape[0]
     system = gram + 0.5 * samples * jnp.eye(width, dtype=jnp.float32)
     factor = jnp.linalg.cholesky(system)

time: 206 us -> 207 us (level)
  waiting for transfers between devices: 73.1 us -> 82.2 us
  starting transfers between devices: 54.4 us -> 46.7 us
    ppermute x9, waiting for transfers between devices: 28.3 us -> 35.1 us  [halve_bit(): kept = mine + lax.ppermute(send, axis, flip)]
    ppermute x9, starting transfers between devices: 17.2 us -> 10.6 us  [halve_bit(): kept = mine + lax.ppermute(send, axis, flip)]
    ppermute x8, starting transfers between devices: 14.9 us -> 11 us  [doubling_psum(): x = x + lax.ppermute(x, axis, pairs)]
    ppermute x8, waiting for transfers between devices: 8.98 us -> 12.5 us  [doubling_psum(): x = x + lax.ppermute(x, axis, pairs)]
    ppermute x8, starting transfers between devices: 20.2 us -> 23.6 us  [front_chain(): lax.ppermute(jnp.concatenate([pheno, gram.reshape(-1)]), axis, flip)]
    unnamed x16 -> x12, local copies, waits for them, and re-layouts: 8.53 us -> 8.47 us
where the time goes in v12:
time: 207 us; the launch traced here: 206 us
  waiting for transfers between devices  82.2 us (40%)
  starting transfers between devices  46.7 us (23%)
  other arithmetic  39 us (19%)
  Pallas kernels  13.9 us (7%)
  local copies, waits for them, and re-layouts  12.6 us (6%)
  matrix products  10.7 us (5%)
    ppermute x9, waiting for transfers between devices, halve_bit(): kept = mine + lax.ppermute(send, axis, flip)  35.1 us
    ppermute x8, waiting for transfers between devices, front_chain(): lax.ppermute(jnp.concatenate([pheno, gram.reshape(-1)]), axis, flip)  26.6 us
    ppermute x8, starting transfers between devices, front_chain(): lax.ppermute(jnp.concatenate([pheno, gram.reshape(-1)]), axis, flip)  23.6 us
    pallas_call x1, Pallas kernels, gather_pheno(): pl.pallas_call(gather_body, grid=(count // TILE,), in_specs=[pl.BlockSpec...  13.9 us
    ppermute x8, waiting for transfers between devices, doubling_psum(): x = x + lax.ppermute(x, axis, pairs)  12.5 us
    another operation x3, other arithmetic, per_device(): factor = jnp.linalg.cholesky(system)  12.4 us
    ppermute x8, starting transfers between devices, doubling_psum(): x = x + lax.ppermute(x, axis, pairs)  11 us
    ppermute x9, starting transfers between devices, halve_bit(): kept = mine + lax.ppermute(send, axis, flip)  10.6 us
  transfers between devices with their start and end apart: 28, of which 22 were waited for; matrix products, arithmetic and copies ran while one was open for 20% of the time, Pallas kernels for 0%

profile of v12, /device:TPU:2, one launch (start us, length us, event | category | flops | bytes accessed | tf_op | source)
XLA Modules:
  0.0 205.5 jit_solution(12726407671880702281)
XLA Ops:
  0.0 1.9 fusion.7
  2.7 1.2 collective-permute-done
  4.6 2.3 %collective-permute-start.1 = (f32[17920]{0:T(1024)S(1)}, f32[17920]{0:T(1024)S(1)}, u32[]{:S(2)}, u32[]{:S(2)}) collective-permute-start(f32[17920]{0:T(1024)S(1)} %pad_maximum_fusion.12), channel_id=1, source_target_pairs={{0,2},{2,0},{4,6},{6,4},{1,3},{3,1},{5,7},{7,5},{8,10},{10,8},{12,... | collective-permute-start | bytes 215048 | tf_op jit(solution)/shard_map/ppermute | solution.py:89
  7.0 2.6 %collective-permute-done.1 = f32[17920]{0:T(1024)S(1)} collective-permute-done((f32[17920]{0:T(1024)S(1)}, f32[17920]{0:T(1024)S(1)}, u32[]{:S(2)}, u32[]{:S(2)}) %collective-permute-start.1) | collective-permute-done | bytes 71712 | tf_op jit(solution)/shard_map/ppermute | solution.py:89
  9.6 1.7 collective-permute-start.2
  11.3 4.3 %collective-permute-done.2 = f32[19456]{0:T(1024)S(1)} collective-permute-done((f32[19456]{0:T(1024)S(1)}, f32[19456]{0:T(1024)S(1)}, u32[]{:S(2)}, u32[]{:S(2)}) %collective-permute-start.2) | collective-permute-done | bytes 77856 | tf_op jit(solution)/shard_map/ppermute | solution.py:89
  15.7 1.5 collective-permute-start.3
  17.2 3.1 %collective-permute-done.3 = f32[22528]{0:T(1024)S(1)} collective-permute-done((f32[22528]{0:T(1024)S(1)}, f32[22528]{0:T(1024)S(1)}, u32[]{:S(2)}, u32[]{:S(2)}) %collective-permute-start.3) | collective-permute-done | bytes 90144 | tf_op jit(solution)/shard_map/ppermute | solution.py:89
  20.3 3.2 %collective-permute-start.4 = (f32[28672]{0:T(1024)S(1)}, f32[28672]{0:T(1024)S(1)}, u32[]{:S(2)}, u32[]{:S(2)}) collective-permute-start(f32[28672]{0:T(1024)S(1)} %pad_maximum_fusion.7), channel_id=1, source_target_pairs={{0,16},{8,24},{16,0},{24,8},{32,48},{40,56},{48,32},{56,40},{1,17}... | collective-permute-start | bytes 344072 | tf_op jit(solution)/shard_map/ppermute | solution.py:89
  23.6 4.0 %collective-permute-done.4 = f32[28672]{0:T(1024)S(1)} collective-permute-done((f32[28672]{0:T(1024)S(1)}, f32[28672]{0:T(1024)S(1)}, u32[]{:S(2)}, u32[]{:S(2)}) %collective-permute-start.4) | collective-permute-done | bytes 114720 | tf_op jit(solution)/shard_map/ppermute | solution.py:89
  27.7 10.1 %collective-permute-start.5 = (f32[40960]{0:T(1024)S(1)}, f32[40960]{0:T(1024)S(1)}, u32[]{:S(2)}, u32[]{:S(2)}) collective-permute-start(f32[40960]{0:T(1024)S(1)} %pad_maximum_fusion.6), channel_id=1, source_target_pairs={{0,32},{8,40},{16,48},{24,56},{32,0},{40,8},{48,16},{56,24},{1,33}... | collective-permute-start | bytes 491528 | tf_op jit(solution)/shard_map/ppermute | solution.py:89
  37.7 5.1 %collective-permute-done.5 = f32[40960]{0:T(1024)S(1)} collective-permute-done((f32[40960]{0:T(1024)S(1)}, f32[40960]{0:T(1024)S(1)}, u32[]{:S(2)}, u32[]{:S(2)}) %collective-permute-start.5) | collective-permute-done | bytes 163872 | tf_op jit(solution)/shard_map/ppermute | solution.py:89
  42.9 1.7 collective-permute-start.6
  44.6 6.6 %copy.34 = s32[3072,512]{0,1:T(8,128)} copy(s32[3072,512]{1,0:T(8,128)} %param.7) | data formatting | bytes 12582912 | tf_op args[3]
  51.2 3.5 %convert_element_type.31 = bf16[3072,512]{0,1:T(8,128)(2,1)S(1)} convert(s32[3072,512]{0,1:T(8,128)} %copy.34) | non-fusion elementwise | flops 1572864 | bytes 9437184 | tf_op jit(solution)/shard_map/convert_element_type | solution.py:146
  54.7 1.8 copy.35
  56.7 3.0 %collective-permute-start.7 = (f32[114688]{0:T(1024)S(1)}, f32[114688]{0:T(1024)S(1)}, u32[]{:S(2)}, u32[]{:S(2)}) collective-permute-start(f32[114688]{0:T(1024)S(1)} %pad_maximum_fusion.2), channel_id=1, source_target_pairs={{0,128},{64,192},{128,0},{192,64},{1,129},{65,193},{129,1},{193,65... | collective-permute-start | bytes 1376264 | tf_op jit(solution)/shard_map/ppermute | solution.py:89
  60.3 6.4 %collective-permute-done.7 = f32[114688]{0:T(1024)S(1)} collective-permute-done((f32[114688]{0:T(1024)S(1)}, f32[114688]{0:T(1024)S(1)}, u32[]{:S(2)}, u32[]{:S(2)}) %collective-permute-start.7) | collective-permute-done | bytes 458784 | tf_op jit(solution)/shard_map/ppermute | solution.py:89
  68.2 0.9 pad_maximum_fusion.1.tab_ref
  69.1 13.9 %shard_map.46 = f32[1,12288]{1,0:T(1,128)} custom-call(s32[1,12288]{1,0:T(1,128)} %bitcast.271, bf16[512,768]{1,0:T(8,128)(2,1)} %pad_maximum_fusion.1.tab_ref), custom_call_target="tpu_custom_call" | custom-call | tf_op jit(solution)/shard_map/pallas_call | solution.py:44
  83.5 1.6 reduce.9
  88.8 1.5 collective-permute-done.11
  90.4 2.1 %collective-permute-start.12 = (f32[128,16]{0,1:T(8,128)S(1)}, f32[128,16]{0,1:T(8,128)S(1)}, u32[]{:S(2)}, u32[]{:S(2)}) collective-permute-start(f32[128,16]{0,1:T(8,128)S(1)} %add.110), channel_id=1, source_target_pairs={{0,4},{2,6},{4,0},{6,2},{1,5},{3,7},{5,1},{7,3},{8,12},{10,14},{12... | collective-permute-start | bytes 24584 | tf_op jit(solution)/shard_map/ppermute | solution.py:64
  93.4 11.7 %cholesky.16 = f32[128,128]{1,0:T(8,128)S(1)} custom-call(f32[128,128]{1,0:T(8,128)S(1)} %fusion.33), custom_call_target="Cholesky" | custom-call | tf_op jit(solution)/shard_map/jit(cholesky)/cholesky | solution.py:179
  105.3 3.6 %collective-permute-done.13 = f32[128,16]{0,1:T(8,128)S(1)} collective-permute-done((f32[128,16]{0,1:T(8,128)S(1)}, f32[128,16]{0,1:T(8,128)S(1)}, u32[]{:S(2)}, u32[]{:S(2)}) %collective-permute-start.13) | collective-permute-done | bytes 8224 | tf_op jit(solution)/shard_map/ppermute | solution.py:64
  110.5 2.9 %collective-permute-done.14 = f32[128,16]{0,1:T(8,128)S(1)} collective-permute-done((f32[128,16]{0,1:T(8,128)S(1)}, f32[128,16]{0,1:T(8,128)S(1)}, u32[]{:S(2)}, u32[]{:S(2)}) %collective-permute-start.14) | collective-permute-done | bytes 8224 | tf_op jit(solution)/shard_map/ppermute | solution.py:64
  113.4 4.2 %collective-permute-start.15 = (f32[128,16]{0,1:T(8,128)S(1)}, f32[128,16]{0,1:T(8,128)S(1)}, u32[]{:S(2)}, u32[]{:S(2)}) collective-permute-start(f32[128,16]{0,1:T(8,128)S(1)} %add.113), channel_id=1, source_target_pairs={{0,32},{8,40},{16,48},{24,56},{32,0},{40,8},{48,16},{56,24},{1,33}... | collective-permute-start | bytes 24584 | tf_op jit(solution)/shard_map/ppermute | solution.py:64
  118.3 9.8 %custom-call.8 = f32[1,128,128]{1,2,0:T(8,128)S(1)} custom-call(f32[1,128,128]{2,1,0:T(8,128)S(1)} %fusion.15), custom_call_target="InvertDiagBlocksLowerTriangular" | custom-call | tf_op jit(solution)/shard_map/triangular_solve | solution.py:13
  129.5 2.5 %collective-permute-done.16 = f32[128,16]{0,1:T(8,128)S(1)} collective-permute-done((f32[128,16]{0,1:T(8,128)S(1)}, f32[128,16]{0,1:T(8,128)S(1)}, u32[]{:S(2)}, u32[]{:S(2)}) %collective-permute-start.16) | collective-permute-done | bytes 8224 | tf_op jit(solution)/shard_map/ppermute | solution.py:64
  131.9 2.9 %collective-permute-start.17 = (f32[128,16]{0,1:T(8,128)S(1)}, f32[128,16]{0,1:T(8,128)S(1)}, u32[]{:S(2)}, u32[]{:S(2)}) collective-permute-start(f32[128,16]{0,1:T(8,128)S(1)} %add.115), channel_id=1, source_target_pairs={{0,128},{64,192},{128,0},{192,64},{1,129},{65,193},{129,1},{193,65... | collective-permute-start | bytes 24584 | tf_op jit(solution)/shard_map/ppermute | solution.py:64
  135.8 1.3 collective-permute-done.17
  137.4 3.8 %collective-permute-done.9 = f32[1536,16]{0,1:T(8,128)S(1)} collective-permute-done((f32[1536,16]{0,1:T(8,128)S(1)}, f32[1536,16]{0,1:T(8,128)S(1)}, u32[]{:S(2)}, u32[]{:S(2)}) %collective-permute-start.9) | collective-permute-done | bytes 98336 | tf_op jit(solution)/shard_map/ppermute | solution.py:74
  141.3 1.4 maximum_subtract_fusion
  142.7 3.4 %multiply_convert_fusion = bf16[3072,128,16]{0,2,1:T(8,128)(2,1)S(1)} fusion(f32[3072,16]{0,1:T(8,128)S(1)} %maximum_subtract_fusion, f32[3072,128]{0,1:T(8,128)S(1)} %copy.33), kind=kLoop, calls=%fused_computation | loop fusion | flops 12582912 | bytes 14352384 | tf_op jit(solution)/shard_map/convert_element_type | solution.py:191
  146.1 6.7 %fusion.42 = f32[2048,512]{0,1:T(8,128)S(1)} fusion(bf16[3072,2048]{0,1:T(8,128)(2,1)S(1)} %bitcast.253, bf16[3072,512]{0,1:T(8,128)(2,1)S(1)} %bitcast.264), kind=kOutput, calls=%fused_computation.124 | convolution fusion | flops 6442450944 | bytes 19922944 | tf_op jit(solution)/shard_map/dot_general | solution.py:150
  153.3 4.1 %collective-permute-done.18 = f32[2048,256]{0,1:T(8,128)S(1)} collective-permute-done((f32[2048,256]{0,1:T(8,128)S(1)}, f32[2048,256]{0,1:T(8,128)S(1)}, u32[]{:S(2)}, u32[]{:S(2)}) %collective-permute-start.18) | collective-permute-done | bytes 2097184 | tf_op jit(solution)/shard_map/ppermute | solution.py:122
  158.3 1.5 collective-permute-start.19
  160.0 12.4 %collective-permute-done.19 = f32[1,128,1024]{2,1,0:T(8,128)S(1)} collective-permute-done((f32[1,128,1024]{2,1,0:T(8,128)S(1)}, f32[1,128,1024]{2,1,0:T(8,128)S(1)}, u32[]{:S(2)}, u32[]{:S(2)}) %collective-permute-start.19) | collective-permute-done | bytes 524320 | tf_op jit(solution)/shard_map/ppermute | solution.py:136
  172.6 1.0 collective-permute-done.23
  174.5 5.6 %collective-permute-done.20 = f32[2,32,1024]{2,1,0:T(8,128)S(1)} collective-permute-done((f32[2,32,1024]{2,1,0:T(8,128)S(1)}, f32[2,32,1024]{2,1,0:T(8,128)S(1)}, u32[]{:S(2)}, u32[]{:S(2)}) %collective-permute-start.20) | collective-permute-done | bytes 262176 | tf_op jit(solution)/shard_map/ppermute | solution.py:136
  180.1 1.5 collective-permute-start.21
  181.7 1.1 collective-permute-start.25
  182.8 3.9 %collective-permute-done.21 = f32[1,32,1024]{2,1,0:T(8,128)S(1)} collective-permute-done((f32[1,32,1024]{2,1,0:T(8,128)S(1)}, f32[1,32,1024]{2,1,0:T(8,128)S(1)}, u32[]{:S(2)}, u32[]{:S(2)}) %collective-permute-start.21) | collective-permute-done | bytes 131104 | tf_op jit(solution)/shard_map/ppermute | solution.py:136
  187.7 2.8 %collective-permute-done.25 = f32[2,16,1024]{2,1,0:T(8,128)S(1)} collective-permute-done((f32[2,16,1024]{2,1,0:T(8,128)S(1)}, f32[2,16,1024]{2,1,0:T(8,128)S(1)}, u32[]{:S(2)}, u32[]{:S(2)}) %collective-permute-start.25) | collective-permute-done | bytes 131104 | tf_op jit(solution)/shard_map/ppermute | solution.py:136
  190.5 2.9 %collective-permute-start.26 = (f32[1,16,1024]{2,1,0:T(8,128)S(1)}, f32[1,16,1024]{2,1,0:T(8,128)S(1)}, u32[]{:S(2)}, u32[]{:S(2)}) collective-permute-start(f32[1,16,1024]{2,1,0:T(8,128)S(1)} %select_bitcast_fusion.7), channel_id=1, source_target_pairs={{0,4},{2,6},{4,0},{6,2},{1,5},{3,7},{5,1},{7,3},{8,12},{10,14},{12... | collective-permute-start | bytes 196616 | tf_op jit(solution)/shard_map/ppermute | solution.py:136
  193.4 2.9 %collective-permute-done.26 = f32[1,16,1024]{2,1,0:T(8,128)S(1)} collective-permute-done((f32[1,16,1024]{2,1,0:T(8,128)S(1)}, f32[1,16,1024]{2,1,0:T(8,128)S(1)}, u32[]{:S(2)}, u32[]{:S(2)}) %collective-permute-start.26) | collective-permute-done | bytes 65568 | tf_op jit(solution)/shard_map/ppermute | solution.py:136
  196.4 1.9 collective-permute-start.27
  198.2 6.4 %collective-permute-done.27 = f32[1,8,2048]{2,1,0:T(8,128)S(1)} collective-permute-done((f32[1,8,2048]{2,1,0:T(8,128)S(1)}, f32[1,8,2048]{2,1,0:T(8,128)S(1)}, u32[]{:S(2)}, u32[]{:S(2)}) %collective-permute-start.27) | collective-permute-done | bytes 65568 | tf_op jit(solution)/shard_map/ppermute | solution.py:136
  (105 shorter events, 18.6 us)
Async XLA Ops:
  0.0 59.6 %copy-start = (s32[16,3072]{1,0:T(8,128)S(1)}, s32[16,3072]{1,0:T(8,128)}, u32[]{:S(2)}) copy-start(s32[16,3072]{1,0:T(8,128)} %param.6) | copy-start | bytes 589828
  2.7 1.3 collective-permute-start
  4.6 4.9 %collective-permute-start.1 = (f32[17920]{0:T(1024)S(1)}, f32[17920]{0:T(1024)S(1)}, u32[]{:S(2)}, u32[]{:S(2)}) collective-permute-start(f32[17920]{0:T(1024)S(1)} %pad_maximum_fusion.12), channel_id=1, source_target_pairs={{0,2},{2,0},{4,6},{6,4},{1,3},{3,1},{5,7},{7,5},{8,10},{10,8},{12,... | collective-permute-start | bytes 215048 | tf_op jit(solution)/shard_map/ppermute | solution.py:89
  9.6 6.0 %collective-permute-start.2 = (f32[19456]{0:T(1024)S(1)}, f32[19456]{0:T(1024)S(1)}, u32[]{:S(2)}, u32[]{:S(2)}) collective-permute-start(f32[19456]{0:T(1024)S(1)} %pad_maximum_fusion.11), channel_id=1, source_target_pairs={{0,4},{2,6},{4,0},{6,2},{1,5},{3,7},{5,1},{7,3},{8,12},{10,14},{12... | collective-permute-start | bytes 233480 | tf_op jit(solution)/shard_map/ppermute | solution.py:89
  15.7 4.6 %collective-permute-start.3 = (f32[22528]{0:T(1024)S(1)}, f32[22528]{0:T(1024)S(1)}, u32[]{:S(2)}, u32[]{:S(2)}) collective-permute-start(f32[22528]{0:T(1024)S(1)} %pad_maximum_fusion.10), channel_id=1, source_target_pairs={{0,8},{8,0},{16,24},{24,16},{32,40},{40,32},{48,56},{56,48},{1,9},... | collective-permute-start | bytes 270344 | tf_op jit(solution)/shard_map/ppermute | solution.py:89
  20.3 7.2 %collective-permute-start.4 = (f32[28672]{0:T(1024)S(1)}, f32[28672]{0:T(1024)S(1)}, u32[]{:S(2)}, u32[]{:S(2)}) collective-permute-start(f32[28672]{0:T(1024)S(1)} %pad_maximum_fusion.7), channel_id=1, source_target_pairs={{0,16},{8,24},{16,0},{24,8},{32,48},{40,56},{48,32},{56,40},{1,17}... | collective-permute-start | bytes 344072 | tf_op jit(solution)/shard_map/ppermute | solution.py:89
  27.7 15.1 %collective-permute-start.5 = (f32[40960]{0:T(1024)S(1)}, f32[40960]{0:T(1024)S(1)}, u32[]{:S(2)}, u32[]{:S(2)}) collective-permute-start(f32[40960]{0:T(1024)S(1)} %pad_maximum_fusion.6), channel_id=1, source_target_pairs={{0,32},{8,40},{16,48},{24,56},{32,0},{40,8},{48,16},{56,24},{1,33}... | collective-permute-start | bytes 491528 | tf_op jit(solution)/shard_map/ppermute | solution.py:89
  42.9 13.6 %collective-permute-start.6 = (f32[65536]{0:T(1024)S(1)}, f32[65536]{0:T(1024)S(1)}, u32[]{:S(2)}, u32[]{:S(2)}) collective-permute-start(f32[65536]{0:T(1024)S(1)} %pad_maximum_fusion.4), channel_id=1, source_target_pairs={{0,64},{64,0},{128,192},{192,128},{1,65},{65,1},{129,193},{193,129... | collective-permute-start | bytes 786440 | tf_op jit(solution)/shard_map/ppermute | solution.py:89
  56.7 10.1 %collective-permute-start.7 = (f32[114688]{0:T(1024)S(1)}, f32[114688]{0:T(1024)S(1)}, u32[]{:S(2)}, u32[]{:S(2)}) collective-permute-start(f32[114688]{0:T(1024)S(1)} %pad_maximum_fusion.2), channel_id=1, source_target_pairs={{0,128},{64,192},{128,0},{192,64},{1,129},{65,193},{129,1},{193,65... | collective-permute-start | bytes 1376264 | tf_op jit(solution)/shard_map/ppermute | solution.py:89
  66.7 0.8 copy-start.3
  68.1 17.1 %copy-start.1 = (f32[3072,128]{1,0:T(8,128)S(1)}, f32[3072,128]{1,0:T(8,128)}, u32[]{:S(2)}) copy-start(f32[3072,128]{1,0:T(8,128)} %param.5) | copy-start | bytes 4718596
  85.5 1.3 collective-permute-start.10
  86.7 3.7 %collective-permute-start.11 = (f32[128,16]{0,1:T(8,128)S(1)}, f32[128,16]{0,1:T(8,128)S(1)}, u32[]{:S(2)}, u32[]{:S(2)}) collective-permute-start(f32[128,16]{0,1:T(8,128)S(1)} %add.109), channel_id=1, source_target_pairs={{0,2},{2,0},{4,6},{6,4},{1,3},{3,1},{5,7},{7,5},{8,10},{10,8},{12,... | collective-permute-start | bytes 24584 | tf_op jit(solution)/shard_map/ppermute | solution.py:64
  90.4 14.7 %collective-permute-start.12 = (f32[128,16]{0,1:T(8,128)S(1)}, f32[128,16]{0,1:T(8,128)S(1)}, u32[]{:S(2)}, u32[]{:S(2)}) collective-permute-start(f32[128,16]{0,1:T(8,128)S(1)} %add.110), channel_id=1, source_target_pairs={{0,4},{2,6},{4,0},{6,2},{1,5},{3,7},{5,1},{7,3},{8,12},{10,14},{12... | collective-permute-start | bytes 24584 | tf_op jit(solution)/shard_map/ppermute | solution.py:64
  105.1 3.7 %collective-permute-start.13 = (f32[128,16]{0,1:T(8,128)S(1)}, f32[128,16]{0,1:T(8,128)S(1)}, u32[]{:S(2)}, u32[]{:S(2)}) collective-permute-start(f32[128,16]{0,1:T(8,128)S(1)} %add.111), channel_id=1, source_target_pairs={{0,8},{8,0},{16,24},{24,16},{32,40},{40,32},{48,56},{56,48},{1,9},... | collective-permute-start | bytes 24584 | tf_op jit(solution)/shard_map/ppermute | solution.py:64
  108.9 4.5 %collective-permute-start.14 = (f32[128,16]{0,1:T(8,128)S(1)}, f32[128,16]{0,1:T(8,128)S(1)}, u32[]{:S(2)}, u32[]{:S(2)}) collective-permute-start(f32[128,16]{0,1:T(8,128)S(1)} %add.112), channel_id=1, source_target_pairs={{0,16},{8,24},{16,0},{24,8},{32,48},{40,56},{48,32},{56,40},{1,17}... | collective-permute-start | bytes 24584 | tf_op jit(solution)/shard_map/ppermute | solution.py:64
  110.1 18.6 %collective-permute-start.8 = (f32[768,16]{0,1:T(8,128)S(1)}, f32[768,16]{0,1:T(8,128)}, u32[]{:S(2)}, u32[]{:S(2)}) collective-permute-start(f32[768,16]{0,1:T(8,128)S(1)} %bitcast.270), channel_id=1, source_target_pairs={{0,64},{64,0},{128,192},{192,128},{1,65},{65,1},{129,193},{193,129... | collective-permute-start | bytes 147464 | tf_op jit(solution)/shard_map/ppermute | solution.py:74
  113.4 14.7 %collective-permute-start.15 = (f32[128,16]{0,1:T(8,128)S(1)}, f32[128,16]{0,1:T(8,128)S(1)}, u32[]{:S(2)}, u32[]{:S(2)}) collective-permute-start(f32[128,16]{0,1:T(8,128)S(1)} %add.113), channel_id=1, source_target_pairs={{0,32},{8,40},{16,48},{24,56},{32,0},{40,8},{48,16},{56,24},{1,33}... | collective-permute-start | bytes 24584 | tf_op jit(solution)/shard_map/ppermute | solution.py:64
  128.1 3.8 %collective-permute-start.16 = (f32[128,16]{0,1:T(8,128)S(1)}, f32[128,16]{0,1:T(8,128)S(1)}, u32[]{:S(2)}, u32[]{:S(2)}) collective-permute-start(f32[128,16]{0,1:T(8,128)S(1)} %add.114), channel_id=1, source_target_pairs={{0,64},{64,0},{128,192},{192,128},{1,65},{65,1},{129,193},{193,129... | collective-permute-start | bytes 24584 | tf_op jit(solution)/shard_map/ppermute | solution.py:64
  131.9 5.2 %collective-permute-start.17 = (f32[128,16]{0,1:T(8,128)S(1)}, f32[128,16]{0,1:T(8,128)S(1)}, u32[]{:S(2)}, u32[]{:S(2)}) collective-permute-start(f32[128,16]{0,1:T(8,128)S(1)} %add.115), channel_id=1, source_target_pairs={{0,128},{64,192},{128,0},{192,64},{1,129},{65,193},{129,1},{193,65... | collective-permute-start | bytes 24584 | tf_op jit(solution)/shard_map/ppermute | solution.py:64
  134.8 6.4 %collective-permute-start.9 = (f32[1536,16]{0,1:T(8,128)S(1)}, f32[1536,16]{0,1:T(8,128)S(1)}, u32[]{:S(2)}, u32[]{:S(2)}) collective-permute-start(f32[1536,16]{0,1:T(8,128)S(1)} %pad_maximum_fusion.9), channel_id=1, source_target_pairs={{0,128},{64,192},{128,0},{192,64},{1,129},{65,193},{129,1},{193,65... | collective-permute-start | bytes 294920 | tf_op jit(solution)/shard_map/ppermute | solution.py:74
  142.7 3.5 %copy-start.2 = (bf16[3072,2,2,2,2,2,2,8]{0,7,6,5,4,3,2,1:T(8,128)(2,1)S(1)}, bf16[3072,2,2,2,2,2,2,8]{0,7,6,5,4,3,2,1:T(8,128)(2,1)}, u32[]{:S(2)}) copy-start(bf16[3072,2,2,2,2,2,2,8]{0,7,6,5,4,3,2,1:T(8,128)(2,1)} %copy.35) | copy-start | bytes 9437188
  153.2 4.2 %collective-permute-start.18 = (f32[2048,256]{0,1:T(8,128)S(1)}, f32[2048,256]{0,1:T(8,128)S(1)}, u32[]{:S(2)}, u32[]{:S(2)}) collective-permute-start(f32[2048,256]{0,1:T(8,128)S(1)} %slice_select_fusion), channel_id=1, source_target_pairs={{0,1},{1,0},{2,3},{3,2},{4,5},{5,4},{6,7},{7,6},{8,9},{9,8},{10,11... | collective-permute-start | bytes 6291464 | tf_op jit(solution)/shard_map/ppermute | solution.py:122
  158.3 14.1 %collective-permute-start.19 = (f32[1,128,1024]{2,1,0:T(8,128)S(1)}, f32[1,128,1024]{2,1,0:T(8,128)S(1)}, u32[]{:S(2)}, u32[]{:S(2)}) collective-permute-start(f32[1,128,1024]{2,1,0:T(8,128)S(1)} %select_bitcast_fusion.1), channel_id=1, source_target_pairs={{0,2},{2,0},{4,6},{6,4},{1,3},{3,1},{5,7},{7,5},{8,10},{10,8},{12,... | collective-permute-start | bytes 1572872 | tf_op jit(solution)/shard_map/ppermute | solution.py:136
  159.9 13.8 %collective-permute-start.23 = (f32[4,32,1024]{2,1,0:T(8,128)S(1)}, f32[4,32,1024]{2,1,0:T(8,128)S(1)}, u32[]{:S(2)}, u32[]{:S(2)}) collective-permute-start(f32[4,32,1024]{2,1,0:T(8,128)S(1)} %select_bitcast_fusion), channel_id=1, source_target_pairs={{0,8},{8,0},{16,24},{24,16},{32,40},{40,32},{48,56},{56,48},{1,9},... | collective-permute-start | bytes 1572872 | tf_op jit(solution)/shard_map/ppermute | solution.py:136
  172.5 7.6 %collective-permute-start.20 = (f32[2,32,1024]{2,1,0:T(8,128)S(1)}, f32[2,32,1024]{2,1,0:T(8,128)S(1)}, u32[]{:S(2)}, u32[]{:S(2)}) collective-permute-start(f32[2,32,1024]{2,1,0:T(8,128)S(1)} %select_bitcast_fusion.3), channel_id=1, source_target_pairs={{0,8},{8,0},{16,24},{24,16},{32,40},{40,32},{48,56},{56,48},{1,9},... | collective-permute-start | bytes 786440 | tf_op jit(solution)/shard_map/ppermute | solution.py:136
  173.8 7.8 %collective-permute-start.24 = (f32[1,64,1024]{2,1,0:T(8,128)S(1)}, f32[1,64,1024]{2,1,0:T(8,128)S(1)}, u32[]{:S(2)}, u32[]{:S(2)}) collective-permute-start(f32[1,64,1024]{2,1,0:T(8,128)S(1)} %select_bitcast_fusion.2), channel_id=1, source_target_pairs={{0,2},{2,0},{4,6},{6,4},{1,3},{3,1},{5,7},{7,5},{8,10},{10,8},{12,... | collective-permute-start | bytes 786440 | tf_op jit(solution)/shard_map/ppermute | solution.py:136
  180.1 6.6 %collective-permute-start.21 = (f32[1,32,1024]{2,1,0:T(8,128)S(1)}, f32[1,32,1024]{2,1,0:T(8,128)S(1)}, u32[]{:S(2)}, u32[]{:S(2)}) collective-permute-start(f32[1,32,1024]{2,1,0:T(8,128)S(1)} %select_bitcast_fusion.5), channel_id=1, source_target_pairs={{0,4},{2,6},{4,0},{6,2},{1,5},{3,7},{5,1},{7,3},{8,12},{10,14},{12... | collective-permute-start | bytes 393224 | tf_op jit(solution)/shard_map/ppermute | solution.py:136
  181.7 8.7 %collective-permute-start.25 = (f32[2,16,1024]{2,1,0:T(8,128)S(1)}, f32[2,16,1024]{2,1,0:T(8,128)S(1)}, u32[]{:S(2)}, u32[]{:S(2)}) collective-permute-start(f32[2,16,1024]{2,1,0:T(8,128)S(1)} %select_bitcast_fusion.4), channel_id=1, source_target_pairs={{0,16},{8,24},{16,0},{24,8},{32,48},{40,56},{48,32},{56,40},{1,17}... | collective-permute-start | bytes 393224 | tf_op jit(solution)/shard_map/ppermute | solution.py:136
  186.7 6.7 %collective-permute-start.22 = (f32[1,16,1024]{2,1,0:T(8,128)S(1)}, f32[1,16,1024]{2,1,0:T(8,128)S(1)}, u32[]{:S(2)}, u32[]{:S(2)}) collective-permute-start(f32[1,16,1024]{2,1,0:T(8,128)S(1)} %select_bitcast_fusion.8), channel_id=1, source_target_pairs={{0,16},{8,24},{16,0},{24,8},{32,48},{40,56},{48,32},{56,40},{1,17}... | collective-permute-start | bytes 196616 | tf_op jit(solution)/shard_map/ppermute | solution.py:136
  190.5 5.9 %collective-permute-start.26 = (f32[1,16,1024]{2,1,0:T(8,128)S(1)}, f32[1,16,1024]{2,1,0:T(8,128)S(1)}, u32[]{:S(2)}, u32[]{:S(2)}) collective-permute-start(f32[1,16,1024]{2,1,0:T(8,128)S(1)} %select_bitcast_fusion.7), channel_id=1, source_target_pairs={{0,4},{2,6},{4,0},{6,2},{1,5},{3,7},{5,1},{7,3},{8,12},{10,14},{12... | collective-permute-start | bytes 196616 | tf_op jit(solution)/shard_map/ppermute | solution.py:136
  196.4 8.3 %collective-permute-start.27 = (f32[1,8,2048]{2,1,0:T(8,128)S(1)}, f32[1,8,2048]{2,1,0:T(8,128)S(1)}, u32[]{:S(2)}, u32[]{:S(2)}) collective-permute-start(f32[1,8,2048]{2,1,0:T(8,128)S(1)} %select_bitcast_fusion.6), channel_id=1, source_target_pairs={{0,32},{8,40},{16,48},{24,56},{32,0},{40,8},{48,16},{56,24},{1,33}... | collective-permute-start | bytes 196616 | tf_op jit(solution)/shard_map/ppermute | solution.py:136

commit v13 on v11

--- a/solution.py
+++ b/solution.py
@@ -177,11 +177,12 @@
     samples = pheno_full.shape[0]
     system = gram + 0.5 * samples * jnp.eye(width, dtype=jnp.float32)
     factor = jnp.linalg.cholesky(system)
+    inverse = chol_solve(factor, jnp.eye(width, dtype=jnp.float32))
     perm_part = lax.dynamic_slice_in_dim(perms, offset_rows, quarter, 1)
     pheno_part = gather_pheno(pheno_full, perm_part).T
     cross_part = jnp.dot(expo_part.T, pheno_part, precision=hi)
     cross = doubling_psum(cross_part, ("core", "x", "z", "vgrp"))
-    coefficients = chol_solve(factor, cross)
+    coefficients = jnp.dot(inverse, cross, precision=hi)
     permuted = doubling_gather(pheno_part, axis_bits(("vgrp",)))
     residuals = permuted - jnp.dot(exposures, coefficients, precision=hi)
     nperm = residuals.shape[1]

time: 206 us -> 226 us (1.097)
  local copies, waits for them, and re-layouts: 12.8 us -> 25.3 us
  waiting for transfers between devices: 73.1 us -> 81.4 us
  starting transfers between devices: 54.4 us -> 46.9 us
  other arithmetic: 39.3 us -> 46.4 us
    ppermute x9, waiting for transfers between devices: 28.3 us -> 37.9 us  [halve_bit(): kept = mine + lax.ppermute(send, axis, flip)]
    slice x5, local copies, waits for them, and re-layouts: 0.49 us -> 8.97 us  [front_chain(): other, other_gram = (packed[:count], packed[count:].reshape(gram.shape))]
    ppermute x8, waiting for transfers between devices: 8.98 us -> 17.3 us  [doubling_psum(): x = x + lax.ppermute(x, axis, pairs)]
    ppermute x9, starting transfers between devices: 17.2 us -> 9.9 us  [halve_bit(): kept = mine + lax.ppermute(send, axis, flip)]
    ppermute x8, waiting for transfers between devices: 27.2 us -> 20.4 us  [front_chain(): lax.ppermute(jnp.concatenate([pheno, gram.reshape(-1)]), axis, flip)]
    concatenate x4, local copies, waits for them, and re-layouts: 0.24 us -> 4.84 us  [front_chain(): pheno = jnp.concatenate([low, high], axis=0)]
    select_n x9, other arithmetic: 1.06 us -> 4.74 us  [front_chain(): low = jnp.where(bit == 0, pheno, other)]
    ppermute x8, starting transfers between devices: 14.9 us -> 11.2 us  [doubling_psum(): x = x + lax.ppermute(x, axis, pairs)]
  transfers between devices with their start and end apart: 28 -> 28, of which waited for: 22 -> 22; matrix products, arithmetic and copies ran while one was open for 20% -> 23% of each run, Pallas kernels for 0% -> 0%
where the time goes in v13:
time: 226 us; the launch traced here: 225 us
  waiting for transfers between devices  81.4 us (36%)
  starting transfers between devices  46.9 us (21%)
  other arithmetic  46.4 us (21%)
  local copies, waits for them, and re-layouts  25.3 us (11%)
  Pallas kernels  13.9 us (6%)
  matrix products  11 us (5%)
    ppermute x9, waiting for transfers between devices, halve_bit(): kept = mine + lax.ppermute(send, axis, flip)  37.9 us
    ppermute x8, starting transfers between devices, front_chain(): lax.ppermute(jnp.concatenate([pheno, gram.reshape(-1)]), axis, flip)  20.5 us
    ppermute x8, waiting for transfers between devices, front_chain(): lax.ppermute(jnp.concatenate([pheno, gram.reshape(-1)]), axis, flip)  20.4 us
    ppermute x8, waiting for transfers between devices, doubling_psum(): x = x + lax.ppermute(x, axis, pairs)  17.3 us
    pallas_call x1, Pallas kernels, gather_pheno(): pl.pallas_call(gather_body, grid=(count // TILE,), in_specs=[pl.BlockSpec...  13.9 us
    another operation x3, other arithmetic, per_device(): factor = jnp.linalg.cholesky(system)  13.2 us
    another operation x2, other arithmetic, chol_solve(): lax.linalg.triangular_solve(factor, middle, left_side=True, lower=True, t...  11.9 us
    ppermute x8, starting transfers between devices, doubling_psum(): x = x + lax.ppermute(x, axis, pairs)  11.2 us
  transfers between devices with their start and end apart: 28, of which 22 were waited for; matrix products, arithmetic and copies ran while one was open for 23% of the time, Pallas kernels for 0%

profile of v13, /device:TPU:2, one launch (start us, length us, event | category | flops | bytes accessed | tf_op | source)
XLA Modules:
  0.0 225.4 jit_solution(8105338921433264349)
XLA Ops:
  0.0 1.9 fusion.7
  4.6 2.3 %collective-permute-start.1 = (f32[17920]{0:T(1024)S(1)}, f32[17920]{0:T(1024)S(1)}, u32[]{:S(2)}, u32[]{:S(2)}) collective-permute-start(f32[17920]{0:T(1024)S(1)} %pad_maximum_fusion.13), channel_id=1, source_target_pairs={{0,2},{2,0},{4,6},{6,4},{1,3},{3,1},{5,7},{7,5},{8,10},{10,8},{12,... | collective-permute-start | bytes 215048 | tf_op jit(solution)/shard_map/ppermute | solution.py:89
  7.0 2.6 %collective-permute-done.1 = f32[17920]{0:T(1024)S(1)} collective-permute-done((f32[17920]{0:T(1024)S(1)}, f32[17920]{0:T(1024)S(1)}, u32[]{:S(2)}, u32[]{:S(2)}) %collective-permute-start.1) | collective-permute-done | bytes 71712 | tf_op jit(solution)/shard_map/ppermute | solution.py:89
  9.6 1.7 collective-permute-start.2
  11.3 4.3 %collective-permute-done.2 = f32[19456]{0:T(1024)S(1)} collective-permute-done((f32[19456]{0:T(1024)S(1)}, f32[19456]{0:T(1024)S(1)}, u32[]{:S(2)}, u32[]{:S(2)}) %collective-permute-start.2) | collective-permute-done | bytes 77856 | tf_op jit(solution)/shard_map/ppermute | solution.py:89
  17.2 3.1 %collective-permute-done.3 = f32[22528]{0:T(1024)S(1)} collective-permute-done((f32[22528]{0:T(1024)S(1)}, f32[22528]{0:T(1024)S(1)}, u32[]{:S(2)}, u32[]{:S(2)}) %collective-permute-start.3) | collective-permute-done | bytes 90144 | tf_op jit(solution)/shard_map/ppermute | solution.py:89
  20.3 3.2 %collective-permute-start.4 = (f32[28672]{0:T(1024)S(1)}, f32[28672]{0:T(1024)S(1)}, u32[]{:S(2)}, u32[]{:S(2)}) collective-permute-start(f32[28672]{0:T(1024)S(1)} %pad_maximum_fusion.8), channel_id=1, source_target_pairs={{0,16},{8,24},{16,0},{24,8},{32,48},{40,56},{48,32},{56,40},{1,17}... | collective-permute-start | bytes 344072 | tf_op jit(solution)/shard_map/ppermute | solution.py:89
  23.6 6.6 %copy.38 = s32[3072,512]{0,1:T(8,128)} copy(s32[3072,512]{1,0:T(8,128)} %param.7) | data formatting | bytes 12582912 | tf_op args[3]
  30.2 3.5 %convert_element_type.32 = bf16[3072,512]{0,1:T(8,128)(2,1)S(1)} convert(s32[3072,512]{0,1:T(8,128)} %copy.38) | non-fusion elementwise | flops 1572864 | bytes 9437184 | tf_op jit(solution)/shard_map/convert_element_type | solution.py:146
  33.7 1.8 copy.39
  35.6 5.2 %collective-permute-start.5 = (f32[40960]{0:T(1024)S(1)}, f32[40960]{0:T(1024)S(1)}, u32[]{:S(2)}, u32[]{:S(2)}) collective-permute-start(f32[40960]{0:T(1024)S(1)} %pad_maximum_fusion.7), channel_id=1, source_target_pairs={{0,32},{8,40},{16,48},{24,56},{32,0},{40,8},{48,16},{56,24},{1,33}... | collective-permute-start | bytes 491528 | tf_op jit(solution)/shard_map/ppermute | solution.py:89
  40.8 4.4 %collective-permute-done.5 = f32[40960]{0:T(1024)S(1)} collective-permute-done((f32[40960]{0:T(1024)S(1)}, f32[40960]{0:T(1024)S(1)}, u32[]{:S(2)}, u32[]{:S(2)}) %collective-permute-start.5) | collective-permute-done | bytes 163872 | tf_op jit(solution)/shard_map/ppermute | solution.py:89
  45.3 1.7 collective-permute-start.6
  47.0 4.8 %collective-permute-done.6 = f32[65536]{0:T(1024)S(1)} collective-permute-done((f32[65536]{0:T(1024)S(1)}, f32[65536]{0:T(1024)S(1)}, u32[]{:S(2)}, u32[]{:S(2)}) %collective-permute-start.6) | collective-permute-done | bytes 262176 | tf_op jit(solution)/shard_map/ppermute | solution.py:89
  53.4 4.8 %collective-permute-start.7 = (f32[114688]{0:T(1024)}, f32[114688]{0:T(1024)}, u32[]{:S(2)}, u32[]{:S(2)}) collective-permute-start(f32[114688]{0:T(1024)} %pad_maximum_fusion.2), channel_id=1, source_target_pairs={{0,128},{64,192},{128,0},{192,64},{1,129},{65,193},{129,1},{193,65... | collective-permute-start | bytes 1376264 | tf_op jit(solution)/shard_map/ppermute | solution.py:89
  62.6 1.6 copy.41
  64.2 1.7 slice.249
  65.9 1.8 copy.42
  67.6 1.9 fusion.15
  70.6 1.8 slice.292
  72.4 1.8 slice.253
  74.2 1.9 copy.44
  78.4 13.9 %shard_map.46 = f32[1,12288]{1,0:T(1,128)} custom-call(s32[1,12288]{1,0:T(1,128)} %bitcast.260, bf16[512,768]{1,0:T(8,128)(2,1)} %pad_maximum_fusion.1.tab_ref), custom_call_target="tpu_custom_call" | custom-call | tf_op jit(solution)/shard_map/pallas_call | solution.py:44
  92.8 2.2 reduce.9
  98.0 12.5 %cholesky.17 = f32[128,128]{1,0:T(8,128)S(1)} custom-call(f32[128,128]{1,0:T(8,128)} %fusion.39), custom_call_target="Cholesky" | custom-call | tf_op jit(solution)/shard_map/jit(cholesky)/cholesky | solution.py:179
  111.2 3.1 %collective-permute-done.11 = f32[128,16]{0,1:T(8,128)S(1)} collective-permute-done((f32[128,16]{0,1:T(8,128)S(1)}, f32[128,16]{0,1:T(8,128)S(1)}, u32[]{:S(2)}, u32[]{:S(2)}) %collective-permute-start.11) | collective-permute-done | bytes 8224 | tf_op jit(solution)/shard_map/ppermute | solution.py:64
  114.3 2.1 collective-permute-start.12
  117.1 2.4 %collective-permute-done.12 = f32[128,16]{0,1:T(8,128)S(1)} collective-permute-done((f32[128,16]{0,1:T(8,128)S(1)}, f32[128,16]{0,1:T(8,128)S(1)}, u32[]{:S(2)}, u32[]{:S(2)}) %collective-permute-start.12) | collective-permute-done | bytes 8224 | tf_op jit(solution)/shard_map/ppermute | solution.py:64
  119.5 2.7 %collective-permute-start.13 = (f32[128,16]{0,1:T(8,128)S(1)}, f32[128,16]{0,1:T(8,128)S(1)}, u32[]{:S(2)}, u32[]{:S(2)}) collective-permute-start(f32[128,16]{0,1:T(8,128)S(1)} %add.111), channel_id=1, source_target_pairs={{0,8},{8,0},{16,24},{24,16},{32,40},{40,32},{48,56},{56,48},{1,9},... | collective-permute-start | bytes 24584 | tf_op jit(solution)/shard_map/ppermute | solution.py:64
  123.4 10.6 %custom-call.8 = f32[1,128,128]{1,2,0:T(8,128)S(1)} custom-call(f32[1,128,128]{2,1,0:T(8,128)} %fusion.21), custom_call_target="InvertDiagBlocksLowerTriangular" | custom-call | tf_op jit(solution)/shard_map/triangular_solve | solution.py:13
  134.1 2.0 collective-permute-start.8
  136.8 3.8 %collective-permute-done.14 = f32[128,16]{0,1:T(8,128)S(1)} collective-permute-done((f32[128,16]{0,1:T(8,128)S(1)}, f32[128,16]{0,1:T(8,128)S(1)}, u32[]{:S(2)}, u32[]{:S(2)}) %collective-permute-start.14) | collective-permute-done | bytes 8224 | tf_op jit(solution)/shard_map/ppermute | solution.py:64
  140.6 4.3 %collective-permute-start.15 = (f32[128,16]{0,1:T(8,128)S(1)}, f32[128,16]{0,1:T(8,128)S(1)}, u32[]{:S(2)}, u32[]{:S(2)}) collective-permute-start(f32[128,16]{0,1:T(8,128)S(1)} %add.113), channel_id=1, source_target_pairs={{0,32},{8,40},{16,48},{24,56},{32,0},{40,8},{48,16},{56,24},{1,33}... | collective-permute-start | bytes 24584 | tf_op jit(solution)/shard_map/ppermute | solution.py:64
  145.1 3.0 %collective-permute-done.15 = f32[128,16]{0,1:T(8,128)S(1)} collective-permute-done((f32[128,16]{0,1:T(8,128)S(1)}, f32[128,16]{0,1:T(8,128)S(1)}, u32[]{:S(2)}, u32[]{:S(2)}) %collective-permute-start.15) | collective-permute-done | bytes 8224 | tf_op jit(solution)/shard_map/ppermute | solution.py:64
  148.3 3.6 %collective-permute-done.16 = f32[128,16]{0,1:T(8,128)S(1)} collective-permute-done((f32[128,16]{0,1:T(8,128)S(1)}, f32[128,16]{0,1:T(8,128)S(1)}, u32[]{:S(2)}, u32[]{:S(2)}) %collective-permute-start.16) | collective-permute-done | bytes 8224 | tf_op jit(solution)/shard_map/ppermute | solution.py:64
  152.5 3.2 %collective-permute-start.9 = (f32[1536,16]{0,1:T(8,128)S(1)}, f32[1536,16]{0,1:T(8,128)S(1)}, u32[]{:S(2)}, u32[]{:S(2)}) collective-permute-start(f32[1536,16]{0,1:T(8,128)S(1)} %pad_maximum_fusion.10), channel_id=1, source_target_pairs={{0,128},{64,192},{128,0},{192,64},{1,129},{65,193},{129,1},{193,65... | collective-permute-start | bytes 294920 | tf_op jit(solution)/shard_map/ppermute | solution.py:74
  157.2 1.7 collective-permute-done.9
  160.4 3.4 %multiply_convert_fusion = bf16[3072,128,16]{0,2,1:T(8,128)(2,1)S(1)} fusion(f32[3072,16]{0,1:T(8,128)S(1)} %maximum_subtract_fusion, f32[3072,128]{0,1:T(8,128)S(1)} %copy.37), kind=kLoop, calls=%fused_computation | loop fusion | flops 12582912 | bytes 14352384 | tf_op jit(solution)/shard_map/convert_element_type | solution.py:192
  163.8 6.7 %fusion.50 = f32[2048,512]{0,1:T(8,128)S(1)} fusion(bf16[3072,2048]{0,1:T(8,128)(2,1)S(1)} %bitcast.242, bf16[3072,512]{0,1:T(8,128)(2,1)S(1)} %bitcast.253), kind=kOutput, calls=%fused_computation.129 | convolution fusion | flops 6442450944 | bytes 19922944 | tf_op jit(solution)/shard_map/dot_general | solution.py:150
  171.0 4.1 %collective-permute-done.18 = f32[2048,256]{0,1:T(8,128)S(1)} collective-permute-done((f32[2048,256]{0,1:T(8,128)S(1)}, f32[2048,256]{0,1:T(8,128)S(1)}, u32[]{:S(2)}, u32[]{:S(2)}) %collective-permute-start.18) | collective-permute-done | bytes 2097184 | tf_op jit(solution)/shard_map/ppermute | solution.py:122
  176.8 13.3 %collective-permute-done.19 = f32[1,128,1024]{2,1,0:T(8,128)S(1)} collective-permute-done((f32[1,128,1024]{2,1,0:T(8,128)S(1)}, f32[1,128,1024]{2,1,0:T(8,128)S(1)}, u32[]{:S(2)}, u32[]{:S(2)}) %collective-permute-start.19) | collective-permute-done | bytes 524320 | tf_op jit(solution)/shard_map/ppermute | solution.py:136
  192.2 5.6 %collective-permute-done.20 = f32[2,32,1024]{2,1,0:T(8,128)S(1)} collective-permute-done((f32[2,32,1024]{2,1,0:T(8,128)S(1)}, f32[2,32,1024]{2,1,0:T(8,128)S(1)}, u32[]{:S(2)}, u32[]{:S(2)}) %collective-permute-start.20) | collective-permute-done | bytes 262176 | tf_op jit(solution)/shard_map/ppermute | solution.py:136
  197.8 2.2 collective-permute-start.21
  200.7 3.7 %collective-permute-done.21 = f32[1,32,1024]{2,1,0:T(8,128)S(1)} collective-permute-done((f32[1,32,1024]{2,1,0:T(8,128)S(1)}, f32[1,32,1024]{2,1,0:T(8,128)S(1)}, u32[]{:S(2)}, u32[]{:S(2)}) %collective-permute-start.21) | collective-permute-done | bytes 131104 | tf_op jit(solution)/shard_map/ppermute | solution.py:136
  205.0 4.6 %collective-permute-done.25 = f32[2,16,1024]{2,1,0:T(8,128)S(1)} collective-permute-done((f32[2,16,1024]{2,1,0:T(8,128)S(1)}, f32[2,16,1024]{2,1,0:T(8,128)S(1)}, u32[]{:S(2)}, u32[]{:S(2)}) %collective-permute-start.25) | collective-permute-done | bytes 131104 | tf_op jit(solution)/shard_map/ppermute | solution.py:136
  210.3 5.2 %collective-permute-done.26 = f32[1,16,1024]{2,1,0:T(8,128)S(1)} collective-permute-done((f32[1,16,1024]{2,1,0:T(8,128)S(1)}, f32[1,16,1024]{2,1,0:T(8,128)S(1)}, u32[]{:S(2)}, u32[]{:S(2)}) %collective-permute-start.26) | collective-permute-done | bytes 65568 | tf_op jit(solution)/shard_map/ppermute | solution.py:136
  215.5 3.6 %collective-permute-start.27 = (f32[1,8,2048]{2,1,0:T(8,128)S(1)}, f32[1,8,2048]{2,1,0:T(8,128)S(1)}, u32[]{:S(2)}, u32[]{:S(2)}) collective-permute-start(f32[1,8,2048]{2,1,0:T(8,128)S(1)} %select_bitcast_fusion.6), channel_id=1, source_target_pairs={{0,32},{8,40},{16,48},{24,56},{32,0},{40,8},{48,16},{56,24},{1,33}... | collective-permute-start | bytes 196616 | tf_op jit(solution)/shard_map/ppermute | solution.py:136
  219.1 5.3 %collective-permute-done.27 = f32[1,8,2048]{2,1,0:T(8,128)S(1)} collective-permute-done((f32[1,8,2048]{2,1,0:T(8,128)S(1)}, f32[1,8,2048]{2,1,0:T(8,128)S(1)}, u32[]{:S(2)}, u32[]{:S(2)}) %collective-permute-start.27) | collective-permute-done | bytes 65568 | tf_op jit(solution)/shard_map/ppermute | solution.py:136
  (116 shorter events, 31.4 us)
Async XLA Ops:
  0.0 58.7 %copy-start = (s32[16,3072]{1,0:T(8,128)S(1)}, s32[16,3072]{1,0:T(8,128)}, u32[]{:S(2)}) copy-start(s32[16,3072]{1,0:T(8,128)} %param.6) | copy-start | bytes 589828
  2.7 1.3 collective-permute-start
  4.6 4.9 %collective-permute-start.1 = (f32[17920]{0:T(1024)S(1)}, f32[17920]{0:T(1024)S(1)}, u32[]{:S(2)}, u32[]{:S(2)}) collective-permute-start(f32[17920]{0:T(1024)S(1)} %pad_maximum_fusion.13), channel_id=1, source_target_pairs={{0,2},{2,0},{4,6},{6,4},{1,3},{3,1},{5,7},{7,5},{8,10},{10,8},{12,... | collective-permute-start | bytes 215048 | tf_op jit(solution)/shard_map/ppermute | solution.py:89
  9.6 6.0 %collective-permute-start.2 = (f32[19456]{0:T(1024)S(1)}, f32[19456]{0:T(1024)S(1)}, u32[]{:S(2)}, u32[]{:S(2)}) collective-permute-start(f32[19456]{0:T(1024)S(1)} %pad_maximum_fusion.12), channel_id=1, source_target_pairs={{0,4},{2,6},{4,0},{6,2},{1,5},{3,7},{5,1},{7,3},{8,12},{10,14},{12... | collective-permute-start | bytes 233480 | tf_op jit(solution)/shard_map/ppermute | solution.py:89
  15.7 4.6 %collective-permute-start.3 = (f32[22528]{0:T(1024)S(1)}, f32[22528]{0:T(1024)S(1)}, u32[]{:S(2)}, u32[]{:S(2)}) collective-permute-start(f32[22528]{0:T(1024)S(1)} %pad_maximum_fusion.11), channel_id=1, source_target_pairs={{0,8},{8,0},{16,24},{24,16},{32,40},{40,32},{48,56},{56,48},{1,9},... | collective-permute-start | bytes 270344 | tf_op jit(solution)/shard_map/ppermute | solution.py:89
  20.3 15.2 %collective-permute-start.4 = (f32[28672]{0:T(1024)S(1)}, f32[28672]{0:T(1024)S(1)}, u32[]{:S(2)}, u32[]{:S(2)}) collective-permute-start(f32[28672]{0:T(1024)S(1)} %pad_maximum_fusion.8), channel_id=1, source_target_pairs={{0,16},{8,24},{16,0},{24,8},{32,48},{40,56},{48,32},{56,40},{1,17}... | collective-permute-start | bytes 344072 | tf_op jit(solution)/shard_map/ppermute | solution.py:89
  35.5 22.6 %copy-start.1 = (f32[3072,128]{1,0:T(8,128)S(1)}, f32[3072,128]{1,0:T(8,128)}, u32[]{:S(2)}) copy-start(f32[3072,128]{1,0:T(8,128)} %param.5) | copy-start | bytes 4718596
  35.6 9.6 %collective-permute-start.5 = (f32[40960]{0:T(1024)S(1)}, f32[40960]{0:T(1024)S(1)}, u32[]{:S(2)}, u32[]{:S(2)}) collective-permute-start(f32[40960]{0:T(1024)S(1)} %pad_maximum_fusion.7), channel_id=1, source_target_pairs={{0,32},{8,40},{16,48},{24,56},{32,0},{40,8},{48,16},{56,24},{1,33}... | collective-permute-start | bytes 491528 | tf_op jit(solution)/shard_map/ppermute | solution.py:89
  45.2 12.9 %copy-start.4 = (f32[40960]{0:T(1024)}, f32[40960]{0:T(1024)S(1)}, u32[]{:S(2)}) copy-start(f32[40960]{0:T(1024)S(1)} %collective-permute-done.5) | copy-start | bytes 491524
  45.3 12.9 %copy-start.3 = (f32[24576]{0:T(1024)}, f32[24576]{0:T(1024)S(1)}, u32[]{:S(2)}) copy-start(f32[24576]{0:T(1024)S(1)} %get-tuple-element.22) | copy-start | bytes 294916
  45.3 6.5 %collective-permute-start.6 = (f32[65536]{0:T(1024)S(1)}, f32[65536]{0:T(1024)S(1)}, u32[]{:S(2)}, u32[]{:S(2)}) collective-permute-start(f32[65536]{0:T(1024)S(1)} %pad_maximum_fusion.5), channel_id=1, source_target_pairs={{0,64},{64,0},{128,192},{192,128},{1,65},{65,1},{129,193},{193,129... | collective-permute-start | bytes 786440 | tf_op jit(solution)/shard_map/ppermute | solution.py:89
  51.8 6.4 %copy-start.5 = (f32[65536]{0:T(1024)}, f32[65536]{0:T(1024)S(1)}, u32[]{:S(2)}) copy-start(f32[65536]{0:T(1024)S(1)} %collective-permute-done.6) | copy-start | bytes 786436
  53.4 16.1 %collective-permute-start.7 = (f32[114688]{0:T(1024)}, f32[114688]{0:T(1024)}, u32[]{:S(2)}, u32[]{:S(2)}) collective-permute-start(f32[114688]{0:T(1024)} %pad_maximum_fusion.2), channel_id=1, source_target_pairs={{0,128},{64,192},{128,0},{192,64},{1,129},{65,193},{129,1},{193,65... | collective-permute-start | bytes 1376264 | tf_op jit(solution)/shard_map/ppermute | solution.py:89
  96.2 14.4 %collective-permute-start.10 = (f32[128,16]{0,1:T(8,128)S(1)}, f32[128,16]{0,1:T(8,128)S(1)}, u32[]{:S(2)}, u32[]{:S(2)}) collective-permute-start(f32[128,16]{0,1:T(8,128)S(1)} %fusion.5), channel_id=1, source_target_pairs={{0,1},{1,0},{2,3},{3,2},{4,5},{5,4},{6,7},{7,6},{8,9},{9,8},{10,11... | collective-permute-start | bytes 24584 | tf_op jit(solution)/shard_map/ppermute | solution.py:64
  110.6 3.7 %collective-permute-start.11 = (f32[128,16]{0,1:T(8,128)S(1)}, f32[128,16]{0,1:T(8,128)S(1)}, u32[]{:S(2)}, u32[]{:S(2)}) collective-permute-start(f32[128,16]{0,1:T(8,128)S(1)} %add.109), channel_id=1, source_target_pairs={{0,2},{2,0},{4,6},{6,4},{1,3},{3,1},{5,7},{7,5},{8,10},{10,8},{12,... | collective-permute-start | bytes 24584 | tf_op jit(solution)/shard_map/ppermute | solution.py:64
  114.3 5.2 %collective-permute-start.12 = (f32[128,16]{0,1:T(8,128)S(1)}, f32[128,16]{0,1:T(8,128)S(1)}, u32[]{:S(2)}, u32[]{:S(2)}) collective-permute-start(f32[128,16]{0,1:T(8,128)S(1)} %add.110), channel_id=1, source_target_pairs={{0,4},{2,6},{4,0},{6,2},{1,5},{3,7},{5,1},{7,3},{8,12},{10,14},{12... | collective-permute-start | bytes 24584 | tf_op jit(solution)/shard_map/ppermute | solution.py:64
  119.5 16.6 %collective-permute-start.13 = (f32[128,16]{0,1:T(8,128)S(1)}, f32[128,16]{0,1:T(8,128)S(1)}, u32[]{:S(2)}, u32[]{:S(2)}) collective-permute-start(f32[128,16]{0,1:T(8,128)S(1)} %add.111), channel_id=1, source_target_pairs={{0,8},{8,0},{16,24},{24,16},{32,40},{40,32},{48,56},{56,48},{1,9},... | collective-permute-start | bytes 24584 | tf_op jit(solution)/shard_map/ppermute | solution.py:64
  134.1 14.2 %collective-permute-start.8 = (f32[768,16]{0,1:T(8,128)S(1)}, f32[768,16]{0,1:T(8,128)S(1)}, u32[]{:S(2)}, u32[]{:S(2)}) collective-permute-start(f32[768,16]{0,1:T(8,128)S(1)} %bitcast.259), channel_id=1, source_target_pairs={{0,64},{64,0},{128,192},{192,128},{1,65},{65,1},{129,193},{193,129... | collective-permute-start | bytes 147464 | tf_op jit(solution)/shard_map/ppermute | solution.py:74
  136.1 4.6 %collective-permute-start.14 = (f32[128,16]{0,1:T(8,128)S(1)}, f32[128,16]{0,1:T(8,128)S(1)}, u32[]{:S(2)}, u32[]{:S(2)}) collective-permute-start(f32[128,16]{0,1:T(8,128)S(1)} %add.112), channel_id=1, source_target_pairs={{0,16},{8,24},{16,0},{24,8},{32,48},{40,56},{48,32},{56,40},{1,17}... | collective-permute-start | bytes 24584 | tf_op jit(solution)/shard_map/ppermute | solution.py:64
  140.6 7.6 %collective-permute-start.15 = (f32[128,16]{0,1:T(8,128)S(1)}, f32[128,16]{0,1:T(8,128)S(1)}, u32[]{:S(2)}, u32[]{:S(2)}) collective-permute-start(f32[128,16]{0,1:T(8,128)S(1)} %add.113), channel_id=1, source_target_pairs={{0,32},{8,40},{16,48},{24,56},{32,0},{40,8},{48,16},{56,24},{1,33}... | collective-permute-start | bytes 24584 | tf_op jit(solution)/shard_map/ppermute | solution.py:64
  148.2 3.7 %collective-permute-start.16 = (f32[128,16]{0,1:T(8,128)S(1)}, f32[128,16]{0,1:T(8,128)S(1)}, u32[]{:S(2)}, u32[]{:S(2)}) collective-permute-start(f32[128,16]{0,1:T(8,128)S(1)} %add.114), channel_id=1, source_target_pairs={{0,64},{64,0},{128,192},{192,128},{1,65},{65,1},{129,193},{193,129... | collective-permute-start | bytes 24584 | tf_op jit(solution)/shard_map/ppermute | solution.py:64
  151.9 5.2 %collective-permute-start.17 = (f32[128,16]{0,1:T(8,128)S(1)}, f32[128,16]{0,1:T(8,128)S(1)}, u32[]{:S(2)}, u32[]{:S(2)}) collective-permute-start(f32[128,16]{0,1:T(8,128)S(1)} %add.115), channel_id=1, source_target_pairs={{0,128},{64,192},{128,0},{192,64},{1,129},{65,193},{129,1},{193,65... | collective-permute-start | bytes 24584 | tf_op jit(solution)/shard_map/ppermute | solution.py:64
  152.5 6.4 %collective-permute-start.9 = (f32[1536,16]{0,1:T(8,128)S(1)}, f32[1536,16]{0,1:T(8,128)S(1)}, u32[]{:S(2)}, u32[]{:S(2)}) collective-permute-start(f32[1536,16]{0,1:T(8,128)S(1)} %pad_maximum_fusion.10), channel_id=1, source_target_pairs={{0,128},{64,192},{128,0},{192,64},{1,129},{65,193},{129,1},{193,65... | collective-permute-start | bytes 294920 | tf_op jit(solution)/shard_map/ppermute | solution.py:74
  160.4 3.5 %copy-start.2 = (bf16[3072,2,2,2,2,2,2,8]{0,7,6,5,4,3,2,1:T(8,128)(2,1)S(1)}, bf16[3072,2,2,2,2,2,2,8]{0,7,6,5,4,3,2,1:T(8,128)(2,1)}, u32[]{:S(2)}) copy-start(bf16[3072,2,2,2,2,2,2,8]{0,7,6,5,4,3,2,1:T(8,128)(2,1)} %copy.39) | copy-start | bytes 9437188
  170.9 4.2 %collective-permute-start.18 = (f32[2048,256]{0,1:T(8,128)S(1)}, f32[2048,256]{0,1:T(8,128)S(1)}, u32[]{:S(2)}, u32[]{:S(2)}) collective-permute-start(f32[2048,256]{0,1:T(8,128)S(1)} %slice_select_fusion), channel_id=1, source_target_pairs={{0,1},{1,0},{2,3},{3,2},{4,5},{5,4},{6,7},{7,6},{8,9},{9,8},{10,11... | collective-permute-start | bytes 6291464 | tf_op jit(solution)/shard_map/ppermute | solution.py:122
  176.0 14.1 %collective-permute-start.19 = (f32[1,128,1024]{2,1,0:T(8,128)S(1)}, f32[1,128,1024]{2,1,0:T(8,128)S(1)}, u32[]{:S(2)}, u32[]{:S(2)}) collective-permute-start(f32[1,128,1024]{2,1,0:T(8,128)S(1)} %select_bitcast_fusion.1), channel_id=1, source_target_pairs={{0,2},{2,0},{4,6},{6,4},{1,3},{3,1},{5,7},{7,5},{8,10},{10,8},{12,... | collective-permute-start | bytes 1572872 | tf_op jit(solution)/shard_map/ppermute | solution.py:136
  176.7 13.8 %collective-permute-start.23 = (f32[4,32,1024]{2,1,0:T(8,128)S(1)}, f32[4,32,1024]{2,1,0:T(8,128)S(1)}, u32[]{:S(2)}, u32[]{:S(2)}) collective-permute-start(f32[4,32,1024]{2,1,0:T(8,128)S(1)} %select_bitcast_fusion), channel_id=1, source_target_pairs={{0,8},{8,0},{16,24},{24,16},{32,40},{40,32},{48,56},{56,48},{1,9},... | collective-permute-start | bytes 1572872 | tf_op jit(solution)/shard_map/ppermute | solution.py:136
  190.2 7.6 %collective-permute-start.20 = (f32[2,32,1024]{2,1,0:T(8,128)S(1)}, f32[2,32,1024]{2,1,0:T(8,128)S(1)}, u32[]{:S(2)}, u32[]{:S(2)}) collective-permute-start(f32[2,32,1024]{2,1,0:T(8,128)S(1)} %select_bitcast_fusion.3), channel_id=1, source_target_pairs={{0,8},{8,0},{16,24},{24,16},{32,40},{40,32},{48,56},{56,48},{1,9},... | collective-permute-start | bytes 786440 | tf_op jit(solution)/shard_map/ppermute | solution.py:136
  190.6 9.5 %collective-permute-start.24 = (f32[1,64,1024]{2,1,0:T(8,128)S(1)}, f32[1,64,1024]{2,1,0:T(8,128)S(1)}, u32[]{:S(2)}, u32[]{:S(2)}) collective-permute-start(f32[1,64,1024]{2,1,0:T(8,128)S(1)} %select_bitcast_fusion.2), channel_id=1, source_target_pairs={{0,2},{2,0},{4,6},{6,4},{1,3},{3,1},{5,7},{7,5},{8,10},{10,8},{12,... | collective-permute-start | bytes 786440 | tf_op jit(solution)/shard_map/ppermute | solution.py:136
  197.8 6.6 %collective-permute-start.21 = (f32[1,32,1024]{2,1,0:T(8,128)S(1)}, f32[1,32,1024]{2,1,0:T(8,128)S(1)}, u32[]{:S(2)}, u32[]{:S(2)}) collective-permute-start(f32[1,32,1024]{2,1,0:T(8,128)S(1)} %select_bitcast_fusion.5), channel_id=1, source_target_pairs={{0,4},{2,6},{4,0},{6,2},{1,5},{3,7},{5,1},{7,3},{8,12},{10,14},{12... | collective-permute-start | bytes 393224 | tf_op jit(solution)/shard_map/ppermute | solution.py:136
  200.1 9.4 %collective-permute-start.25 = (f32[2,16,1024]{2,1,0:T(8,128)S(1)}, f32[2,16,1024]{2,1,0:T(8,128)S(1)}, u32[]{:S(2)}, u32[]{:S(2)}) collective-permute-start(f32[2,16,1024]{2,1,0:T(8,128)S(1)} %select_bitcast_fusion.4), channel_id=1, source_target_pairs={{0,16},{8,24},{16,0},{24,8},{32,48},{40,56},{48,32},{56,40},{1,17}... | collective-permute-start | bytes 393224 | tf_op jit(solution)/shard_map/ppermute | solution.py:136
  204.4 5.8 %collective-permute-start.22 = (f32[1,16,1024]{2,1,0:T(8,128)S(1)}, f32[1,16,1024]{2,1,0:T(8,128)S(1)}, u32[]{:S(2)}, u32[]{:S(2)}) collective-permute-start(f32[1,16,1024]{2,1,0:T(8,128)S(1)} %select_bitcast_fusion.8), channel_id=1, source_target_pairs={{0,16},{8,24},{16,0},{24,8},{32,48},{40,56},{48,32},{56,40},{1,17}... | collective-permute-start | bytes 196616 | tf_op jit(solution)/shard_map/ppermute | solution.py:136
  209.6 5.9 %collective-permute-start.26 = (f32[1,16,1024]{2,1,0:T(8,128)S(1)}, f32[1,16,1024]{2,1,0:T(8,128)S(1)}, u32[]{:S(2)}, u32[]{:S(2)}) collective-permute-start(f32[1,16,1024]{2,1,0:T(8,128)S(1)} %select_bitcast_fusion.7), channel_id=1, source_target_pairs={{0,4},{2,6},{4,0},{6,2},{1,5},{3,7},{5,1},{7,3},{8,12},{10,14},{12... | collective-permute-start | bytes 196616 | tf_op jit(solution)/shard_map/ppermute | solution.py:136
  215.5 9.0 %collective-permute-start.27 = (f32[1,8,2048]{2,1,0:T(8,128)S(1)}, f32[1,8,2048]{2,1,0:T(8,128)S(1)}, u32[]{:S(2)}, u32[]{:S(2)}) collective-permute-start(f32[1,8,2048]{2,1,0:T(8,128)S(1)} %select_bitcast_fusion.6), channel_id=1, source_target_pairs={{0,32},{8,40},{16,48},{24,56},{32,0},{40,8},{48,16},{56,24},{1,33}... | collective-permute-start | bytes 196616 | tf_op jit(solution)/shard_map/ppermute | solution.py:136
